TPU v7x, 32 devices: a whole 2x2x4 slice. The times are simulated.
32 devices in a mesh: gx: 4 (over z), gy: 8 (over y, x, core).
Axes of the slice: x: 2, y: 2, z: 4, core: 2. Of those that a mesh axis runs over, the one named last changes fastest.
Arguments:
- forcing: float32 [2, 16, 64, 1024], P(None, None, 'gx', 'gy'), may hold values from -6 to 6
- viscosity: float32 [16, 64, 1024], P(None, 'gx', 'gy'), may hold values from 0.05 to 0.5
- observed: float32 [2, 64, 1024], P(None, 'gx', 'gy'), may hold values from -6 to 6
- beta_tiles: float32 [4, 128], P('gx', 'gy'), may hold values from 1 to 30
- ice_mask: int32 [64, 1024], P('gx', 'gy'), may hold values 0 or 1
- tile_owner: int32 [64, 1024], P('gx', 'gy'), may hold values from 0 to 127
Outputs:
- velocity: float32 [2, 16, 64, 1024], P(None, None, 'gx', 'gy')
- adjoint: float32 [2, 16, 64, 1024], P(None, None, 'gx', 'gy')
- grad_tiles: float32 [4, 128], P('gx', 'gy')
All inputs are finite; a program needn't handle non-finite values. No bound on the sum of `ice_mask` on one device may be relied on, other than what follows from the above.
Results may differ from a plain program's by a relative error of at most 0.000025.
Values sent between devices are 32-bit elements; how exact they have to be, the bound alone decides.
No kernel may reach another device: no remote copies, remote signals or barrier semaphores. Data moves between devices by JAX's collectives and lax.ppermute only.
A program may use at most 64 MiB of HBM per device.

v0:
```python
import jax
import jax.numpy as jnp
from jax import lax
from jax.sharding import PartitionSpec as P

PASSES = 4


OMEGA = 0.8
VERTICAL = 16.0


def with_halo(cells, sides, width):
    for axis, dim in sides:
        count = lax.axis_size(axis)
        ends = count - 1
        head = lax.slice_in_dim(cells, 0, width, axis=dim)
        tail = lax.slice_in_dim(cells, cells.shape[dim] - width, cells.shape[dim], axis=dim)
        cells = jnp.concatenate(
            [
                lax.ppermute(tail, axis, [(i, (i + 1) % count) for i in range(ends)]),
                cells,
                lax.ppermute(head, axis, [((i + 1) % count, i) for i in range(ends)]),
            ],
            axis=dim,
        )
    return cells


def lateral_terms(visc_pad):
    centre_visc = visc_pad[:, 1:-1, 1:-1]
    west_face = 0.5 * (centre_visc + visc_pad[:, :-2, 1:-1])
    east_face = 0.5 * (centre_visc + visc_pad[:, 2:, 1:-1])
    south_face = 0.5 * (centre_visc + visc_pad[:, 1:-1, :-2])
    north_face = 0.5 * (centre_visc + visc_pad[:, 1:-1, 2:])
    return (west_face, east_face, south_face, north_face)


def weights_xy():
    along_x = jnp.array([4.0, 1.0], jnp.float32).reshape(2, 1, 1, 1)
    along_y = jnp.array([1.0, 4.0], jnp.float32).reshape(2, 1, 1, 1)
    return (along_x, along_y)


def prepare(visc_pad, beta_col, ice_cover):
    faces = lateral_terms(visc_pad)
    west_face, east_face, south_face, north_face = faces
    along_x, along_y = weights_xy()
    centre_visc = visc_pad[:, 1:-1, 1:-1]
    vertical = VERTICAL * 0.5 * (centre_visc[:-1] + centre_visc[1:])
    zero_row = jnp.zeros_like(centre_visc[:1])
    upper_link = jnp.concatenate([vertical, zero_row], 0)
    lower_link = jnp.concatenate([zero_row, vertical], 0)
    basal = jnp.concatenate([jnp.zeros_like(centre_visc[:-1]), beta_col[None]], 0)
    diagonal = along_x * (west_face + east_face) + along_y * (south_face + north_face)
    diagonal = diagonal + upper_link + lower_link + basal + (1.0 - ice_cover)
    layer_count = visc_pad.shape[0]
    ratio_list = []
    inverse_list = []
    for layer_idx in range(layer_count):
        pivot = diagonal[:, layer_idx]
        if layer_idx > 0:
            pivot = pivot + lower_link[layer_idx] * ratio_list[-1]
        inverse = 1.0 / pivot
        inverse_list.append(inverse)
        ratio_list.append(-upper_link[layer_idx] * inverse)
    return (faces, lower_link, jnp.stack(ratio_list, 1), jnp.stack(inverse_list, 1))


def relax(vel_pad, rhs_field, faces, lower_link, ratios, inverses, ice_cover):
    west_face, east_face, south_face, north_face = faces
    along_x, along_y = weights_xy()
    lateral = along_x * (west_face * vel_pad[:, :, :-2, 1:-1] + east_face * vel_pad[:, :, 2:, 1:-1])
    lateral = lateral + along_y * (
        south_face * vel_pad[:, :, 1:-1, :-2] + north_face * vel_pad[:, :, 1:-1, 2:]
    )
    right_side = rhs_field + lateral
    layer_count = right_side.shape[1]
    forward_list = []
    for layer_idx in range(layer_count):
        value = right_side[:, layer_idx]
        if layer_idx > 0:
            value = value + lower_link[layer_idx] * forward_list[-1]
        forward_list.append(value * inverses[:, layer_idx])
    solved = [None] * layer_count
    solved[layer_count - 1] = forward_list[layer_count - 1]
    for layer_idx in range(layer_count - 2, -1, -1):
        solved[layer_idx] = forward_list[layer_idx] - ratios[:, layer_idx] * solved[layer_idx + 1]
    line_value = jnp.stack(solved, 1)
    centre = vel_pad[:, :, 1:-1, 1:-1]
    return ice_cover * ((1.0 - OMEGA) * centre + OMEGA * line_value)


def pad_cells(field):
    return jnp.pad(field, [(0, 0)] * (field.ndim - 2) + [(1, 1), (1, 1)])


def local(forcing, viscosity, observed, beta_tiles, ice_mask, tile_owner):
    ice_cover = ice_mask.astype(jnp.float32)
    friction_row = lax.all_gather(beta_tiles, "gy", axis=1, tiled=True)
    beta_col = jnp.take(friction_row[0], tile_owner, axis=0)
    visc_rim = with_halo(viscosity, (("gx", 1), ("gy", 2)), 1)
    faces, lower_link, ratios, inverses = prepare(visc_rim, beta_col, ice_cover)

    def advance(field, rhs_field, first):
        if first:
            field_rim = pad_cells(field)
        else:
            field_rim = with_halo(field, (("gx", 2), ("gy", 3)), 1)
        return relax(field_rim, rhs_field, faces, lower_link, ratios, inverses, ice_cover)

    velocity = jnp.zeros_like(forcing)
    for sweep_idx in range(PASSES):
        velocity = advance(velocity, forcing, sweep_idx == 0)
    misfit = velocity[:, 0] - observed
    adjoint_rhs = jnp.zeros_like(forcing).at[:, 0].set(misfit)
    adjoint = jnp.zeros_like(forcing)
    for sweep_idx in range(PASSES):
        adjoint = advance(adjoint, adjoint_rhs, sweep_idx == 0)
    grad_col = -ice_cover * beta_col * jnp.sum(adjoint[:, -1] * velocity[:, -1], axis=0)
    tile_count = friction_row.shape[1]
    partial_sum = jax.ops.segment_sum(
        grad_col.reshape(-1), tile_owner.reshape(-1), num_segments=tile_count
    )[None]
    grad_tiles = lax.psum_scatter(partial_sum, "gy", scatter_dimension=1, tiled=True)
    return (velocity, adjoint, grad_tiles)


def solution(mesh):
    in_specs = (
        P(None, None, "gx", "gy"),
        P(None, "gx", "gy"),
        P(None, "gx", "gy"),
        P("gx", "gy"),
        P("gx", "gy"),
        P("gx", "gy"),
    )
    out_specs = (P(None, None, "gx", "gy"), P(None, None, "gx", "gy"), P("gx", "gy"))
    return jax.shard_map(local, mesh=mesh, in_specs=in_specs, out_specs=out_specs, check_vma=False)
```

profile of v0, /device:TPU:0, one launch (start us, length us, event | category | flops | bytes accessed | tf_op | source)
XLA Modules:
  0.0 241.7 jit_solution(5458424872420051510)
XLA Ops:
  7.2 0.9 fusion.302
  8.1 4.9 %collective-permute-start = (f32[16,1,128]{2,1,0:T(1,128)S(1)}, f32[16,1,128]{2,1,0:T(1,128)S(1)}, u32[]{:S(2)}, u32[]{:S(2)}) collective-permute-start(f32[16,1,128]{2,1,0:T(1,128)S(1)} %get-tuple-element.252), channel_id=1, source_target_pairs={{0,8},{8,16},{16,24},{1,9},{9,17},{17,25},{2,10},{10,18},{18,26},{... | collective-permute-start | bytes 24584 | tf_op jit(solution)/shard_map/ppermute | solution.py:21
  13.0 1.3 collective-permute-start.1
  14.3 1.0 add_multiply_fusion.6
  15.4 0.6 copy-done.10
  16.0 0.6 dynamic-slice.11
  17.3 0.6 copy-done.9
  18.0 13.4 %all-reduce.4 = f32[128]{0:T(128)S(1)} all-reduce(f32[128]{0:T(128)S(1)} %bitcast_dynamic-update-slice_fusion), channel_id=1, replica_groups=mesh['gx'=4,'gy'=8] {'gy'}, use_global_device_ids=true, to_apply=%add.4 | all-reduce | flops 128 | bytes 1024 | tf_op jit(solution)/shard_map/squeeze | solution.py:101
  31.4 12.6 %gather_fusion = f32[2048]{0:T(1024)S(1)} fusion(f32[128]{0:T(128)S(1)} %all-reduce.4, s32[2048]{0:T(1024)S(1)} %bitcast_clamp_fusion), kind=kCustom, calls=%fused_computation | custom fusion | bytes 24576 | tf_op jit(solution)/shard_map/jit(_take)/gather | solution.py:101
  44.0 0.7 copy-done.4
  44.8 0.9 copy-done.1
  45.8 1.3 collective-permute-start.2
  47.1 1.3 collective-permute-start.3
  48.5 1.9 collective-permute-done.3
  50.4 0.2 fusion.283
  50.7 0.6 copy-done.6
  51.3 0.2 fusion.282
  52.0 4.3 %collective-permute-start.4 = (f32[2,16,1,128]{3,2,1,0:T(1,128)S(1)}, f32[2,16,1,128]{3,2,1,0:T(1,128)S(1)}, u32[]{:S(2)}, u32[]{:S(2)}) collective-permute-start(f32[2,16,1,128]{3,2,1,0:T(1,128)S(1)} %get-tuple-element.245), channel_id=1, source_target_pairs={{0,8},{8,16},{16,24},{1,9},{9,17},{17,25},{2,10},{10,18},{18,26},{... | collective-permute-start | bytes 49160 | tf_op jit(solution)/shard_map/ppermute | solution.py:21
  56.3 1.3 collective-permute-start.5
  57.7 4.2 %collective-permute-done.5 = f32[2,16,1,128]{3,2,1,0:T(1,128)S(1)} collective-permute-done((f32[2,16,1,128]{3,2,1,0:T(1,128)S(1)}, f32[2,16,1,128]{3,2,1,0:T(1,128)S(1)}, u32[]{:S(2)}, u32[]{:S(2)}) %collective-permute-start.5) | collective-permute-done | bytes 16416 | tf_op jit(solution)/shard_map/ppermute | solution.py:23
  62.1 4.7 %collective-permute-start.6 = (f32[2,16,18,1]{3,2,1,0:T(8,128)S(1)}, f32[2,16,18,1]{3,2,1,0:T(8,128)S(1)}, u32[]{:S(2)}, u32[]{:S(2)}) collective-permute-start(f32[2,16,18,1]{3,2,1,0:T(8,128)S(1)} %get-tuple-element.233), channel_id=1, source_target_pairs={{0,1},{1,2},{2,3},{3,4},{4,5},{5,6},{6,7},{8,9},{9,10},{10,11},{11... | collective-permute-start | bytes 6920 | tf_op jit(solution)/shard_map/ppermute | solution.py:21
  66.9 1.3 collective-permute-start.7
  68.2 3.0 %collective-permute-done.7 = f32[2,16,18,1]{3,2,1,0:T(8,128)S(1)} collective-permute-done((f32[2,16,18,1]{3,2,1,0:T(8,128)S(1)}, f32[2,16,18,1]{3,2,1,0:T(8,128)S(1)}, u32[]{:S(2)}, u32[]{:S(2)}) %collective-permute-start.7) | collective-permute-done | bytes 2336 | tf_op jit(solution)/shard_map/ppermute | solution.py:23
  71.2 0.4 fusion.51
  72.1 3.5 %collective-permute-start.8 = (f32[2,16,1,128]{3,2,1,0:T(1,128)S(1)}, f32[2,16,1,128]{3,2,1,0:T(1,128)S(1)}, u32[]{:S(2)}, u32[]{:S(2)}) collective-permute-start(f32[2,16,1,128]{3,2,1,0:T(1,128)S(1)} %get-tuple-element.243), channel_id=1, source_target_pairs={{0,8},{8,16},{16,24},{1,9},{9,17},{17,25},{2,10},{10,18},{18,26},{... | collective-permute-start | bytes 49160 | tf_op jit(solution)/shard_map/ppermute | solution.py:21
  75.6 1.3 collective-permute-start.9
  77.0 4.2 %collective-permute-done.9 = f32[2,16,1,128]{3,2,1,0:T(1,128)S(1)} collective-permute-done((f32[2,16,1,128]{3,2,1,0:T(1,128)S(1)}, f32[2,16,1,128]{3,2,1,0:T(1,128)S(1)}, u32[]{:S(2)}, u32[]{:S(2)}) %collective-permute-start.9) | collective-permute-done | bytes 16416 | tf_op jit(solution)/shard_map/ppermute | solution.py:23
  81.4 9.5 %collective-permute-start.10 = (f32[2,16,18,1]{3,2,1,0:T(8,128)S(1)}, f32[2,16,18,1]{3,2,1,0:T(8,128)S(1)}, u32[]{:S(2)}, u32[]{:S(2)}) collective-permute-start(f32[2,16,18,1]{3,2,1,0:T(8,128)S(1)} %get-tuple-element.231), channel_id=1, source_target_pairs={{0,1},{1,2},{2,3},{3,4},{4,5},{5,6},{6,7},{8,9},{9,10},{10,11},{11... | collective-permute-start | bytes 6920 | tf_op jit(solution)/shard_map/ppermute | solution.py:21
  90.9 1.3 collective-permute-start.11
  92.2 3.2 %collective-permute-done.11 = f32[2,16,18,1]{3,2,1,0:T(8,128)S(1)} collective-permute-done((f32[2,16,18,1]{3,2,1,0:T(8,128)S(1)}, f32[2,16,18,1]{3,2,1,0:T(8,128)S(1)}, u32[]{:S(2)}, u32[]{:S(2)}) %collective-permute-start.11) | collective-permute-done | bytes 2336 | tf_op jit(solution)/shard_map/ppermute | solution.py:23
  95.4 0.4 fusion.41
  96.3 3.5 %collective-permute-start.12 = (f32[2,16,1,128]{3,2,1,0:T(1,128)S(1)}, f32[2,16,1,128]{3,2,1,0:T(1,128)S(1)}, u32[]{:S(2)}, u32[]{:S(2)}) collective-permute-start(f32[2,16,1,128]{3,2,1,0:T(1,128)S(1)} %get-tuple-element.241), channel_id=1, source_target_pairs={{0,8},{8,16},{16,24},{1,9},{9,17},{17,25},{2,10},{10,18},{18,26},{... | collective-permute-start | bytes 49160 | tf_op jit(solution)/shard_map/ppermute | solution.py:21
  99.7 1.3 collective-permute-start.13
  101.2 4.2 %collective-permute-done.13 = f32[2,16,1,128]{3,2,1,0:T(1,128)S(1)} collective-permute-done((f32[2,16,1,128]{3,2,1,0:T(1,128)S(1)}, f32[2,16,1,128]{3,2,1,0:T(1,128)S(1)}, u32[]{:S(2)}, u32[]{:S(2)}) %collective-permute-start.13) | collective-permute-done | bytes 16416 | tf_op jit(solution)/shard_map/ppermute | solution.py:23
  105.6 8.3 %collective-permute-start.14 = (f32[2,16,18,1]{3,2,1,0:T(8,128)S(1)}, f32[2,16,18,1]{3,2,1,0:T(8,128)S(1)}, u32[]{:S(2)}, u32[]{:S(2)}) collective-permute-start(f32[2,16,18,1]{3,2,1,0:T(8,128)S(1)} %get-tuple-element.229), channel_id=1, source_target_pairs={{0,1},{1,2},{2,3},{3,4},{4,5},{5,6},{6,7},{8,9},{9,10},{10,11},{11... | collective-permute-start | bytes 6920 | tf_op jit(solution)/shard_map/ppermute | solution.py:21
  113.9 1.3 collective-permute-start.15
  115.2 3.2 %collective-permute-done.15 = f32[2,16,18,1]{3,2,1,0:T(8,128)S(1)} collective-permute-done((f32[2,16,18,1]{3,2,1,0:T(8,128)S(1)}, f32[2,16,18,1]{3,2,1,0:T(8,128)S(1)}, u32[]{:S(2)}, u32[]{:S(2)}) %collective-permute-start.15) | collective-permute-done | bytes 2336 | tf_op jit(solution)/shard_map/ppermute | solution.py:23
  118.4 0.4 fusion.31
  119.3 0.6 copy-done.8
  120.3 1.8 collective-permute-start.16
  122.1 1.3 collective-permute-start.17
  123.5 4.2 %collective-permute-done.17 = f32[2,16,1,128]{3,2,1,0:T(1,128)S(1)} collective-permute-done((f32[2,16,1,128]{3,2,1,0:T(1,128)S(1)}, f32[2,16,1,128]{3,2,1,0:T(1,128)S(1)}, u32[]{:S(2)}, u32[]{:S(2)}) %collective-permute-start.17) | collective-permute-done | bytes 16416 | tf_op jit(solution)/shard_map/ppermute | solution.py:23
  128.0 7.5 %collective-permute-start.18 = (f32[2,16,18,1]{3,2,1,0:T(8,128)S(1)}, f32[2,16,18,1]{3,2,1,0:T(8,128)S(1)}, u32[]{:S(2)}, u32[]{:S(2)}) collective-permute-start(f32[2,16,18,1]{3,2,1,0:T(8,128)S(1)} %get-tuple-element.227), channel_id=1, source_target_pairs={{0,1},{1,2},{2,3},{3,4},{4,5},{5,6},{6,7},{8,9},{9,10},{10,11},{11... | collective-permute-start | bytes 6920 | tf_op jit(solution)/shard_map/ppermute | solution.py:21
  135.5 1.3 collective-permute-start.19
  136.8 3.2 %collective-permute-done.19 = f32[2,16,18,1]{3,2,1,0:T(8,128)S(1)} collective-permute-done((f32[2,16,18,1]{3,2,1,0:T(8,128)S(1)}, f32[2,16,18,1]{3,2,1,0:T(8,128)S(1)}, u32[]{:S(2)}, u32[]{:S(2)}) %collective-permute-start.19) | collective-permute-done | bytes 2336 | tf_op jit(solution)/shard_map/ppermute | solution.py:23
  140.0 0.4 fusion.21
  140.8 1.8 collective-permute-start.20
  142.6 1.3 collective-permute-start.21
  144.1 4.2 %collective-permute-done.21 = f32[2,16,1,128]{3,2,1,0:T(1,128)S(1)} collective-permute-done((f32[2,16,1,128]{3,2,1,0:T(1,128)S(1)}, f32[2,16,1,128]{3,2,1,0:T(1,128)S(1)}, u32[]{:S(2)}, u32[]{:S(2)}) %collective-permute-start.21) | collective-permute-done | bytes 16416 | tf_op jit(solution)/shard_map/ppermute | solution.py:23
  148.5 7.4 %collective-permute-start.22 = (f32[2,16,18,1]{3,2,1,0:T(8,128)S(1)}, f32[2,16,18,1]{3,2,1,0:T(8,128)S(1)}, u32[]{:S(2)}, u32[]{:S(2)}) collective-permute-start(f32[2,16,18,1]{3,2,1,0:T(8,128)S(1)} %get-tuple-element.225), channel_id=1, source_target_pairs={{0,1},{1,2},{2,3},{3,4},{4,5},{5,6},{6,7},{8,9},{9,10},{10,11},{11... | collective-permute-start | bytes 6920 | tf_op jit(solution)/shard_map/ppermute | solution.py:21
  155.9 1.3 collective-permute-start.23
  157.2 3.2 %collective-permute-done.23 = f32[2,16,18,1]{3,2,1,0:T(8,128)S(1)} collective-permute-done((f32[2,16,18,1]{3,2,1,0:T(8,128)S(1)}, f32[2,16,18,1]{3,2,1,0:T(8,128)S(1)}, u32[]{:S(2)}, u32[]{:S(2)}) %collective-permute-start.23) | collective-permute-done | bytes 2336 | tf_op jit(solution)/shard_map/ppermute | solution.py:23
  160.4 0.4 fusion.12
  161.2 1.8 collective-permute-start.24
  163.0 1.3 collective-permute-start.25
  164.5 4.2 %collective-permute-done.25 = f32[2,16,1,128]{3,2,1,0:T(1,128)S(1)} collective-permute-done((f32[2,16,1,128]{3,2,1,0:T(1,128)S(1)}, f32[2,16,1,128]{3,2,1,0:T(1,128)S(1)}, u32[]{:S(2)}, u32[]{:S(2)}) %collective-permute-start.25) | collective-permute-done | bytes 16416 | tf_op jit(solution)/shard_map/ppermute | solution.py:23
  168.9 7.4 %collective-permute-start.26 = (f32[2,16,18,1]{3,2,1,0:T(8,128)S(1)}, f32[2,16,18,1]{3,2,1,0:T(8,128)S(1)}, u32[]{:S(2)}, u32[]{:S(2)}) collective-permute-start(f32[2,16,18,1]{3,2,1,0:T(8,128)S(1)} %get-tuple-element.223), channel_id=1, source_target_pairs={{0,1},{1,2},{2,3},{3,4},{4,5},{5,6},{6,7},{8,9},{9,10},{10,11},{11... | collective-permute-start | bytes 6920 | tf_op jit(solution)/shard_map/ppermute | solution.py:21
  176.3 1.3 collective-permute-start.27
  177.6 3.2 %collective-permute-done.27 = f32[2,16,18,1]{3,2,1,0:T(8,128)S(1)} collective-permute-done((f32[2,16,18,1]{3,2,1,0:T(8,128)S(1)}, f32[2,16,18,1]{3,2,1,0:T(8,128)S(1)}, u32[]{:S(2)}, u32[]{:S(2)}) %collective-permute-start.27) | collective-permute-done | bytes 2336 | tf_op jit(solution)/shard_map/ppermute | solution.py:23
  180.8 0.4 fusion.3
  181.7 14.7 %scatter_custom_fusion = f32[128]{0:T(128)S(1)} fusion(s32[2048]{0:T(1024)S(1)} %bitcast.90, f32[2048]{0:T(1024)S(1)} %multiply_bitcast_fusion, f32[]{:T(128)} %constant.56.clone.1), kind=kCustom, calls=%fused_computation.711 | custom fusion | flops 2048 | bytes 516 | tf_op jit(solution)/shard_map/scatter-add | solution.py:122
  196.3 0.7 copy.27
  197.1 36.5 %reduce-scatter.4.cloned.1.call-done = f32[16,1]{1,0:T(8,128)} async-done(((f32[128,1]{1,0:T(8,128)}), f32[16,1]{1,0:T(8,128)}) %reduce-scatter.4.cloned.1.call-update) | async-done | bytes 80
  233.5 1.3 copy.28
  (211 shorter events, 5.3 us)
Async XLA Ops:
  7.2 226.4 %reduce-scatter.4.cloned.1.call-start = ((), (), s32[]{:S(2)}) async-start(), calls=%async_computation.1 | async-start | bytes 73728
  8.1 36.6 %collective-permute-start = (f32[16,1,128]{2,1,0:T(1,128)S(1)}, f32[16,1,128]{2,1,0:T(1,128)S(1)}, u32[]{:S(2)}, u32[]{:S(2)}) collective-permute-start(f32[16,1,128]{2,1,0:T(1,128)S(1)} %get-tuple-element.252), channel_id=1, source_target_pairs={{0,8},{8,16},{16,24},{1,9},{9,17},{17,25},{2,10},{10,18},{18,26},{... | collective-permute-start | bytes 24584 | tf_op jit(solution)/shard_map/ppermute | solution.py:21
  13.0 31.7 %collective-permute-start.1 = (f32[16,1,128]{2,1,0:T(1,128)S(1)}, f32[16,1,128]{2,1,0:T(1,128)S(1)}, u32[]{:S(2)}, u32[]{:S(2)}) collective-permute-start(f32[16,1,128]{2,1,0:T(1,128)S(1)} %get-tuple-element.253), channel_id=1, source_target_pairs={{8,0},{16,8},{24,16},{9,1},{17,9},{25,17},{10,2},{18,10},{26,18},{... | collective-permute-start | bytes 24584 | tf_op jit(solution)/shard_map/ppermute | solution.py:23
  15.4 0.7 copy-start.10
  15.4 16.0 %copy-start.5 = (s32[16,128]{1,0:T(8,128)S(1)}, s32[16,128]{1,0:T(8,128)}, u32[]{:S(2)}) copy-start(s32[16,128]{1,0:T(8,128)} %param.31) | copy-start | bytes 24580
  17.3 0.7 copy-start.9
  44.0 0.7 copy-start.4
  44.7 0.9 copy-start.1
  45.8 2.7 %collective-permute-start.2 = (f32[16,18,1]{2,1,0:T(8,128)S(1)}, f32[16,18,1]{2,1,0:T(8,128)S(1)}, u32[]{:S(2)}, u32[]{:S(2)}) collective-permute-start(f32[16,18,1]{2,1,0:T(8,128)S(1)} %get-tuple-element.247), channel_id=1, source_target_pairs={{0,1},{1,2},{2,3},{3,4},{4,5},{5,6},{6,7},{8,9},{9,10},{10,11},{11... | collective-permute-start | bytes 3464 | tf_op jit(solution)/shard_map/ppermute | solution.py:21
  47.1 3.3 %collective-permute-start.3 = (f32[16,18,1]{2,1,0:T(8,128)S(1)}, f32[16,18,1]{2,1,0:T(8,128)S(1)}, u32[]{:S(2)}, u32[]{:S(2)}) collective-permute-start(f32[16,18,1]{2,1,0:T(8,128)S(1)} %get-tuple-element.248), channel_id=1, source_target_pairs={{1,0},{2,1},{3,2},{4,3},{5,4},{6,5},{7,6},{9,8},{10,9},{11,10},{12... | collective-permute-start | bytes 3464 | tf_op jit(solution)/shard_map/ppermute | solution.py:23
  48.5 2.2 copy-start
  50.6 0.7 copy-start.6
  50.6 0.7 copy-start.7
  52.0 5.7 %collective-permute-start.4 = (f32[2,16,1,128]{3,2,1,0:T(1,128)S(1)}, f32[2,16,1,128]{3,2,1,0:T(1,128)S(1)}, u32[]{:S(2)}, u32[]{:S(2)}) collective-permute-start(f32[2,16,1,128]{3,2,1,0:T(1,128)S(1)} %get-tuple-element.245), channel_id=1, source_target_pairs={{0,8},{8,16},{16,24},{1,9},{9,17},{17,25},{2,10},{10,18},{18,26},{... | collective-permute-start | bytes 49160 | tf_op jit(solution)/shard_map/ppermute | solution.py:21
  56.3 5.6 %collective-permute-start.5 = (f32[2,16,1,128]{3,2,1,0:T(1,128)S(1)}, f32[2,16,1,128]{3,2,1,0:T(1,128)S(1)}, u32[]{:S(2)}, u32[]{:S(2)}) collective-permute-start(f32[2,16,1,128]{3,2,1,0:T(1,128)S(1)} %get-tuple-element.246), channel_id=1, source_target_pairs={{8,0},{16,8},{24,16},{9,1},{17,9},{25,17},{10,2},{18,10},{26,18},{... | collective-permute-start | bytes 49160 | tf_op jit(solution)/shard_map/ppermute | solution.py:23
  62.1 6.0 %collective-permute-start.6 = (f32[2,16,18,1]{3,2,1,0:T(8,128)S(1)}, f32[2,16,18,1]{3,2,1,0:T(8,128)S(1)}, u32[]{:S(2)}, u32[]{:S(2)}) collective-permute-start(f32[2,16,18,1]{3,2,1,0:T(8,128)S(1)} %get-tuple-element.233), channel_id=1, source_target_pairs={{0,1},{1,2},{2,3},{3,4},{4,5},{5,6},{6,7},{8,9},{9,10},{10,11},{11... | collective-permute-start | bytes 6920 | tf_op jit(solution)/shard_map/ppermute | solution.py:21
  66.9 4.4 %collective-permute-start.7 = (f32[2,16,18,1]{3,2,1,0:T(8,128)S(1)}, f32[2,16,18,1]{3,2,1,0:T(8,128)S(1)}, u32[]{:S(2)}, u32[]{:S(2)}) collective-permute-start(f32[2,16,18,1]{3,2,1,0:T(8,128)S(1)} %get-tuple-element.234), channel_id=1, source_target_pairs={{1,0},{2,1},{3,2},{4,3},{5,4},{6,5},{7,6},{9,8},{10,9},{11,10},{12... | collective-permute-start | bytes 6920 | tf_op jit(solution)/shard_map/ppermute | solution.py:23
  72.1 4.9 %collective-permute-start.8 = (f32[2,16,1,128]{3,2,1,0:T(1,128)S(1)}, f32[2,16,1,128]{3,2,1,0:T(1,128)S(1)}, u32[]{:S(2)}, u32[]{:S(2)}) collective-permute-start(f32[2,16,1,128]{3,2,1,0:T(1,128)S(1)} %get-tuple-element.243), channel_id=1, source_target_pairs={{0,8},{8,16},{16,24},{1,9},{9,17},{17,25},{2,10},{10,18},{18,26},{... | collective-permute-start | bytes 49160 | tf_op jit(solution)/shard_map/ppermute | solution.py:21
  75.6 5.6 %collective-permute-start.9 = (f32[2,16,1,128]{3,2,1,0:T(1,128)S(1)}, f32[2,16,1,128]{3,2,1,0:T(1,128)S(1)}, u32[]{:S(2)}, u32[]{:S(2)}) collective-permute-start(f32[2,16,1,128]{3,2,1,0:T(1,128)S(1)} %get-tuple-element.244), channel_id=1, source_target_pairs={{8,0},{16,8},{24,16},{9,1},{17,9},{25,17},{10,2},{18,10},{26,18},{... | collective-permute-start | bytes 49160 | tf_op jit(solution)/shard_map/ppermute | solution.py:23
  81.4 10.8 %collective-permute-start.10 = (f32[2,16,18,1]{3,2,1,0:T(8,128)S(1)}, f32[2,16,18,1]{3,2,1,0:T(8,128)S(1)}, u32[]{:S(2)}, u32[]{:S(2)}) collective-permute-start(f32[2,16,18,1]{3,2,1,0:T(8,128)S(1)} %get-tuple-element.231), channel_id=1, source_target_pairs={{0,1},{1,2},{2,3},{3,4},{4,5},{5,6},{6,7},{8,9},{9,10},{10,11},{11... | collective-permute-start | bytes 6920 | tf_op jit(solution)/shard_map/ppermute | solution.py:21
  90.9 4.5 %collective-permute-start.11 = (f32[2,16,18,1]{3,2,1,0:T(8,128)S(1)}, f32[2,16,18,1]{3,2,1,0:T(8,128)S(1)}, u32[]{:S(2)}, u32[]{:S(2)}) collective-permute-start(f32[2,16,18,1]{3,2,1,0:T(8,128)S(1)} %get-tuple-element.232), channel_id=1, source_target_pairs={{1,0},{2,1},{3,2},{4,3},{5,4},{6,5},{7,6},{9,8},{10,9},{11,10},{12... | collective-permute-start | bytes 6920 | tf_op jit(solution)/shard_map/ppermute | solution.py:23
  96.3 4.9 %collective-permute-start.12 = (f32[2,16,1,128]{3,2,1,0:T(1,128)S(1)}, f32[2,16,1,128]{3,2,1,0:T(1,128)S(1)}, u32[]{:S(2)}, u32[]{:S(2)}) collective-permute-start(f32[2,16,1,128]{3,2,1,0:T(1,128)S(1)} %get-tuple-element.241), channel_id=1, source_target_pairs={{0,8},{8,16},{16,24},{1,9},{9,17},{17,25},{2,10},{10,18},{18,26},{... | collective-permute-start | bytes 49160 | tf_op jit(solution)/shard_map/ppermute | solution.py:21
  99.7 5.6 %collective-permute-start.13 = (f32[2,16,1,128]{3,2,1,0:T(1,128)S(1)}, f32[2,16,1,128]{3,2,1,0:T(1,128)S(1)}, u32[]{:S(2)}, u32[]{:S(2)}) collective-permute-start(f32[2,16,1,128]{3,2,1,0:T(1,128)S(1)} %get-tuple-element.242), channel_id=1, source_target_pairs={{8,0},{16,8},{24,16},{9,1},{17,9},{25,17},{10,2},{18,10},{26,18},{... | collective-permute-start | bytes 49160 | tf_op jit(solution)/shard_map/ppermute | solution.py:23
  105.6 9.6 %collective-permute-start.14 = (f32[2,16,18,1]{3,2,1,0:T(8,128)S(1)}, f32[2,16,18,1]{3,2,1,0:T(8,128)S(1)}, u32[]{:S(2)}, u32[]{:S(2)}) collective-permute-start(f32[2,16,18,1]{3,2,1,0:T(8,128)S(1)} %get-tuple-element.229), channel_id=1, source_target_pairs={{0,1},{1,2},{2,3},{3,4},{4,5},{5,6},{6,7},{8,9},{9,10},{10,11},{11... | collective-permute-start | bytes 6920 | tf_op jit(solution)/shard_map/ppermute | solution.py:21
  113.9 4.5 %collective-permute-start.15 = (f32[2,16,18,1]{3,2,1,0:T(8,128)S(1)}, f32[2,16,18,1]{3,2,1,0:T(8,128)S(1)}, u32[]{:S(2)}, u32[]{:S(2)}) collective-permute-start(f32[2,16,18,1]{3,2,1,0:T(8,128)S(1)} %get-tuple-element.230), channel_id=1, source_target_pairs={{1,0},{2,1},{3,2},{4,3},{5,4},{6,5},{7,6},{9,8},{10,9},{11,10},{12... | collective-permute-start | bytes 6920 | tf_op jit(solution)/shard_map/ppermute | solution.py:23
  119.2 0.7 copy-start.8
  119.2 62.4 %copy-start.2 = (f32[2,16,16,128]{3,2,1,0:T(8,128)}, f32[2,16,16,128]{3,2,1,0:T(8,128)S(1)}, u32[]{:S(2)}) copy-start(f32[2,16,16,128]{3,2,1,0:T(8,128)S(1)} %add_multiply_fusion.3) | copy-start | bytes 786436
  120.3 3.2 %collective-permute-start.16 = (f32[2,16,1,128]{3,2,1,0:T(1,128)S(1)}, f32[2,16,1,128]{3,2,1,0:T(1,128)S(1)}, u32[]{:S(2)}, u32[]{:S(2)}) collective-permute-start(f32[2,16,1,128]{3,2,1,0:T(1,128)S(1)} %get-tuple-element.239), channel_id=1, source_target_pairs={{0,8},{8,16},{16,24},{1,9},{9,17},{17,25},{2,10},{10,18},{18,26},{... | collective-permute-start | bytes 49160 | tf_op jit(solution)/shard_map/ppermute | solution.py:21
  122.1 5.6 %collective-permute-start.17 = (f32[2,16,1,128]{3,2,1,0:T(1,128)S(1)}, f32[2,16,1,128]{3,2,1,0:T(1,128)S(1)}, u32[]{:S(2)}, u32[]{:S(2)}) collective-permute-start(f32[2,16,1,128]{3,2,1,0:T(1,128)S(1)} %get-tuple-element.240), channel_id=1, source_target_pairs={{8,0},{16,8},{24,16},{9,1},{17,9},{25,17},{10,2},{18,10},{26,18},{... | collective-permute-start | bytes 49160 | tf_op jit(solution)/shard_map/ppermute | solution.py:23
  128.0 8.8 %collective-permute-start.18 = (f32[2,16,18,1]{3,2,1,0:T(8,128)S(1)}, f32[2,16,18,1]{3,2,1,0:T(8,128)S(1)}, u32[]{:S(2)}, u32[]{:S(2)}) collective-permute-start(f32[2,16,18,1]{3,2,1,0:T(8,128)S(1)} %get-tuple-element.227), channel_id=1, source_target_pairs={{0,1},{1,2},{2,3},{3,4},{4,5},{5,6},{6,7},{8,9},{9,10},{10,11},{11... | collective-permute-start | bytes 6920 | tf_op jit(solution)/shard_map/ppermute | solution.py:21
  135.5 4.5 %collective-permute-start.19 = (f32[2,16,18,1]{3,2,1,0:T(8,128)S(1)}, f32[2,16,18,1]{3,2,1,0:T(8,128)S(1)}, u32[]{:S(2)}, u32[]{:S(2)}) collective-permute-start(f32[2,16,18,1]{3,2,1,0:T(8,128)S(1)} %get-tuple-element.228), channel_id=1, source_target_pairs={{1,0},{2,1},{3,2},{4,3},{5,4},{6,5},{7,6},{9,8},{10,9},{11,10},{12... | collective-permute-start | bytes 6920 | tf_op jit(solution)/shard_map/ppermute | solution.py:23
  140.8 3.2 %collective-permute-start.20 = (f32[2,16,1,128]{3,2,1,0:T(1,128)S(1)}, f32[2,16,1,128]{3,2,1,0:T(1,128)S(1)}, u32[]{:S(2)}, u32[]{:S(2)}) collective-permute-start(f32[2,16,1,128]{3,2,1,0:T(1,128)S(1)} %get-tuple-element.237), channel_id=1, source_target_pairs={{0,8},{8,16},{16,24},{1,9},{9,17},{17,25},{2,10},{10,18},{18,26},{... | collective-permute-start | bytes 49160 | tf_op jit(solution)/shard_map/ppermute | solution.py:21
  142.6 5.6 %collective-permute-start.21 = (f32[2,16,1,128]{3,2,1,0:T(1,128)S(1)}, f32[2,16,1,128]{3,2,1,0:T(1,128)S(1)}, u32[]{:S(2)}, u32[]{:S(2)}) collective-permute-start(f32[2,16,1,128]{3,2,1,0:T(1,128)S(1)} %get-tuple-element.238), channel_id=1, source_target_pairs={{8,0},{16,8},{24,16},{9,1},{17,9},{25,17},{10,2},{18,10},{26,18},{... | collective-permute-start | bytes 49160 | tf_op jit(solution)/shard_map/ppermute | solution.py:23
  148.5 8.7 %collective-permute-start.22 = (f32[2,16,18,1]{3,2,1,0:T(8,128)S(1)}, f32[2,16,18,1]{3,2,1,0:T(8,128)S(1)}, u32[]{:S(2)}, u32[]{:S(2)}) collective-permute-start(f32[2,16,18,1]{3,2,1,0:T(8,128)S(1)} %get-tuple-element.225), channel_id=1, source_target_pairs={{0,1},{1,2},{2,3},{3,4},{4,5},{5,6},{6,7},{8,9},{9,10},{10,11},{11... | collective-permute-start | bytes 6920 | tf_op jit(solution)/shard_map/ppermute | solution.py:21
  155.9 4.5 %collective-permute-start.23 = (f32[2,16,18,1]{3,2,1,0:T(8,128)S(1)}, f32[2,16,18,1]{3,2,1,0:T(8,128)S(1)}, u32[]{:S(2)}, u32[]{:S(2)}) collective-permute-start(f32[2,16,18,1]{3,2,1,0:T(8,128)S(1)} %get-tuple-element.226), channel_id=1, source_target_pairs={{1,0},{2,1},{3,2},{4,3},{5,4},{6,5},{7,6},{9,8},{10,9},{11,10},{12... | collective-permute-start | bytes 6920 | tf_op jit(solution)/shard_map/ppermute | solution.py:23
  161.2 3.2 %collective-permute-start.24 = (f32[2,16,1,128]{3,2,1,0:T(1,128)S(1)}, f32[2,16,1,128]{3,2,1,0:T(1,128)S(1)}, u32[]{:S(2)}, u32[]{:S(2)}) collective-permute-start(f32[2,16,1,128]{3,2,1,0:T(1,128)S(1)} %get-tuple-element.235), channel_id=1, source_target_pairs={{0,8},{8,16},{16,24},{1,9},{9,17},{17,25},{2,10},{10,18},{18,26},{... | collective-permute-start | bytes 49160 | tf_op jit(solution)/shard_map/ppermute | solution.py:21
  163.0 5.6 %collective-permute-start.25 = (f32[2,16,1,128]{3,2,1,0:T(1,128)S(1)}, f32[2,16,1,128]{3,2,1,0:T(1,128)S(1)}, u32[]{:S(2)}, u32[]{:S(2)}) collective-permute-start(f32[2,16,1,128]{3,2,1,0:T(1,128)S(1)} %get-tuple-element.236), channel_id=1, source_target_pairs={{8,0},{16,8},{24,16},{9,1},{17,9},{25,17},{10,2},{18,10},{26,18},{... | collective-permute-start | bytes 49160 | tf_op jit(solution)/shard_map/ppermute | solution.py:23
  168.9 8.7 %collective-permute-start.26 = (f32[2,16,18,1]{3,2,1,0:T(8,128)S(1)}, f32[2,16,18,1]{3,2,1,0:T(8,128)S(1)}, u32[]{:S(2)}, u32[]{:S(2)}) collective-permute-start(f32[2,16,18,1]{3,2,1,0:T(8,128)S(1)} %get-tuple-element.223), channel_id=1, source_target_pairs={{0,1},{1,2},{2,3},{3,4},{4,5},{5,6},{6,7},{8,9},{9,10},{10,11},{11... | collective-permute-start | bytes 6920 | tf_op jit(solution)/shard_map/ppermute | solution.py:21
  176.3 4.5 %collective-permute-start.27 = (f32[2,16,18,1]{3,2,1,0:T(8,128)S(1)}, f32[2,16,18,1]{3,2,1,0:T(8,128)S(1)}, u32[]{:S(2)}, u32[]{:S(2)}) collective-permute-start(f32[2,16,18,1]{3,2,1,0:T(8,128)S(1)} %get-tuple-element.224), channel_id=1, source_target_pairs={{1,0},{2,1},{3,2},{4,3},{5,4},{6,5},{7,6},{9,8},{10,9},{11,10},{12... | collective-permute-start | bytes 6920 | tf_op jit(solution)/shard_map/ppermute | solution.py:23
  181.6 53.2 %copy-start.3 = (f32[2,16,16,128]{3,2,1,0:T(8,128)}, f32[2,16,16,128]{3,2,1,0:T(8,128)S(1)}, u32[]{:S(2)}) copy-start(f32[2,16,16,128]{3,2,1,0:T(8,128)S(1)} %add_multiply_fusion) | copy-start | bytes 786436
Sparse Core Ops, SparseCore 0:
  197.2 36.2 reduce-scatter.3
where the time goes:
time: 243 us; the launch traced here: 242 us
  starting transfers between devices  85.7 us (35%)
  waiting for transfers between devices  83.4 us (34%)
  local copies, waits for them, and re-layouts  22.2 us (9%)
  other arithmetic  20.7 us (9%)
  between operations  16.3 us (7%)
  blocking collectives  13.4 us (6%)
    ppermute x14, starting transfers between devices, with_halo(): lax.ppermute(tail, axis, [(i, (i + 1) % count) for i in range(ends)])  67.6 us
    ppermute x14, waiting for transfers between devices, with_halo(): lax.ppermute(head, axis, [((i + 1) % count, i) for i in range(ends)])  46.1 us
    unnamed x2, waiting for transfers between devices  36.5 us
    ppermute x14, starting transfers between devices, with_halo(): lax.ppermute(head, axis, [((i + 1) % count, i) for i in range(ends)])  18.1 us
    scatter-add x1, other arithmetic, local(): jax.ops.segment_sum(grad_col.reshape(-1), tile_owner.reshape(-1), num_seg...  14.7 us
    squeeze x1, blocking collectives, local(): beta_col = jnp.take(friction_row[0], tile_owner, axis=0)  13.4 us
    gather x1, local copies, waits for them, and re-layouts, local(): beta_col = jnp.take(friction_row[0], tile_owner, axis=0)  12.6 us
    unnamed x139, local copies, waits for them, and re-layouts  7.19 us
  transfers between devices with their start and end apart: 29, of which 20 were waited for; matrix products, arithmetic and copies ran while one was open for 6% of the time, Pallas kernels for 0%

commit v1 on v0

--- a/solution.py
+++ b/solution.py
@@ -8,6 +8,7 @@
 
 OMEGA = 0.8
 VERTICAL = 16.0
+HALO = 2 * PASSES - 1
 
 
 def with_halo(cells, sides, width):
@@ -96,32 +97,73 @@
 
 
 def local(forcing, viscosity, observed, beta_tiles, ice_mask, tile_owner):
-    ice_cover = ice_mask.astype(jnp.float32)
-    friction_row = lax.all_gather(beta_tiles, "gy", axis=1, tiled=True)
-    beta_col = jnp.take(friction_row[0], tile_owner, axis=0)
-    visc_rim = with_halo(viscosity, (("gx", 1), ("gy", 2)), 1)
-    faces, lower_link, ratios, inverses = prepare(visc_rim, beta_col, ice_cover)
+    comps, layers, rows, cols = forcing.shape
+    strip_count = lax.axis_size("gx")
+    strips_near = jnp.concatenate(
+        [
+            lax.ppermute(beta_tiles, "gx", [(i, i + 1) for i in range(strip_count - 1)]),
+            beta_tiles,
+            lax.ppermute(beta_tiles, "gx", [(i + 1, i) for i in range(strip_count - 1)]),
+        ],
+        axis=0,
+    )
+    friction_rows = lax.all_gather(strips_near, "gy", axis=1, tiled=True)
+    tile_count = friction_rows.shape[1]
 
-    def advance(field, rhs_field, first):
-        if first:
-            field_rim = pad_cells(field)
-        else:
-            field_rim = with_halo(field, (("gx", 2), ("gy", 3)), 1)
-        return relax(field_rim, rhs_field, faces, lower_link, ratios, inverses, ice_cover)
+    packed = jnp.concatenate(
+        [
+            forcing.reshape(comps * layers, rows, cols),
+            viscosity,
+            observed,
+            ice_mask.astype(jnp.float32)[None],
+            tile_owner.astype(jnp.float32)[None],
+        ],
+        axis=0,
+    )
+    packed = with_halo(packed, (("gx", 1), ("gy", 2)), HALO)
+    ext_rows, ext_cols = packed.shape[1], packed.shape[2]
+    at = 0
+    forcing_ext = packed[at:at + comps * layers].reshape(comps, layers, ext_rows, ext_cols)
+    at += comps * layers
+    visc_ext = packed[at:at + layers]
+    at += layers
+    observed_ext = packed[at:at + comps]
+    at += comps
+    ice_cover = packed[at]
+    owner_ext = packed[at + 1].astype(jnp.int32)
 
-    velocity = jnp.zeros_like(forcing)
+    tiles = lax.broadcasted_iota(jnp.int32, (1, 1, tile_count), 2)
+    owner_match = owner_ext[:, :, None] == tiles
+    row_strip = jnp.concatenate(
+        [
+            jnp.broadcast_to(friction_rows[0], (HALO, tile_count)),
+            jnp.broadcast_to(friction_rows[1], (rows, tile_count)),
+            jnp.broadcast_to(friction_rows[2], (HALO, tile_count)),
+        ],
+        axis=0,
+    )
+    beta_col = jnp.sum(jnp.where(owner_match, row_strip[:, None, :], 0.0), axis=-1)
+
+    faces, lower_link, ratios, inverses = prepare(pad_cells(visc_ext), beta_col, ice_cover)
+
+    def advance(field, rhs_field):
+        return relax(pad_cells(field), rhs_field, faces, lower_link, ratios, inverses, ice_cover)
+
+    velocity = jnp.zeros_like(forcing_ext)
     for sweep_idx in range(PASSES):
-        velocity = advance(velocity, forcing, sweep_idx == 0)
-    misfit = velocity[:, 0] - observed
-    adjoint_rhs = jnp.zeros_like(forcing).at[:, 0].set(misfit)
-    adjoint = jnp.zeros_like(forcing)
+        velocity = advance(velocity, forcing_ext)
+    misfit = velocity[:, 0] - observed_ext
+    adjoint_rhs = jnp.zeros_like(forcing_ext).at[:, 0].set(misfit)
+    adjoint = jnp.zeros_like(forcing_ext)
     for sweep_idx in range(PASSES):
-        adjoint = advance(adjoint, adjoint_rhs, sweep_idx == 0)
-    grad_col = -ice_cover * beta_col * jnp.sum(adjoint[:, -1] * velocity[:, -1], axis=0)
-    tile_count = friction_row.shape[1]
-    partial_sum = jax.ops.segment_sum(
-        grad_col.reshape(-1), tile_owner.reshape(-1), num_segments=tile_count
-    )[None]
+        adjoint = advance(adjoint, adjoint_rhs)
+
+    inner = (slice(HALO, HALO + rows), slice(HALO, HALO + cols))
+    velocity = velocity[:, :, inner[0], inner[1]]
+    adjoint = adjoint[:, :, inner[0], inner[1]]
+    grad_col = -ice_cover[inner] * beta_col[inner] * jnp.sum(adjoint[:, -1] * velocity[:, -1], axis=0)
+    block_match = owner_match[inner[0], inner[1]]
+    partial_sum = jnp.sum(jnp.where(block_match, grad_col[:, :, None], 0.0), axis=(0, 1))[None]
     grad_tiles = lax.psum_scatter(partial_sum, "gy", scatter_dimension=1, tiled=True)
     return (velocity, adjoint, grad_tiles)
 

time: 243 us -> 109 us (0.45)
  starting transfers between devices: 85.7 us -> 15.6 us
  waiting for transfers between devices: 83.4 us -> 37.6 us
  local copies, waits for them, and re-layouts: 22.2 us -> 12 us
  blocking collectives: 13.4 us -> 8.91 us
    ppermute x14 -> x2, starting transfers between devices: 67.6 us -> 6.79 us  [with_halo(): lax.ppermute(tail, axis, [(i, (i + 1) % count) for i in range(ends)])]
    ppermute x14 -> x2, waiting for transfers between devices: 46.1 us -> 1.79 us  [with_halo(): lax.ppermute(head, axis, [((i + 1) % count, i) for i in range(ends)])]
    ppermute x14 -> x2, starting transfers between devices: 18.1 us -> 2.58 us  [with_halo(): lax.ppermute(head, axis, [((i + 1) % count, i) for i in range(ends)])]
    scatter-add x1 -> x0, other arithmetic: 14.7 us -> none  [local(): jax.ops.segment_sum(grad_col.reshape(-1), tile_owner.reshape(-1), num_seg...]
    squeeze x1 -> x0, blocking collectives: 13.4 us -> none  [local(): beta_col = jnp.take(friction_row[0], tile_owner, axis=0)]
    gather x1 -> x0, local copies, waits for them, and re-layouts: 12.6 us -> none  [local(): beta_col = jnp.take(friction_row[0], tile_owner, axis=0)]
    all_gather x0 -> x1, blocking collectives: none -> 8.91 us  [local(): friction_rows = lax.all_gather(strips_near, 'gy', axis=1, tiled=True)]
    ppermute x0 -> x2, starting transfers between devices: none -> 6.22 us  [the longest x1 4.93 us: local(): lax.ppermute(beta_tiles, 'gx', [(i, i + 1) for i in range(strip_count - 1)])]
  transfers between devices with their start and end apart: 29 -> 7, of which waited for: 20 -> 2; matrix products, arithmetic and copies ran while one was open for 6% -> 8% of each run, Pallas kernels for 0% -> 0%
where the time goes in v1:
time: 109 us
  waiting for transfers between devices  37.6 us (34%)
  other arithmetic  19.2 us (18%)
  starting transfers between devices  15.6 us (14%)
  between operations  15.5 us (14%)
  local copies, waits for them, and re-layouts  12 us (11%)
  blocking collectives  8.91 us (8%)
    unnamed x2, waiting for transfers between devices  35.8 us
    all_gather x1, blocking collectives, local(): friction_rows = lax.all_gather(strips_near, 'gy', axis=1, tiled=True)  8.91 us
    unnamed x128, local copies, waits for them, and re-layouts  7.01 us
    ppermute x2, starting transfers between devices, with_halo(): lax.ppermute(tail, axis, [(i, (i + 1) % count) for i in range(ends)])  6.79 us
    ppermute x1, starting transfers between devices, local(): lax.ppermute(beta_tiles, 'gx', [(i, i + 1) for i in range(strip_count - 1)])  4.93 us
    add x4, other arithmetic, relax(): right_side = rhs_field + lateral  3.61 us
    unnamed x10, other arithmetic  3.13 us
    add x3, other arithmetic, relax(): lateral + along_y * (south_face * vel_pad[:, :, 1:-1, :-2] + north_face *...  2.78 us
  transfers between devices with their start and end apart: 7, of which 2 were waited for; matrix products, arithmetic and copies ran while one was open for 8% of the time, Pallas kernels for 0%

profile of v1, /device:TPU:0, one launch (start us, length us, event | category | flops | bytes accessed | tf_op | source)
XLA Modules:
  0.0 108.7 jit_solution(3275133596863738168)
XLA Ops:
  7.2 4.9 %collective-permute-start.4 = (f32[1,16]{1,0:T(1,128)}, f32[1,16]{1,0:T(1,128)S(1)}, u32[]{:S(2)}, u32[]{:S(2)}) collective-permute-start(f32[1,16]{1,0:T(1,128)} %param.29), channel_id=1, source_target_pairs={{0,8},{8,16},{16,24},{1,9},{9,17},{17,25},{2,10},{10,18},{18,26},{... | collective-permute-start | bytes 200 | tf_op jit(solution)/shard_map/ppermute | solution.py:104
  12.2 1.3 %collective-permute-start.5 = (f32[1,16]{1,0:T(1,128)}, f32[1,16]{1,0:T(1,128)S(1)}, u32[]{:S(2)}, u32[]{:S(2)}) collective-permute-start(f32[1,16]{1,0:T(1,128)} %param.29), channel_id=1, source_target_pairs={{8,0},{16,8},{24,16},{9,1},{17,9},{25,17},{10,2},{18,10},{26,18},{... | collective-permute-start | bytes 200 | tf_op jit(solution)/shard_map/ppermute | solution.py:106
  13.5 1.0 constant_dynamic-update-slice_fusion.4
  14.4 0.9 constant_dynamic-update-slice_fusion.3
  15.3 0.7 constant_dynamic-update-slice_fusion.2
  16.1 0.7 constant_dynamic-update-slice_fusion.1
  16.8 0.7 constant_dynamic-update-slice_fusion
  17.5 4.6 %collective-permute-start = (f32[52,7,128]{2,1,0:T(8,128)S(1)}, f32[52,7,128]{2,1,0:T(8,128)S(1)}, u32[]{:S(2)}, u32[]{:S(2)}) collective-permute-start(f32[52,7,128]{2,1,0:T(8,128)S(1)} %get-tuple-element.271), channel_id=1, source_target_pairs={{0,8},{8,16},{16,24},{1,9},{9,17},{17,25},{2,10},{10,18},{18,26},{... | collective-permute-start | bytes 559112 | tf_op jit(solution)/shard_map/ppermute | solution.py:22
  22.1 1.3 %collective-permute-start.1 = (f32[52,7,128]{2,1,0:T(8,128)S(1)}, f32[52,7,128]{2,1,0:T(8,128)S(1)}, u32[]{:S(2)}, u32[]{:S(2)}) collective-permute-start(f32[52,7,128]{2,1,0:T(8,128)S(1)} %get-tuple-element.272), channel_id=1, source_target_pairs={{8,0},{16,8},{24,16},{9,1},{17,9},{25,17},{10,2},{18,10},{26,18},{... | collective-permute-start | bytes 559112 | tf_op jit(solution)/shard_map/ppermute | solution.py:24
  23.5 8.9 %all-gather = f32[8,16,3]{1,2,0:T(4,128)S(1)} all-gather(f32[1,16,3]{1,2,0:T(4,128)S(1)} %maximum_bitcast_fusion.1), channel_id=1, replica_groups=mesh['gx'=4,'gy'=8] {'gy'}, dimensions={0}, use_global_device_ids=true | all-gather | bytes 1728 | tf_op jit(solution)/shard_map/all_gather | solution.py:110
  32.5 0.1 pad_maximum_fusion.1
  32.6 0.3 fusion.218
  33.0 0.6 copy.51
  33.6 2.2 %collective-permute-start.2 = (f32[52,30,7]{0,1,2:T(8,128)S(1)}, f32[52,30,7]{0,1,2:T(8,128)S(1)}, u32[]{:S(2)}, u32[]{:S(2)}) collective-permute-start(f32[52,30,7]{0,1,2:T(8,128)S(1)} %copy.51), channel_id=1, source_target_pairs={{0,1},{1,2},{2,3},{3,4},{4,5},{5,6},{6,7},{8,9},{9,10},{10,11},{11... | collective-permute-start | bytes 131048 | tf_op jit(solution)/shard_map/ppermute | solution.py:22
  35.8 0.6 copy.52
  36.4 1.3 %collective-permute-start.3 = (f32[52,30,7]{0,1,2:T(8,128)S(1)}, f32[52,30,7]{0,1,2:T(8,128)S(1)}, u32[]{:S(2)}, u32[]{:S(2)}) collective-permute-start(f32[52,30,7]{0,1,2:T(8,128)S(1)} %copy.52), channel_id=1, source_target_pairs={{1,0},{2,1},{3,2},{4,3},{5,4},{6,5},{7,6},{9,8},{10,9},{11,10},{12... | collective-permute-start | bytes 131048 | tf_op jit(solution)/shard_map/ppermute | solution.py:24
  37.8 0.8 copy.53
  38.6 1.8 %collective-permute-done.3 = f32[52,30,7]{0,1,2:T(8,128)S(1)} collective-permute-done((f32[52,30,7]{0,1,2:T(8,128)S(1)}, f32[52,30,7]{0,1,2:T(8,128)S(1)}, u32[]{:S(2)}, u32[]{:S(2)}) %collective-permute-start.3) | collective-permute-done | bytes 43712 | tf_op jit(solution)/shard_map/ppermute | solution.py:24
  40.4 0.8 copy.54
  41.2 1.0 pad_maximum_fusion
  42.3 0.1 slice.1032
  42.5 0.5 fusion.216
  43.1 0.1 fusion.141
  43.2 0.9 iota_compare_fusion
  44.1 2.2 %select_reduce_fusion = f32[30,142]{1,0:T(8,128)S(1)} fusion(f32[30,128]{1,0:T(8,128)S(1)} %pad_maximum_fusion.2, s32[30,142]{1,0:T(8,128)S(1)} %fusion.141), kind=kLoop, calls=%fused_computation | loop fusion | flops 1631580 | bytes 49440 | tf_op jit(solution)/shard_map/reduce_sum | solution.py:145
  46.4 0.1 broadcast_multiply_fusion.2
  46.5 0.9 copy_add_fusion
  47.4 0.3 fusion.116
  47.7 0.3 constant_dynamic-update-slice_fusion.20
  48.2 0.1 broadcast_multiply_fusion.1
  48.4 0.9 add_add_fusion.2
  49.3 0.2 fusion.98
  49.4 0.3 constant_dynamic-update-slice_fusion.36
  50.0 0.3 add_multiply_fusion.5
  50.3 0.9 add_add_fusion.1
  51.2 0.2 fusion.83
  51.4 0.3 constant_dynamic-update-slice_fusion.52
  51.9 0.3 add_multiply_fusion.4
  52.2 0.9 add_add_fusion
  53.1 0.2 fusion.68
  53.3 0.3 constant_dynamic-update-slice_fusion.68
  53.8 0.3 add_multiply_fusion.3
  54.1 0.2 fusion.52
  54.4 0.3 constant_dynamic-update-slice_fusion.84
  55.0 0.9 multiply_add_fusion.2
  55.9 0.2 fusion.36
  56.1 0.3 constant_dynamic-update-slice_fusion.100
  56.7 0.2 add_multiply_fusion.2
  56.9 0.9 multiply_add_fusion.1
  57.8 0.2 fusion.20
  58.0 0.3 constant_dynamic-update-slice_fusion.116
  58.5 0.2 add_multiply_fusion.1
  58.8 0.9 multiply_add_fusion
  59.7 0.2 fusion.4
  59.9 0.3 constant_dynamic-update-slice_fusion.132
  60.4 0.2 add_multiply_fusion
  60.8 0.4 select_reduce_fusion.1
  61.2 0.8 copy.63
  61.9 0.1 slice.1193
  62.1 1.3 %slice.1131 = f32[2,16,16,128]{3,2,0,1:T(8,128)S(1)} slice(f32[2,16,30,142]{3,2,0,1:T(8,128)} %copy-done), slice={[0:2], [0:16], [7:23], [7:135]} | slice | bytes 524288 | tf_op jit(solution)/shard_map/slice | solution.py:162
  63.4 0.7 copy.62
  64.1 0.7 copy.61
  64.8 35.8 %reduce-scatter.4.cloned.1.call-done = f32[16,1]{1,0:T(8,128)} async-done(((f32[128,1]{1,0:T(8,128)}), f32[16,1]{1,0:T(8,128)}) %reduce-scatter.4.cloned.1.call-update) | async-done | bytes 80
  100.6 1.3 %copy.64 = f32[1,16]{1,0:T(1,128)} copy(f32[1,16]{0,1:T(8,128)} %bitcast.103) | data formatting | bytes 128
  (155 shorter events, 1.7 us)
Async XLA Ops:
  7.2 16.3 %copy-start.3 = (f32[1,16]{1,0:T(1,128)S(1)}, f32[1,16]{1,0:T(1,128)}, u32[]{:S(2)}) copy-start(f32[1,16]{1,0:T(1,128)} %param.29) | copy-start | bytes 196
  7.2 93.4 %reduce-scatter.4.cloned.1.call-start = ((), (), s32[]{:S(2)}) async-start(), calls=%async_computation.1 | async-start | bytes 73728
  7.2 16.2 %collective-permute-start.4 = (f32[1,16]{1,0:T(1,128)}, f32[1,16]{1,0:T(1,128)S(1)}, u32[]{:S(2)}, u32[]{:S(2)}) collective-permute-start(f32[1,16]{1,0:T(1,128)} %param.29), channel_id=1, source_target_pairs={{0,8},{8,16},{16,24},{1,9},{9,17},{17,25},{2,10},{10,18},{18,26},{... | collective-permute-start | bytes 200 | tf_op jit(solution)/shard_map/ppermute | solution.py:104
  12.2 11.3 %collective-permute-start.5 = (f32[1,16]{1,0:T(1,128)}, f32[1,16]{1,0:T(1,128)S(1)}, u32[]{:S(2)}, u32[]{:S(2)}) collective-permute-start(f32[1,16]{1,0:T(1,128)} %param.29), channel_id=1, source_target_pairs={{8,0},{16,8},{24,16},{9,1},{17,9},{25,17},{10,2},{18,10},{26,18},{... | collective-permute-start | bytes 200 | tf_op jit(solution)/shard_map/ppermute | solution.py:106
  17.5 15.0 %collective-permute-start = (f32[52,7,128]{2,1,0:T(8,128)S(1)}, f32[52,7,128]{2,1,0:T(8,128)S(1)}, u32[]{:S(2)}, u32[]{:S(2)}) collective-permute-start(f32[52,7,128]{2,1,0:T(8,128)S(1)} %get-tuple-element.271), channel_id=1, source_target_pairs={{0,8},{8,16},{16,24},{1,9},{9,17},{17,25},{2,10},{10,18},{18,26},{... | collective-permute-start | bytes 559112 | tf_op jit(solution)/shard_map/ppermute | solution.py:22
  22.1 10.4 %collective-permute-start.1 = (f32[52,7,128]{2,1,0:T(8,128)S(1)}, f32[52,7,128]{2,1,0:T(8,128)S(1)}, u32[]{:S(2)}, u32[]{:S(2)}) collective-permute-start(f32[52,7,128]{2,1,0:T(8,128)S(1)} %get-tuple-element.272), channel_id=1, source_target_pairs={{8,0},{16,8},{24,16},{9,1},{17,9},{25,17},{10,2},{18,10},{26,18},{... | collective-permute-start | bytes 559112 | tf_op jit(solution)/shard_map/ppermute | solution.py:24
  33.6 4.2 %collective-permute-start.2 = (f32[52,30,7]{0,1,2:T(8,128)S(1)}, f32[52,30,7]{0,1,2:T(8,128)S(1)}, u32[]{:S(2)}, u32[]{:S(2)}) collective-permute-start(f32[52,30,7]{0,1,2:T(8,128)S(1)} %copy.51), channel_id=1, source_target_pairs={{0,1},{1,2},{2,3},{3,4},{4,5},{5,6},{6,7},{8,9},{9,10},{10,11},{11... | collective-permute-start | bytes 131048 | tf_op jit(solution)/shard_map/ppermute | solution.py:22
  36.4 4.0 %collective-permute-start.3 = (f32[52,30,7]{0,1,2:T(8,128)S(1)}, f32[52,30,7]{0,1,2:T(8,128)S(1)}, u32[]{:S(2)}, u32[]{:S(2)}) collective-permute-start(f32[52,30,7]{0,1,2:T(8,128)S(1)} %copy.52), channel_id=1, source_target_pairs={{1,0},{2,1},{3,2},{4,3},{5,4},{6,5},{7,6},{9,8},{10,9},{11,10},{12... | collective-permute-start | bytes 131048 | tf_op jit(solution)/shard_map/ppermute | solution.py:24
  44.1 2.4 %copy-start.1 = (f32[2]{0:T(128)S(1)}, f32[2]{0:T(128)}, u32[]{:S(2)}) copy-start(f32[2]{0:T(128)} %constant.48.clone) | copy-start | bytes 28
  44.1 2.4 %copy-start.2 = (f32[2]{0:T(128)S(1)}, f32[2]{0:T(128)}, u32[]{:S(2)}) copy-start(f32[2]{0:T(128)} %constant.49.clone) | copy-start | bytes 28
  54.1 6.5 %copy-start = (f32[2,16,30,142]{3,2,0,1:T(8,128)}, f32[2,16,30,142]{3,2,0,1:T(8,128)S(1)}, u32[]{:S(2)}) copy-start(f32[2,16,30,142]{3,2,0,1:T(8,128)S(1)} %add_multiply_fusion.3) | copy-start | bytes 1635844
Sparse Core Ops, SparseCore 0:
  62.1 38.4 reduce-scatter.3

commit v2 on v1

--- a/solution.py
+++ b/solution.py
@@ -163,8 +163,12 @@
     adjoint = adjoint[:, :, inner[0], inner[1]]
     grad_col = -ice_cover[inner] * beta_col[inner] * jnp.sum(adjoint[:, -1] * velocity[:, -1], axis=0)
     block_match = owner_match[inner[0], inner[1]]
-    partial_sum = jnp.sum(jnp.where(block_match, grad_col[:, :, None], 0.0), axis=(0, 1))[None]
-    grad_tiles = lax.psum_scatter(partial_sum, "gy", scatter_dimension=1, tiled=True)
+    partial_sum = jnp.sum(jnp.where(block_match, grad_col[:, :, None], 0.0), axis=(0, 1))
+    owners = lax.axis_size("gy")
+    chunk = tile_count // owners
+    gathered = lax.all_gather(partial_sum.reshape(owners, chunk), "gy")
+    mine = lax.dynamic_index_in_dim(gathered, lax.axis_index("gy"), axis=1, keepdims=False)
+    grad_tiles = jnp.sum(mine, axis=0)[None]
     return (velocity, adjoint, grad_tiles)
 
 

time: 109 us -> 69.6 us (0.64)
  waiting for transfers between devices: 37.6 us -> 1.8 us
  between operations: 15.5 us -> 2.06 us
  blocking collectives: 8.91 us -> 20.5 us
  local copies, waits for them, and re-layouts: 12 us -> 8.86 us
    unnamed x2 -> x0, waiting for transfers between devices: 35.8 us -> none
    all_gather x0 -> x1, blocking collectives: none -> 11.6 us  [local(): gathered = lax.all_gather(partial_sum.reshape(owners, chunk), 'gy')]
    unnamed x128 -> x124, local copies, waits for them, and re-layouts: 7.01 us -> 4.97 us
    slice x1, local copies, waits for them, and re-layouts: 1.27 us -> 0.13 us  [local(): velocity = velocity[:, :, inner[0], inner[1]]]
  transfers between devices with their start and end apart: 7 -> 6, of which waited for: 2 -> 1; matrix products, arithmetic and copies ran while one was open for 8% -> 8% of each run, Pallas kernels for 0% -> 0%
where the time goes in v2:
time: 69.6 us; the launch traced here: 68.9 us
  blocking collectives  20.5 us (29%)
  other arithmetic  20 us (29%)
  starting transfers between devices  15.6 us (22%)
  local copies, waits for them, and re-layouts  8.86 us (13%)
  between operations  2.06 us (3%)
  waiting for transfers between devices  1.8 us (3%)
    all_gather x1, blocking collectives, local(): gathered = lax.all_gather(partial_sum.reshape(owners, chunk), 'gy')  11.6 us
    all_gather x1, blocking collectives, local(): friction_rows = lax.all_gather(strips_near, 'gy', axis=1, tiled=True)  8.91 us
    ppermute x2, starting transfers between devices, with_halo(): lax.ppermute(tail, axis, [(i, (i + 1) % count) for i in range(ends)])  6.79 us
    unnamed x124, local copies, waits for them, and re-layouts  4.97 us
    ppermute x1, starting transfers between devices, local(): lax.ppermute(beta_tiles, 'gx', [(i, i + 1) for i in range(strip_count - 1)])  4.93 us
    add x4, other arithmetic, relax(): right_side = rhs_field + lateral  3.87 us
    unnamed x10, other arithmetic  3.17 us
    add x3, other arithmetic, relax(): lateral + along_y * (south_face * vel_pad[:, :, 1:-1, :-2] + north_face *...  2.78 us
  transfers between devices with their start and end apart: 6, of which 1 were waited for; matrix products, arithmetic and copies ran while one was open for 8% of the time, Pallas kernels for 0%

profile of v2, /device:TPU:0, one launch (start us, length us, event | category | flops | bytes accessed | tf_op | source)
XLA Modules:
  0.0 68.9 jit_solution(2016773956054153151)
XLA Ops:
  0.6 4.9 %collective-permute-start.4 = (f32[1,16]{1,0:T(1,128)}, f32[1,16]{1,0:T(1,128)S(1)}, u32[]{:S(2)}, u32[]{:S(2)}) collective-permute-start(f32[1,16]{1,0:T(1,128)} %param.29), channel_id=1, source_target_pairs={{0,8},{8,16},{16,24},{1,9},{9,17},{17,25},{2,10},{10,18},{18,26},{... | collective-permute-start | bytes 200 | tf_op jit(solution)/shard_map/ppermute | solution.py:104
  5.6 1.3 %collective-permute-start.5 = (f32[1,16]{1,0:T(1,128)}, f32[1,16]{1,0:T(1,128)S(1)}, u32[]{:S(2)}, u32[]{:S(2)}) collective-permute-start(f32[1,16]{1,0:T(1,128)} %param.29), channel_id=1, source_target_pairs={{8,0},{16,8},{24,16},{9,1},{17,9},{25,17},{10,2},{18,10},{26,18},{... | collective-permute-start | bytes 200 | tf_op jit(solution)/shard_map/ppermute | solution.py:106
  6.9 1.0 %constant_dynamic-update-slice_fusion.4 = f32[52,16,128]{2,1,0:T(8,128)S(1)} fusion(f32[32,16,128]{2,1,0:T(8,128)} %bitcast.98), kind=kLoop, calls=%fused_computation.32 | loop fusion | bytes 524288
  7.8 0.9 %constant_dynamic-update-slice_fusion.3 = f32[52,16,128]{2,1,0:T(8,128)S(1)} fusion(f32[52,16,128]{2,1,0:T(8,128)S(1)} %constant_dynamic-update-slice_fusion.4, f32[16,16,128]{2,1,0:T(8,128)} %param.27), kind=kLoop, calls=%fused_computation.31 | loop fusion | bytes 262144
  8.8 0.7 %constant_dynamic-update-slice_fusion.2 = f32[52,16,128]{2,1,0:T(8,128)S(1)} fusion(f32[52,16,128]{2,1,0:T(8,128)S(1)} %constant_dynamic-update-slice_fusion.3, f32[2,16,128]{2,1,0:T(8,128)} %param.28), kind=kLoop, calls=%fused_computation.30 | loop fusion | bytes 32768
  9.5 0.7 %constant_dynamic-update-slice_fusion.1 = f32[52,16,128]{2,1,0:T(8,128)S(1)} fusion(f32[52,16,128]{2,1,0:T(8,128)S(1)} %constant_dynamic-update-slice_fusion.2, s32[16,128]{1,0:T(8,128)} %param.30), kind=kLoop, calls=%fused_computation.29 | loop fusion | flops 2048 | bytes 16384
  10.2 0.7 %constant_dynamic-update-slice_fusion = f32[52,16,128]{2,1,0:T(8,128)S(1)} fusion(f32[52,16,128]{2,1,0:T(8,128)S(1)} %constant_dynamic-update-slice_fusion.1, s32[16,128]{1,0:T(8,128)} %param.31), kind=kLoop, calls=%fused_computation.28 | loop fusion | flops 2048 | bytes 16384 | tf_op jit(solution)/shard_map/concatenate | solution.py:113
  10.9 4.6 %collective-permute-start = (f32[52,7,128]{2,1,0:T(8,128)S(1)}, f32[52,7,128]{2,1,0:T(8,128)S(1)}, u32[]{:S(2)}, u32[]{:S(2)}) collective-permute-start(f32[52,7,128]{2,1,0:T(8,128)S(1)} %get-tuple-element.271), channel_id=1, source_target_pairs={{0,8},{8,16},{16,24},{1,9},{9,17},{17,25},{2,10},{10,18},{18,26},{... | collective-permute-start | bytes 559112 | tf_op jit(solution)/shard_map/ppermute | solution.py:22
  15.5 1.3 %collective-permute-start.1 = (f32[52,7,128]{2,1,0:T(8,128)S(1)}, f32[52,7,128]{2,1,0:T(8,128)S(1)}, u32[]{:S(2)}, u32[]{:S(2)}) collective-permute-start(f32[52,7,128]{2,1,0:T(8,128)S(1)} %get-tuple-element.272), channel_id=1, source_target_pairs={{8,0},{16,8},{24,16},{9,1},{17,9},{25,17},{10,2},{18,10},{26,18},{... | collective-permute-start | bytes 559112 | tf_op jit(solution)/shard_map/ppermute | solution.py:24
  16.9 8.9 %all-gather = f32[8,16,3]{1,2,0:T(4,128)S(1)} all-gather(f32[1,16,3]{1,2,0:T(4,128)S(1)} %maximum_bitcast_fusion.1), channel_id=1, replica_groups=mesh['gx'=4,'gy'=8] {'gy'}, dimensions={0}, use_global_device_ids=true | all-gather | bytes 1728 | tf_op jit(solution)/shard_map/all_gather | solution.py:110
  25.9 0.1 pad_maximum_fusion.1
  26.1 0.3 fusion.218
  26.4 0.6 copy.51
  27.0 2.2 %collective-permute-start.2 = (f32[52,30,7]{0,1,2:T(8,128)S(1)}, f32[52,30,7]{0,1,2:T(8,128)S(1)}, u32[]{:S(2)}, u32[]{:S(2)}) collective-permute-start(f32[52,30,7]{0,1,2:T(8,128)S(1)} %copy.51), channel_id=1, source_target_pairs={{0,1},{1,2},{2,3},{3,4},{4,5},{5,6},{6,7},{8,9},{9,10},{10,11},{11... | collective-permute-start | bytes 131048 | tf_op jit(solution)/shard_map/ppermute | solution.py:22
  29.2 0.6 copy.52
  29.8 1.3 %collective-permute-start.3 = (f32[52,30,7]{0,1,2:T(8,128)S(1)}, f32[52,30,7]{0,1,2:T(8,128)S(1)}, u32[]{:S(2)}, u32[]{:S(2)}) collective-permute-start(f32[52,30,7]{0,1,2:T(8,128)S(1)} %copy.52), channel_id=1, source_target_pairs={{1,0},{2,1},{3,2},{4,3},{5,4},{6,5},{7,6},{9,8},{10,9},{11,10},{12... | collective-permute-start | bytes 131048 | tf_op jit(solution)/shard_map/ppermute | solution.py:24
  31.2 0.8 %copy.53 = f32[52,30,7]{2,1,0:T(8,128)S(1)} copy(f32[52,30,7]{0,1,2:T(8,128)S(1)} %collective-permute-done.2) | data formatting | bytes 87360 | tf_op jit(solution)/shard_map/ppermute | solution.py:22
  32.0 1.8 %collective-permute-done.3 = f32[52,30,7]{0,1,2:T(8,128)S(1)} collective-permute-done((f32[52,30,7]{0,1,2:T(8,128)S(1)}, f32[52,30,7]{0,1,2:T(8,128)S(1)}, u32[]{:S(2)}, u32[]{:S(2)}) %collective-permute-start.3) | collective-permute-done | bytes 43712 | tf_op jit(solution)/shard_map/ppermute | solution.py:24
  33.8 0.8 %copy.54 = f32[52,30,7]{2,1,0:T(8,128)S(1)} copy(f32[52,30,7]{0,1,2:T(8,128)S(1)} %collective-permute-done.3) | data formatting | bytes 87360 | tf_op jit(solution)/shard_map/ppermute | solution.py:24
  34.7 1.0 %pad_maximum_fusion = f32[52,30,142]{2,1,0:T(8,128)S(1)} fusion(f32[52,30,7]{2,1,0:T(8,128)S(1)} %copy.54, f32[52,7,128]{2,1,0:T(8,128)S(1)} %collective-permute-done.1, f32[52,16,128]{2,1,0:T(8,128)S(1)} %constant_dynamic-update-slice_fusion, f32[52,7,128]{2,1,0:T(8,128)S(1)} %collective-permute-done, f32[52,30,7]{2,1,0:T(8,128)S(1)} %copy.53), kind=kLoop, calls=%fused_computation.2 | loop fusion | flops 886080 | bytes 1772160 | tf_op jit(solution)/shard_map/concatenate | solution.py:20
  35.7 0.1 slice.1032
  36.0 0.6 fusion.216
  36.5 0.1 fusion.141
  36.6 0.9 %iota_compare_fusion = pred[30,142,128]{2,1,0:T(8,128)(4,1)S(1)} fusion(s32[30,142]{1,0:T(8,128)S(1)} %fusion.141), kind=kLoop, calls=%fused_computation.1 | loop fusion | flops 545280 | bytes 562320 | tf_op jit(solution)/shard_map/eq | solution.py:136
  37.5 2.2 %select_reduce_fusion = f32[30,142]{1,0:T(8,128)S(1)} fusion(f32[30,128]{1,0:T(8,128)S(1)} %pad_maximum_fusion.2, s32[30,142]{1,0:T(8,128)S(1)} %fusion.141), kind=kLoop, calls=%fused_computation | loop fusion | flops 1631580 | bytes 49440 | tf_op jit(solution)/shard_map/reduce_sum | solution.py:145
  39.8 0.1 broadcast_multiply_fusion.2
  39.9 1.2 %copy_add_fusion = (f32[2,16,30,142]{3,2,0,1:T(8,128)S(1)}, f32[2,16,30,142]{3,2,0,1:T(8,128)S(1)}, f32[2,16,30,142]{3,2,0,1:T(8,128)S(1)}) fusion(f32[2,16,30,142]{3,2,1,0:T(8,128)S(1)} %bitcast.94, f32[30,142]{1,0:T(8,128)S(1)} %get-tuple-element.276, f32[16,30,142]{2,1,0:T(8,128)S(1)} %get-tuple-element.237, f32[30,142]{1,0:T(8,128)S(1)} %get-tuple-element.275, ...), kind=kLoop, calls=%fused_computation.18 | loop fusion | flops 2317440 | bytes 4720096 | tf_op jit(solution)/shard_map/add | solution.py:78
  41.1 0.3 fusion.116
  41.4 0.3 constant_dynamic-update-slice_fusion.20
  42.0 0.1 broadcast_multiply_fusion.1
  42.1 0.9 %add_add_fusion.2 = f32[2,16,30,142]{3,2,0,1:T(8,128)S(1)} fusion(f32[2,16,30,142]{3,2,0,1:T(8,128)S(1)} %broadcast_multiply_fusion.1, f32[2,16,30,142]{3,2,1,0:T(8,128)S(1)} %bitcast.95, f32[16,30,142]{2,1,0:T(8,128)S(1)} %get-tuple-element.237, f32[16,30,142]{2,1,0:T(8,128)S(1)} %get-tuple-element.238, f32[2]{0:T(128)S(1)} %copy-done.1, ...), kind=kLoop, calls=%fused_computation.15 | loop fusion | flops 1363200 | bytes 2726416 | tf_op jit(solution)/shard_map/add | solution.py:78
  43.0 0.2 fusion.98
  43.2 0.3 constant_dynamic-update-slice_fusion.36
  43.7 0.2 add_multiply_fusion.5
  43.9 0.9 %add_add_fusion.1 = f32[2,16,30,142]{3,2,0,1:T(8,128)S(1)} fusion(f32[2,16,30,142]{3,2,0,1:T(8,128)S(1)} %add_multiply_fusion.5, f32[2,16,30,142]{3,2,1,0:T(8,128)S(1)} %bitcast.96, f32[16,30,142]{2,1,0:T(8,128)S(1)} %get-tuple-element.237, f32[16,30,142]{2,1,0:T(8,128)S(1)} %get-tuple-element.238, f32[2]{0:T(128)S(1)} %copy-done.1, ...), kind=kLoop, calls=%fused_computation.13 | loop fusion | flops 1363200 | bytes 2726416 | tf_op jit(solution)/shard_map/add | solution.py:78
  44.8 0.2 fusion.83
  45.0 0.3 constant_dynamic-update-slice_fusion.52
  45.5 0.3 add_multiply_fusion.4
  45.8 0.9 %add_add_fusion = f32[2,16,30,142]{3,2,0,1:T(8,128)S(1)} fusion(f32[2,16,30,142]{3,2,0,1:T(8,128)S(1)} %add_multiply_fusion.4, f32[2,16,30,142]{3,2,1,0:T(8,128)S(1)} %bitcast.97, f32[16,30,142]{2,1,0:T(8,128)S(1)} %get-tuple-element.237, f32[16,30,142]{2,1,0:T(8,128)S(1)} %get-tuple-element.238, f32[2]{0:T(128)S(1)} %copy-done.1, ...), kind=kLoop, calls=%fused_computation.11 | loop fusion | flops 1363200 | bytes 2726416 | tf_op jit(solution)/shard_map/add | solution.py:78
  46.8 0.2 fusion.68
  46.9 0.3 constant_dynamic-update-slice_fusion.68
  47.5 0.3 add_multiply_fusion.3
  47.8 0.2 fusion.52
  48.0 0.3 constant_dynamic-update-slice_fusion.84
  48.6 0.1 broadcast_multiply_fusion
  48.7 0.9 %multiply_add_fusion.2 = f32[2,16,30,142]{3,2,0,1:T(8,128)S(1)} fusion(f32[2,16,30,142]{3,2,0,1:T(8,128)S(1)} %broadcast_multiply_fusion, f32[16,30,142]{2,1,0:T(8,128)S(1)} %get-tuple-element.237, f32[16,30,142]{2,1,0:T(8,128)S(1)} %get-tuple-element.238, f32[2]{0:T(128)S(1)} %copy-done.1, f32[16,30,142]{2,1,0:T(8,128)S(1)} %get-tuple-element.229, ...), kind=kLoop, calls=%fused_computation.9 | loop fusion | flops 1226880 | bytes 2181136 | tf_op jit(solution)/shard_map/add | solution.py:75
  49.6 0.2 fusion.36
  49.8 0.3 constant_dynamic-update-slice_fusion.100
  50.3 0.2 add_multiply_fusion.2
  50.6 0.9 %multiply_add_fusion.1 = f32[2,16,30,142]{3,2,0,1:T(8,128)S(1)} fusion(f32[2,16,30,142]{3,2,0,1:T(8,128)S(1)} %add_multiply_fusion.2, f32[16,30,142]{2,1,0:T(8,128)S(1)} %get-tuple-element.237, f32[16,30,142]{2,1,0:T(8,128)S(1)} %get-tuple-element.238, f32[2]{0:T(128)S(1)} %copy-done.1, f32[16,30,142]{2,1,0:T(8,128)S(1)} %get-tuple-element.229, ...), kind=kLoop, calls=%fused_computation.7 | loop fusion | flops 1226880 | bytes 2181136 | tf_op jit(solution)/shard_map/add | solution.py:75
  51.5 0.2 fusion.20
  51.7 0.3 constant_dynamic-update-slice_fusion.116
  52.2 0.2 add_multiply_fusion.1
  52.4 0.9 %multiply_add_fusion = f32[2,16,30,142]{3,2,0,1:T(8,128)S(1)} fusion(f32[2,16,30,142]{3,2,0,1:T(8,128)S(1)} %add_multiply_fusion.1, f32[16,30,142]{2,1,0:T(8,128)S(1)} %get-tuple-element.237, f32[16,30,142]{2,1,0:T(8,128)S(1)} %get-tuple-element.238, f32[2]{0:T(128)S(1)} %copy-done.1, f32[16,30,142]{2,1,0:T(8,128)S(1)} %get-tuple-element.229, ...), kind=kLoop, calls=%fused_computation.5 | loop fusion | flops 1226880 | bytes 2181136 | tf_op jit(solution)/shard_map/add | solution.py:75
  53.4 0.2 fusion.4
  53.5 0.3 constant_dynamic-update-slice_fusion.132
  54.1 0.3 add_multiply_fusion
  54.5 0.1 slice.1193
  54.6 0.1 slice.1131
  54.8 0.4 select_reduce_fusion.1
  55.3 11.6 %all_gather.7 = f32[8,8,16]{2,1,0:T(8,128)S(1)} all-gather(f32[1,8,16]{2,1,0:T(8,128)S(1)} %all_gather_reshape.3), channel_id=1, replica_groups=mesh['gx'=4,'gy'=8] {'gy'}, dimensions={0}, use_global_device_ids=true | all-gather | bytes 4608 | tf_op jit(solution)/shard_map/all_gather | solution.py:169
  66.9 0.7 %copy.62 = f32[2,16,16,128]{3,2,1,0:T(8,128)} copy(f32[2,16,16,128]{3,2,0,1:T(8,128)S(1)} %slice.1193) | data formatting | bytes 524288
  67.6 0.7 %copy.61 = f32[2,16,16,128]{3,2,1,0:T(8,128)} copy(f32[2,16,16,128]{3,2,0,1:T(8,128)S(1)} %slice.1131) | data formatting | bytes 524288
  68.3 0.5 dynamic-slice_reduce_fusion
  (151 shorter events, 1.6 us)
Async XLA Ops:
  0.6 16.3 %copy-start.2 = (f32[1,16]{1,0:T(1,128)S(1)}, f32[1,16]{1,0:T(1,128)}, u32[]{:S(2)}) copy-start(f32[1,16]{1,0:T(1,128)} %param.29) | copy-start | bytes 196
  0.6 16.2 %collective-permute-start.4 = (f32[1,16]{1,0:T(1,128)}, f32[1,16]{1,0:T(1,128)S(1)}, u32[]{:S(2)}, u32[]{:S(2)}) collective-permute-start(f32[1,16]{1,0:T(1,128)} %param.29), channel_id=1, source_target_pairs={{0,8},{8,16},{16,24},{1,9},{9,17},{17,25},{2,10},{10,18},{18,26},{... | collective-permute-start | bytes 200 | tf_op jit(solution)/shard_map/ppermute | solution.py:104
  5.6 11.3 %collective-permute-start.5 = (f32[1,16]{1,0:T(1,128)}, f32[1,16]{1,0:T(1,128)S(1)}, u32[]{:S(2)}, u32[]{:S(2)}) collective-permute-start(f32[1,16]{1,0:T(1,128)} %param.29), channel_id=1, source_target_pairs={{8,0},{16,8},{24,16},{9,1},{17,9},{25,17},{10,2},{18,10},{26,18},{... | collective-permute-start | bytes 200 | tf_op jit(solution)/shard_map/ppermute | solution.py:106
  10.9 15.0 %collective-permute-start = (f32[52,7,128]{2,1,0:T(8,128)S(1)}, f32[52,7,128]{2,1,0:T(8,128)S(1)}, u32[]{:S(2)}, u32[]{:S(2)}) collective-permute-start(f32[52,7,128]{2,1,0:T(8,128)S(1)} %get-tuple-element.271), channel_id=1, source_target_pairs={{0,8},{8,16},{16,24},{1,9},{9,17},{17,25},{2,10},{10,18},{18,26},{... | collective-permute-start | bytes 559112 | tf_op jit(solution)/shard_map/ppermute | solution.py:22
  15.5 10.5 %collective-permute-start.1 = (f32[52,7,128]{2,1,0:T(8,128)S(1)}, f32[52,7,128]{2,1,0:T(8,128)S(1)}, u32[]{:S(2)}, u32[]{:S(2)}) collective-permute-start(f32[52,7,128]{2,1,0:T(8,128)S(1)} %get-tuple-element.272), channel_id=1, source_target_pairs={{8,0},{16,8},{24,16},{9,1},{17,9},{25,17},{10,2},{18,10},{26,18},{... | collective-permute-start | bytes 559112 | tf_op jit(solution)/shard_map/ppermute | solution.py:24
  27.0 4.2 %collective-permute-start.2 = (f32[52,30,7]{0,1,2:T(8,128)S(1)}, f32[52,30,7]{0,1,2:T(8,128)S(1)}, u32[]{:S(2)}, u32[]{:S(2)}) collective-permute-start(f32[52,30,7]{0,1,2:T(8,128)S(1)} %copy.51), channel_id=1, source_target_pairs={{0,1},{1,2},{2,3},{3,4},{4,5},{5,6},{6,7},{8,9},{9,10},{10,11},{11... | collective-permute-start | bytes 131048 | tf_op jit(solution)/shard_map/ppermute | solution.py:22
  29.8 4.0 %collective-permute-start.3 = (f32[52,30,7]{0,1,2:T(8,128)S(1)}, f32[52,30,7]{0,1,2:T(8,128)S(1)}, u32[]{:S(2)}, u32[]{:S(2)}) collective-permute-start(f32[52,30,7]{0,1,2:T(8,128)S(1)} %copy.52), channel_id=1, source_target_pairs={{1,0},{2,1},{3,2},{4,3},{5,4},{6,5},{7,6},{9,8},{10,9},{11,10},{12... | collective-permute-start | bytes 131048 | tf_op jit(solution)/shard_map/ppermute | solution.py:24
  37.5 2.4 %copy-start = (f32[2]{0:T(128)S(1)}, f32[2]{0:T(128)}, u32[]{:S(2)}) copy-start(f32[2]{0:T(128)} %constant.58.clone) | copy-start | bytes 28
  37.5 2.4 %copy-start.1 = (f32[2]{0:T(128)S(1)}, f32[2]{0:T(128)}, u32[]{:S(2)}) copy-start(f32[2]{0:T(128)} %constant.59.clone) | copy-start | bytes 28

commit v3 on v2

--- a/solution.py
+++ b/solution.py
@@ -96,31 +96,51 @@
     return jnp.pad(field, [(0, 0)] * (field.ndim - 2) + [(1, 1), (1, 1)])
 
 
+def shifted(piece, axis, down):
+    count = lax.axis_size(axis)
+    if down:
+        pairs = [(i, i + 1) for i in range(count - 1)]
+    else:
+        pairs = [(i + 1, i) for i in range(count - 1)]
+    return lax.ppermute(piece, axis, pairs)
+
+
 def local(forcing, viscosity, observed, beta_tiles, ice_mask, tile_owner):
     comps, layers, rows, cols = forcing.shape
-    strip_count = lax.axis_size("gx")
-    strips_near = jnp.concatenate(
-        [
-            lax.ppermute(beta_tiles, "gx", [(i, i + 1) for i in range(strip_count - 1)]),
-            beta_tiles,
-            lax.ppermute(beta_tiles, "gx", [(i + 1, i) for i in range(strip_count - 1)]),
-        ],
-        axis=0,
+    tiles_here = beta_tiles.shape[1]
+    planes = [
+        forcing.reshape(comps * layers, rows, cols),
+        viscosity,
+        observed,
+        ice_mask.astype(jnp.float32)[None],
+        tile_owner.astype(jnp.float32)[None],
+    ]
+    plane_count = sum(p.shape[0] for p in planes)
+
+    beta_plane = jnp.pad(beta_tiles, ((0, HALO - 1), (0, cols - tiles_here)))[None]
+    head = jnp.concatenate([p[:, :HALO] for p in planes] + [beta_plane], axis=0)
+    tail = jnp.concatenate([p[:, rows - HALO:] for p in planes] + [beta_plane], axis=0)
+    from_above = shifted(tail, "gx", True)
+    from_below = shifted(head, "gx", False)
+
+    def stack_rows(lo, hi):
+        return jnp.concatenate(
+            [from_above[:plane_count, :, lo:hi]]
+            + [jnp.concatenate([p[:, :, lo:hi] for p in planes], axis=0)]
+            + [from_below[:plane_count, :, lo:hi]],
+            axis=1,
+        )
+
+    from_left = shifted(stack_rows(cols - HALO, cols), "gy", True)
+    from_right = shifted(stack_rows(0, HALO), "gy", False)
+
+    strips_near = jnp.stack(
+        [from_above[plane_count, 0, :tiles_here], beta_tiles[0], from_below[plane_count, 0, :tiles_here]]
     )
     friction_rows = lax.all_gather(strips_near, "gy", axis=1, tiled=True)
     tile_count = friction_rows.shape[1]
 
-    packed = jnp.concatenate(
-        [
-            forcing.reshape(comps * layers, rows, cols),
-            viscosity,
-            observed,
-            ice_mask.astype(jnp.float32)[None],
-            tile_owner.astype(jnp.float32)[None],
-        ],
-        axis=0,
-    )
-    packed = with_halo(packed, (("gx", 1), ("gy", 2)), HALO)
+    packed = jnp.concatenate([from_left, stack_rows(0, cols), from_right], axis=2)
     ext_rows, ext_cols = packed.shape[1], packed.shape[2]
     at = 0
     forcing_ext = packed[at:at + comps * layers].reshape(comps, layers, ext_rows, ext_cols)

time: 69.6 us -> 69.6 us (level)
  starting transfers between devices: 15.6 us -> 8.81 us
  local copies, waits for them, and re-layouts: 8.86 us -> 13.8 us
  waiting for transfers between devices: 1.8 us -> 3.09 us
    ppermute x6 -> x4, starting transfers between devices: 15.6 us -> 8.81 us  [shifted(): return lax.ppermute(piece, axis, pairs)]
    all_gather x1, blocking collectives: 8.91 us -> 12.8 us  [local(): friction_rows = lax.all_gather(strips_near, 'gy', axis=1, tiled=True)]
    all_gather x1, blocking collectives: 11.6 us -> 8.15 us  [local(): gathered = lax.all_gather(partial_sum.reshape(owners, chunk), 'gy')]
    unnamed x124 -> x145, local copies, waits for them, and re-layouts: 4.97 us -> 6.99 us
    slice x5 -> x19, local copies, waits for them, and re-layouts: 1.61 us -> 3.6 us  [the longest x11 2.74 us: stack_rows(): p[:, :, lo:hi]]
    broadcast_in_dim x0 -> x2, other arithmetic: none -> 1.4 us  [the longest x1 0.7 us: local(): ice_mask.astype(jnp.float32)[None]]
    ppermute x6 -> x4, waiting for transfers between devices: 1.8 us -> 3.09 us  [shifted(): return lax.ppermute(piece, axis, pairs)]
    concatenate x0 -> x3, local copies, waits for them, and re-layouts: none -> 0.93 us  [the longest x1 0.66 us: local(): jnp.concatenate([p[:, rows - HALO:] for p in planes] + [beta_plane], axis=0)]
  transfers between devices with their start and end apart: 6 -> 4, of which waited for: 1 -> 1; matrix products, arithmetic and copies ran while one was open for 8% -> 8% of each run, Pallas kernels for 0% -> 0%
where the time goes in v3:
time: 69.6 us; the launch traced here: 69.1 us
  blocking collectives  20.9 us (30%)
  other arithmetic  20.3 us (29%)
  local copies, waits for them, and re-layouts  13.8 us (20%)
  starting transfers between devices  8.81 us (13%)
  waiting for transfers between devices  3.09 us (4%)
  between operations  2.2 us (3%)
    all_gather x1, blocking collectives, local(): friction_rows = lax.all_gather(strips_near, 'gy', axis=1, tiled=True)  12.8 us
    ppermute x4, starting transfers between devices, shifted(): return lax.ppermute(piece, axis, pairs)  8.81 us
    all_gather x1, blocking collectives, local(): gathered = lax.all_gather(partial_sum.reshape(owners, chunk), 'gy')  8.15 us
    unnamed x145, local copies, waits for them, and re-layouts  6.99 us
    add x4, other arithmetic, relax(): right_side = rhs_field + lateral  3.88 us
    ppermute x4, waiting for transfers between devices, shifted(): return lax.ppermute(piece, axis, pairs)  3.09 us
    add x3, other arithmetic, relax(): lateral + along_y * (south_face * vel_pad[:, :, 1:-1, :-2] + north_face *...  3 us
    slice x11, local copies, waits for them, and re-layouts, stack_rows(): p[:, :, lo:hi]  2.74 us
  transfers between devices with their start and end apart: 4, of which 1 were waited for; matrix products, arithmetic and copies ran while one was open for 8% of the time, Pallas kernels for 0%

profile of v3, /device:TPU:0, one launch (start us, length us, event | category | flops | bytes accessed | tf_op | source)
XLA Modules:
  0.0 69.1 jit_solution(12364120944737393506)
XLA Ops:
  0.7 1.0 %constant_dynamic-update-slice_fusion.5 = (f32[53,7,128]{2,1,0:T(8,128)S(1)}, f32[53,7,128]{2,1,0:T(8,128)S(1)}) fusion(f32[32,16,128]{2,1,0:T(8,128)} %bitcast.109), kind=kLoop, calls=%fused_computation.32 | loop fusion | bytes 491520
  1.7 0.7 %convert_bitcast_fusion.1 = f32[1,16,128]{2,1,0:T(8,128)S(1)} fusion(s32[16,128]{1,0:T(8,128)} %param.30), kind=kLoop, calls=%fused_computation.618 | loop fusion | flops 2048 | bytes 16384 | tf_op jit(solution)/shard_map/broadcast_in_dim | solution.py:115
  2.4 0.7 %convert_bitcast_fusion = f32[1,16,128]{2,1,0:T(8,128)S(1)} fusion(s32[16,128]{1,0:T(8,128)} %param.31), kind=kLoop, calls=%fused_computation.617 | loop fusion | flops 2048 | bytes 16384 | tf_op jit(solution)/shard_map/broadcast_in_dim | solution.py:116
  3.1 0.9 %constant_dynamic-update-slice_fusion.4 = (f32[53,7,128]{2,1,0:T(8,128)S(1)}, f32[53,7,128]{2,1,0:T(8,128)S(1)}) fusion(f32[53,7,128]{2,1,0:T(8,128)S(1)} %get-tuple-element.271, f32[16,16,128]{2,1,0:T(8,128)} %param.27, f32[53,7,128]{2,1,0:T(8,128)S(1)} %get-tuple-element.272), kind=kLoop, calls=%fused_computation.31 | loop fusion | bytes 245760
  4.0 0.7 %constant_dynamic-update-slice_fusion.3 = (f32[53,7,128]{2,1,0:T(8,128)S(1)}, f32[53,7,128]{2,1,0:T(8,128)S(1)}) fusion(f32[53,7,128]{2,1,0:T(8,128)S(1)} %get-tuple-element.279, f32[2,16,128]{2,1,0:T(8,128)} %param.28, f32[53,7,128]{2,1,0:T(8,128)S(1)} %get-tuple-element.280), kind=kLoop, calls=%fused_computation.30 | loop fusion | bytes 30720
  4.7 0.7 constant_dynamic-update-slice_fusion
  5.4 4.9 %collective-permute-start = (f32[53,7,128]{2,1,0:T(8,128)S(1)}, f32[53,7,128]{2,1,0:T(8,128)S(1)}, u32[]{:S(2)}, u32[]{:S(2)}) collective-permute-start(f32[53,7,128]{2,1,0:T(8,128)S(1)} %get-tuple-element.301), channel_id=1, source_target_pairs={{0,8},{8,16},{16,24},{1,9},{9,17},{17,25},{2,10},{10,18},{18,26},{... | collective-permute-start | bytes 569864 | tf_op jit(solution)/shard_map/ppermute | solution.py:105
  10.3 1.3 %collective-permute-start.1 = (f32[53,7,128]{2,1,0:T(8,128)S(1)}, f32[53,7,128]{2,1,0:T(8,128)S(1)}, u32[]{:S(2)}, u32[]{:S(2)}) collective-permute-start(f32[53,7,128]{2,1,0:T(8,128)S(1)} %get-tuple-element.302), channel_id=1, source_target_pairs={{8,0},{16,8},{24,16},{9,1},{17,9},{25,17},{10,2},{18,10},{26,18},{... | collective-permute-start | bytes 569864 | tf_op jit(solution)/shard_map/ppermute | solution.py:105
  11.6 1.2 %fusion.219 = (f32[32,16,7]{2,1,0:T(8,128)S(1)}, f32[32,16,7]{2,1,0:T(8,128)S(1)}) fusion(f32[32,16,128]{2,1,0:T(8,128)} %bitcast.110), kind=kLoop, calls=%fused_computation.629 | loop fusion | bytes 57344 | tf_op jit(solution)/shard_map/slice | solution.py:129
  13.2 0.2 copy.77
  13.4 0.2 copy.78
  13.6 0.2 copy.79
  13.8 0.2 copy.101
  14.0 0.2 copy.102
  14.2 0.2 copy.84
  14.4 0.2 copy.85
  14.6 0.2 copy.86
  14.9 0.2 copy.103
  15.1 0.2 copy.104
  15.9 3.1 %collective-permute-done.1 = f32[53,7,128]{2,1,0:T(8,128)S(1)} collective-permute-done((f32[53,7,128]{2,1,0:T(8,128)S(1)}, f32[53,7,128]{2,1,0:T(8,128)S(1)}, u32[]{:S(2)}, u32[]{:S(2)}) %collective-permute-start.1) | collective-permute-done | bytes 189984 | tf_op jit(solution)/shard_map/ppermute | solution.py:105
  19.3 1.3 %collective-permute-start.2 = (f32[52,30,7]{0,1,2:T(8,128)S(1)}, f32[52,30,7]{0,1,2:T(8,128)S(1)}, u32[]{:S(2)}, u32[]{:S(2)}) collective-permute-start(f32[52,30,7]{0,1,2:T(8,128)S(1)} %pad_maximum_fusion.1), channel_id=1, source_target_pairs={{0,1},{1,2},{2,3},{3,4},{4,5},{5,6},{6,7},{8,9},{9,10},{10,11},{11... | collective-permute-start | bytes 131048 | tf_op jit(solution)/shard_map/ppermute | solution.py:105
  21.0 1.3 %collective-permute-start.3 = (f32[52,30,7]{0,1,2:T(8,128)S(1)}, f32[52,30,7]{0,1,2:T(8,128)S(1)}, u32[]{:S(2)}, u32[]{:S(2)}) collective-permute-start(f32[52,30,7]{0,1,2:T(8,128)S(1)} %pad_maximum_fusion.2), channel_id=1, source_target_pairs={{1,0},{2,1},{3,2},{4,3},{5,4},{6,5},{7,6},{9,8},{10,9},{11,10},{12... | collective-permute-start | bytes 131048 | tf_op jit(solution)/shard_map/ppermute | solution.py:105
  22.3 12.8 %all-gather = f32[8,16,3]{1,2,0:T(4,128)S(1)} all-gather(f32[1,16,3]{1,2,0:T(4,128)S(1)} %maximum_bitcast_fusion.1), channel_id=1, replica_groups=mesh['gx'=4,'gy'=8] {'gy'}, dimensions={0}, use_global_device_ids=true | all-gather | bytes 1728 | tf_op jit(solution)/shard_map/all_gather | solution.py:140
  35.3 0.8 %copy.89 = f32[52,30,7]{2,1,0:T(8,128)S(1)} copy(f32[52,30,7]{0,1,2:T(8,128)S(1)} %collective-permute-done.2) | data formatting | bytes 87360 | tf_op jit(solution)/shard_map/ppermute | solution.py:105
  36.2 0.9 %copy.90 = f32[52,30,7]{2,1,0:T(8,128)S(1)} copy(f32[52,30,7]{0,1,2:T(8,128)S(1)} %collective-permute-done.3) | data formatting | bytes 87360 | tf_op jit(solution)/shard_map/ppermute | solution.py:105
  37.1 1.0 %pad_maximum_fusion = f32[52,30,142]{2,1,0:T(8,128)S(1)} fusion(f32[52,30,7]{2,1,0:T(8,128)S(1)} %copy.90, f32[52,7,128]{2,1,0:T(8,128)S(1)} %slice.1136, f32[52,16,128]{2,1,0:T(8,128)S(1)} %constant_dynamic-update-slice_fusion.12, f32[52,7,128]{2,1,0:T(8,128)S(1)} %slice.1135, f32[52,30,7]{2,1,0:T(8,128)S(1)} %copy.89), kind=kLoop, calls=%fused_computation.2 | loop fusion | flops 886080 | bytes 1772160 | tf_op jit(solution)/shard_map/concatenate | solution.py:143
  38.3 1.1 %copy-done = f32[52,30,142]{2,1,0:T(8,128)} copy-done((f32[52,30,142]{2,1,0:T(8,128)}, f32[52,30,142]{2,1,0:T(8,128)S(1)}, u32[]{:S(2)}) %copy-start) | copy-done | bytes 886104
  39.6 0.9 %iota_compare_fusion = pred[30,142,128]{2,1,0:T(8,128)(4,1)S(1)} fusion(s32[30,142]{1,0:T(8,128)S(1)} %fusion.141), kind=kLoop, calls=%fused_computation.1 | loop fusion | flops 545280 | bytes 562320 | tf_op jit(solution)/shard_map/eq | solution.py:156
  40.4 2.2 %select_reduce_fusion = f32[30,142]{1,0:T(8,128)S(1)} fusion(f32[30,128]{1,0:T(8,128)S(1)} %pad_maximum_fusion.3, s32[30,142]{1,0:T(8,128)S(1)} %fusion.141), kind=kLoop, calls=%fused_computation | loop fusion | flops 1631580 | bytes 49440 | tf_op jit(solution)/shard_map/reduce_sum | solution.py:165
  42.7 0.5 fusion.216
  43.4 1.2 %copy_add_fusion = (f32[2,16,30,142]{3,2,0,1:T(8,128)S(1)}, f32[2,16,30,142]{3,2,0,1:T(8,128)S(1)}, f32[2,16,30,142]{3,2,0,1:T(8,128)S(1)}) fusion(f32[2,16,30,142]{3,2,1,0:T(8,128)S(1)} %bitcast.105, f32[30,142]{1,0:T(8,128)S(1)} %get-tuple-element.284, f32[16,30,142]{2,1,0:T(8,128)S(1)} %get-tuple-element.235, f32[30,142]{1,0:T(8,128)S(1)} %get-tuple-element.283, ...), kind=kLoop, calls=%fused_computation.18 | loop fusion | flops 2317440 | bytes 4720096 | tf_op jit(solution)/shard_map/add | solution.py:78
  44.6 0.3 fusion.116
  44.9 0.3 constant_dynamic-update-slice_fusion.32
  45.6 0.9 %add_add_fusion.2 = f32[2,16,30,142]{3,2,0,1:T(8,128)S(1)} fusion(f32[2,16,30,142]{3,2,0,1:T(8,128)S(1)} %broadcast_multiply_fusion.1, f32[2,16,30,142]{3,2,1,0:T(8,128)S(1)} %bitcast.106, f32[16,30,142]{2,1,0:T(8,128)S(1)} %get-tuple-element.235, f32[16,30,142]{2,1,0:T(8,128)S(1)} %get-tuple-element.236, f32[2]{0:T(128)S(1)} %copy-done.7, ...), kind=kLoop, calls=%fused_computation.15 | loop fusion | flops 1363200 | bytes 2726416 | tf_op jit(solution)/shard_map/add | solution.py:78
  46.5 0.2 fusion.98
  46.7 0.3 constant_dynamic-update-slice_fusion.48
  47.2 0.2 add_multiply_fusion.5
  47.4 0.9 %add_add_fusion.1 = f32[2,16,30,142]{3,2,0,1:T(8,128)S(1)} fusion(f32[2,16,30,142]{3,2,0,1:T(8,128)S(1)} %add_multiply_fusion.5, f32[2,16,30,142]{3,2,1,0:T(8,128)S(1)} %bitcast.107, f32[16,30,142]{2,1,0:T(8,128)S(1)} %get-tuple-element.235, f32[16,30,142]{2,1,0:T(8,128)S(1)} %get-tuple-element.236, f32[2]{0:T(128)S(1)} %copy-done.7, ...), kind=kLoop, calls=%fused_computation.13 | loop fusion | flops 1363200 | bytes 2726416 | tf_op jit(solution)/shard_map/add | solution.py:78
  48.3 0.2 fusion.83
  48.5 0.3 constant_dynamic-update-slice_fusion.64
  49.0 0.3 add_multiply_fusion.4
  49.3 0.9 %add_add_fusion = f32[2,16,30,142]{3,2,0,1:T(8,128)S(1)} fusion(f32[2,16,30,142]{3,2,0,1:T(8,128)S(1)} %add_multiply_fusion.4, f32[2,16,30,142]{3,2,1,0:T(8,128)S(1)} %bitcast.108, f32[16,30,142]{2,1,0:T(8,128)S(1)} %get-tuple-element.235, f32[16,30,142]{2,1,0:T(8,128)S(1)} %get-tuple-element.236, f32[2]{0:T(128)S(1)} %copy-done.7, ...), kind=kLoop, calls=%fused_computation.11 | loop fusion | flops 1363200 | bytes 2726416 | tf_op jit(solution)/shard_map/add | solution.py:78
  50.3 0.2 fusion.68
  50.4 0.3 constant_dynamic-update-slice_fusion.80
  51.0 0.3 add_multiply_fusion.3
  51.3 0.2 fusion.52
  51.5 0.3 constant_dynamic-update-slice_fusion.96
  52.2 0.9 %multiply_add_fusion.2 = f32[2,16,30,142]{3,2,0,1:T(8,128)S(1)} fusion(f32[2,16,30,142]{3,2,0,1:T(8,128)S(1)} %broadcast_multiply_fusion, f32[16,30,142]{2,1,0:T(8,128)S(1)} %get-tuple-element.235, f32[16,30,142]{2,1,0:T(8,128)S(1)} %get-tuple-element.236, f32[2]{0:T(128)S(1)} %copy-done.7, f32[16,30,142]{2,1,0:T(8,128)S(1)} %get-tuple-element.229, ...), kind=kLoop, calls=%fused_computation.9 | loop fusion | flops 1226880 | bytes 2181136 | tf_op jit(solution)/shard_map/add | solution.py:75
  53.1 0.2 fusion.36
  53.3 0.3 constant_dynamic-update-slice_fusion.112
  53.8 0.2 add_multiply_fusion.2
  54.1 0.9 %multiply_add_fusion.1 = f32[2,16,30,142]{3,2,0,1:T(8,128)S(1)} fusion(f32[2,16,30,142]{3,2,0,1:T(8,128)S(1)} %add_multiply_fusion.2, f32[16,30,142]{2,1,0:T(8,128)S(1)} %get-tuple-element.235, f32[16,30,142]{2,1,0:T(8,128)S(1)} %get-tuple-element.236, f32[2]{0:T(128)S(1)} %copy-done.7, f32[16,30,142]{2,1,0:T(8,128)S(1)} %get-tuple-element.229, ...), kind=kLoop, calls=%fused_computation.7 | loop fusion | flops 1226880 | bytes 2181136 | tf_op jit(solution)/shard_map/add | solution.py:75
  55.0 0.2 fusion.20
  55.2 0.3 constant_dynamic-update-slice_fusion.128
  55.7 0.2 add_multiply_fusion.1
  55.9 1.1 %multiply_add_fusion = f32[2,16,30,142]{3,2,0,1:T(8,128)S(1)} fusion(f32[2,16,30,142]{3,2,0,1:T(8,128)S(1)} %add_multiply_fusion.1, f32[16,30,142]{2,1,0:T(8,128)S(1)} %get-tuple-element.235, f32[16,30,142]{2,1,0:T(8,128)S(1)} %get-tuple-element.236, f32[2]{0:T(128)S(1)} %copy-done.7, f32[16,30,142]{2,1,0:T(8,128)S(1)} %get-tuple-element.229, ...), kind=kLoop, calls=%fused_computation.5 | loop fusion | flops 1226880 | bytes 2181136 | tf_op jit(solution)/shard_map/add | solution.py:75
  57.1 0.2 fusion.4
  57.3 0.3 constant_dynamic-update-slice_fusion.144
  57.8 0.3 add_multiply_fusion
  58.5 0.4 select_reduce_fusion.1
  59.0 8.1 %all_gather.7 = f32[8,8,16]{2,1,0:T(8,128)S(1)} all-gather(f32[1,8,16]{2,1,0:T(8,128)S(1)} %all_gather_reshape.3), channel_id=1, replica_groups=mesh['gx'=4,'gy'=8] {'gy'}, dimensions={0}, use_global_device_ids=true | all-gather | bytes 4608 | tf_op jit(solution)/shard_map/all_gather | solution.py:189
  67.1 0.7 %copy.98 = f32[2,16,16,128]{3,2,1,0:T(8,128)} copy(f32[2,16,16,128]{3,2,0,1:T(8,128)S(1)} %slice.1305) | data formatting | bytes 524288
  67.9 0.7 %copy.97 = f32[2,16,16,128]{3,2,1,0:T(8,128)} copy(f32[2,16,16,128]{3,2,0,1:T(8,128)S(1)} %slice.1243) | data formatting | bytes 524288
  68.6 0.5 dynamic-slice_reduce_fusion
  (191 shorter events, 3.9 us)
Async XLA Ops:
  0.6 12.5 %copy-start.1 = (f32[2,16,16,128]{3,2,1,0:T(8,128)S(1)}, f32[2,16,16,128]{3,2,1,0:T(8,128)}, u32[]{:S(2)}) copy-start(f32[2,16,16,128]{3,2,1,0:T(8,128)} %param.26) | copy-start | bytes 786436
  0.6 12.3 %copy-start.2 = (f32[16,16,128]{2,1,0:T(8,128)S(1)}, f32[16,16,128]{2,1,0:T(8,128)}, u32[]{:S(2)}) copy-start(f32[16,16,128]{2,1,0:T(8,128)} %param.27) | copy-start | bytes 393220
  0.7 12.4 %copy-start.3 = (f32[2,16,128]{2,1,0:T(8,128)S(1)}, f32[2,16,128]{2,1,0:T(8,128)}, u32[]{:S(2)}) copy-start(f32[2,16,128]{2,1,0:T(8,128)} %param.28) | copy-start | bytes 49156
  5.4 10.3 %collective-permute-start = (f32[53,7,128]{2,1,0:T(8,128)S(1)}, f32[53,7,128]{2,1,0:T(8,128)S(1)}, u32[]{:S(2)}, u32[]{:S(2)}) collective-permute-start(f32[53,7,128]{2,1,0:T(8,128)S(1)} %get-tuple-element.301), channel_id=1, source_target_pairs={{0,8},{8,16},{16,24},{1,9},{9,17},{17,25},{2,10},{10,18},{18,26},{... | collective-permute-start | bytes 569864 | tf_op jit(solution)/shard_map/ppermute | solution.py:105
  10.3 8.7 %collective-permute-start.1 = (f32[53,7,128]{2,1,0:T(8,128)S(1)}, f32[53,7,128]{2,1,0:T(8,128)S(1)}, u32[]{:S(2)}, u32[]{:S(2)}) collective-permute-start(f32[53,7,128]{2,1,0:T(8,128)S(1)} %get-tuple-element.302), channel_id=1, source_target_pairs={{8,0},{16,8},{24,16},{9,1},{17,9},{25,17},{10,2},{18,10},{26,18},{... | collective-permute-start | bytes 569864 | tf_op jit(solution)/shard_map/ppermute | solution.py:105
  12.8 2.5 %copy-start.4 = (s32[16,128]{1,0:T(8,128)S(1)}, s32[16,128]{1,0:T(8,128)}, u32[]{:S(2)}) copy-start(s32[16,128]{1,0:T(8,128)} %param.30) | copy-start | bytes 24580
  12.9 2.7 %copy-start.5 = (s32[16,128]{1,0:T(8,128)S(1)}, s32[16,128]{1,0:T(8,128)}, u32[]{:S(2)}) copy-start(s32[16,128]{1,0:T(8,128)} %param.31) | copy-start | bytes 24580
  15.5 6.8 %copy-start.8 = (f32[1,16]{1,0:T(1,128)S(1)}, f32[1,16]{1,0:T(1,128)}, u32[]{:S(2)}) copy-start(f32[1,16]{1,0:T(1,128)} %param.29) | copy-start | bytes 196
  19.3 16.0 %collective-permute-start.2 = (f32[52,30,7]{0,1,2:T(8,128)S(1)}, f32[52,30,7]{0,1,2:T(8,128)S(1)}, u32[]{:S(2)}, u32[]{:S(2)}) collective-permute-start(f32[52,30,7]{0,1,2:T(8,128)S(1)} %pad_maximum_fusion.1), channel_id=1, source_target_pairs={{0,1},{1,2},{2,3},{3,4},{4,5},{5,6},{6,7},{8,9},{9,10},{10,11},{11... | collective-permute-start | bytes 131048 | tf_op jit(solution)/shard_map/ppermute | solution.py:105
  21.0 15.2 %collective-permute-start.3 = (f32[52,30,7]{0,1,2:T(8,128)S(1)}, f32[52,30,7]{0,1,2:T(8,128)S(1)}, u32[]{:S(2)}, u32[]{:S(2)}) collective-permute-start(f32[52,30,7]{0,1,2:T(8,128)S(1)} %pad_maximum_fusion.2), channel_id=1, source_target_pairs={{1,0},{2,1},{3,2},{4,3},{5,4},{6,5},{7,6},{9,8},{10,9},{11,10},{12... | collective-permute-start | bytes 131048 | tf_op jit(solution)/shard_map/ppermute | solution.py:105
  38.1 1.2 %copy-start = (f32[52,30,142]{2,1,0:T(8,128)}, f32[52,30,142]{2,1,0:T(8,128)S(1)}, u32[]{:S(2)}) copy-start(f32[52,30,142]{2,1,0:T(8,128)S(1)} %pad_maximum_fusion) | copy-start | bytes 2658244
  39.4 3.2 %slice-start = ((f32[52,30,142]{2,1,0:T(8,128)}), f32[16,30,142]{2,1,0:T(8,128)S(1)}, s32[]{:S(2)}) async-start(f32[52,30,142]{2,1,0:T(8,128)} %copy-done), calls=%async_computation | async-start | bytes 1048576 | tf_op jit(solution)/shard_map/slice | solution.py:148
  42.7 0.7 %copy-start.6 = (f32[2]{0:T(128)S(1)}, f32[2]{0:T(128)}, u32[]{:S(2)}) copy-start(f32[2]{0:T(128)} %constant.58.clone) | copy-start | bytes 28
  42.7 0.7 %copy-start.7 = (f32[2]{0:T(128)S(1)}, f32[2]{0:T(128)}, u32[]{:S(2)}) copy-start(f32[2]{0:T(128)} %constant.59.clone) | copy-start | bytes 28

commit v4 on v3

--- a/solution.py
+++ b/solution.py
@@ -1,6 +1,8 @@
 import jax
 import jax.numpy as jnp
 from jax import lax
+from jax.experimental import pallas as pl
+from jax.experimental.pallas import tpu as pltpu
 from jax.sharding import PartitionSpec as P
 
 PASSES = 4
@@ -96,6 +98,123 @@
     return jnp.pad(field, [(0, 0)] * (field.ndim - 2) + [(1, 1), (1, 1)])
 
 
+WEIGHTS = ((4.0, 1.0), (1.0, 4.0))
+
+
+def passes_kernel(forcing_ref, visc_ref, obs_ref, ice_ref, beta_ref, vel_ref, adj_ref,
+                  face_ref, link_ref, ratio_ref, inv_ref, iter_ref, fwd_ref, misfit_ref):
+    comps, layers, tall, wide = forcing_ref.shape
+    rows, cols = vel_ref.shape[2], vel_ref.shape[3]
+    ice = ice_ref[...]
+
+    def along_rows(x, step):
+        return pltpu.roll(x, step % tall, 0)
+
+    def along_cols(x, step):
+        return pltpu.roll(x, step % wide, 1)
+
+    for k in range(layers):
+        visc = visc_ref[k]
+        face_ref[0, k] = 0.5 * (visc + along_rows(visc, 1))
+        face_ref[1, k] = 0.5 * (visc + along_rows(visc, -1))
+        face_ref[2, k] = 0.5 * (visc + along_cols(visc, 1))
+        face_ref[3, k] = 0.5 * (visc + along_cols(visc, -1))
+        if k == 0:
+            link_ref[0] = jnp.zeros_like(visc)
+        else:
+            link_ref[k] = (VERTICAL * 0.5) * (visc_ref[k - 1] + visc)
+
+    open_water = 1.0 - ice
+    for c in range(comps):
+        wx, wy = WEIGHTS[c]
+        ratio_prev = None
+        for k in range(layers):
+            diag = wx * (face_ref[0, k] + face_ref[1, k]) + wy * (face_ref[2, k] + face_ref[3, k])
+            lower = link_ref[k]
+            upper = link_ref[k + 1] if k < layers - 1 else None
+            if upper is not None:
+                diag = diag + upper
+            diag = diag + lower
+            if k == layers - 1:
+                diag = diag + beta_ref[...]
+            diag = diag + open_water
+            pivot = diag if k == 0 else diag + lower * ratio_prev
+            inverse = 1.0 / pivot
+            inv_ref[c, k] = inverse
+            ratio_prev = -upper * inverse if upper is not None else jnp.zeros_like(inverse)
+            ratio_ref[c, k] = ratio_prev
+
+    def run_pass(src, dst, forced, first):
+        for c in range(comps):
+            wx, wy = WEIGHTS[c]
+
+            def right_side(k, base):
+                if first:
+                    return base
+                u = iter_ref[src, c, k]
+                lateral = wx * (face_ref[0, k] * along_rows(u, 1) + face_ref[1, k] * along_rows(u, -1))
+                lateral = lateral + wy * (face_ref[2, k] * along_cols(u, 1) + face_ref[3, k] * along_cols(u, -1))
+                return lateral if base is None else base + lateral
+
+            if forced:
+                base0 = forcing_ref[c, 0]
+            else:
+                base0 = misfit_ref[c]
+            f0 = right_side(0, base0) * inv_ref[c, 0]
+            fwd_ref[0] = f0
+
+            def down(k, f_prev):
+                base = forcing_ref[c, k] if forced else None
+                value = right_side(k, base)
+                if value is None:
+                    value = jnp.zeros_like(f_prev)
+                value = value + link_ref[k] * f_prev
+                f = value * inv_ref[c, k]
+                fwd_ref[k] = f
+                return f
+
+            lax.fori_loop(1, layers, down, f0)
+
+            def put(k, line):
+                if first:
+                    iter_ref[dst, c, k] = ice * (OMEGA * line)
+                else:
+                    iter_ref[dst, c, k] = ice * ((1.0 - OMEGA) * iter_ref[src, c, k] + OMEGA * line)
+
+            last = fwd_ref[layers - 1]
+            put(layers - 1, last)
+
+            def up(j, s_next):
+                k = layers - 2 - j
+                line = fwd_ref[k] - ratio_ref[c, k] * s_next
+                put(k, line)
+                return line
+
+            lax.fori_loop(0, layers - 1, up, last)
+
+    def inner(x):
+        x = along_cols(along_rows(x, -HALO), -HALO)
+        return x[:rows, :cols]
+
+    buf = 0
+    for sweep_idx in range(PASSES):
+        run_pass(1 - buf, buf, True, sweep_idx == 0)
+        buf = 1 - buf
+    velocity_buf = 1 - buf
+    for c in range(comps):
+        misfit_ref[c] = iter_ref[velocity_buf, c, 0] - obs_ref[c]
+        for k in range(layers):
+            vel_ref[c, k] = inner(iter_ref[velocity_buf, c, k])
+    buf = 0
+    for sweep_idx in range(PASSES):
+        run_pass(1 - buf, buf, False, sweep_idx == 0)
+        buf = 1 - buf
+    adjoint_buf = 1 - buf
+    for c in range(comps):
+        for k in range(layers):
+            adj_ref[c, k] = inner(iter_ref[adjoint_buf, c, k])
+
+
 def shifted(piece, axis, down):
     count = lax.axis_size(axis)
     if down:
@@ -164,23 +283,30 @@
     )
     beta_col = jnp.sum(jnp.where(owner_match, row_strip[:, None, :], 0.0), axis=-1)
 
-    faces, lower_link, ratios, inverses = prepare(pad_cells(visc_ext), beta_col, ice_cover)
-
-    def advance(field, rhs_field):
-        return relax(pad_cells(field), rhs_field, faces, lower_link, ratios, inverses, ice_cover)
-
-    velocity = jnp.zeros_like(forcing_ext)
-    for sweep_idx in range(PASSES):
-        velocity = advance(velocity, forcing_ext)
-    misfit = velocity[:, 0] - observed_ext
-    adjoint_rhs = jnp.zeros_like(forcing_ext).at[:, 0].set(misfit)
-    adjoint = jnp.zeros_like(forcing_ext)
-    for sweep_idx in range(PASSES):
-        adjoint = advance(adjoint, adjoint_rhs)
+    tall = -(-ext_rows // 8) * 8
+    wide = -(-ext_cols // 128) * 128
+
+    def fit(x):
+        return jnp.pad(x, [(0, 0)] * (x.ndim - 2) + [(0, tall - ext_rows), (0, wide - ext_cols)])
+
+    grid_shape = (comps, layers, tall, wide)
+    scratch = [
+        pltpu.VMEM((4, layers, tall, wide), jnp.float32),
+        pltpu.VMEM((layers, tall, wide), jnp.float32),
+        pltpu.VMEM(grid_shape, jnp.float32),
+        pltpu.VMEM(grid_shape, jnp.float32),
+        pltpu.VMEM((2,) + grid_shape, jnp.float32),
+        pltpu.VMEM((layers, tall, wide), jnp.float32),
+        pltpu.VMEM((comps, tall, wide), jnp.float32),
+    ]
+    out_shape = jax.ShapeDtypeStruct(forcing.shape, jnp.float32)
+    velocity, adjoint = pl.pallas_call(
+        passes_kernel,
+        out_shape=(out_shape, out_shape),
+        scratch_shapes=scratch,
+    )(fit(forcing_ext), fit(visc_ext), fit(observed_ext), fit(ice_cover), fit(beta_col))
 
     inner = (slice(HALO, HALO + rows), slice(HALO, HALO + cols))
-    velocity = velocity[:, :, inner[0], inner[1]]
-    adjoint = adjoint[:, :, inner[0], inner[1]]
     grad_col = -ice_cover[inner] * beta_col[inner] * jnp.sum(adjoint[:, -1] * velocity[:, -1], axis=0)
     block_match = owner_match[inner[0], inner[1]]
     partial_sum = jnp.sum(jnp.where(block_match, grad_col[:, :, None], 0.0), axis=(0, 1))

time: 69.6 us -> 84.6 us (1.22)
  Pallas kernels: 0 us -> 24.3 us
  other arithmetic: 20.3 us -> 7.94 us
  blocking collectives: 20.9 us -> 23 us
  starting transfers between devices: 8.81 us -> 10.5 us
  between operations: 2.2 us -> 1.01 us
    pallas_call x0 -> x1, Pallas kernels: none -> 24.3 us  [local(): pl.pallas_call(passes_kernel, out_shape=(out_shape, out_shape), scratch_s...]
    add x8 -> x0, other arithmetic: 7.42 us -> none  [the longest x4 3.88 us: relax(): right_side = rhs_field + lateral]
    all_gather x1, blocking collectives: 8.15 us -> 14.1 us  [local(): gathered = lax.all_gather(partial_sum.reshape(owners, chunk), 'gy')]
    all_gather x1, blocking collectives: 12.8 us -> 8.91 us  [local(): friction_rows = lax.all_gather(strips_near, 'gy', axis=1, tiled=True)]
    mul x20 -> x0, other arithmetic: 3.53 us -> none  [the longest x9 1.84 us: relax(): return ice_cover * ((1.0 - OMEGA) * centre + OMEGA * line_value)]
    pad x0 -> x4, local copies, waits for them, and re-layouts: none -> 3.15 us  [fit(): jnp.pad(x, [(0, 0)] * (x.ndim - 2) + [(0, tall - ext_rows), (0, wide - ex...]
    unnamed x145 -> x27, local copies, waits for them, and re-layouts: 6.99 us -> 3.9 us
    unnamed x10 -> x2, other arithmetic: 2.48 us -> 0.01 us
  transfers between devices with their start and end apart: 4 -> 4, of which waited for: 1 -> 2; matrix products, arithmetic and copies ran while one was open for 8% -> 7% of each run, Pallas kernels for 0% -> 0%
where the time goes in v4:
time: 84.6 us; the launch traced here: 84 us
  Pallas kernels  24.3 us (29%)
  blocking collectives  23 us (27%)
  local copies, waits for them, and re-layouts  14.2 us (17%)
  starting transfers between devices  10.5 us (12%)
  other arithmetic  7.94 us (9%)
  waiting for transfers between devices  3.02 us (4%)
  between operations  1.01 us (1%)
    pallas_call x1, Pallas kernels, local(): pl.pallas_call(passes_kernel, out_shape=(out_shape, out_shape), scratch_s...  24.3 us
    all_gather x1, blocking collectives, local(): gathered = lax.all_gather(partial_sum.reshape(owners, chunk), 'gy')  14.1 us
    ppermute x4, starting transfers between devices, shifted(): return lax.ppermute(piece, axis, pairs)  10.5 us
    all_gather x1, blocking collectives, local(): friction_rows = lax.all_gather(strips_near, 'gy', axis=1, tiled=True)  8.91 us
    unnamed x27, local copies, waits for them, and re-layouts  3.9 us
    slice x11, local copies, waits for them, and re-layouts, stack_rows(): p[:, :, lo:hi]  3.48 us
    pad x4, local copies, waits for them, and re-layouts, fit(): jnp.pad(x, [(0, 0)] * (x.ndim - 2) + [(0, tall - ext_rows), (0, wide - ex...  3.15 us
    ppermute x4, waiting for transfers between devices, shifted(): return lax.ppermute(piece, axis, pairs)  3.02 us
  transfers between devices with their start and end apart: 4, of which 2 were waited for; matrix products, arithmetic and copies ran while one was open for 7% of the time, Pallas kernels for 0%

profile of v4, /device:TPU:0, one launch (start us, length us, event | category | flops | bytes accessed | tf_op | source)
XLA Modules:
  0.0 84.0 jit_solution(283763356774186895)
XLA Ops:
  0.6 0.0 copy-start.1
  0.6 0.7 convert_bitcast_fusion.1
  1.4 0.7 convert_bitcast_fusion
  2.1 1.0 %slice_dynamic-update-slice_fusion.1 = (f32[53,7,128]{2,1,0:T(8,128)S(1)}, f32[53,7,128]{2,1,0:T(8,128)S(1)}) fusion(f32[32,16,128]{2,1,0:T(8,128)} %bitcast.36), kind=kLoop, calls=%fused_computation.5 | loop fusion | bytes 491520
  3.1 0.0 copy-start.2
  3.1 0.9 %slice_dynamic-update-slice_fusion.3 = (f32[53,7,128]{2,1,0:T(8,128)S(1)}, f32[53,7,128]{2,1,0:T(8,128)S(1)}) fusion(f32[53,7,128]{2,1,0:T(8,128)S(1)} %get-tuple-element.11, f32[16,16,128]{2,1,0:T(8,128)} %param.7, f32[53,7,128]{2,1,0:T(8,128)S(1)} %get-tuple-element.12), kind=kLoop, calls=%fused_computation.22 | loop fusion | bytes 245760
  4.0 0.0 copy-start.3
  4.0 0.8 constant_dynamic-update-slice_fusion.3
  4.8 0.7 constant_dynamic-update-slice_fusion
  5.5 4.9 %collective-permute-start = (f32[53,7,128]{2,1,0:T(8,128)S(1)}, f32[53,7,128]{2,1,0:T(8,128)S(1)}, u32[]{:S(2)}, u32[]{:S(2)}) collective-permute-start(f32[53,7,128]{2,1,0:T(8,128)S(1)} %get-tuple-element.36), channel_id=1, source_target_pairs={{0,8},{8,16},{16,24},{1,9},{9,17},{17,25},{2,10},{10,18},{18,26},{... | collective-permute-start | bytes 569864 | tf_op jit(solution)/shard_map/ppermute | solution.py:224
  10.4 1.3 %collective-permute-start.1 = (f32[53,7,128]{2,1,0:T(8,128)S(1)}, f32[53,7,128]{2,1,0:T(8,128)S(1)}, u32[]{:S(2)}, u32[]{:S(2)}) collective-permute-start(f32[53,7,128]{2,1,0:T(8,128)S(1)} %get-tuple-element.37), channel_id=1, source_target_pairs={{8,0},{16,8},{24,16},{9,1},{17,9},{25,17},{10,2},{18,10},{26,18},{... | collective-permute-start | bytes 569864 | tf_op jit(solution)/shard_map/ppermute | solution.py:224
  11.7 0.1 fusion.16
  11.8 0.1 fusion.17
  11.9 0.9 %fusion.15 = (f32[2,16,7]{2,1,0:T(8,128)S(1)}, f32[2,16,7]{2,1,0:T(8,128)S(1)}) fusion(f32[2,16,128]{2,1,0:T(8,128)} %param.8), kind=kLoop, calls=%fused_computation.57 | loop fusion | bytes 3584 | tf_op jit(solution)/shard_map/slice | solution.py:248
  12.7 1.1 %fusion.14 = (f32[16,16,7]{2,1,0:T(8,128)S(1)}, f32[16,16,7]{2,1,0:T(8,128)S(1)}) fusion(f32[16,16,128]{2,1,0:T(8,128)} %param.7), kind=kLoop, calls=%fused_computation.56 | loop fusion | bytes 28672 | tf_op jit(solution)/shard_map/slice | solution.py:248
  13.8 0.0 copy-start.5
  13.9 0.1 fusion.11
  14.0 0.2 copy.45
  14.2 0.2 copy.30
  14.4 0.2 copy.31
  14.6 0.2 copy.47
  14.9 0.2 copy.37
  15.1 0.2 copy.38
  15.3 0.0 copy-start.6
  15.3 0.2 copy.44
  15.5 0.2 copy.46
  15.8 0.2 copy.29
  16.0 0.2 copy.36
  16.2 0.1 concatenate.31
  16.3 0.1 concatenate.36
  16.5 0.0 collective-permute-done
  16.5 0.1 fusion.12
  16.6 0.2 copy.32
  16.8 0.2 copy.39
  16.9 2.2 %collective-permute-done.1 = f32[53,7,128]{2,1,0:T(8,128)S(1)} collective-permute-done((f32[53,7,128]{2,1,0:T(8,128)S(1)}, f32[53,7,128]{2,1,0:T(8,128)S(1)}, u32[]{:S(2)}, u32[]{:S(2)}) %collective-permute-start.1) | collective-permute-done | bytes 189984 | tf_op jit(solution)/shard_map/ppermute | solution.py:224
  19.1 8.9 %all-gather = f32[8,16,3]{1,2,0:T(4,128)S(1)} all-gather(f32[1,16,3]{1,2,0:T(4,128)S(1)} %maximum_bitcast_fusion.1), channel_id=1, replica_groups=mesh['gx'=4,'gy'=8] {'gy'}, dimensions={0}, use_global_device_ids=true | all-gather | bytes 1728 | tf_op jit(solution)/shard_map/all_gather | solution.py:259
  28.0 0.1 reshape.24
  28.1 0.1 fusion.13
  28.2 0.2 copy.33
  28.4 0.2 copy.40
  28.6 1.3 %collective-permute-start.3 = (f32[52,30,7]{0,1,2:T(8,128)S(1)}, f32[52,30,7]{0,1,2:T(8,128)S(1)}, u32[]{:S(2)}, u32[]{:S(2)}) collective-permute-start(f32[52,30,7]{0,1,2:T(8,128)S(1)} %pad_maximum_fusion.2), channel_id=1, source_target_pairs={{1,0},{2,1},{3,2},{4,3},{5,4},{6,5},{7,6},{9,8},{10,9},{11,10},{12... | collective-permute-start | bytes 131048 | tf_op jit(solution)/shard_map/ppermute | solution.py:224
  29.9 3.0 %collective-permute-start.2 = (f32[52,30,7]{0,1,2:T(8,128)S(1)}, f32[52,30,7]{0,1,2:T(8,128)S(1)}, u32[]{:S(2)}, u32[]{:S(2)}) collective-permute-start(f32[52,30,7]{0,1,2:T(8,128)S(1)} %pad_maximum_fusion.1), channel_id=1, source_target_pairs={{0,1},{1,2},{2,3},{3,4},{4,5},{5,6},{6,7},{8,9},{9,10},{10,11},{11... | collective-permute-start | bytes 131048 | tf_op jit(solution)/shard_map/ppermute | solution.py:224
  33.1 0.8 %collective-permute-done.2 = f32[52,30,7]{0,1,2:T(8,128)S(1)} collective-permute-done((f32[52,30,7]{0,1,2:T(8,128)S(1)}, f32[52,30,7]{0,1,2:T(8,128)S(1)}, u32[]{:S(2)}, u32[]{:S(2)}) %collective-permute-start.2) | collective-permute-done | bytes 43712 | tf_op jit(solution)/shard_map/ppermute | solution.py:224
  33.9 0.8 %copy.41 = f32[52,30,7]{2,1,0:T(8,128)S(1)} copy(f32[52,30,7]{0,1,2:T(8,128)S(1)} %collective-permute-done.2) | data formatting | bytes 87360 | tf_op jit(solution)/shard_map/ppermute | solution.py:224
  34.8 0.0 collective-permute-done.3
  34.8 0.9 %copy.42 = f32[52,30,7]{2,1,0:T(8,128)S(1)} copy(f32[52,30,7]{0,1,2:T(8,128)S(1)} %collective-permute-done.3) | data formatting | bytes 87360 | tf_op jit(solution)/shard_map/ppermute | solution.py:224
  35.6 0.7 select_maximum_fusion.obs_ref
  36.4 0.1 fusion.9
  36.5 1.0 %pad_maximum_fusion = f32[52,30,142]{2,1,0:T(8,128)S(1)} fusion(f32[52,30,7]{2,1,0:T(8,128)S(1)} %copy.42, f32[52,7,128]{2,1,0:T(8,128)S(1)} %slice.176, f32[52,16,128]{2,1,0:T(8,128)S(1)} %constant_dynamic-update-slice_fusion.8, f32[52,7,128]{2,1,0:T(8,128)S(1)} %slice.175, f32[52,30,7]{2,1,0:T(8,128)S(1)} %copy.41), kind=kLoop, calls=%fused_computation.2 | loop fusion | flops 886080 | bytes 1772160 | tf_op jit(solution)/shard_map/concatenate | solution.py:262
  37.5 0.1 slice.182
  37.5 0.9 %iota_compare_fusion = pred[30,142,128]{2,1,0:T(8,128)(4,1)S(1)} fusion(s32[30,142]{1,0:T(8,128)S(1)} %get-tuple-element.7), kind=kLoop, calls=%fused_computation.1 | loop fusion | flops 545280 | bytes 562320 | tf_op jit(solution)/shard_map/eq | solution.py:275
  38.4 0.2 copy-done
  38.7 2.0 %select_reduce_fusion = f32[30,142]{1,0:T(8,128)S(1)} fusion(f32[30,128]{1,0:T(8,128)S(1)} %pad_maximum_fusion.3, s32[30,142]{1,0:T(8,128)S(1)} %get-tuple-element.7), kind=kLoop, calls=%fused_computation | loop fusion | flops 1631580 | bytes 49440 | tf_op jit(solution)/shard_map/reduce_sum | solution.py:284
  40.7 0.6 pad.28.beta_ref
  41.3 0.6 pad.27.ice_ref
  41.9 1.1 %pad.24.forcing_ref = f32[2,16,32,256]{3,2,1,0:T(8,128)} pad(f32[2,16,30,142]{3,2,1,0:T(8,128)S(1)} %bitcast.35, f32[]{:T(128)} %constant.4.clone.1), padding=0_0x0_0x0_2x0_114 | pad | bytes 1593860 | tf_op jit(solution)/shard_map/jit(_pad)/pad | solution.py:290
  43.0 0.8 pad.25.visc_ref
  43.9 24.3 %shard_map.85 = (f32[2,16,16,128]{3,2,1,0:T(8,128)}, f32[2,16,16,128]{3,2,1,0:T(8,128)}) custom-call(f32[2,16,32,256]{3,2,1,0:T(8,128)} %pad.24.forcing_ref, f32[16,32,256]{2,1,0:T(8,128)} %pad.25.visc_ref, f32[2,32,256]{2,1,0:T(8,128)} %select_maximum_fusion.obs_ref, f32[32,256]{1,0:T(8,128)} %pad.27.ice_ref, f32[32,256]{1,0:T(8,128)} %pad.28.beta_ref), custom_call_target="tpu_custom_call" | custom-call | tf_op jit(solution)/shard_map/pallas_call | solution.py:303
  68.2 0.7 multiply_reduce_fusion
  68.9 0.1 fusion.10
  69.0 0.4 select_reduce_fusion.1
  69.3 0.1 all_gather_reshape.3
  69.4 14.1 %all_gather.7 = f32[8,8,16]{2,1,0:T(8,128)S(1)} all-gather(f32[1,8,16]{2,1,0:T(8,128)S(1)} %all_gather_reshape.3), channel_id=1, replica_groups=mesh['gx'=4,'gy'=8] {'gy'}, dimensions={0}, use_global_device_ids=true | all-gather | bytes 4608 | tf_op jit(solution)/shard_map/all_gather | solution.py:315
  83.5 0.5 dynamic-slice_reduce_fusion
  (30 shorter events, 0.2 us)
Async XLA Ops:
  0.6 13.2 %copy-start.1 = (f32[2,16,16,128]{3,2,1,0:T(8,128)S(1)}, f32[2,16,16,128]{3,2,1,0:T(8,128)}, u32[]{:S(2)}) copy-start(f32[2,16,16,128]{3,2,1,0:T(8,128)} %param.6) | copy-start | bytes 786436
  3.1 12.6 %copy-start.2 = (f32[16,16,128]{2,1,0:T(8,128)S(1)}, f32[16,16,128]{2,1,0:T(8,128)}, u32[]{:S(2)}) copy-start(f32[16,16,128]{2,1,0:T(8,128)} %param.7) | copy-start | bytes 393220
  4.0 11.7 %copy-start.3 = (f32[2,16,128]{2,1,0:T(8,128)S(1)}, f32[2,16,128]{2,1,0:T(8,128)}, u32[]{:S(2)}) copy-start(f32[2,16,128]{2,1,0:T(8,128)} %param.8) | copy-start | bytes 49156
  4.8 11.0 %copy-start.4 = (s32[16,128]{1,0:T(8,128)S(1)}, s32[16,128]{1,0:T(8,128)}, u32[]{:S(2)}) copy-start(s32[16,128]{1,0:T(8,128)} %param.10) | copy-start | bytes 24580
  5.5 11.0 %collective-permute-start = (f32[53,7,128]{2,1,0:T(8,128)S(1)}, f32[53,7,128]{2,1,0:T(8,128)S(1)}, u32[]{:S(2)}, u32[]{:S(2)}) collective-permute-start(f32[53,7,128]{2,1,0:T(8,128)S(1)} %get-tuple-element.36), channel_id=1, source_target_pairs={{0,8},{8,16},{16,24},{1,9},{9,17},{17,25},{2,10},{10,18},{18,26},{... | collective-permute-start | bytes 569864 | tf_op jit(solution)/shard_map/ppermute | solution.py:224
  10.4 8.7 %collective-permute-start.1 = (f32[53,7,128]{2,1,0:T(8,128)S(1)}, f32[53,7,128]{2,1,0:T(8,128)S(1)}, u32[]{:S(2)}, u32[]{:S(2)}) collective-permute-start(f32[53,7,128]{2,1,0:T(8,128)S(1)} %get-tuple-element.37), channel_id=1, source_target_pairs={{8,0},{16,8},{24,16},{9,1},{17,9},{25,17},{10,2},{18,10},{26,18},{... | collective-permute-start | bytes 569864 | tf_op jit(solution)/shard_map/ppermute | solution.py:224
  13.8 2.6 %copy-start.5 = (s32[16,128]{1,0:T(8,128)S(1)}, s32[16,128]{1,0:T(8,128)}, u32[]{:S(2)}) copy-start(s32[16,128]{1,0:T(8,128)} %param.11) | copy-start | bytes 24580
  15.3 3.8 %copy-start.6 = (f32[1,16]{1,0:T(1,128)S(1)}, f32[1,16]{1,0:T(1,128)}, u32[]{:S(2)}) copy-start(f32[1,16]{1,0:T(1,128)} %param.9) | copy-start | bytes 196
  28.6 6.2 %collective-permute-start.3 = (f32[52,30,7]{0,1,2:T(8,128)S(1)}, f32[52,30,7]{0,1,2:T(8,128)S(1)}, u32[]{:S(2)}, u32[]{:S(2)}) collective-permute-start(f32[52,30,7]{0,1,2:T(8,128)S(1)} %pad_maximum_fusion.2), channel_id=1, source_target_pairs={{1,0},{2,1},{3,2},{4,3},{5,4},{6,5},{7,6},{9,8},{10,9},{11,10},{12... | collective-permute-start | bytes 131048 | tf_op jit(solution)/shard_map/ppermute | solution.py:224
  29.9 4.0 %collective-permute-start.2 = (f32[52,30,7]{0,1,2:T(8,128)S(1)}, f32[52,30,7]{0,1,2:T(8,128)S(1)}, u32[]{:S(2)}, u32[]{:S(2)}) collective-permute-start(f32[52,30,7]{0,1,2:T(8,128)S(1)} %pad_maximum_fusion.1), channel_id=1, source_target_pairs={{0,1},{1,2},{2,3},{3,4},{4,5},{5,6},{6,7},{8,9},{9,10},{10,11},{11... | collective-permute-start | bytes 131048 | tf_op jit(solution)/shard_map/ppermute | solution.py:224
  37.5 1.2 %copy-start = (f32[52,30,142]{2,1,0:T(8,128)}, f32[52,30,142]{2,1,0:T(8,128)S(1)}, u32[]{:S(2)}) copy-start(f32[52,30,142]{2,1,0:T(8,128)S(1)} %pad_maximum_fusion) | copy-start | bytes 2658244
  40.7 2.3 %slice-start = ((f32[52,30,142]{2,1,0:T(8,128)}), f32[16,30,142]{2,1,0:T(8,128)S(1)}, s32[]{:S(2)}) async-start(f32[52,30,142]{2,1,0:T(8,128)} %copy-done), calls=%async_computation | async-start | bytes 1048576 | tf_op jit(solution)/shard_map/slice | solution.py:267

commit v5 on v3

--- a/solution.py
+++ b/solution.py
@@ -92,6 +92,61 @@
     return ice_cover * ((1.0 - OMEGA) * centre + OMEGA * line_value)
 
 
+def lane_weights(comps, width):
+    along_x = jnp.concatenate([jnp.full((width,), (4.0, 1.0)[c], jnp.float32) for c in range(comps)])
+    along_y = jnp.concatenate([jnp.full((width,), (1.0, 4.0)[c], jnp.float32) for c in range(comps)])
+    return (along_x, along_y)
+
+
+def prepare_lanes(visc_pad, beta_col, ice_cover, weights):
+    faces = lateral_terms(visc_pad)
+    west_face, east_face, south_face, north_face = faces
+    along_x, along_y = weights
+    centre_visc = visc_pad[:, 1:-1, 1:-1]
+    vertical = VERTICAL * 0.5 * (centre_visc[:-1] + centre_visc[1:])
+    zero_row = jnp.zeros_like(centre_visc[:1])
+    upper_link = jnp.concatenate([vertical, zero_row], 0)
+    lower_link = jnp.concatenate([zero_row, vertical], 0)
+    basal = jnp.concatenate([jnp.zeros_like(centre_visc[:-1]), beta_col[None]], 0)
+    diagonal = along_x * (west_face + east_face) + along_y * (south_face + north_face)
+    diagonal = diagonal + upper_link + lower_link + basal + (1.0 - ice_cover)
+    layer_count = visc_pad.shape[0]
+    ratio_list = []
+    inverse_list = []
+    for layer_idx in range(layer_count):
+        pivot = diagonal[layer_idx]
+        if layer_idx > 0:
+            pivot = pivot + lower_link[layer_idx] * ratio_list[-1]
+        inverse = 1.0 / pivot
+        inverse_list.append(inverse)
+        ratio_list.append(-upper_link[layer_idx] * inverse)
+    return (faces, lower_link, ratio_list, inverse_list)
+
+
+def relax_lanes(vel_pad, rhs_field, faces, lower_link, ratios, inverses, ice_cover, weights):
+    west_face, east_face, south_face, north_face = faces
+    along_x, along_y = weights
+    lateral = along_x * (west_face * vel_pad[:, :-2, 1:-1] + east_face * vel_pad[:, 2:, 1:-1])
+    lateral = lateral + along_y * (
+        south_face * vel_pad[:, 1:-1, :-2] + north_face * vel_pad[:, 1:-1, 2:]
+    )
+    right_side = rhs_field + lateral
+    layer_count = right_side.shape[0]
+    forward_list = []
+    for layer_idx in range(layer_count):
+        value = right_side[layer_idx]
+        if layer_idx > 0:
+            value = value + lower_link[layer_idx] * forward_list[-1]
+        forward_list.append(value * inverses[layer_idx])
+    solved = [None] * layer_count
+    solved[layer_count - 1] = forward_list[layer_count - 1]
+    for layer_idx in range(layer_count - 2, -1, -1):
+        solved[layer_idx] = forward_list[layer_idx] - ratios[layer_idx] * solved[layer_idx + 1]
+    line_value = jnp.stack(solved, 0)
+    centre = vel_pad[:, 1:-1, 1:-1]
+    return ice_cover * ((1.0 - OMEGA) * centre + OMEGA * line_value)
+
+
 def pad_cells(field):
     return jnp.pad(field, [(0, 0)] * (field.ndim - 2) + [(1, 1), (1, 1)])
 
@@ -164,23 +219,40 @@
     )
     beta_col = jnp.sum(jnp.where(owner_match, row_strip[:, None, :], 0.0), axis=-1)
 
-    faces, lower_link, ratios, inverses = prepare(pad_cells(visc_ext), beta_col, ice_cover)
+    def side_by_side(per_comp):
+        return jnp.concatenate([per_comp[c] for c in range(comps)], axis=-1)
+
+    weights = lane_weights(comps, ext_cols)
+    visc_lanes = side_by_side([visc_ext] * comps)
+    ice_lanes = side_by_side([ice_cover] * comps)
+    beta_lanes = side_by_side([beta_col] * comps)
+    forcing_lanes = side_by_side([forcing_ext[c] for c in range(comps)])
+    observed_lanes = side_by_side([observed_ext[c] for c in range(comps)])
+    faces, lower_link, ratios, inverses = prepare_lanes(
+        pad_cells(visc_lanes), beta_lanes, ice_lanes, weights
+    )
 
     def advance(field, rhs_field):
-        return relax(pad_cells(field), rhs_field, faces, lower_link, ratios, inverses, ice_cover)
-
-    velocity = jnp.zeros_like(forcing_ext)
+        return relax_lanes(pad_cells(field), rhs_field, faces, lower_link, ratios, inverses, ice_lanes, weights)
+
+    velocity = jnp.zeros_like(forcing_lanes)
     for sweep_idx in range(PASSES):
-        velocity = advance(velocity, forcing_ext)
-    misfit = velocity[:, 0] - observed_ext
-    adjoint_rhs = jnp.zeros_like(forcing_ext).at[:, 0].set(misfit)
-    adjoint = jnp.zeros_like(forcing_ext)
+        velocity = advance(velocity, forcing_lanes)
+    misfit = velocity[0] - observed_lanes
+    adjoint_rhs = jnp.zeros_like(forcing_lanes).at[0].set(misfit)
+    adjoint = jnp.zeros_like(forcing_lanes)
     for sweep_idx in range(PASSES):
         adjoint = advance(adjoint, adjoint_rhs)
 
     inner = (slice(HALO, HALO + rows), slice(HALO, HALO + cols))
-    velocity = velocity[:, :, inner[0], inner[1]]
-    adjoint = adjoint[:, :, inner[0], inner[1]]
+
+    def split(field):
+        return jnp.stack(
+            [field[:, inner[0], c * ext_cols + HALO:c * ext_cols + HALO + cols] for c in range(comps)]
+        )
+
+    velocity = split(velocity)
+    adjoint = split(adjoint)
     grad_col = -ice_cover[inner] * beta_col[inner] * jnp.sum(adjoint[:, -1] * velocity[:, -1], axis=0)
     block_match = owner_match[inner[0], inner[1]]
     partial_sum = jnp.sum(jnp.where(block_match, grad_col[:, :, None], 0.0), axis=(0, 1))

time: 69.6 us -> 62.7 us (0.901)
  local copies, waits for them, and re-layouts: 13.8 us -> 10.7 us
  waiting for transfers between devices: 3.09 us -> 0.15 us
  blocking collectives: 20.9 us -> 18.3 us
  starting transfers between devices: 8.81 us -> 11.2 us
    all_gather x1, blocking collectives: 12.8 us -> 9.22 us  [local(): friction_rows = lax.all_gather(strips_near, 'gy', axis=1, tiled=True)]
    unnamed x145 -> x85, local copies, waits for them, and re-layouts: 6.99 us -> 4 us
    ppermute x4, waiting for transfers between devices: 3.09 us -> 0.15 us  [shifted(): return lax.ppermute(piece, axis, pairs)]
    ppermute x4, starting transfers between devices: 8.81 us -> 11.2 us  [shifted(): return lax.ppermute(piece, axis, pairs)]
    another operation x4 -> x2, other arithmetic: 0.07 us -> 1.44 us  [split(): jnp.stack([field[:, inner[0], c * ext_cols + HALO:c * ext_cols + HALO + c...]
    add x8, other arithmetic: 7.42 us -> 6.33 us  [the longest x4 3.53 us: relax_lanes(): right_side = rhs_field + lateral]
    all_gather x1, blocking collectives: 8.15 us -> 9.05 us  [local(): gathered = lax.all_gather(partial_sum.reshape(owners, chunk), 'gy')]
    unnamed x10 -> x66, other arithmetic: 2.48 us -> 1.96 us
  transfers between devices with their start and end apart: 4 -> 4, of which waited for: 1 -> 1; matrix products, arithmetic and copies ran while one was open for 8% -> 9% of each run, Pallas kernels for 0% -> 0%
where the time goes in v5:
time: 62.7 us; the launch traced here: 62.2 us
  other arithmetic  19.8 us (32%)
  blocking collectives  18.3 us (29%)
  starting transfers between devices  11.2 us (18%)
  local copies, waits for them, and re-layouts  10.7 us (17%)
  between operations  2.1 us (3%)
    ppermute x4, starting transfers between devices, shifted(): return lax.ppermute(piece, axis, pairs)  11.2 us
    all_gather x1, blocking collectives, local(): friction_rows = lax.all_gather(strips_near, 'gy', axis=1, tiled=True)  9.22 us
    all_gather x1, blocking collectives, local(): gathered = lax.all_gather(partial_sum.reshape(owners, chunk), 'gy')  9.05 us
    unnamed x85, local copies, waits for them, and re-layouts  4 us
    add x4, other arithmetic, relax_lanes(): right_side = rhs_field + lateral  3.53 us
    slice x11, local copies, waits for them, and re-layouts, stack_rows(): p[:, :, lo:hi]  2.73 us
    add x3, other arithmetic, relax_lanes(): lateral + along_y * (south_face * vel_pad[:, 1:-1, :-2] + north_face * ve...  2.36 us
    reduce_sum x1, other arithmetic, local(): jnp.sum(jnp.where(owner_match, row_strip[:, None, :], 0.0), axis=-1)  2.23 us
  transfers between devices with their start and end apart: 4, of which 1 were waited for; matrix products, arithmetic and copies ran while one was open for 9% of the time, Pallas kernels for 0%

profile of v5, /device:TPU:0, one launch (start us, length us, event | category | flops | bytes accessed | tf_op | source)
XLA Modules:
  0.0 62.2 jit_solution(16249956630649542287)
XLA Ops:
  0.7 1.0 %constant_dynamic-update-slice_fusion.5 = (f32[53,7,128]{2,1,0:T(8,128)S(1)}, f32[53,7,128]{2,1,0:T(8,128)S(1)}) fusion(f32[32,16,128]{2,1,0:T(8,128)} %bitcast.44), kind=kLoop, calls=%fused_computation.45 | loop fusion | bytes 491520
  1.7 0.7 %convert_bitcast_fusion.1 = f32[1,16,128]{2,1,0:T(8,128)S(1)} fusion(s32[16,128]{1,0:T(8,128)} %param.12), kind=kLoop, calls=%fused_computation.635 | loop fusion | flops 2048 | bytes 16384 | tf_op jit(solution)/shard_map/broadcast_in_dim | solution.py:170
  2.4 0.7 %convert_bitcast_fusion = f32[1,16,128]{2,1,0:T(8,128)S(1)} fusion(s32[16,128]{1,0:T(8,128)} %param.13), kind=kLoop, calls=%fused_computation.634 | loop fusion | flops 2048 | bytes 16384 | tf_op jit(solution)/shard_map/broadcast_in_dim | solution.py:171
  3.1 0.9 %constant_dynamic-update-slice_fusion.4 = (f32[53,7,128]{2,1,0:T(8,128)S(1)}, f32[53,7,128]{2,1,0:T(8,128)S(1)}) fusion(f32[53,7,128]{2,1,0:T(8,128)S(1)} %get-tuple-element.250, f32[16,16,128]{2,1,0:T(8,128)} %param.9, f32[53,7,128]{2,1,0:T(8,128)S(1)} %get-tuple-element.251), kind=kLoop, calls=%fused_computation.44 | loop fusion | bytes 245760
  4.0 0.7 %constant_dynamic-update-slice_fusion.3 = (f32[53,7,128]{2,1,0:T(8,128)S(1)}, f32[53,7,128]{2,1,0:T(8,128)S(1)}) fusion(f32[53,7,128]{2,1,0:T(8,128)S(1)} %get-tuple-element.258, f32[2,16,128]{2,1,0:T(8,128)} %param.10, f32[53,7,128]{2,1,0:T(8,128)S(1)} %get-tuple-element.259), kind=kLoop, calls=%fused_computation.43 | loop fusion | bytes 30720
  4.7 0.7 %constant_dynamic-update-slice_fusion = (f32[53,7,128]{2,1,0:T(8,128)S(1)}, f32[53,7,128]{2,1,0:T(8,128)S(1)}) fusion(f32[53,7,128]{2,1,0:T(8,128)S(1)} %get-tuple-element.275, f32[1,16]{1,0:T(1,128)} %param.11, f32[53,7,128]{2,1,0:T(8,128)S(1)} %get-tuple-element.276), kind=kLoop, calls=%fused_computation.40 | loop fusion | bytes 8256 | tf_op jit(solution)/shard_map/concatenate | solution.py:177
  5.4 1.3 %collective-permute-start.1 = (f32[53,7,128]{2,1,0:T(8,128)S(1)}, f32[53,7,128]{2,1,0:T(8,128)S(1)}, u32[]{:S(2)}, u32[]{:S(2)}) collective-permute-start(f32[53,7,128]{2,1,0:T(8,128)S(1)} %get-tuple-element.283), channel_id=1, source_target_pairs={{8,0},{16,8},{24,16},{9,1},{17,9},{25,17},{10,2},{18,10},{26,18},{... | collective-permute-start | bytes 569864 | tf_op jit(solution)/shard_map/ppermute | solution.py:160
  6.7 5.6 %collective-permute-start = (f32[53,7,128]{2,1,0:T(8,128)S(1)}, f32[53,7,128]{2,1,0:T(8,128)S(1)}, u32[]{:S(2)}, u32[]{:S(2)}) collective-permute-start(f32[53,7,128]{2,1,0:T(8,128)S(1)} %get-tuple-element.282), channel_id=1, source_target_pairs={{0,8},{8,16},{16,24},{1,9},{9,17},{17,25},{2,10},{10,18},{18,26},{... | collective-permute-start | bytes 569864 | tf_op jit(solution)/shard_map/ppermute | solution.py:160
  12.3 1.2 %fusion.285 = (f32[32,16,7]{2,1,0:T(8,128)S(1)}, f32[32,16,7]{2,1,0:T(8,128)S(1)}) fusion(f32[32,16,128]{2,1,0:T(8,128)} %bitcast.45), kind=kLoop, calls=%fused_computation.645 | loop fusion | bytes 57344 | tf_op jit(solution)/shard_map/slice | solution.py:184
  13.8 0.2 copy.56
  14.0 0.2 copy.66
  14.2 0.2 copy.67
  14.4 0.2 copy.57
  14.6 0.2 copy.58
  14.9 0.2 copy.49
  15.1 0.2 copy.64
  15.3 0.2 copy.65
  15.5 0.2 copy.50
  15.7 0.2 copy.51
  17.1 1.3 %collective-permute-start.3 = (f32[52,30,7]{0,1,2:T(8,128)S(1)}, f32[52,30,7]{0,1,2:T(8,128)S(1)}, u32[]{:S(2)}, u32[]{:S(2)}) collective-permute-start(f32[52,30,7]{0,1,2:T(8,128)S(1)} %pad_maximum_fusion.6), channel_id=1, source_target_pairs={{1,0},{2,1},{3,2},{4,3},{5,4},{6,5},{7,6},{9,8},{10,9},{11,10},{12... | collective-permute-start | bytes 131048 | tf_op jit(solution)/shard_map/ppermute | solution.py:160
  18.6 0.2 copy.52
  18.8 3.0 %collective-permute-start.2 = (f32[52,30,7]{0,1,2:T(8,128)S(1)}, f32[52,30,7]{0,1,2:T(8,128)S(1)}, u32[]{:S(2)}, u32[]{:S(2)}) collective-permute-start(f32[52,30,7]{0,1,2:T(8,128)S(1)} %pad_maximum_fusion.5), channel_id=1, source_target_pairs={{0,1},{1,2},{2,3},{3,4},{4,5},{5,6},{6,7},{8,9},{9,10},{10,11},{11... | collective-permute-start | bytes 131048 | tf_op jit(solution)/shard_map/ppermute | solution.py:160
  21.9 9.2 %all-gather = f32[8,16,3]{1,2,0:T(4,128)S(1)} all-gather(f32[1,16,3]{1,2,0:T(4,128)S(1)} %maximum_bitcast_fusion.2), channel_id=1, replica_groups=mesh['gx'=4,'gy'=8] {'gy'}, dimensions={0}, use_global_device_ids=true | all-gather | bytes 1728 | tf_op jit(solution)/shard_map/all_gather | solution.py:195
  31.3 0.8 %copy.62 = f32[52,30,7]{2,1,0:T(8,128)S(1)} copy(f32[52,30,7]{0,1,2:T(8,128)S(1)} %collective-permute-done.3) | data formatting | bytes 87360 | tf_op jit(solution)/shard_map/ppermute | solution.py:160
  32.2 0.9 %copy.61 = f32[52,30,7]{2,1,0:T(8,128)S(1)} copy(f32[52,30,7]{0,1,2:T(8,128)S(1)} %collective-permute-done.2) | data formatting | bytes 87360 | tf_op jit(solution)/shard_map/ppermute | solution.py:160
  33.0 1.0 %pad_maximum_fusion = f32[52,30,142]{2,1,0:T(8,128)S(1)} fusion(f32[52,30,7]{2,1,0:T(8,128)S(1)} %copy.62, f32[52,7,128]{2,1,0:T(8,128)S(1)} %slice.1151, f32[52,16,128]{2,1,0:T(8,128)S(1)} %constant_dynamic-update-slice_fusion.12, f32[52,7,128]{2,1,0:T(8,128)S(1)} %slice.1150, f32[52,30,7]{2,1,0:T(8,128)S(1)} %copy.61), kind=kLoop, calls=%fused_computation.2 | loop fusion | flops 886080 | bytes 1772160 | tf_op jit(solution)/shard_map/concatenate | solution.py:198
  34.1 0.2 pad_maximum_fusion.1
  34.3 0.3 fusion.2
  34.8 0.9 %iota_compare_fusion = pred[30,142,128]{2,1,0:T(8,128)(4,1)S(1)} fusion(s32[30,142]{1,0:T(8,128)S(1)} %get-tuple-element.240), kind=kLoop, calls=%fused_computation.1 | loop fusion | flops 545280 | bytes 562320 | tf_op jit(solution)/shard_map/eq | solution.py:211
  35.7 2.2 %select_reduce_fusion = f32[30,142]{1,0:T(8,128)S(1)} fusion(f32[30,128]{1,0:T(8,128)S(1)} %pad_maximum_fusion.16, s32[30,142]{1,0:T(8,128)S(1)} %get-tuple-element.240), kind=kLoop, calls=%fused_computation | loop fusion | flops 1631580 | bytes 49440 | tf_op jit(solution)/shard_map/reduce_sum | solution.py:220
  38.1 0.8 %fusion.155 = (f32[16,30,284]{2,1,0:T(8,128)S(1)}, f32[16,30,284]{2,1,0:T(8,128)S(1)}, f32[16,30,284]{2,1,0:T(8,128)S(1)}, f32[16,30,284]{2,1,0:T(8,128)S(1)}, f...) fusion(f32[16,30,142]{2,1,0:T(8,128)S(1)} %get-tuple-element.242, f32[16,30,142]{2,1,0:T(8,128)S(1)} %get-tuple-element.243, ...), kind=kLoop, calls=%fused_computation.643 | loop fusion | flops 2044800 | bytes 4500832 | tf_op jit(solution)/shard_map/add | solution.py:133
  38.9 0.4 add_add_fusion.3
  39.4 0.3 fusion.124
  40.1 0.9 %add_add_fusion.2 = f32[16,30,284]{2,1,0:T(8,128)S(1)} fusion(f32[16,30,284]{2,1,0:T(8,128)S(1)} %broadcast_multiply_fusion.1, f32[16,30,284]{2,1,0:T(8,128)S(1)} %get-tuple-element.238, f32[16,30,284]{2,1,0:T(8,128)S(1)} %get-tuple-element.237, f32[16,30,284]{2,1,0:T(8,128)S(1)} %get-tuple-element.236, f32[16,30,284]{2,1,0:T(8,128)S(1)} %get-tuple-element.235, ...), kind=kLoop, calls=%fused_computation.21 | loop fusion | flops 2044800 | bytes 3819232 | tf_op jit(solution)/shard_map/add | solution.py:133
  41.1 0.2 fusion.106
  41.6 0.2 add_multiply_fusion.5
  41.8 0.9 %add_add_fusion.1 = f32[16,30,284]{2,1,0:T(8,128)S(1)} fusion(f32[16,30,284]{2,1,0:T(8,128)S(1)} %add_multiply_fusion.5, f32[16,30,284]{2,1,0:T(8,128)S(1)} %get-tuple-element.238, f32[16,30,284]{2,1,0:T(8,128)S(1)} %get-tuple-element.237, f32[16,30,284]{2,1,0:T(8,128)S(1)} %get-tuple-element.236, f32[16,30,284]{2,1,0:T(8,128)S(1)} %get-tuple-element.235, ...), kind=kLoop, calls=%fused_computation.19 | loop fusion | flops 2044800 | bytes 3819232 | tf_op jit(solution)/shard_map/add | solution.py:133
  42.7 0.2 fusion.91
  42.9 0.2 constant_dynamic-update-slice_fusion.64
  43.3 0.2 add_multiply_fusion.4
  43.5 0.9 %add_add_fusion = f32[16,30,284]{2,1,0:T(8,128)S(1)} fusion(f32[16,30,284]{2,1,0:T(8,128)S(1)} %add_multiply_fusion.4, f32[16,30,284]{2,1,0:T(8,128)S(1)} %get-tuple-element.238, f32[16,30,284]{2,1,0:T(8,128)S(1)} %get-tuple-element.237, f32[16,30,284]{2,1,0:T(8,128)S(1)} %get-tuple-element.236, f32[16,30,284]{2,1,0:T(8,128)S(1)} %get-tuple-element.235, ...), kind=kLoop, calls=%fused_computation.17 | loop fusion | flops 2044800 | bytes 3819232 | tf_op jit(solution)/shard_map/add | solution.py:133
  44.4 0.2 fusion.76
  44.5 0.2 constant_dynamic-update-slice_fusion.80
  44.9 0.2 add_multiply_fusion.3
  45.1 0.2 fusion.58
  45.3 0.2 constant_dynamic-update-slice_fusion.96
  45.8 0.8 %multiply_add_fusion.2 = f32[16,30,284]{2,1,0:T(8,128)S(1)} fusion(f32[16,30,284]{2,1,0:T(8,128)S(1)} %broadcast_multiply_fusion, f32[16,30,284]{2,1,0:T(8,128)S(1)} %get-tuple-element.238, f32[16,30,284]{2,1,0:T(8,128)S(1)} %get-tuple-element.237, f32[16,30,284]{2,1,0:T(8,128)S(1)} %get-tuple-element.236, f32[16,30,284]{2,1,0:T(8,128)S(1)} %get-tuple-element.235, ...), kind=kLoop, calls=%fused_computation.15 | loop fusion | flops 1772160 | bytes 3273952 | tf_op jit(solution)/shard_map/add | solution.py:130
  46.6 0.2 fusion.42
  46.8 0.2 constant_dynamic-update-slice_fusion.112
  47.2 0.2 add_multiply_fusion.2
  47.3 0.8 %multiply_add_fusion.1 = f32[16,30,284]{2,1,0:T(8,128)S(1)} fusion(f32[16,30,284]{2,1,0:T(8,128)S(1)} %add_multiply_fusion.2, f32[16,30,284]{2,1,0:T(8,128)S(1)} %get-tuple-element.238, f32[16,30,284]{2,1,0:T(8,128)S(1)} %get-tuple-element.237, f32[16,30,284]{2,1,0:T(8,128)S(1)} %get-tuple-element.236, f32[16,30,284]{2,1,0:T(8,128)S(1)} %get-tuple-element.235, ...), kind=kLoop, calls=%fused_computation.13 | loop fusion | flops 1772160 | bytes 3273952 | tf_op jit(solution)/shard_map/add | solution.py:130
  48.1 0.2 fusion.26
  48.3 0.2 constant_dynamic-update-slice_fusion.128
  48.7 0.2 add_multiply_fusion.1
  48.9 0.8 %multiply_add_fusion = f32[16,30,284]{2,1,0:T(8,128)S(1)} fusion(f32[16,30,284]{2,1,0:T(8,128)S(1)} %add_multiply_fusion.1, f32[16,30,284]{2,1,0:T(8,128)S(1)} %get-tuple-element.238, f32[16,30,284]{2,1,0:T(8,128)S(1)} %get-tuple-element.237, f32[16,30,284]{2,1,0:T(8,128)S(1)} %get-tuple-element.236, f32[16,30,284]{2,1,0:T(8,128)S(1)} %get-tuple-element.235, ...), kind=kLoop, calls=%fused_computation.11 | loop fusion | flops 1772160 | bytes 3273952 | tf_op jit(solution)/shard_map/add | solution.py:130
  49.7 0.2 fusion.10
  49.9 0.2 constant_dynamic-update-slice_fusion.144
  50.3 0.2 add_multiply_fusion
  50.5 0.2 slice_bitcast_fusion.1
  50.7 0.7 %pad_maximum_fusion.3 = f32[2,16,16,128]{3,2,1,0:T(8,128)} fusion(f32[1,16,16,128]{3,2,1,0:T(8,128)S(1)} %get-tuple-element.284, f32[1,16,16,128]{3,2,1,0:T(8,128)S(1)} %get-tuple-element.285), kind=kLoop, calls=%fused_computation.35 | loop fusion | flops 65536 | bytes 524288 | tf_op jit(solution)/shard_map/stack | solution.py:250
  51.4 0.7 %pad_maximum_fusion.4 = f32[2,16,16,128]{3,2,1,0:T(8,128)} fusion(f32[1,16,16,128]{3,2,1,0:T(8,128)S(1)} %get-tuple-element.245, f32[1,16,16,128]{3,2,1,0:T(8,128)S(1)} %get-tuple-element.244), kind=kLoop, calls=%fused_computation.38 | loop fusion | flops 65536 | bytes 524288 | tf_op jit(solution)/shard_map/stack | solution.py:250
  52.2 0.4 select_reduce_fusion.1
  52.7 9.0 %all_gather.7 = f32[8,8,16]{2,1,0:T(8,128)S(1)} all-gather(f32[1,8,16]{2,1,0:T(8,128)S(1)} %all_gather_reshape.3), channel_id=1, replica_groups=mesh['gx'=4,'gy'=8] {'gy'}, dimensions={0}, use_global_device_ids=true | all-gather | bytes 4608 | tf_op jit(solution)/shard_map/all_gather | solution.py:261
  61.7 0.5 dynamic-slice_reduce_fusion
  (185 shorter events, 3.9 us)
Async XLA Ops:
  0.6 13.1 %copy-start = (f32[2,16,16,128]{3,2,1,0:T(8,128)S(1)}, f32[2,16,16,128]{3,2,1,0:T(8,128)}, u32[]{:S(2)}) copy-start(f32[2,16,16,128]{3,2,1,0:T(8,128)} %param.8) | copy-start | bytes 786436
  0.6 12.8 %copy-start.1 = (f32[16,16,128]{2,1,0:T(8,128)S(1)}, f32[16,16,128]{2,1,0:T(8,128)}, u32[]{:S(2)}) copy-start(f32[16,16,128]{2,1,0:T(8,128)} %param.9) | copy-start | bytes 393220
  0.7 12.9 %copy-start.2 = (f32[2,16,128]{2,1,0:T(8,128)S(1)}, f32[2,16,128]{2,1,0:T(8,128)}, u32[]{:S(2)}) copy-start(f32[2,16,128]{2,1,0:T(8,128)} %param.10) | copy-start | bytes 49156
  4.0 10.9 %copy-start.5 = (s32[16,128]{1,0:T(8,128)S(1)}, s32[16,128]{1,0:T(8,128)}, u32[]{:S(2)}) copy-start(s32[16,128]{1,0:T(8,128)} %param.12) | copy-start | bytes 24580
  5.4 11.0 %collective-permute-start.1 = (f32[53,7,128]{2,1,0:T(8,128)S(1)}, f32[53,7,128]{2,1,0:T(8,128)S(1)}, u32[]{:S(2)}, u32[]{:S(2)}) collective-permute-start(f32[53,7,128]{2,1,0:T(8,128)S(1)} %get-tuple-element.283), channel_id=1, source_target_pairs={{8,0},{16,8},{24,16},{9,1},{17,9},{25,17},{10,2},{18,10},{26,18},{... | collective-permute-start | bytes 569864 | tf_op jit(solution)/shard_map/ppermute | solution.py:160
  6.7 10.1 %collective-permute-start = (f32[53,7,128]{2,1,0:T(8,128)S(1)}, f32[53,7,128]{2,1,0:T(8,128)S(1)}, u32[]{:S(2)}, u32[]{:S(2)}) collective-permute-start(f32[53,7,128]{2,1,0:T(8,128)S(1)} %get-tuple-element.282), channel_id=1, source_target_pairs={{0,8},{8,16},{16,24},{1,9},{9,17},{17,25},{2,10},{10,18},{18,26},{... | collective-permute-start | bytes 569864 | tf_op jit(solution)/shard_map/ppermute | solution.py:160
  13.5 2.8 %copy-start.6 = (s32[16,128]{1,0:T(8,128)S(1)}, s32[16,128]{1,0:T(8,128)}, u32[]{:S(2)}) copy-start(s32[16,128]{1,0:T(8,128)} %param.13) | copy-start | bytes 24580
  16.2 5.6 %copy-start.7 = (f32[1,16]{1,0:T(1,128)S(1)}, f32[1,16]{1,0:T(1,128)}, u32[]{:S(2)}) copy-start(f32[1,16]{1,0:T(1,128)} %param.11) | copy-start | bytes 196
  17.1 14.2 %collective-permute-start.3 = (f32[52,30,7]{0,1,2:T(8,128)S(1)}, f32[52,30,7]{0,1,2:T(8,128)S(1)}, u32[]{:S(2)}, u32[]{:S(2)}) collective-permute-start(f32[52,30,7]{0,1,2:T(8,128)S(1)} %pad_maximum_fusion.6), channel_id=1, source_target_pairs={{1,0},{2,1},{3,2},{4,3},{5,4},{6,5},{7,6},{9,8},{10,9},{11,10},{12... | collective-permute-start | bytes 131048 | tf_op jit(solution)/shard_map/ppermute | solution.py:160
  18.8 13.4 %collective-permute-start.2 = (f32[52,30,7]{0,1,2:T(8,128)S(1)}, f32[52,30,7]{0,1,2:T(8,128)S(1)}, u32[]{:S(2)}, u32[]{:S(2)}) collective-permute-start(f32[52,30,7]{0,1,2:T(8,128)S(1)} %pad_maximum_fusion.5), channel_id=1, source_target_pairs={{0,1},{1,2},{2,3},{3,4},{4,5},{5,6},{6,7},{8,9},{9,10},{10,11},{11... | collective-permute-start | bytes 131048 | tf_op jit(solution)/shard_map/ppermute | solution.py:160
  34.7 3.4 %copy-start.3 = (f32[284]{0:T(512)S(1)}, f32[284]{0:T(512)}, u32[]{:S(2)}) copy-start(f32[284]{0:T(512)} %constant.51.clone.1) | copy-start | bytes 3412
  34.7 3.4 %copy-start.4 = (f32[284]{0:T(512)S(1)}, f32[284]{0:T(512)}, u32[]{:S(2)}) copy-start(f32[284]{0:T(512)} %constant.49.clone.1) | copy-start | bytes 3412

commit v6 on v5

--- a/solution.py
+++ b/solution.py
@@ -207,17 +207,17 @@
     ice_cover = packed[at]
     owner_ext = packed[at + 1].astype(jnp.int32)
 
-    tiles = lax.broadcasted_iota(jnp.int32, (1, 1, tile_count), 2)
-    owner_match = owner_ext[:, :, None] == tiles
+    tiles = lax.broadcasted_iota(jnp.int32, (tile_count, 1, 1), 0)
+    owner_match = owner_ext[None] == tiles
     row_strip = jnp.concatenate(
         [
-            jnp.broadcast_to(friction_rows[0], (HALO, tile_count)),
-            jnp.broadcast_to(friction_rows[1], (rows, tile_count)),
-            jnp.broadcast_to(friction_rows[2], (HALO, tile_count)),
+            jnp.broadcast_to(friction_rows[0][:, None], (tile_count, HALO)),
+            jnp.broadcast_to(friction_rows[1][:, None], (tile_count, rows)),
+            jnp.broadcast_to(friction_rows[2][:, None], (tile_count, HALO)),
         ],
-        axis=0,
-    )
-    beta_col = jnp.sum(jnp.where(owner_match, row_strip[:, None, :], 0.0), axis=-1)
+        axis=1,
+    )
+    beta_col = jnp.sum(jnp.where(owner_match, row_strip[:, :, None], 0.0), axis=0)
 
     def side_by_side(per_comp):
         return jnp.concatenate([per_comp[c] for c in range(comps)], axis=-1)
@@ -254,8 +254,8 @@
     velocity = split(velocity)
     adjoint = split(adjoint)
     grad_col = -ice_cover[inner] * beta_col[inner] * jnp.sum(adjoint[:, -1] * velocity[:, -1], axis=0)
-    block_match = owner_match[inner[0], inner[1]]
-    partial_sum = jnp.sum(jnp.where(block_match, grad_col[:, :, None], 0.0), axis=(0, 1))
+    block_match = owner_match[:, inner[0], inner[1]]
+    partial_sum = jnp.sum(jnp.where(block_match, grad_col[None], 0.0), axis=(1, 2))
     owners = lax.axis_size("gy")
     chunk = tile_count // owners
     gathered = lax.all_gather(partial_sum.reshape(owners, chunk), "gy")

time: 62.7 us -> 62.7 us (level)
  no operation moved by 1% of the time
where the time goes in v6:
time: 62.7 us; the launch traced here: 62.2 us
  other arithmetic  19.8 us (32%)
  blocking collectives  18.3 us (29%)
  starting transfers between devices  11.2 us (18%)
  local copies, waits for them, and re-layouts  10.7 us (17%)
  between operations  2.1 us (3%)
    ppermute x4, starting transfers between devices, shifted(): return lax.ppermute(piece, axis, pairs)  11.2 us
    all_gather x1, blocking collectives, local(): friction_rows = lax.all_gather(strips_near, 'gy', axis=1, tiled=True)  9.22 us
    all_gather x1, blocking collectives, local(): gathered = lax.all_gather(partial_sum.reshape(owners, chunk), 'gy')  9.05 us
    unnamed x85, local copies, waits for them, and re-layouts  4 us
    add x4, other arithmetic, relax_lanes(): right_side = rhs_field + lateral  3.53 us
    slice x11, local copies, waits for them, and re-layouts, stack_rows(): p[:, :, lo:hi]  2.73 us
    add x3, other arithmetic, relax_lanes(): lateral + along_y * (south_face * vel_pad[:, 1:-1, :-2] + north_face * ve...  2.36 us
    reduce_sum x1, other arithmetic, local(): jnp.sum(jnp.where(owner_match, row_strip[:, :, None], 0.0), axis=0)  2.23 us
  transfers between devices with their start and end apart: 4, of which 1 were waited for; matrix products, arithmetic and copies ran while one was open for 9% of the time, Pallas kernels for 0%

profile of v6, /device:TPU:0, one launch (start us, length us, event | category | flops | bytes accessed | tf_op | source)
XLA Modules:
  0.0 62.2 jit_solution(16249956630649542287)
XLA Ops:
  0.7 1.0 %constant_dynamic-update-slice_fusion.5 = (f32[53,7,128]{2,1,0:T(8,128)S(1)}, f32[53,7,128]{2,1,0:T(8,128)S(1)}) fusion(f32[32,16,128]{2,1,0:T(8,128)} %bitcast.44), kind=kLoop, calls=%fused_computation.45 | loop fusion | bytes 491520
  1.7 0.7 %convert_bitcast_fusion.1 = f32[1,16,128]{2,1,0:T(8,128)S(1)} fusion(s32[16,128]{1,0:T(8,128)} %param.12), kind=kLoop, calls=%fused_computation.635 | loop fusion | flops 2048 | bytes 16384 | tf_op jit(solution)/shard_map/broadcast_in_dim | solution.py:170
  2.4 0.7 %convert_bitcast_fusion = f32[1,16,128]{2,1,0:T(8,128)S(1)} fusion(s32[16,128]{1,0:T(8,128)} %param.13), kind=kLoop, calls=%fused_computation.634 | loop fusion | flops 2048 | bytes 16384 | tf_op jit(solution)/shard_map/broadcast_in_dim | solution.py:171
  3.1 0.9 %constant_dynamic-update-slice_fusion.4 = (f32[53,7,128]{2,1,0:T(8,128)S(1)}, f32[53,7,128]{2,1,0:T(8,128)S(1)}) fusion(f32[53,7,128]{2,1,0:T(8,128)S(1)} %get-tuple-element.250, f32[16,16,128]{2,1,0:T(8,128)} %param.9, f32[53,7,128]{2,1,0:T(8,128)S(1)} %get-tuple-element.251), kind=kLoop, calls=%fused_computation.44 | loop fusion | bytes 245760
  4.0 0.7 %constant_dynamic-update-slice_fusion.3 = (f32[53,7,128]{2,1,0:T(8,128)S(1)}, f32[53,7,128]{2,1,0:T(8,128)S(1)}) fusion(f32[53,7,128]{2,1,0:T(8,128)S(1)} %get-tuple-element.258, f32[2,16,128]{2,1,0:T(8,128)} %param.10, f32[53,7,128]{2,1,0:T(8,128)S(1)} %get-tuple-element.259), kind=kLoop, calls=%fused_computation.43 | loop fusion | bytes 30720
  4.7 0.7 %constant_dynamic-update-slice_fusion = (f32[53,7,128]{2,1,0:T(8,128)S(1)}, f32[53,7,128]{2,1,0:T(8,128)S(1)}) fusion(f32[53,7,128]{2,1,0:T(8,128)S(1)} %get-tuple-element.275, f32[1,16]{1,0:T(1,128)} %param.11, f32[53,7,128]{2,1,0:T(8,128)S(1)} %get-tuple-element.276), kind=kLoop, calls=%fused_computation.40 | loop fusion | bytes 8256 | tf_op jit(solution)/shard_map/concatenate | solution.py:177
  5.4 1.3 %collective-permute-start.1 = (f32[53,7,128]{2,1,0:T(8,128)S(1)}, f32[53,7,128]{2,1,0:T(8,128)S(1)}, u32[]{:S(2)}, u32[]{:S(2)}) collective-permute-start(f32[53,7,128]{2,1,0:T(8,128)S(1)} %get-tuple-element.283), channel_id=1, source_target_pairs={{8,0},{16,8},{24,16},{9,1},{17,9},{25,17},{10,2},{18,10},{26,18},{... | collective-permute-start | bytes 569864 | tf_op jit(solution)/shard_map/ppermute | solution.py:160
  6.7 5.6 %collective-permute-start = (f32[53,7,128]{2,1,0:T(8,128)S(1)}, f32[53,7,128]{2,1,0:T(8,128)S(1)}, u32[]{:S(2)}, u32[]{:S(2)}) collective-permute-start(f32[53,7,128]{2,1,0:T(8,128)S(1)} %get-tuple-element.282), channel_id=1, source_target_pairs={{0,8},{8,16},{16,24},{1,9},{9,17},{17,25},{2,10},{10,18},{18,26},{... | collective-permute-start | bytes 569864 | tf_op jit(solution)/shard_map/ppermute | solution.py:160
  12.3 1.2 %fusion.285 = (f32[32,16,7]{2,1,0:T(8,128)S(1)}, f32[32,16,7]{2,1,0:T(8,128)S(1)}) fusion(f32[32,16,128]{2,1,0:T(8,128)} %bitcast.45), kind=kLoop, calls=%fused_computation.645 | loop fusion | bytes 57344 | tf_op jit(solution)/shard_map/slice | solution.py:184
  13.8 0.2 copy.58
  14.0 0.2 copy.70
  14.2 0.2 copy.71
  14.4 0.2 copy.59
  14.6 0.2 copy.60
  14.9 0.2 copy.51
  15.1 0.2 copy.68
  15.3 0.2 copy.69
  15.5 0.2 copy.52
  15.7 0.2 copy.53
  17.1 1.3 %collective-permute-start.3 = (f32[52,30,7]{0,1,2:T(8,128)S(1)}, f32[52,30,7]{0,1,2:T(8,128)S(1)}, u32[]{:S(2)}, u32[]{:S(2)}) collective-permute-start(f32[52,30,7]{0,1,2:T(8,128)S(1)} %pad_maximum_fusion.6), channel_id=1, source_target_pairs={{1,0},{2,1},{3,2},{4,3},{5,4},{6,5},{7,6},{9,8},{10,9},{11,10},{12... | collective-permute-start | bytes 131048 | tf_op jit(solution)/shard_map/ppermute | solution.py:160
  18.6 0.2 copy.54
  18.8 3.0 %collective-permute-start.2 = (f32[52,30,7]{0,1,2:T(8,128)S(1)}, f32[52,30,7]{0,1,2:T(8,128)S(1)}, u32[]{:S(2)}, u32[]{:S(2)}) collective-permute-start(f32[52,30,7]{0,1,2:T(8,128)S(1)} %pad_maximum_fusion.5), channel_id=1, source_target_pairs={{0,1},{1,2},{2,3},{3,4},{4,5},{5,6},{6,7},{8,9},{9,10},{10,11},{11... | collective-permute-start | bytes 131048 | tf_op jit(solution)/shard_map/ppermute | solution.py:160
  21.9 9.2 %all-gather = f32[8,16,3]{1,2,0:T(4,128)S(1)} all-gather(f32[1,16,3]{1,2,0:T(4,128)S(1)} %maximum_bitcast_fusion.2), channel_id=1, replica_groups=mesh['gx'=4,'gy'=8] {'gy'}, dimensions={0}, use_global_device_ids=true | all-gather | bytes 1728 | tf_op jit(solution)/shard_map/all_gather | solution.py:195
  31.3 0.8 %copy.64 = f32[52,30,7]{2,1,0:T(8,128)S(1)} copy(f32[52,30,7]{0,1,2:T(8,128)S(1)} %collective-permute-done.3) | data formatting | bytes 87360 | tf_op jit(solution)/shard_map/ppermute | solution.py:160
  32.2 0.9 %copy.63 = f32[52,30,7]{2,1,0:T(8,128)S(1)} copy(f32[52,30,7]{0,1,2:T(8,128)S(1)} %collective-permute-done.2) | data formatting | bytes 87360 | tf_op jit(solution)/shard_map/ppermute | solution.py:160
  33.0 1.0 %pad_maximum_fusion = f32[52,30,142]{2,1,0:T(8,128)S(1)} fusion(f32[52,30,7]{2,1,0:T(8,128)S(1)} %copy.64, f32[52,7,128]{2,1,0:T(8,128)S(1)} %slice.1151, f32[52,16,128]{2,1,0:T(8,128)S(1)} %constant_dynamic-update-slice_fusion.12, f32[52,7,128]{2,1,0:T(8,128)S(1)} %slice.1150, f32[52,30,7]{2,1,0:T(8,128)S(1)} %copy.63), kind=kLoop, calls=%fused_computation.2 | loop fusion | flops 886080 | bytes 1772160 | tf_op jit(solution)/shard_map/concatenate | solution.py:198
  34.1 0.2 pad_maximum_fusion.1
  34.3 0.3 fusion.2
  34.8 0.9 %iota_compare_fusion = pred[128,30,142]{0,2,1:T(8,128)(4,1)S(1)} fusion(s32[30,142]{1,0:T(8,128)S(1)} %get-tuple-element.240), kind=kLoop, calls=%fused_computation.1 | loop fusion | flops 545280 | bytes 562320 | tf_op jit(solution)/shard_map/eq | solution.py:211
  35.7 2.2 %select_reduce_fusion = f32[30,142]{1,0:T(8,128)S(1)} fusion(f32[128,30]{0,1:T(8,128)S(1)} %pad_maximum_fusion.16, s32[30,142]{1,0:T(8,128)S(1)} %get-tuple-element.240), kind=kLoop, calls=%fused_computation | loop fusion | flops 1631580 | bytes 49440 | tf_op jit(solution)/shard_map/reduce_sum | solution.py:220
  38.1 0.8 %fusion.155 = (f32[16,30,284]{2,1,0:T(8,128)S(1)}, f32[16,30,284]{2,1,0:T(8,128)S(1)}, f32[16,30,284]{2,1,0:T(8,128)S(1)}, f32[16,30,284]{2,1,0:T(8,128)S(1)}, f...) fusion(f32[16,30,142]{2,1,0:T(8,128)S(1)} %get-tuple-element.242, f32[16,30,142]{2,1,0:T(8,128)S(1)} %get-tuple-element.243, ...), kind=kLoop, calls=%fused_computation.643 | loop fusion | flops 2044800 | bytes 4500832 | tf_op jit(solution)/shard_map/add | solution.py:133
  38.9 0.4 add_add_fusion.3
  39.4 0.3 fusion.124
  40.1 0.9 %add_add_fusion.2 = f32[16,30,284]{2,1,0:T(8,128)S(1)} fusion(f32[16,30,284]{2,1,0:T(8,128)S(1)} %broadcast_multiply_fusion.1, f32[16,30,284]{2,1,0:T(8,128)S(1)} %get-tuple-element.238, f32[16,30,284]{2,1,0:T(8,128)S(1)} %get-tuple-element.237, f32[16,30,284]{2,1,0:T(8,128)S(1)} %get-tuple-element.236, f32[16,30,284]{2,1,0:T(8,128)S(1)} %get-tuple-element.235, ...), kind=kLoop, calls=%fused_computation.21 | loop fusion | flops 2044800 | bytes 3819232 | tf_op jit(solution)/shard_map/add | solution.py:133
  41.1 0.2 fusion.106
  41.6 0.2 add_multiply_fusion.5
  41.8 0.9 %add_add_fusion.1 = f32[16,30,284]{2,1,0:T(8,128)S(1)} fusion(f32[16,30,284]{2,1,0:T(8,128)S(1)} %add_multiply_fusion.5, f32[16,30,284]{2,1,0:T(8,128)S(1)} %get-tuple-element.238, f32[16,30,284]{2,1,0:T(8,128)S(1)} %get-tuple-element.237, f32[16,30,284]{2,1,0:T(8,128)S(1)} %get-tuple-element.236, f32[16,30,284]{2,1,0:T(8,128)S(1)} %get-tuple-element.235, ...), kind=kLoop, calls=%fused_computation.19 | loop fusion | flops 2044800 | bytes 3819232 | tf_op jit(solution)/shard_map/add | solution.py:133
  42.7 0.2 fusion.91
  42.9 0.2 constant_dynamic-update-slice_fusion.64
  43.3 0.2 add_multiply_fusion.4
  43.5 0.9 %add_add_fusion = f32[16,30,284]{2,1,0:T(8,128)S(1)} fusion(f32[16,30,284]{2,1,0:T(8,128)S(1)} %add_multiply_fusion.4, f32[16,30,284]{2,1,0:T(8,128)S(1)} %get-tuple-element.238, f32[16,30,284]{2,1,0:T(8,128)S(1)} %get-tuple-element.237, f32[16,30,284]{2,1,0:T(8,128)S(1)} %get-tuple-element.236, f32[16,30,284]{2,1,0:T(8,128)S(1)} %get-tuple-element.235, ...), kind=kLoop, calls=%fused_computation.17 | loop fusion | flops 2044800 | bytes 3819232 | tf_op jit(solution)/shard_map/add | solution.py:133
  44.4 0.2 fusion.76
  44.5 0.2 constant_dynamic-update-slice_fusion.80
  44.9 0.2 add_multiply_fusion.3
  45.1 0.2 fusion.58
  45.3 0.2 constant_dynamic-update-slice_fusion.96
  45.8 0.8 %multiply_add_fusion.2 = f32[16,30,284]{2,1,0:T(8,128)S(1)} fusion(f32[16,30,284]{2,1,0:T(8,128)S(1)} %broadcast_multiply_fusion, f32[16,30,284]{2,1,0:T(8,128)S(1)} %get-tuple-element.238, f32[16,30,284]{2,1,0:T(8,128)S(1)} %get-tuple-element.237, f32[16,30,284]{2,1,0:T(8,128)S(1)} %get-tuple-element.236, f32[16,30,284]{2,1,0:T(8,128)S(1)} %get-tuple-element.235, ...), kind=kLoop, calls=%fused_computation.15 | loop fusion | flops 1772160 | bytes 3273952 | tf_op jit(solution)/shard_map/add | solution.py:130
  46.6 0.2 fusion.42
  46.8 0.2 constant_dynamic-update-slice_fusion.112
  47.2 0.2 add_multiply_fusion.2
  47.3 0.8 %multiply_add_fusion.1 = f32[16,30,284]{2,1,0:T(8,128)S(1)} fusion(f32[16,30,284]{2,1,0:T(8,128)S(1)} %add_multiply_fusion.2, f32[16,30,284]{2,1,0:T(8,128)S(1)} %get-tuple-element.238, f32[16,30,284]{2,1,0:T(8,128)S(1)} %get-tuple-element.237, f32[16,30,284]{2,1,0:T(8,128)S(1)} %get-tuple-element.236, f32[16,30,284]{2,1,0:T(8,128)S(1)} %get-tuple-element.235, ...), kind=kLoop, calls=%fused_computation.13 | loop fusion | flops 1772160 | bytes 3273952 | tf_op jit(solution)/shard_map/add | solution.py:130
  48.1 0.2 fusion.26
  48.3 0.2 constant_dynamic-update-slice_fusion.128
  48.7 0.2 add_multiply_fusion.1
  48.9 0.8 %multiply_add_fusion = f32[16,30,284]{2,1,0:T(8,128)S(1)} fusion(f32[16,30,284]{2,1,0:T(8,128)S(1)} %add_multiply_fusion.1, f32[16,30,284]{2,1,0:T(8,128)S(1)} %get-tuple-element.238, f32[16,30,284]{2,1,0:T(8,128)S(1)} %get-tuple-element.237, f32[16,30,284]{2,1,0:T(8,128)S(1)} %get-tuple-element.236, f32[16,30,284]{2,1,0:T(8,128)S(1)} %get-tuple-element.235, ...), kind=kLoop, calls=%fused_computation.11 | loop fusion | flops 1772160 | bytes 3273952 | tf_op jit(solution)/shard_map/add | solution.py:130
  49.7 0.2 fusion.10
  49.9 0.2 constant_dynamic-update-slice_fusion.144
  50.3 0.2 add_multiply_fusion
  50.5 0.2 slice_bitcast_fusion.1
  50.7 0.7 %pad_maximum_fusion.3 = f32[2,16,16,128]{3,2,1,0:T(8,128)} fusion(f32[1,16,16,128]{3,2,1,0:T(8,128)S(1)} %get-tuple-element.284, f32[1,16,16,128]{3,2,1,0:T(8,128)S(1)} %get-tuple-element.285), kind=kLoop, calls=%fused_computation.35 | loop fusion | flops 65536 | bytes 524288 | tf_op jit(solution)/shard_map/stack | solution.py:250
  51.4 0.7 %pad_maximum_fusion.4 = f32[2,16,16,128]{3,2,1,0:T(8,128)} fusion(f32[1,16,16,128]{3,2,1,0:T(8,128)S(1)} %get-tuple-element.245, f32[1,16,16,128]{3,2,1,0:T(8,128)S(1)} %get-tuple-element.244), kind=kLoop, calls=%fused_computation.38 | loop fusion | flops 65536 | bytes 524288 | tf_op jit(solution)/shard_map/stack | solution.py:250
  52.2 0.4 select_reduce_fusion.1
  52.7 9.0 %all_gather.7 = f32[8,8,16]{2,1,0:T(8,128)S(1)} all-gather(f32[1,8,16]{2,1,0:T(8,128)S(1)} %all_gather_reshape.3), channel_id=1, replica_groups=mesh['gx'=4,'gy'=8] {'gy'}, dimensions={0}, use_global_device_ids=true | all-gather | bytes 4608 | tf_op jit(solution)/shard_map/all_gather | solution.py:261
  61.7 0.5 dynamic-slice_reduce_fusion
  (185 shorter events, 3.9 us)
Async XLA Ops:
  0.6 13.1 %copy-start = (f32[2,16,16,128]{3,2,1,0:T(8,128)S(1)}, f32[2,16,16,128]{3,2,1,0:T(8,128)}, u32[]{:S(2)}) copy-start(f32[2,16,16,128]{3,2,1,0:T(8,128)} %param.8) | copy-start | bytes 786436
  0.6 12.8 %copy-start.1 = (f32[16,16,128]{2,1,0:T(8,128)S(1)}, f32[16,16,128]{2,1,0:T(8,128)}, u32[]{:S(2)}) copy-start(f32[16,16,128]{2,1,0:T(8,128)} %param.9) | copy-start | bytes 393220
  0.7 12.9 %copy-start.2 = (f32[2,16,128]{2,1,0:T(8,128)S(1)}, f32[2,16,128]{2,1,0:T(8,128)}, u32[]{:S(2)}) copy-start(f32[2,16,128]{2,1,0:T(8,128)} %param.10) | copy-start | bytes 49156
  4.0 10.9 %copy-start.5 = (s32[16,128]{1,0:T(8,128)S(1)}, s32[16,128]{1,0:T(8,128)}, u32[]{:S(2)}) copy-start(s32[16,128]{1,0:T(8,128)} %param.12) | copy-start | bytes 24580
  5.4 11.0 %collective-permute-start.1 = (f32[53,7,128]{2,1,0:T(8,128)S(1)}, f32[53,7,128]{2,1,0:T(8,128)S(1)}, u32[]{:S(2)}, u32[]{:S(2)}) collective-permute-start(f32[53,7,128]{2,1,0:T(8,128)S(1)} %get-tuple-element.283), channel_id=1, source_target_pairs={{8,0},{16,8},{24,16},{9,1},{17,9},{25,17},{10,2},{18,10},{26,18},{... | collective-permute-start | bytes 569864 | tf_op jit(solution)/shard_map/ppermute | solution.py:160
  6.7 10.1 %collective-permute-start = (f32[53,7,128]{2,1,0:T(8,128)S(1)}, f32[53,7,128]{2,1,0:T(8,128)S(1)}, u32[]{:S(2)}, u32[]{:S(2)}) collective-permute-start(f32[53,7,128]{2,1,0:T(8,128)S(1)} %get-tuple-element.282), channel_id=1, source_target_pairs={{0,8},{8,16},{16,24},{1,9},{9,17},{17,25},{2,10},{10,18},{18,26},{... | collective-permute-start | bytes 569864 | tf_op jit(solution)/shard_map/ppermute | solution.py:160
  13.5 2.8 %copy-start.6 = (s32[16,128]{1,0:T(8,128)S(1)}, s32[16,128]{1,0:T(8,128)}, u32[]{:S(2)}) copy-start(s32[16,128]{1,0:T(8,128)} %param.13) | copy-start | bytes 24580
  16.2 5.6 %copy-start.7 = (f32[1,16]{1,0:T(1,128)S(1)}, f32[1,16]{1,0:T(1,128)}, u32[]{:S(2)}) copy-start(f32[1,16]{1,0:T(1,128)} %param.11) | copy-start | bytes 196
  17.1 14.2 %collective-permute-start.3 = (f32[52,30,7]{0,1,2:T(8,128)S(1)}, f32[52,30,7]{0,1,2:T(8,128)S(1)}, u32[]{:S(2)}, u32[]{:S(2)}) collective-permute-start(f32[52,30,7]{0,1,2:T(8,128)S(1)} %pad_maximum_fusion.6), channel_id=1, source_target_pairs={{1,0},{2,1},{3,2},{4,3},{5,4},{6,5},{7,6},{9,8},{10,9},{11,10},{12... | collective-permute-start | bytes 131048 | tf_op jit(solution)/shard_map/ppermute | solution.py:160
  18.8 13.4 %collective-permute-start.2 = (f32[52,30,7]{0,1,2:T(8,128)S(1)}, f32[52,30,7]{0,1,2:T(8,128)S(1)}, u32[]{:S(2)}, u32[]{:S(2)}) collective-permute-start(f32[52,30,7]{0,1,2:T(8,128)S(1)} %pad_maximum_fusion.5), channel_id=1, source_target_pairs={{0,1},{1,2},{2,3},{3,4},{4,5},{5,6},{6,7},{8,9},{9,10},{10,11},{11... | collective-permute-start | bytes 131048 | tf_op jit(solution)/shard_map/ppermute | solution.py:160
  34.7 3.4 %copy-start.3 = (f32[284]{0:T(512)S(1)}, f32[284]{0:T(512)}, u32[]{:S(2)}) copy-start(f32[284]{0:T(512)} %constant.51.clone.1) | copy-start | bytes 3412
  34.7 3.4 %copy-start.4 = (f32[284]{0:T(512)S(1)}, f32[284]{0:T(512)}, u32[]{:S(2)}) copy-start(f32[284]{0:T(512)} %constant.49.clone.1) | copy-start | bytes 3412

commit v7 on v6

--- a/solution.py
+++ b/solution.py
@@ -207,17 +207,24 @@
     ice_cover = packed[at]
     owner_ext = packed[at + 1].astype(jnp.int32)
 
-    tiles = lax.broadcasted_iota(jnp.int32, (tile_count, 1, 1), 0)
-    owner_match = owner_ext[None] == tiles
-    row_strip = jnp.concatenate(
-        [
-            jnp.broadcast_to(friction_rows[0][:, None], (tile_count, HALO)),
-            jnp.broadcast_to(friction_rows[1][:, None], (tile_count, rows)),
-            jnp.broadcast_to(friction_rows[2][:, None], (tile_count, HALO)),
-        ],
-        axis=1,
-    )
-    beta_col = jnp.sum(jnp.where(owner_match, row_strip[:, :, None], 0.0), axis=0)
+    strip_table = friction_rows.T
+    high = lax.reduce_precision(strip_table, exponent_bits=8, mantissa_bits=7)
+    rest = strip_table - high
+    middle = lax.reduce_precision(rest, exponent_bits=8, mantissa_bits=7)
+    low = rest - middle
+    parts = jnp.concatenate([high, middle, low], axis=1).astype(jnp.bfloat16)
+    tiles = lax.broadcasted_iota(jnp.int32, (1, 1, tile_count), 2)
+    one_hot = (owner_ext[:, :, None] == tiles).astype(jnp.bfloat16)
+    looked_up = lax.dot_general(
+        one_hot, parts, (((2,), (0,)), ((), ())), preferred_element_type=jnp.float32
+    )
+    band = lax.broadcasted_iota(jnp.int32, (ext_rows, 1), 0)
+    strip_of_row = jnp.where(band < HALO, 0, jnp.where(band < HALO + rows, 1, 2))
+    near = friction_rows.shape[0]
+    beta_col = sum(
+        jnp.where(strip_of_row == k, looked_up[:, :, k] + looked_up[:, :, near + k] + looked_up[:, :, 2 * near + k], 0.0)
+        for k in range(near)
+    )
 
     def side_by_side(per_comp):
         return jnp.concatenate([per_comp[c] for c in range(comps)], axis=-1)
@@ -254,7 +261,7 @@
     velocity = split(velocity)
     adjoint = split(adjoint)
     grad_col = -ice_cover[inner] * beta_col[inner] * jnp.sum(adjoint[:, -1] * velocity[:, -1], axis=0)
-    block_match = owner_match[:, inner[0], inner[1]]
+    block_match = tile_owner[None] == lax.broadcasted_iota(jnp.int32, (tile_count, 1, 1), 0)
     partial_sum = jnp.sum(jnp.where(block_match, grad_col[None], 0.0), axis=(1, 2))
     owners = lax.axis_size("gy")
     chunk = tile_count // owners

time: 62.7 us -> 64.8 us (1.033)
  waiting for transfers between devices: 0.15 us -> 2.94 us
  blocking collectives: 18.3 us -> 20.9 us
  starting transfers between devices: 11.2 us -> 8.81 us
  other arithmetic: 19.8 us -> 17.7 us
  matrix products: 0 us -> 1.16 us
    all_gather x1, blocking collectives: 9.22 us -> 12.8 us  [local(): friction_rows = lax.all_gather(strips_near, 'gy', axis=1, tiled=True)]
    ppermute x4, waiting for transfers between devices: 0.15 us -> 2.94 us  [shifted(): return lax.ppermute(piece, axis, pairs)]
    ppermute x4, starting transfers between devices: 11.2 us -> 8.81 us  [shifted(): return lax.ppermute(piece, axis, pairs)]
    reduce_sum x1 -> x0, other arithmetic: 2.23 us -> none  [local(): jnp.sum(jnp.where(owner_match, row_strip[:, :, None], 0.0), axis=0)]
    dot_general x0 -> x1, matrix products: none -> 1.16 us  [local(): lax.dot_general(one_hot, parts, (((2,), (0,)), ((), ())), preferred_eleme...]
    all_gather x1, blocking collectives: 9.05 us -> 8.14 us  [local(): gathered = lax.all_gather(partial_sum.reshape(owners, chunk), 'gy')]
    eq x1 -> x2, other arithmetic: 0.88 us -> 0.01 us  [local(): strip_of_row == k]
    reduce_sum x1, other arithmetic: 0.35 us -> 1.03 us  [local(): jnp.sum(jnp.where(block_match, grad_col[None], 0.0), axis=(1, 2))]
where the time goes in v7:
time: 64.8 us; the launch traced here: 64.3 us
  blocking collectives  20.9 us (32%)
  other arithmetic  17.7 us (27%)
  local copies, waits for them, and re-layouts  10.8 us (17%)
  starting transfers between devices  8.81 us (14%)
  waiting for transfers between devices  2.94 us (5%)
  between operations  2.08 us (3%)
  matrix products  1.16 us (2%)
    all_gather x1, blocking collectives, local(): friction_rows = lax.all_gather(strips_near, 'gy', axis=1, tiled=True)  12.8 us
    ppermute x4, starting transfers between devices, shifted(): return lax.ppermute(piece, axis, pairs)  8.81 us
    all_gather x1, blocking collectives, local(): gathered = lax.all_gather(partial_sum.reshape(owners, chunk), 'gy')  8.14 us
    unnamed x84, local copies, waits for them, and re-layouts  3.93 us
    add x4, other arithmetic, relax_lanes(): right_side = rhs_field + lateral  3.53 us
    ppermute x4, waiting for transfers between devices, shifted(): return lax.ppermute(piece, axis, pairs)  2.94 us
    slice x11, local copies, waits for them, and re-layouts, stack_rows(): p[:, :, lo:hi]  2.74 us
    add x3, other arithmetic, relax_lanes(): lateral + along_y * (south_face * vel_pad[:, 1:-1, :-2] + north_face * ve...  2.36 us
  transfers between devices with their start and end apart: 4, of which 1 were waited for; matrix products, arithmetic and copies ran while one was open for 9% of the time, Pallas kernels for 0%

profile of v7, /device:TPU:0, one launch (start us, length us, event | category | flops | bytes accessed | tf_op | source)
XLA Modules:
  0.0 64.3 jit_solution(2047232747821911269)
XLA Ops:
  0.7 1.0 %constant_dynamic-update-slice_fusion.5 = (f32[53,7,128]{2,1,0:T(8,128)S(1)}, f32[53,7,128]{2,1,0:T(8,128)S(1)}) fusion(f32[32,16,128]{2,1,0:T(8,128)} %bitcast.58), kind=kLoop, calls=%fused_computation.47 | loop fusion | bytes 491520
  1.7 0.7 %convert_bitcast_fusion.1 = f32[1,16,128]{2,1,0:T(8,128)S(1)} fusion(s32[16,128]{1,0:T(8,128)} %param.12), kind=kLoop, calls=%fused_computation.649 | loop fusion | flops 2048 | bytes 16384 | tf_op jit(solution)/shard_map/broadcast_in_dim | solution.py:170
  2.4 0.7 %convert_bitcast_fusion = f32[1,16,128]{2,1,0:T(8,128)S(1)} fusion(s32[16,128]{1,0:T(8,128)} %param.13), kind=kLoop, calls=%fused_computation.648 | loop fusion | flops 2048 | bytes 16384 | tf_op jit(solution)/shard_map/broadcast_in_dim | solution.py:171
  3.1 0.9 %constant_dynamic-update-slice_fusion.4 = (f32[53,7,128]{2,1,0:T(8,128)S(1)}, f32[53,7,128]{2,1,0:T(8,128)S(1)}) fusion(f32[53,7,128]{2,1,0:T(8,128)S(1)} %get-tuple-element.254, f32[16,16,128]{2,1,0:T(8,128)} %param.9, f32[53,7,128]{2,1,0:T(8,128)S(1)} %get-tuple-element.255), kind=kLoop, calls=%fused_computation.46 | loop fusion | bytes 245760
  4.0 0.7 %constant_dynamic-update-slice_fusion.3 = (f32[53,7,128]{2,1,0:T(8,128)S(1)}, f32[53,7,128]{2,1,0:T(8,128)S(1)}) fusion(f32[53,7,128]{2,1,0:T(8,128)S(1)} %get-tuple-element.262, f32[2,16,128]{2,1,0:T(8,128)} %param.10, f32[53,7,128]{2,1,0:T(8,128)S(1)} %get-tuple-element.263), kind=kLoop, calls=%fused_computation.45 | loop fusion | bytes 30720
  4.7 0.7 %constant_dynamic-update-slice_fusion = (f32[53,7,128]{2,1,0:T(8,128)S(1)}, f32[53,7,128]{2,1,0:T(8,128)S(1)}) fusion(f32[53,7,128]{2,1,0:T(8,128)S(1)} %get-tuple-element.279, f32[1,16]{1,0:T(1,128)} %param.11, f32[53,7,128]{2,1,0:T(8,128)S(1)} %get-tuple-element.280), kind=kLoop, calls=%fused_computation.42 | loop fusion | bytes 8256 | tf_op jit(solution)/shard_map/concatenate | solution.py:177
  5.4 4.9 %collective-permute-start = (f32[53,7,128]{2,1,0:T(8,128)S(1)}, f32[53,7,128]{2,1,0:T(8,128)S(1)}, u32[]{:S(2)}, u32[]{:S(2)}) collective-permute-start(f32[53,7,128]{2,1,0:T(8,128)S(1)} %get-tuple-element.286), channel_id=1, source_target_pairs={{0,8},{8,16},{16,24},{1,9},{9,17},{17,25},{2,10},{10,18},{18,26},{... | collective-permute-start | bytes 569864 | tf_op jit(solution)/shard_map/ppermute | solution.py:160
  10.3 1.3 %collective-permute-start.1 = (f32[53,7,128]{2,1,0:T(8,128)S(1)}, f32[53,7,128]{2,1,0:T(8,128)S(1)}, u32[]{:S(2)}, u32[]{:S(2)}) collective-permute-start(f32[53,7,128]{2,1,0:T(8,128)S(1)} %get-tuple-element.287), channel_id=1, source_target_pairs={{8,0},{16,8},{24,16},{9,1},{17,9},{25,17},{10,2},{18,10},{26,18},{... | collective-permute-start | bytes 569864 | tf_op jit(solution)/shard_map/ppermute | solution.py:160
  11.6 1.2 %fusion.299 = (f32[32,16,7]{2,1,0:T(8,128)S(1)}, f32[32,16,7]{2,1,0:T(8,128)S(1)}) fusion(f32[32,16,128]{2,1,0:T(8,128)} %bitcast.59), kind=kLoop, calls=%fused_computation.672 | loop fusion | bytes 57344 | tf_op jit(solution)/shard_map/slice | solution.py:184
  13.2 0.2 copy.41
  13.4 0.2 copy.42
  13.6 0.2 copy.43
  13.8 0.2 copy.63
  14.0 0.2 copy.64
  14.3 0.2 copy.48
  14.5 0.2 copy.49
  14.7 0.2 copy.50
  14.9 0.2 copy.65
  15.1 0.2 copy.66
  16.1 2.9 %collective-permute-done.1 = f32[53,7,128]{2,1,0:T(8,128)S(1)} collective-permute-done((f32[53,7,128]{2,1,0:T(8,128)S(1)}, f32[53,7,128]{2,1,0:T(8,128)S(1)}, u32[]{:S(2)}, u32[]{:S(2)}) %collective-permute-start.1) | collective-permute-done | bytes 189984 | tf_op jit(solution)/shard_map/ppermute | solution.py:160
  19.3 1.3 %collective-permute-start.2 = (f32[52,30,7]{0,1,2:T(8,128)S(1)}, f32[52,30,7]{0,1,2:T(8,128)S(1)}, u32[]{:S(2)}, u32[]{:S(2)}) collective-permute-start(f32[52,30,7]{0,1,2:T(8,128)S(1)} %pad_maximum_fusion.5), channel_id=1, source_target_pairs={{0,1},{1,2},{2,3},{3,4},{4,5},{5,6},{6,7},{8,9},{9,10},{10,11},{11... | collective-permute-start | bytes 131048 | tf_op jit(solution)/shard_map/ppermute | solution.py:160
  20.8 0.2 copy.52
  21.0 1.3 %collective-permute-start.3 = (f32[52,30,7]{0,1,2:T(8,128)S(1)}, f32[52,30,7]{0,1,2:T(8,128)S(1)}, u32[]{:S(2)}, u32[]{:S(2)}) collective-permute-start(f32[52,30,7]{0,1,2:T(8,128)S(1)} %pad_maximum_fusion.6), channel_id=1, source_target_pairs={{1,0},{2,1},{3,2},{4,3},{5,4},{6,5},{7,6},{9,8},{10,9},{11,10},{12... | collective-permute-start | bytes 131048 | tf_op jit(solution)/shard_map/ppermute | solution.py:160
  22.3 12.8 %all-gather = f32[8,16,3]{1,2,0:T(4,128)S(1)} all-gather(f32[1,16,3]{1,2,0:T(4,128)S(1)} %maximum_bitcast_fusion.4), channel_id=1, replica_groups=mesh['gx'=4,'gy'=8] {'gy'}, dimensions={0}, use_global_device_ids=true | all-gather | bytes 1728 | tf_op jit(solution)/shard_map/all_gather | solution.py:195
  35.3 0.8 %copy.53 = f32[52,30,7]{2,1,0:T(8,128)S(1)} copy(f32[52,30,7]{0,1,2:T(8,128)S(1)} %collective-permute-done.2) | data formatting | bytes 87360 | tf_op jit(solution)/shard_map/ppermute | solution.py:160
  36.1 0.9 %copy.54 = f32[52,30,7]{2,1,0:T(8,128)S(1)} copy(f32[52,30,7]{0,1,2:T(8,128)S(1)} %collective-permute-done.3) | data formatting | bytes 87360 | tf_op jit(solution)/shard_map/ppermute | solution.py:160
  37.1 1.0 %pad_maximum_fusion = f32[52,30,142]{2,1,0:T(8,128)S(1)} fusion(f32[52,30,7]{2,1,0:T(8,128)S(1)} %copy.54, f32[52,7,128]{2,1,0:T(8,128)S(1)} %slice.1171, f32[52,16,128]{2,1,0:T(8,128)S(1)} %constant_dynamic-update-slice_fusion.12, f32[52,7,128]{2,1,0:T(8,128)S(1)} %slice.1170, f32[52,30,7]{2,1,0:T(8,128)S(1)} %copy.53), kind=kLoop, calls=%fused_computation.2 | loop fusion | flops 886080 | bytes 1772160 | tf_op jit(solution)/shard_map/concatenate | solution.py:198
  38.2 0.2 pad_maximum_fusion.1
  38.4 0.3 fusion.4
  38.8 1.2 %fusion = f32[30,142,9]{1,2,0:T(8,128)S(1)} fusion(s32[30,142]{1,0:T(8,128)S(1)} %get-tuple-element.237, bf16[128,3]{0,1:T(4,128)(2,1)S(1)} %get-tuple-element.284, bf16[128,3]{0,1:T(4,128)(2,1)S(1)} %get-tuple-element.285, bf16[128,3]{0,1:T(4,128)(2,1)S(1)} %get-tuple-element.283), kind=kOutput, calls=%fused_computation.1 | convolution fusion | flops 10367232 | bytes 172704 | tf_op jit(solution)/shard_map/dot_general | solution.py:218
  39.9 0.2 slice_add_fusion.143
  40.4 0.8 %fusion.169 = (f32[16,30,284]{2,1,0:T(8,128)S(1)}, f32[16,30,284]{2,1,0:T(8,128)S(1)}, f32[16,30,284]{2,1,0:T(8,128)S(1)}, f32[16,30,284]{2,1,0:T(8,128)S(1)}, f...) fusion(f32[16,30,142]{2,1,0:T(8,128)S(1)} %get-tuple-element.239, f32[16,30,142]{2,1,0:T(8,128)S(1)} %get-tuple-element.240, ...), kind=kLoop, calls=%fused_computation.670 | loop fusion | flops 2044800 | bytes 4500832 | tf_op jit(solution)/shard_map/add | solution.py:133
  41.2 0.4 add_add_fusion.3
  41.6 0.3 fusion.126
  42.4 0.9 %add_add_fusion.2 = f32[16,30,284]{2,1,0:T(8,128)S(1)} fusion(f32[16,30,284]{2,1,0:T(8,128)S(1)} %broadcast_multiply_fusion.1, f32[16,30,284]{2,1,0:T(8,128)S(1)} %get-tuple-element.235, f32[16,30,284]{2,1,0:T(8,128)S(1)} %get-tuple-element.234, f32[16,30,284]{2,1,0:T(8,128)S(1)} %get-tuple-element.233, f32[16,30,284]{2,1,0:T(8,128)S(1)} %get-tuple-element.232, ...), kind=kLoop, calls=%fused_computation.23 | loop fusion | flops 2044800 | bytes 3819232 | tf_op jit(solution)/shard_map/add | solution.py:133
  43.3 0.2 fusion.108
  43.9 0.2 add_multiply_fusion.5
  44.1 0.9 %add_add_fusion.1 = f32[16,30,284]{2,1,0:T(8,128)S(1)} fusion(f32[16,30,284]{2,1,0:T(8,128)S(1)} %add_multiply_fusion.5, f32[16,30,284]{2,1,0:T(8,128)S(1)} %get-tuple-element.235, f32[16,30,284]{2,1,0:T(8,128)S(1)} %get-tuple-element.234, f32[16,30,284]{2,1,0:T(8,128)S(1)} %get-tuple-element.233, f32[16,30,284]{2,1,0:T(8,128)S(1)} %get-tuple-element.232, ...), kind=kLoop, calls=%fused_computation.21 | loop fusion | flops 2044800 | bytes 3819232 | tf_op jit(solution)/shard_map/add | solution.py:133
  45.0 0.2 fusion.93
  45.1 0.2 constant_dynamic-update-slice_fusion.64
  45.5 0.2 add_multiply_fusion.4
  45.7 0.9 %add_add_fusion = f32[16,30,284]{2,1,0:T(8,128)S(1)} fusion(f32[16,30,284]{2,1,0:T(8,128)S(1)} %add_multiply_fusion.4, f32[16,30,284]{2,1,0:T(8,128)S(1)} %get-tuple-element.235, f32[16,30,284]{2,1,0:T(8,128)S(1)} %get-tuple-element.234, f32[16,30,284]{2,1,0:T(8,128)S(1)} %get-tuple-element.233, f32[16,30,284]{2,1,0:T(8,128)S(1)} %get-tuple-element.232, ...), kind=kLoop, calls=%fused_computation.19 | loop fusion | flops 2044800 | bytes 3819232 | tf_op jit(solution)/shard_map/add | solution.py:133
  46.6 0.2 fusion.78
  46.8 0.2 constant_dynamic-update-slice_fusion.80
  47.2 0.2 add_multiply_fusion.3
  47.5 0.2 fusion.60
  47.7 0.2 constant_dynamic-update-slice_fusion.96
  48.2 0.8 %multiply_add_fusion.2 = f32[16,30,284]{2,1,0:T(8,128)S(1)} fusion(f32[16,30,284]{2,1,0:T(8,128)S(1)} %broadcast_multiply_fusion, f32[16,30,284]{2,1,0:T(8,128)S(1)} %get-tuple-element.235, f32[16,30,284]{2,1,0:T(8,128)S(1)} %get-tuple-element.234, f32[16,30,284]{2,1,0:T(8,128)S(1)} %get-tuple-element.233, f32[16,30,284]{2,1,0:T(8,128)S(1)} %get-tuple-element.232, ...), kind=kLoop, calls=%fused_computation.17 | loop fusion | flops 1772160 | bytes 3273952 | tf_op jit(solution)/shard_map/add | solution.py:130
  49.0 0.2 fusion.44
  49.2 0.2 constant_dynamic-update-slice_fusion.112
  49.6 0.2 add_multiply_fusion.2
  49.8 0.8 %multiply_add_fusion.1 = f32[16,30,284]{2,1,0:T(8,128)S(1)} fusion(f32[16,30,284]{2,1,0:T(8,128)S(1)} %add_multiply_fusion.2, f32[16,30,284]{2,1,0:T(8,128)S(1)} %get-tuple-element.235, f32[16,30,284]{2,1,0:T(8,128)S(1)} %get-tuple-element.234, f32[16,30,284]{2,1,0:T(8,128)S(1)} %get-tuple-element.233, f32[16,30,284]{2,1,0:T(8,128)S(1)} %get-tuple-element.232, ...), kind=kLoop, calls=%fused_computation.15 | loop fusion | flops 1772160 | bytes 3273952 | tf_op jit(solution)/shard_map/add | solution.py:130
  50.6 0.2 fusion.28
  50.7 0.2 constant_dynamic-update-slice_fusion.128
  51.1 0.2 add_multiply_fusion.1
  51.3 0.8 %multiply_add_fusion = f32[16,30,284]{2,1,0:T(8,128)S(1)} fusion(f32[16,30,284]{2,1,0:T(8,128)S(1)} %add_multiply_fusion.1, f32[16,30,284]{2,1,0:T(8,128)S(1)} %get-tuple-element.235, f32[16,30,284]{2,1,0:T(8,128)S(1)} %get-tuple-element.234, f32[16,30,284]{2,1,0:T(8,128)S(1)} %get-tuple-element.233, f32[16,30,284]{2,1,0:T(8,128)S(1)} %get-tuple-element.232, ...), kind=kLoop, calls=%fused_computation.13 | loop fusion | flops 1772160 | bytes 3273952 | tf_op jit(solution)/shard_map/add | solution.py:130
  52.1 0.2 fusion.12
  52.3 0.2 constant_dynamic-update-slice_fusion.144
  52.7 0.2 add_multiply_fusion
  53.0 0.7 %pad_maximum_fusion.4 = f32[2,16,16,128]{3,2,1,0:T(8,128)} fusion(f32[1,16,16,128]{3,2,1,0:T(8,128)S(1)} %get-tuple-element.242, f32[1,16,16,128]{3,2,1,0:T(8,128)S(1)} %get-tuple-element.241), kind=kLoop, calls=%fused_computation.40 | loop fusion | flops 65536 | bytes 524288 | tf_op jit(solution)/shard_map/stack | solution.py:257
  53.7 0.7 %pad_maximum_fusion.3 = f32[2,16,16,128]{3,2,1,0:T(8,128)} fusion(f32[1,16,16,128]{3,2,1,0:T(8,128)S(1)} %get-tuple-element.244, f32[1,16,16,128]{3,2,1,0:T(8,128)S(1)} %get-tuple-element.243), kind=kLoop, calls=%fused_computation.37 | loop fusion | flops 65536 | bytes 524288 | tf_op jit(solution)/shard_map/stack | solution.py:257
  54.5 1.0 %select_reduce_fusion = f32[128]{0:T(128)S(1)} fusion(f32[16,128]{1,0:T(8,128)S(1)} %fusion.162, s32[16,128]{1,0:T(8,128)S(1)} %copy-done.5), kind=kLoop, calls=%fused_computation.4 | loop fusion | flops 786304 | bytes 16896 | tf_op jit(solution)/shard_map/reduce_sum | solution.py:265
  55.7 8.1 %all_gather.7 = f32[8,8,16]{2,1,0:T(8,128)S(1)} all-gather(f32[1,8,16]{2,1,0:T(8,128)S(1)} %all_gather_reshape.3), channel_id=1, replica_groups=mesh['gx'=4,'gy'=8] {'gy'}, dimensions={0}, use_global_device_ids=true | all-gather | bytes 4608 | tf_op jit(solution)/shard_map/all_gather | solution.py:268
  63.8 0.5 dynamic-slice_reduce_fusion
  (185 shorter events, 4.1 us)
Async XLA Ops:
  0.6 12.5 %copy-start = (f32[2,16,16,128]{3,2,1,0:T(8,128)S(1)}, f32[2,16,16,128]{3,2,1,0:T(8,128)}, u32[]{:S(2)}) copy-start(f32[2,16,16,128]{3,2,1,0:T(8,128)} %param.8) | copy-start | bytes 786436
  0.6 12.3 %copy-start.1 = (f32[16,16,128]{2,1,0:T(8,128)S(1)}, f32[16,16,128]{2,1,0:T(8,128)}, u32[]{:S(2)}) copy-start(f32[16,16,128]{2,1,0:T(8,128)} %param.9) | copy-start | bytes 393220
  0.7 12.4 %copy-start.2 = (f32[2,16,128]{2,1,0:T(8,128)S(1)}, f32[2,16,128]{2,1,0:T(8,128)}, u32[]{:S(2)}) copy-start(f32[2,16,128]{2,1,0:T(8,128)} %param.10) | copy-start | bytes 49156
  5.4 10.4 %collective-permute-start = (f32[53,7,128]{2,1,0:T(8,128)S(1)}, f32[53,7,128]{2,1,0:T(8,128)S(1)}, u32[]{:S(2)}, u32[]{:S(2)}) collective-permute-start(f32[53,7,128]{2,1,0:T(8,128)S(1)} %get-tuple-element.286), channel_id=1, source_target_pairs={{0,8},{8,16},{16,24},{1,9},{9,17},{17,25},{2,10},{10,18},{18,26},{... | collective-permute-start | bytes 569864 | tf_op jit(solution)/shard_map/ppermute | solution.py:160
  10.3 8.7 %collective-permute-start.1 = (f32[53,7,128]{2,1,0:T(8,128)S(1)}, f32[53,7,128]{2,1,0:T(8,128)S(1)}, u32[]{:S(2)}, u32[]{:S(2)}) collective-permute-start(f32[53,7,128]{2,1,0:T(8,128)S(1)} %get-tuple-element.287), channel_id=1, source_target_pairs={{8,0},{16,8},{24,16},{9,1},{17,9},{25,17},{10,2},{18,10},{26,18},{... | collective-permute-start | bytes 569864 | tf_op jit(solution)/shard_map/ppermute | solution.py:160
  12.8 2.6 %copy-start.6 = (s32[16,128]{1,0:T(8,128)S(1)}, s32[16,128]{1,0:T(8,128)}, u32[]{:S(2)}) copy-start(s32[16,128]{1,0:T(8,128)} %param.12) | copy-start | bytes 24580
  13.1 2.7 %copy-start.5 = (s32[16,128]{1,0:T(8,128)S(1)}, s32[16,128]{1,0:T(8,128)}, u32[]{:S(2)}) copy-start(s32[16,128]{1,0:T(8,128)} %param.13) | copy-start | bytes 24580
  15.6 6.7 %copy-start.7 = (f32[1,16]{1,0:T(1,128)S(1)}, f32[1,16]{1,0:T(1,128)}, u32[]{:S(2)}) copy-start(f32[1,16]{1,0:T(1,128)} %param.11) | copy-start | bytes 196
  19.3 15.9 %collective-permute-start.2 = (f32[52,30,7]{0,1,2:T(8,128)S(1)}, f32[52,30,7]{0,1,2:T(8,128)S(1)}, u32[]{:S(2)}, u32[]{:S(2)}) collective-permute-start(f32[52,30,7]{0,1,2:T(8,128)S(1)} %pad_maximum_fusion.5), channel_id=1, source_target_pairs={{0,1},{1,2},{2,3},{3,4},{4,5},{5,6},{6,7},{8,9},{9,10},{10,11},{11... | collective-permute-start | bytes 131048 | tf_op jit(solution)/shard_map/ppermute | solution.py:160
  21.0 15.1 %collective-permute-start.3 = (f32[52,30,7]{0,1,2:T(8,128)S(1)}, f32[52,30,7]{0,1,2:T(8,128)S(1)}, u32[]{:S(2)}, u32[]{:S(2)}) collective-permute-start(f32[52,30,7]{0,1,2:T(8,128)S(1)} %pad_maximum_fusion.6), channel_id=1, source_target_pairs={{1,0},{2,1},{3,2},{4,3},{5,4},{6,5},{7,6},{9,8},{10,9},{11,10},{12... | collective-permute-start | bytes 131048 | tf_op jit(solution)/shard_map/ppermute | solution.py:160
  38.4 1.9 %copy-start.3 = (f32[284]{0:T(512)S(1)}, f32[284]{0:T(512)}, u32[]{:S(2)}) copy-start(f32[284]{0:T(512)} %constant.56.clone.1) | copy-start | bytes 3412
  38.4 1.9 %copy-start.4 = (f32[284]{0:T(512)S(1)}, f32[284]{0:T(512)}, u32[]{:S(2)}) copy-start(f32[284]{0:T(512)} %constant.58.clone.1) | copy-start | bytes 3412

commit v8 on v7

--- a/solution.py
+++ b/solution.py
@@ -160,6 +160,19 @@
     return lax.ppermute(piece, axis, pairs)
 
 
+def gather_by_doubling(piece, axis):
+    count = lax.axis_size(axis)
+    if count & (count - 1):
+        return lax.all_gather(piece, axis).reshape(-1)
+    slots = lax.broadcasted_iota(jnp.int32, (count, 1), 0)
+    gathered = jnp.where(slots == lax.axis_index(axis), piece[None, :], 0.0)
+    step = 1
+    while step < count:
+        gathered = gathered + lax.ppermute(gathered, axis, [(i, i ^ step) for i in range(count)])
+        step *= 2
+    return gathered.reshape(-1)
+
+
 def local(forcing, viscosity, observed, beta_tiles, ice_mask, tile_owner):
     comps, layers, rows, cols = forcing.shape
     tiles_here = beta_tiles.shape[1]
@@ -172,9 +185,8 @@
     ]
     plane_count = sum(p.shape[0] for p in planes)
 
-    beta_plane = jnp.pad(beta_tiles, ((0, HALO - 1), (0, cols - tiles_here)))[None]
-    head = jnp.concatenate([p[:, :HALO] for p in planes] + [beta_plane], axis=0)
-    tail = jnp.concatenate([p[:, rows - HALO:] for p in planes] + [beta_plane], axis=0)
+    head = jnp.concatenate([p[:, :HALO] for p in planes], axis=0)
+    tail = jnp.concatenate([p[:, rows - HALO:] for p in planes], axis=0)
     from_above = shifted(tail, "gx", True)
     from_below = shifted(head, "gx", False)
 
@@ -189,10 +201,8 @@
     from_left = shifted(stack_rows(cols - HALO, cols), "gy", True)
     from_right = shifted(stack_rows(0, HALO), "gy", False)
 
-    strips_near = jnp.stack(
-        [from_above[plane_count, 0, :tiles_here], beta_tiles[0], from_below[plane_count, 0, :tiles_here]]
-    )
-    friction_rows = lax.all_gather(strips_near, "gy", axis=1, tiled=True)
+    own_row = gather_by_doubling(beta_tiles[0], "gy")
+    friction_rows = jnp.stack([shifted(own_row, "gx", True), own_row, shifted(own_row, "gx", False)])
     tile_count = friction_rows.shape[1]
 
     packed = jnp.concatenate([from_left, stack_rows(0, cols), from_right], axis=2)

time: 64.8 us -> 69 us (1.065)
  starting transfers between devices: 8.81 us -> 20 us
  blocking collectives: 20.9 us -> 12.7 us
  other arithmetic: 17.7 us -> 18.6 us
    all_gather x1 -> x0, blocking collectives: 12.8 us -> none  [local(): friction_rows = lax.all_gather(strips_near, 'gy', axis=1, tiled=True)]
    ppermute x4 -> x6, starting transfers between devices: 8.81 us -> 16.6 us  [shifted(): return lax.ppermute(piece, axis, pairs)]
    all_gather x1, blocking collectives: 8.14 us -> 12.7 us  [local(): gathered = lax.all_gather(partial_sum.reshape(owners, chunk), 'gy')]
    ppermute x0 -> x3, starting transfers between devices: none -> 3.47 us  [gather_by_doubling(): lax.ppermute(gathered, axis, [(i, i ^ step) for i in range(count)])]
    ppermute x0 -> x3, waiting for transfers between devices: none -> 2.04 us  [gather_by_doubling(): lax.ppermute(gathered, axis, [(i, i ^ step) for i in range(count)])]
    ppermute x4 -> x6, waiting for transfers between devices: 2.94 us -> 0.91 us  [shifted(): return lax.ppermute(piece, axis, pairs)]
    select_n x0 -> x1, other arithmetic: none -> 0.77 us  [gather_by_doubling(): gathered = jnp.where(slots == lax.axis_index(axis), piece[None, :], 0.0)]
    slice x11, local copies, waits for them, and re-layouts: 2.74 us -> 3.48 us  [stack_rows(): p[:, :, lo:hi]]
  transfers between devices with their start and end apart: 4 -> 9, of which waited for: 1 -> 3; matrix products, arithmetic and copies ran while one was open for 9% -> 16% of each run, Pallas kernels for 0% -> 0%
where the time goes in v8:
time: 69 us; the launch traced here: 68.4 us
  starting transfers between devices  20 us (29%)
  other arithmetic  18.6 us (27%)
  blocking collectives  12.7 us (18%)
  local copies, waits for them, and re-layouts  10.9 us (16%)
  waiting for transfers between devices  2.95 us (4%)
  between operations  2.08 us (3%)
  matrix products  1.14 us (2%)
    ppermute x6, starting transfers between devices, shifted(): return lax.ppermute(piece, axis, pairs)  16.6 us
    all_gather x1, blocking collectives, local(): gathered = lax.all_gather(partial_sum.reshape(owners, chunk), 'gy')  12.7 us
    unnamed x83, local copies, waits for them, and re-layouts  3.88 us
    add x4, other arithmetic, relax_lanes(): right_side = rhs_field + lateral  3.52 us
    slice x11, local copies, waits for them, and re-layouts, stack_rows(): p[:, :, lo:hi]  3.48 us
    ppermute x3, starting transfers between devices, gather_by_doubling(): lax.ppermute(gathered, axis, [(i, i ^ step) for i in range(count)])  3.47 us
    add x3, other arithmetic, relax_lanes(): lateral + along_y * (south_face * vel_pad[:, 1:-1, :-2] + north_face * ve...  2.35 us
    ppermute x3, waiting for transfers between devices, gather_by_doubling(): lax.ppermute(gathered, axis, [(i, i ^ step) for i in range(count)])  2.04 us
  transfers between devices with their start and end apart: 9, of which 3 were waited for; matrix products, arithmetic and copies ran while one was open for 16% of the time, Pallas kernels for 0%

profile of v8, /device:TPU:0, one launch (start us, length us, event | category | flops | bytes accessed | tf_op | source)
XLA Modules:
  0.0 68.4 jit_solution(11406121166317930402)
XLA Ops:
  0.7 0.8 %broadcast_select_fusion = f32[8,16]{1,0:T(8,128)S(1)} fusion(f32[16]{0:T(128)} %bitcast.59, pred[8]{0:T(512)(128)(4,1)S(1)} %iota_compare_fusion.3), kind=kLoop, calls=%fused_computation.660 | loop fusion | flops 128 | bytes 584 | tf_op jit(solution)/shard_map/jit(_where)/select_n | solution.py:168
  1.4 0.5 collective-permute-start.4
  1.9 0.7 %convert_bitcast_fusion.1 = f32[1,16,128]{2,1,0:T(8,128)S(1)} fusion(s32[16,128]{1,0:T(8,128)} %param.12), kind=kLoop, calls=%fused_computation.647 | loop fusion | flops 2048 | bytes 16384 | tf_op jit(solution)/shard_map/broadcast_in_dim | solution.py:183
  2.6 0.7 %convert_bitcast_fusion = f32[1,16,128]{2,1,0:T(8,128)S(1)} fusion(s32[16,128]{1,0:T(8,128)} %param.13), kind=kLoop, calls=%fused_computation.646 | loop fusion | flops 2048 | bytes 16384 | tf_op jit(solution)/shard_map/broadcast_in_dim | solution.py:184
  3.3 1.0 %constant_dynamic-update-slice_fusion.4 = (f32[52,7,128]{2,1,0:T(8,128)S(1)}, f32[52,7,128]{2,1,0:T(8,128)S(1)}) fusion(f32[32,16,128]{2,1,0:T(8,128)} %bitcast.56), kind=kLoop, calls=%fused_computation.46 | loop fusion | bytes 491520
  4.4 0.9 %constant_dynamic-update-slice_fusion.3 = (f32[52,7,128]{2,1,0:T(8,128)S(1)}, f32[52,7,128]{2,1,0:T(8,128)S(1)}) fusion(f32[52,7,128]{2,1,0:T(8,128)S(1)} %get-tuple-element.254, f32[16,16,128]{2,1,0:T(8,128)} %param.9, f32[52,7,128]{2,1,0:T(8,128)S(1)} %get-tuple-element.255), kind=kLoop, calls=%fused_computation.45 | loop fusion | bytes 245760
  5.3 0.7 %constant_dynamic-update-slice_fusion.2 = (f32[52,7,128]{2,1,0:T(8,128)S(1)}, f32[52,7,128]{2,1,0:T(8,128)S(1)}) fusion(f32[52,7,128]{2,1,0:T(8,128)S(1)} %get-tuple-element.262, f32[2,16,128]{2,1,0:T(8,128)} %param.10, f32[52,7,128]{2,1,0:T(8,128)S(1)} %get-tuple-element.263), kind=kLoop, calls=%fused_computation.44 | loop fusion | bytes 30720
  6.0 4.5 %collective-permute-start = (f32[52,7,128]{2,1,0:T(8,128)S(1)}, f32[52,7,128]{2,1,0:T(8,128)S(1)}, u32[]{:S(2)}, u32[]{:S(2)}) collective-permute-start(f32[52,7,128]{2,1,0:T(8,128)S(1)} %get-tuple-element.279), channel_id=1, source_target_pairs={{0,8},{8,16},{16,24},{1,9},{9,17},{17,25},{2,10},{10,18},{18,26},{... | collective-permute-start | bytes 559112 | tf_op jit(solution)/shard_map/ppermute | solution.py:160
  10.5 1.3 %collective-permute-start.1 = (f32[52,7,128]{2,1,0:T(8,128)S(1)}, f32[52,7,128]{2,1,0:T(8,128)S(1)}, u32[]{:S(2)}, u32[]{:S(2)}) collective-permute-start(f32[52,7,128]{2,1,0:T(8,128)S(1)} %get-tuple-element.280), channel_id=1, source_target_pairs={{8,0},{16,8},{24,16},{9,1},{17,9},{25,17},{10,2},{18,10},{26,18},{... | collective-permute-start | bytes 559112 | tf_op jit(solution)/shard_map/ppermute | solution.py:160
  11.9 0.9 %fusion.304 = (f32[2,16,7]{2,1,0:T(8,128)S(1)}, f32[2,16,7]{2,1,0:T(8,128)S(1)}) fusion(f32[2,16,128]{2,1,0:T(8,128)} %param.10), kind=kLoop, calls=%fused_computation.675 | loop fusion | bytes 3584 | tf_op jit(solution)/shard_map/slice | solution.py:196
  12.8 1.1 %fusion.303 = (f32[16,16,7]{2,1,0:T(8,128)S(1)}, f32[16,16,7]{2,1,0:T(8,128)S(1)}) fusion(f32[16,16,128]{2,1,0:T(8,128)} %param.9), kind=kLoop, calls=%fused_computation.674 | loop fusion | bytes 28672 | tf_op jit(solution)/shard_map/slice | solution.py:196
  14.3 0.2 copy.61
  14.6 1.5 %collective-permute-start.5 = (f32[8,16]{1,0:T(8,128)S(1)}, f32[8,16]{1,0:T(8,128)S(1)}, u32[]{:S(2)}, u32[]{:S(2)}) collective-permute-start(f32[8,16]{1,0:T(8,128)S(1)} %fusion.168), channel_id=1, source_target_pairs={{0,2},{1,3},{2,0},{3,1},{4,6},{5,7},{6,4},{7,5},{8,10},{9,11},{10,... | collective-permute-start | bytes 1544 | tf_op jit(solution)/shard_map/ppermute | solution.py:171
  16.1 0.2 copy.40
  16.3 0.2 copy.41
  16.5 0.2 copy.63
  16.7 0.2 copy.47
  17.0 0.2 copy.48
  17.2 1.0 %collective-permute-done.5 = f32[8,16]{1,0:T(8,128)S(1)} collective-permute-done((f32[8,16]{1,0:T(8,128)S(1)}, f32[8,16]{1,0:T(8,128)S(1)}, u32[]{:S(2)}, u32[]{:S(2)}) %collective-permute-start.5) | collective-permute-done | bytes 544 | tf_op jit(solution)/shard_map/ppermute | solution.py:171
  18.3 1.5 %collective-permute-start.6 = (f32[8,16]{1,0:T(8,128)S(1)}, f32[8,16]{1,0:T(8,128)S(1)}, u32[]{:S(2)}, u32[]{:S(2)}) collective-permute-start(f32[8,16]{1,0:T(8,128)S(1)} %fusion.307), channel_id=1, source_target_pairs={{0,4},{1,5},{2,6},{3,7},{4,0},{5,1},{6,2},{7,3},{8,12},{9,13},{10,... | collective-permute-start | bytes 1544 | tf_op jit(solution)/shard_map/ppermute | solution.py:171
  19.8 0.2 copy.60
  20.0 0.2 copy.62
  20.2 0.2 copy.39
  20.4 0.2 copy.46
  20.9 1.0 %collective-permute-done.6 = f32[8,16]{1,0:T(8,128)S(1)} collective-permute-done((f32[8,16]{1,0:T(8,128)S(1)}, f32[8,16]{1,0:T(8,128)S(1)}, u32[]{:S(2)}, u32[]{:S(2)}) %collective-permute-start.6) | collective-permute-done | bytes 544 | tf_op jit(solution)/shard_map/ppermute | solution.py:171
  22.1 1.3 %collective-permute-start.8 = (f32[128]{0:T(128)S(1)}, f32[128]{0:T(128)S(1)}, u32[]{:S(2)}, u32[]{:S(2)}) collective-permute-start(f32[128]{0:T(128)S(1)} %reshape.111), channel_id=1, source_target_pairs={{8,0},{16,8},{24,16},{9,1},{17,9},{25,17},{10,2},{18,10},{26,18},{... | collective-permute-start | bytes 1544 | tf_op jit(solution)/shard_map/ppermute | solution.py:160
  23.3 5.2 %collective-permute-start.7 = (f32[128]{0:T(128)S(1)}, f32[128]{0:T(128)S(1)}, u32[]{:S(2)}, u32[]{:S(2)}) collective-permute-start(f32[128]{0:T(128)S(1)} %reshape.111), channel_id=1, source_target_pairs={{0,8},{8,16},{16,24},{1,9},{9,17},{17,25},{2,10},{10,18},{18,26},{... | collective-permute-start | bytes 1544 | tf_op jit(solution)/shard_map/ppermute | solution.py:160
  29.5 1.3 %collective-permute-start.3 = (f32[52,30,7]{0,1,2:T(8,128)S(1)}, f32[52,30,7]{0,1,2:T(8,128)S(1)}, u32[]{:S(2)}, u32[]{:S(2)}) collective-permute-start(f32[52,30,7]{0,1,2:T(8,128)S(1)} %pad_maximum_fusion.6), channel_id=1, source_target_pairs={{1,0},{2,1},{3,2},{4,3},{5,4},{6,5},{7,6},{9,8},{10,9},{11,10},{12... | collective-permute-start | bytes 131048 | tf_op jit(solution)/shard_map/ppermute | solution.py:160
  30.8 3.0 %collective-permute-start.2 = (f32[52,30,7]{0,1,2:T(8,128)S(1)}, f32[52,30,7]{0,1,2:T(8,128)S(1)}, u32[]{:S(2)}, u32[]{:S(2)}) collective-permute-start(f32[52,30,7]{0,1,2:T(8,128)S(1)} %pad_maximum_fusion.5), channel_id=1, source_target_pairs={{0,1},{1,2},{2,3},{3,4},{4,5},{5,6},{6,7},{8,9},{9,10},{10,11},{11... | collective-permute-start | bytes 131048 | tf_op jit(solution)/shard_map/ppermute | solution.py:160
  33.9 0.9 %collective-permute-done.2 = f32[52,30,7]{0,1,2:T(8,128)S(1)} collective-permute-done((f32[52,30,7]{0,1,2:T(8,128)S(1)}, f32[52,30,7]{0,1,2:T(8,128)S(1)}, u32[]{:S(2)}, u32[]{:S(2)}) %collective-permute-start.2) | collective-permute-done | bytes 43712 | tf_op jit(solution)/shard_map/ppermute | solution.py:160
  34.8 0.8 %copy.51 = f32[52,30,7]{2,1,0:T(8,128)S(1)} copy(f32[52,30,7]{0,1,2:T(8,128)S(1)} %collective-permute-done.2) | data formatting | bytes 87360 | tf_op jit(solution)/shard_map/ppermute | solution.py:160
  35.7 0.9 %copy.52 = f32[52,30,7]{2,1,0:T(8,128)S(1)} copy(f32[52,30,7]{0,1,2:T(8,128)S(1)} %collective-permute-done.3) | data formatting | bytes 87360 | tf_op jit(solution)/shard_map/ppermute | solution.py:160
  36.5 1.0 %pad_maximum_fusion = f32[52,30,142]{2,1,0:T(8,128)S(1)} fusion(f32[52,30,7]{2,1,0:T(8,128)S(1)} %copy.52, f32[52,7,128]{2,1,0:T(8,128)S(1)} %collective-permute-done.1, f32[52,16,128]{2,1,0:T(8,128)S(1)} %constant_dynamic-update-slice_fusion.10, f32[52,7,128]{2,1,0:T(8,128)S(1)} %collective-permute-done, f32[52,30,7]{2,1,0:T(8,128)S(1)} %copy.51), kind=kLoop, calls=%fused_computation.2 | loop fusion | flops 886080 | bytes 1772160 | tf_op jit(solution)/shard_map/concatenate | solution.py:208
  37.6 0.3 fusion.4
  37.9 0.2 pad_maximum_fusion.1
  38.4 1.1 %fusion = f32[30,142,9]{1,2,0:T(8,128)S(1)} fusion(s32[30,142]{1,0:T(8,128)S(1)} %get-tuple-element.237, bf16[128,3]{0,1:T(4,128)(2,1)S(1)} %get-tuple-element.285, bf16[128,3]{0,1:T(4,128)(2,1)S(1)} %get-tuple-element.284, bf16[128,3]{0,1:T(4,128)(2,1)S(1)} %get-tuple-element.283), kind=kOutput, calls=%fused_computation.1 | convolution fusion | flops 10367232 | bytes 172704 | tf_op jit(solution)/shard_map/dot_general | solution.py:228
  39.5 0.2 slice_add_fusion.143
  39.9 0.8 %fusion.170 = (f32[16,30,284]{2,1,0:T(8,128)S(1)}, f32[16,30,284]{2,1,0:T(8,128)S(1)}, f32[16,30,284]{2,1,0:T(8,128)S(1)}, f32[16,30,284]{2,1,0:T(8,128)S(1)}, f...) fusion(f32[16,30,142]{2,1,0:T(8,128)S(1)} %get-tuple-element.239, f32[16,30,142]{2,1,0:T(8,128)S(1)} %get-tuple-element.240, ...), kind=kLoop, calls=%fused_computation.669 | loop fusion | flops 2044800 | bytes 4500832 | tf_op jit(solution)/shard_map/add | solution.py:133
  40.7 0.4 add_add_fusion.3
  41.1 0.3 fusion.126
  41.9 0.9 %add_add_fusion.2 = f32[16,30,284]{2,1,0:T(8,128)S(1)} fusion(f32[16,30,284]{2,1,0:T(8,128)S(1)} %broadcast_multiply_fusion.1, f32[16,30,284]{2,1,0:T(8,128)S(1)} %get-tuple-element.235, f32[16,30,284]{2,1,0:T(8,128)S(1)} %get-tuple-element.234, f32[16,30,284]{2,1,0:T(8,128)S(1)} %get-tuple-element.233, f32[16,30,284]{2,1,0:T(8,128)S(1)} %get-tuple-element.232, ...), kind=kLoop, calls=%fused_computation.23 | loop fusion | flops 2044800 | bytes 3819232 | tf_op jit(solution)/shard_map/add | solution.py:133
  42.8 0.2 fusion.108
  43.6 0.9 %add_add_fusion.1 = f32[16,30,284]{2,1,0:T(8,128)S(1)} fusion(f32[16,30,284]{2,1,0:T(8,128)S(1)} %add_multiply_fusion.5, f32[16,30,284]{2,1,0:T(8,128)S(1)} %get-tuple-element.235, f32[16,30,284]{2,1,0:T(8,128)S(1)} %get-tuple-element.234, f32[16,30,284]{2,1,0:T(8,128)S(1)} %get-tuple-element.233, f32[16,30,284]{2,1,0:T(8,128)S(1)} %get-tuple-element.232, ...), kind=kLoop, calls=%fused_computation.21 | loop fusion | flops 2044800 | bytes 3819232 | tf_op jit(solution)/shard_map/add | solution.py:133
  44.5 0.2 fusion.93
  44.6 0.2 constant_dynamic-update-slice_fusion.62
  45.0 0.2 add_multiply_fusion.4
  45.2 0.9 %add_add_fusion = f32[16,30,284]{2,1,0:T(8,128)S(1)} fusion(f32[16,30,284]{2,1,0:T(8,128)S(1)} %add_multiply_fusion.4, f32[16,30,284]{2,1,0:T(8,128)S(1)} %get-tuple-element.235, f32[16,30,284]{2,1,0:T(8,128)S(1)} %get-tuple-element.234, f32[16,30,284]{2,1,0:T(8,128)S(1)} %get-tuple-element.233, f32[16,30,284]{2,1,0:T(8,128)S(1)} %get-tuple-element.232, ...), kind=kLoop, calls=%fused_computation.19 | loop fusion | flops 2044800 | bytes 3819232 | tf_op jit(solution)/shard_map/add | solution.py:133
  46.1 0.2 fusion.78
  46.7 0.2 add_multiply_fusion.3
  47.0 0.2 fusion.60
  47.7 0.8 %multiply_add_fusion.2 = f32[16,30,284]{2,1,0:T(8,128)S(1)} fusion(f32[16,30,284]{2,1,0:T(8,128)S(1)} %broadcast_multiply_fusion, f32[16,30,284]{2,1,0:T(8,128)S(1)} %get-tuple-element.235, f32[16,30,284]{2,1,0:T(8,128)S(1)} %get-tuple-element.234, f32[16,30,284]{2,1,0:T(8,128)S(1)} %get-tuple-element.233, f32[16,30,284]{2,1,0:T(8,128)S(1)} %get-tuple-element.232, ...), kind=kLoop, calls=%fused_computation.17 | loop fusion | flops 1772160 | bytes 3273952 | tf_op jit(solution)/shard_map/add | solution.py:130
  48.5 0.2 fusion.44
  49.1 0.2 add_multiply_fusion.2
  49.2 0.8 %multiply_add_fusion.1 = f32[16,30,284]{2,1,0:T(8,128)S(1)} fusion(f32[16,30,284]{2,1,0:T(8,128)S(1)} %add_multiply_fusion.2, f32[16,30,284]{2,1,0:T(8,128)S(1)} %get-tuple-element.235, f32[16,30,284]{2,1,0:T(8,128)S(1)} %get-tuple-element.234, f32[16,30,284]{2,1,0:T(8,128)S(1)} %get-tuple-element.233, f32[16,30,284]{2,1,0:T(8,128)S(1)} %get-tuple-element.232, ...), kind=kLoop, calls=%fused_computation.15 | loop fusion | flops 1772160 | bytes 3273952 | tf_op jit(solution)/shard_map/add | solution.py:130
  50.0 0.2 fusion.28
  50.6 0.2 add_multiply_fusion.1
  50.8 0.8 %multiply_add_fusion = f32[16,30,284]{2,1,0:T(8,128)S(1)} fusion(f32[16,30,284]{2,1,0:T(8,128)S(1)} %add_multiply_fusion.1, f32[16,30,284]{2,1,0:T(8,128)S(1)} %get-tuple-element.235, f32[16,30,284]{2,1,0:T(8,128)S(1)} %get-tuple-element.234, f32[16,30,284]{2,1,0:T(8,128)S(1)} %get-tuple-element.233, f32[16,30,284]{2,1,0:T(8,128)S(1)} %get-tuple-element.232, ...), kind=kLoop, calls=%fused_computation.13 | loop fusion | flops 1772160 | bytes 3273952 | tf_op jit(solution)/shard_map/add | solution.py:130
  51.6 0.2 fusion.12
  52.2 0.2 add_multiply_fusion
  52.5 0.7 %pad_maximum_fusion.3 = f32[2,16,16,128]{3,2,1,0:T(8,128)} fusion(f32[1,16,16,128]{3,2,1,0:T(8,128)S(1)} %get-tuple-element.244, f32[1,16,16,128]{3,2,1,0:T(8,128)S(1)} %get-tuple-element.243), kind=kLoop, calls=%fused_computation.37 | loop fusion | flops 65536 | bytes 524288 | tf_op jit(solution)/shard_map/stack | solution.py:267
  53.2 0.7 %pad_maximum_fusion.4 = f32[2,16,16,128]{3,2,1,0:T(8,128)} fusion(f32[1,16,16,128]{3,2,1,0:T(8,128)S(1)} %get-tuple-element.242, f32[1,16,16,128]{3,2,1,0:T(8,128)S(1)} %get-tuple-element.241), kind=kLoop, calls=%fused_computation.40 | loop fusion | flops 65536 | bytes 524288 | tf_op jit(solution)/shard_map/stack | solution.py:267
  54.0 1.0 %select_reduce_fusion = f32[128]{0:T(128)S(1)} fusion(f32[16,128]{1,0:T(8,128)S(1)} %fusion.162, s32[16,128]{1,0:T(8,128)S(1)} %copy-done.5), kind=kLoop, calls=%fused_computation.4 | loop fusion | flops 786304 | bytes 16896 | tf_op jit(solution)/shard_map/reduce_sum | solution.py:275
  55.1 12.7 %all_gather.3 = f32[8,8,16]{2,1,0:T(8,128)S(1)} all-gather(f32[1,8,16]{2,1,0:T(8,128)S(1)} %all_gather_reshape.3), channel_id=1, replica_groups=mesh['gx'=4,'gy'=8] {'gy'}, dimensions={0}, use_global_device_ids=true | all-gather | bytes 4608 | tf_op jit(solution)/shard_map/all_gather | solution.py:278
  67.9 0.5 dynamic-slice_reduce_fusion
  (193 shorter events, 5.4 us)
Async XLA Ops:
  0.6 13.3 %copy-start = (f32[2,16,16,128]{3,2,1,0:T(8,128)S(1)}, f32[2,16,16,128]{3,2,1,0:T(8,128)}, u32[]{:S(2)}) copy-start(f32[2,16,16,128]{3,2,1,0:T(8,128)} %param.8) | copy-start | bytes 786436
  1.4 13.1 %collective-permute-start.4 = (f32[8,16]{1,0:T(8,128)S(1)}, f32[8,16]{1,0:T(8,128)S(1)}, u32[]{:S(2)}, u32[]{:S(2)}) collective-permute-start(f32[8,16]{1,0:T(8,128)S(1)} %broadcast_select_fusion), channel_id=1, source_target_pairs={{0,1},{1,0},{2,3},{3,2},{4,5},{5,4},{6,7},{7,6},{8,9},{9,8},{10,11... | collective-permute-start | bytes 1544 | tf_op jit(solution)/shard_map/ppermute | solution.py:171
  2.6 11.6 %copy-start.1 = (f32[16,16,128]{2,1,0:T(8,128)S(1)}, f32[16,16,128]{2,1,0:T(8,128)}, u32[]{:S(2)}) copy-start(f32[16,16,128]{2,1,0:T(8,128)} %param.9) | copy-start | bytes 393220
  3.3 10.9 %copy-start.2 = (f32[2,16,128]{2,1,0:T(8,128)S(1)}, f32[2,16,128]{2,1,0:T(8,128)}, u32[]{:S(2)}) copy-start(f32[2,16,128]{2,1,0:T(8,128)} %param.10) | copy-start | bytes 49156
  4.3 9.9 %copy-start.6 = (s32[16,128]{1,0:T(8,128)S(1)}, s32[16,128]{1,0:T(8,128)}, u32[]{:S(2)}) copy-start(s32[16,128]{1,0:T(8,128)} %param.12) | copy-start | bytes 24580
  4.3 9.9 %copy-start.5 = (s32[16,128]{1,0:T(8,128)S(1)}, s32[16,128]{1,0:T(8,128)}, u32[]{:S(2)}) copy-start(s32[16,128]{1,0:T(8,128)} %param.13) | copy-start | bytes 24580
  4.3 10.2 %copy-start.7 = (f32[1,16]{1,0:T(1,128)S(1)}, f32[1,16]{1,0:T(1,128)}, u32[]{:S(2)}) copy-start(f32[1,16]{1,0:T(1,128)} %param.11) | copy-start | bytes 196
  6.0 23.0 %collective-permute-start = (f32[52,7,128]{2,1,0:T(8,128)S(1)}, f32[52,7,128]{2,1,0:T(8,128)S(1)}, u32[]{:S(2)}, u32[]{:S(2)}) collective-permute-start(f32[52,7,128]{2,1,0:T(8,128)S(1)} %get-tuple-element.279), channel_id=1, source_target_pairs={{0,8},{8,16},{16,24},{1,9},{9,17},{17,25},{2,10},{10,18},{18,26},{... | collective-permute-start | bytes 559112 | tf_op jit(solution)/shard_map/ppermute | solution.py:160
  10.5 18.0 %collective-permute-start.1 = (f32[52,7,128]{2,1,0:T(8,128)S(1)}, f32[52,7,128]{2,1,0:T(8,128)S(1)}, u32[]{:S(2)}, u32[]{:S(2)}) collective-permute-start(f32[52,7,128]{2,1,0:T(8,128)S(1)} %get-tuple-element.280), channel_id=1, source_target_pairs={{8,0},{16,8},{24,16},{9,1},{17,9},{25,17},{10,2},{18,10},{26,18},{... | collective-permute-start | bytes 559112 | tf_op jit(solution)/shard_map/ppermute | solution.py:160
  14.6 3.6 %collective-permute-start.5 = (f32[8,16]{1,0:T(8,128)S(1)}, f32[8,16]{1,0:T(8,128)S(1)}, u32[]{:S(2)}, u32[]{:S(2)}) collective-permute-start(f32[8,16]{1,0:T(8,128)S(1)} %fusion.168), channel_id=1, source_target_pairs={{0,2},{1,3},{2,0},{3,1},{4,6},{5,7},{6,4},{7,5},{8,10},{9,11},{10,... | collective-permute-start | bytes 1544 | tf_op jit(solution)/shard_map/ppermute | solution.py:171
  18.3 3.6 %collective-permute-start.6 = (f32[8,16]{1,0:T(8,128)S(1)}, f32[8,16]{1,0:T(8,128)S(1)}, u32[]{:S(2)}, u32[]{:S(2)}) collective-permute-start(f32[8,16]{1,0:T(8,128)S(1)} %fusion.307), channel_id=1, source_target_pairs={{0,4},{1,5},{2,6},{3,7},{4,0},{5,1},{6,2},{7,3},{8,12},{9,13},{10,... | collective-permute-start | bytes 1544 | tf_op jit(solution)/shard_map/ppermute | solution.py:171
  22.1 11.8 %collective-permute-start.8 = (f32[128]{0:T(128)S(1)}, f32[128]{0:T(128)S(1)}, u32[]{:S(2)}, u32[]{:S(2)}) collective-permute-start(f32[128]{0:T(128)S(1)} %reshape.111), channel_id=1, source_target_pairs={{8,0},{16,8},{24,16},{9,1},{17,9},{25,17},{10,2},{18,10},{26,18},{... | collective-permute-start | bytes 1544 | tf_op jit(solution)/shard_map/ppermute | solution.py:160
  23.3 10.5 %collective-permute-start.7 = (f32[128]{0:T(128)S(1)}, f32[128]{0:T(128)S(1)}, u32[]{:S(2)}, u32[]{:S(2)}) collective-permute-start(f32[128]{0:T(128)S(1)} %reshape.111), channel_id=1, source_target_pairs={{0,8},{8,16},{16,24},{1,9},{9,17},{17,25},{2,10},{10,18},{18,26},{... | collective-permute-start | bytes 1544 | tf_op jit(solution)/shard_map/ppermute | solution.py:160
  29.5 6.2 %collective-permute-start.3 = (f32[52,30,7]{0,1,2:T(8,128)S(1)}, f32[52,30,7]{0,1,2:T(8,128)S(1)}, u32[]{:S(2)}, u32[]{:S(2)}) collective-permute-start(f32[52,30,7]{0,1,2:T(8,128)S(1)} %pad_maximum_fusion.6), channel_id=1, source_target_pairs={{1,0},{2,1},{3,2},{4,3},{5,4},{6,5},{7,6},{9,8},{10,9},{11,10},{12... | collective-permute-start | bytes 131048 | tf_op jit(solution)/shard_map/ppermute | solution.py:160
  30.8 4.0 %collective-permute-start.2 = (f32[52,30,7]{0,1,2:T(8,128)S(1)}, f32[52,30,7]{0,1,2:T(8,128)S(1)}, u32[]{:S(2)}, u32[]{:S(2)}) collective-permute-start(f32[52,30,7]{0,1,2:T(8,128)S(1)} %pad_maximum_fusion.5), channel_id=1, source_target_pairs={{0,1},{1,2},{2,3},{3,4},{4,5},{5,6},{6,7},{8,9},{9,10},{10,11},{11... | collective-permute-start | bytes 131048 | tf_op jit(solution)/shard_map/ppermute | solution.py:160
  38.2 1.7 %copy-start.3 = (f32[284]{0:T(512)S(1)}, f32[284]{0:T(512)}, u32[]{:S(2)}) copy-start(f32[284]{0:T(512)} %constant.58.clone.1) | copy-start | bytes 3412
  38.2 1.7 %copy-start.4 = (f32[284]{0:T(512)S(1)}, f32[284]{0:T(512)}, u32[]{:S(2)}) copy-start(f32[284]{0:T(512)} %constant.55.clone.1) | copy-start | bytes 3412

commit v9 on v7

--- a/solution.py
+++ b/solution.py
@@ -195,17 +195,22 @@
     friction_rows = lax.all_gather(strips_near, "gy", axis=1, tiled=True)
     tile_count = friction_rows.shape[1]
 
-    packed = jnp.concatenate([from_left, stack_rows(0, cols), from_right], axis=2)
-    ext_rows, ext_cols = packed.shape[1], packed.shape[2]
+    own_planes = jnp.concatenate(planes, axis=0)
+    ext_rows, ext_cols = rows + 2 * HALO, cols + 2 * HALO
+
+    def extended(lo, hi):
+        middle = jnp.concatenate([from_above[lo:hi], own_planes[lo:hi], from_below[lo:hi]], axis=1)
+        return jnp.concatenate([from_left[lo:hi], middle, from_right[lo:hi]], axis=2)
+
     at = 0
-    forcing_ext = packed[at:at + comps * layers].reshape(comps, layers, ext_rows, ext_cols)
+    forcing_ext = extended(at, at + comps * layers).reshape(comps, layers, ext_rows, ext_cols)
     at += comps * layers
-    visc_ext = packed[at:at + layers]
+    visc_ext = extended(at, at + layers)
     at += layers
-    observed_ext = packed[at:at + comps]
+    observed_ext = extended(at, at + comps)
     at += comps
-    ice_cover = packed[at]
-    owner_ext = packed[at + 1].astype(jnp.int32)
+    ice_cover = extended(at, at + 1)[0]
+    owner_ext = extended(at + 1, at + 2)[0].astype(jnp.int32)
 
     strip_table = friction_rows.T
     high = lax.reduce_precision(strip_table, exponent_bits=8, mantissa_bits=7)

time: 64.8 us -> 72.4 us (1.12)
  local copies, waits for them, and re-layouts: 10.8 us -> 14.6 us
  blocking collectives: 20.9 us -> 23 us
  starting transfers between devices: 8.81 us -> 10.5 us
    all_gather x1, blocking collectives: 8.14 us -> 14.1 us  [local(): gathered = lax.all_gather(partial_sum.reshape(owners, chunk), 'gy')]
    unnamed x84 -> x93, local copies, waits for them, and re-layouts: 3.93 us -> 8.1 us
    all_gather x1, blocking collectives: 12.8 us -> 8.91 us  [local(): friction_rows = lax.all_gather(strips_near, 'gy', axis=1, tiled=True)]
    ppermute x4, starting transfers between devices: 8.81 us -> 10.5 us  [shifted(): return lax.ppermute(piece, axis, pairs)]
    ppermute x2 -> x0, local copies, waits for them, and re-layouts: 1.7 us -> none  [shifted(): return lax.ppermute(piece, axis, pairs)]
    concatenate x0 -> x2, local copies, waits for them, and re-layouts: none -> 1.01 us  [side_by_side(): return jnp.concatenate([per_comp[c] for c in range(comps)], axis=-1)]
    unnamed x66 -> x65, other arithmetic: 1.96 us -> 1.99 us
  transfers between devices with their start and end apart: 4 -> 4, of which waited for: 1 -> 2; matrix products, arithmetic and copies ran while one was open for 9% -> 7% of each run, Pallas kernels for 0% -> 0%
where the time goes in v9:
time: 72.4 us; the launch traced here: 71.7 us
  blocking collectives  23 us (32%)
  other arithmetic  17 us (23%)
  local copies, waits for them, and re-layouts  14.6 us (20%)
  starting transfers between devices  10.5 us (15%)
  waiting for transfers between devices  3.43 us (5%)
  between operations  2.16 us (3%)
  matrix products  0.98 us (1%)
    all_gather x1, blocking collectives, local(): gathered = lax.all_gather(partial_sum.reshape(owners, chunk), 'gy')  14.1 us
    ppermute x4, starting transfers between devices, shifted(): return lax.ppermute(piece, axis, pairs)  10.5 us
    all_gather x1, blocking collectives, local(): friction_rows = lax.all_gather(strips_near, 'gy', axis=1, tiled=True)  8.91 us
    unnamed x93, local copies, waits for them, and re-layouts  8.1 us
    add x4, other arithmetic, relax_lanes(): right_side = rhs_field + lateral  3.5 us
    ppermute x4, waiting for transfers between devices, shifted(): return lax.ppermute(piece, axis, pairs)  3.43 us
    slice x11, local copies, waits for them, and re-layouts, stack_rows(): p[:, :, lo:hi]  2.53 us
    add x3, other arithmetic, relax_lanes(): lateral + along_y * (south_face * vel_pad[:, 1:-1, :-2] + north_face * ve...  2.36 us
  transfers between devices with their start and end apart: 4, of which 2 were waited for; matrix products, arithmetic and copies ran while one was open for 7% of the time, Pallas kernels for 0%

profile of v9, /device:TPU:0, one launch (start us, length us, event | category | flops | bytes accessed | tf_op | source)
XLA Modules:
  0.0 71.7 jit_solution(16809989718618460771)
XLA Ops:
  0.7 0.8 %convert_bitcast_fusion.1 = f32[1,16,128]{2,1,0:T(8,128)S(1)} fusion(s32[16,128]{1,0:T(8,128)} %param.12), kind=kLoop, calls=%fused_computation.631 | loop fusion | flops 2048 | bytes 16384 | tf_op jit(solution)/shard_map/broadcast_in_dim | solution.py:170
  1.4 0.7 convert_bitcast_fusion
  2.1 1.0 %constant_dynamic-update-slice_fusion.5 = (f32[53,7,128]{2,1,0:T(8,128)S(1)}, f32[53,7,128]{2,1,0:T(8,128)S(1)}) fusion(f32[32,16,128]{2,1,0:T(8,128)} %bitcast.60), kind=kLoop, calls=%fused_computation.40 | loop fusion | bytes 491520
  3.1 0.9 %constant_dynamic-update-slice_fusion.4 = (f32[53,7,128]{2,1,0:T(8,128)S(1)}, f32[53,7,128]{2,1,0:T(8,128)S(1)}) fusion(f32[53,7,128]{2,1,0:T(8,128)S(1)} %get-tuple-element.251, f32[16,16,128]{2,1,0:T(8,128)} %param.9, f32[53,7,128]{2,1,0:T(8,128)S(1)} %get-tuple-element.252), kind=kLoop, calls=%fused_computation.39 | loop fusion | bytes 245760
  4.0 0.7 %constant_dynamic-update-slice_fusion.3 = (f32[53,7,128]{2,1,0:T(8,128)S(1)}, f32[53,7,128]{2,1,0:T(8,128)S(1)}) fusion(f32[53,7,128]{2,1,0:T(8,128)S(1)} %get-tuple-element.263, f32[2,16,128]{2,1,0:T(8,128)} %param.10, f32[53,7,128]{2,1,0:T(8,128)S(1)} %get-tuple-element.264), kind=kLoop, calls=%fused_computation.38 | loop fusion | bytes 30720
  4.7 0.7 constant_dynamic-update-slice_fusion
  5.4 4.9 %collective-permute-start = (f32[53,7,128]{2,1,0:T(8,128)S(1)}, f32[53,7,128]{2,1,0:T(8,128)S(1)}, u32[]{:S(2)}, u32[]{:S(2)}) collective-permute-start(f32[53,7,128]{2,1,0:T(8,128)S(1)} %get-tuple-element.292), channel_id=1, source_target_pairs={{0,8},{8,16},{16,24},{1,9},{9,17},{17,25},{2,10},{10,18},{18,26},{... | collective-permute-start | bytes 569864 | tf_op jit(solution)/shard_map/ppermute | solution.py:160
  10.3 1.3 %collective-permute-start.1 = (f32[53,7,128]{2,1,0:T(8,128)S(1)}, f32[53,7,128]{2,1,0:T(8,128)S(1)}, u32[]{:S(2)}, u32[]{:S(2)}) collective-permute-start(f32[53,7,128]{2,1,0:T(8,128)S(1)} %get-tuple-element.293), channel_id=1, source_target_pairs={{8,0},{16,8},{24,16},{9,1},{17,9},{25,17},{10,2},{18,10},{26,18},{... | collective-permute-start | bytes 569864 | tf_op jit(solution)/shard_map/ppermute | solution.py:160
  11.8 0.9 %fusion.302 = (f32[2,16,7]{2,1,0:T(8,128)S(1)}, f32[2,16,7]{2,1,0:T(8,128)S(1)}) fusion(f32[2,16,128]{2,1,0:T(8,128)} %param.10), kind=kLoop, calls=%fused_computation.663 | loop fusion | bytes 3584 | tf_op jit(solution)/shard_map/slice | solution.py:184
  12.9 0.2 copy.80
  13.1 0.2 copy.50
  13.3 0.2 copy.51
  13.6 0.2 copy.83
  13.8 0.2 copy.58
  14.0 0.2 copy.59
  14.2 0.2 copy.79
  14.4 0.2 copy.82
  14.6 0.2 copy.49
  14.8 0.2 copy.57
  15.9 3.1 %collective-permute-done.1 = f32[53,7,128]{2,1,0:T(8,128)S(1)} collective-permute-done((f32[53,7,128]{2,1,0:T(8,128)S(1)}, f32[53,7,128]{2,1,0:T(8,128)S(1)}, u32[]{:S(2)}, u32[]{:S(2)}) %collective-permute-start.1) | collective-permute-done | bytes 189984 | tf_op jit(solution)/shard_map/ppermute | solution.py:160
  19.0 8.9 %all-gather = f32[8,16,3]{1,2,0:T(4,128)S(1)} all-gather(f32[1,16,3]{1,2,0:T(4,128)S(1)} %maximum_bitcast_fusion.5), channel_id=1, replica_groups=mesh['gx'=4,'gy'=8] {'gy'}, dimensions={0}, use_global_device_ids=true | all-gather | bytes 1728 | tf_op jit(solution)/shard_map/all_gather | solution.py:195
  28.5 1.3 %collective-permute-start.3 = (f32[52,30,7]{0,1,2:T(8,128)S(1)}, f32[52,30,7]{0,1,2:T(8,128)S(1)}, u32[]{:S(2)}, u32[]{:S(2)}) collective-permute-start(f32[52,30,7]{0,1,2:T(8,128)S(1)} %pad_maximum_fusion.6), channel_id=1, source_target_pairs={{1,0},{2,1},{3,2},{4,3},{5,4},{6,5},{7,6},{9,8},{10,9},{11,10},{12... | collective-permute-start | bytes 131048 | tf_op jit(solution)/shard_map/ppermute | solution.py:160
  29.9 3.0 %collective-permute-start.2 = (f32[52,30,7]{0,1,2:T(8,128)S(1)}, f32[52,30,7]{0,1,2:T(8,128)S(1)}, u32[]{:S(2)}, u32[]{:S(2)}) collective-permute-start(f32[52,30,7]{0,1,2:T(8,128)S(1)} %pad_maximum_fusion.5), channel_id=1, source_target_pairs={{0,1},{1,2},{2,3},{3,4},{4,5},{5,6},{6,7},{8,9},{9,10},{10,11},{11... | collective-permute-start | bytes 131048 | tf_op jit(solution)/shard_map/ppermute | solution.py:160
  33.2 0.3 copy.98
  33.5 0.4 collective-permute-done.2
  33.9 0.3 copy.97
  34.5 0.4 copy.87
  34.9 0.4 copy.88
  35.4 0.3 copy.81
  35.7 0.3 copy.89
  36.2 0.3 copy.84
  36.5 0.3 copy.90
  37.1 1.0 %fusion = f32[30,142,9]{1,2,0:T(8,128)S(1)} fusion(s32[30,142]{1,0:T(8,128)S(1)} %get-tuple-element.295, bf16[128,3]{0,1:T(4,128)(2,1)S(1)} %get-tuple-element.290, bf16[128,3]{0,1:T(4,128)(2,1)S(1)} %get-tuple-element.291, bf16[128,3]{0,1:T(4,128)(2,1)S(1)} %get-tuple-element.289), kind=kOutput, calls=%fused_computation.1 | convolution fusion | flops 10367232 | bytes 172704 | tf_op jit(solution)/shard_map/dot_general | solution.py:223
  38.1 0.2 slice_add_fusion.144
  38.4 0.5 copy.85
  39.0 0.5 copy.86
  39.5 0.6 pad_maximum_fusion
  40.3 0.9 %concatenate.104 = f32[16,30,284]{2,1,0:T(8,128)S(1)} concatenate(f32[16,30,7]{2,1,0:T(8,128)S(1)} %copy.87, f32[16,30,128]{2,1,0:T(8,128)S(1)} %pad_maximum_fusion.4, f32[16,30,7]{2,1,0:T(8,128)S(1)} %copy.88, f32[16,30,7]{2,1,0:T(8,128)S(1)} %copy.87, f32[16,30,128]{2,1,0:T(8,128)S(1)} %pad_maximum_fusion.4, f32[16,30,7]{2,1,0:T(8,128)S(1)} %copy.88), dimensions={2} | concatenate | bytes 1090560 | tf_op jit(solution)/shard_map/concatenate | solution.py:235
  41.3 0.6 copy-done.5
  41.9 0.8 %fusion.164 = (f32[16,30,284]{2,1,0:T(8,128)S(1)}, f32[16,30,284]{2,1,0:T(8,128)S(1)}, f32[16,30,284]{2,1,0:T(8,128)S(1)}, f32[16,30,284]{2,1,0:T(8,128)S(1)}, f...) fusion(f32[16,30,142]{2,1,0:T(8,128)S(1)} %get-tuple-element.237, f32[16,30,142]{2,1,0:T(8,128)S(1)} %get-tuple-element.236, ...), kind=kLoop, calls=%fused_computation.652 | loop fusion | flops 2044800 | bytes 4500832 | tf_op jit(solution)/shard_map/add | solution.py:133
  42.7 0.4 add_add_fusion.3
  43.1 0.3 fusion.121
  43.4 0.2 constant_dynamic-update-slice_fusion.27
  43.9 0.9 %add_add_fusion.2 = f32[16,30,284]{2,1,0:T(8,128)S(1)} fusion(f32[16,30,284]{2,1,0:T(8,128)S(1)} %broadcast_multiply_fusion.1, f32[16,30,284]{2,1,0:T(8,128)S(1)} %get-tuple-element.235, f32[16,30,284]{2,1,0:T(8,128)S(1)} %get-tuple-element.234, f32[16,30,284]{2,1,0:T(8,128)S(1)} %get-tuple-element.233, f32[16,30,284]{2,1,0:T(8,128)S(1)} %get-tuple-element.232, ...), kind=kLoop, calls=%fused_computation.18 | loop fusion | flops 2044800 | bytes 3819232 | tf_op jit(solution)/shard_map/add | solution.py:133
  44.8 0.2 fusion.103
  45.6 0.9 %add_add_fusion.1 = f32[16,30,284]{2,1,0:T(8,128)S(1)} fusion(f32[16,30,284]{2,1,0:T(8,128)S(1)} %add_multiply_fusion.5, f32[16,30,284]{2,1,0:T(8,128)S(1)} %get-tuple-element.235, f32[16,30,284]{2,1,0:T(8,128)S(1)} %get-tuple-element.234, f32[16,30,284]{2,1,0:T(8,128)S(1)} %get-tuple-element.233, f32[16,30,284]{2,1,0:T(8,128)S(1)} %get-tuple-element.232, ...), kind=kLoop, calls=%fused_computation.16 | loop fusion | flops 2044800 | bytes 3819232 | tf_op jit(solution)/shard_map/add | solution.py:133
  47.1 0.2 add_multiply_fusion.4
  47.2 0.9 %add_add_fusion = f32[16,30,284]{2,1,0:T(8,128)S(1)} fusion(f32[16,30,284]{2,1,0:T(8,128)S(1)} %add_multiply_fusion.4, f32[16,30,284]{2,1,0:T(8,128)S(1)} %get-tuple-element.235, f32[16,30,284]{2,1,0:T(8,128)S(1)} %get-tuple-element.234, f32[16,30,284]{2,1,0:T(8,128)S(1)} %get-tuple-element.233, f32[16,30,284]{2,1,0:T(8,128)S(1)} %get-tuple-element.232, ...), kind=kLoop, calls=%fused_computation.14 | loop fusion | flops 2044800 | bytes 3819232 | tf_op jit(solution)/shard_map/add | solution.py:133
  48.7 0.2 add_multiply_fusion.3
  49.0 0.2 fusion.57
  49.7 0.8 %multiply_add_fusion.2 = f32[16,30,284]{2,1,0:T(8,128)S(1)} fusion(f32[16,30,284]{2,1,0:T(8,128)S(1)} %broadcast_multiply_fusion, f32[16,30,284]{2,1,0:T(8,128)S(1)} %get-tuple-element.235, f32[16,30,284]{2,1,0:T(8,128)S(1)} %get-tuple-element.234, f32[16,30,284]{2,1,0:T(8,128)S(1)} %get-tuple-element.233, f32[16,30,284]{2,1,0:T(8,128)S(1)} %get-tuple-element.232, ...), kind=kLoop, calls=%fused_computation.12 | loop fusion | flops 1772160 | bytes 3273952 | tf_op jit(solution)/shard_map/add | solution.py:130
  50.4 0.2 fusion.41
  51.0 0.2 add_multiply_fusion.2
  51.2 0.8 %multiply_add_fusion.1 = f32[16,30,284]{2,1,0:T(8,128)S(1)} fusion(f32[16,30,284]{2,1,0:T(8,128)S(1)} %add_multiply_fusion.2, f32[16,30,284]{2,1,0:T(8,128)S(1)} %get-tuple-element.235, f32[16,30,284]{2,1,0:T(8,128)S(1)} %get-tuple-element.234, f32[16,30,284]{2,1,0:T(8,128)S(1)} %get-tuple-element.233, f32[16,30,284]{2,1,0:T(8,128)S(1)} %get-tuple-element.232, ...), kind=kLoop, calls=%fused_computation.10 | loop fusion | flops 1772160 | bytes 3273952 | tf_op jit(solution)/shard_map/add | solution.py:130
  52.0 0.2 fusion.25
  52.6 0.2 add_multiply_fusion.1
  52.8 0.8 %multiply_add_fusion = f32[16,30,284]{2,1,0:T(8,128)S(1)} fusion(f32[16,30,284]{2,1,0:T(8,128)S(1)} %add_multiply_fusion.1, f32[16,30,284]{2,1,0:T(8,128)S(1)} %get-tuple-element.235, f32[16,30,284]{2,1,0:T(8,128)S(1)} %get-tuple-element.234, f32[16,30,284]{2,1,0:T(8,128)S(1)} %get-tuple-element.233, f32[16,30,284]{2,1,0:T(8,128)S(1)} %get-tuple-element.232, ...), kind=kLoop, calls=%fused_computation.8 | loop fusion | flops 1772160 | bytes 3273952 | tf_op jit(solution)/shard_map/add | solution.py:130
  53.6 0.2 fusion.9
  54.2 0.2 add_multiply_fusion
  54.5 0.7 %pad_maximum_fusion.2 = f32[2,16,16,128]{3,2,1,0:T(8,128)} fusion(f32[1,16,16,128]{3,2,1,0:T(8,128)S(1)} %get-tuple-element.241, f32[1,16,16,128]{3,2,1,0:T(8,128)S(1)} %get-tuple-element.240), kind=kLoop, calls=%fused_computation.30 | loop fusion | flops 65536 | bytes 524288 | tf_op jit(solution)/shard_map/stack | solution.py:262
  55.2 0.7 %pad_maximum_fusion.3 = f32[2,16,16,128]{3,2,1,0:T(8,128)} fusion(f32[1,16,16,128]{3,2,1,0:T(8,128)S(1)} %get-tuple-element.239, f32[1,16,16,128]{3,2,1,0:T(8,128)S(1)} %get-tuple-element.238), kind=kLoop, calls=%fused_computation.33 | loop fusion | flops 65536 | bytes 524288 | tf_op jit(solution)/shard_map/stack | solution.py:262
  56.0 1.0 %select_reduce_fusion = f32[128]{0:T(128)S(1)} fusion(f32[16,128]{1,0:T(8,128)S(1)} %fusion.157, s32[16,128]{1,0:T(8,128)S(1)} %copy-done.7), kind=kLoop, calls=%fused_computation.4 | loop fusion | flops 786304 | bytes 16896 | tf_op jit(solution)/shard_map/reduce_sum | solution.py:270
  57.1 14.1 %all_gather.7 = f32[8,8,16]{2,1,0:T(8,128)S(1)} all-gather(f32[1,8,16]{2,1,0:T(8,128)S(1)} %all_gather_reshape.3), channel_id=1, replica_groups=mesh['gx'=4,'gy'=8] {'gy'}, dimensions={0}, use_global_device_ids=true | all-gather | bytes 4608 | tf_op jit(solution)/shard_map/all_gather | solution.py:273
  71.2 0.5 dynamic-slice_reduce_fusion
  (210 shorter events, 6.5 us)
Async XLA Ops:
  0.6 12.1 %copy-start = (f32[2,16,16,128]{3,2,1,0:T(8,128)S(1)}, f32[2,16,16,128]{3,2,1,0:T(8,128)}, u32[]{:S(2)}) copy-start(f32[2,16,16,128]{3,2,1,0:T(8,128)} %param.8) | copy-start | bytes 786436
  0.6 12.0 %copy-start.1 = (f32[16,16,128]{2,1,0:T(8,128)S(1)}, f32[16,16,128]{2,1,0:T(8,128)}, u32[]{:S(2)}) copy-start(f32[16,16,128]{2,1,0:T(8,128)} %param.9) | copy-start | bytes 393220
  5.4 10.1 %collective-permute-start = (f32[53,7,128]{2,1,0:T(8,128)S(1)}, f32[53,7,128]{2,1,0:T(8,128)S(1)}, u32[]{:S(2)}, u32[]{:S(2)}) collective-permute-start(f32[53,7,128]{2,1,0:T(8,128)S(1)} %get-tuple-element.292), channel_id=1, source_target_pairs={{0,8},{8,16},{16,24},{1,9},{9,17},{17,25},{2,10},{10,18},{18,26},{... | collective-permute-start | bytes 569864 | tf_op jit(solution)/shard_map/ppermute | solution.py:160
  10.3 8.7 %collective-permute-start.1 = (f32[53,7,128]{2,1,0:T(8,128)S(1)}, f32[53,7,128]{2,1,0:T(8,128)S(1)}, u32[]{:S(2)}, u32[]{:S(2)}) collective-permute-start(f32[53,7,128]{2,1,0:T(8,128)S(1)} %get-tuple-element.293), channel_id=1, source_target_pairs={{8,0},{16,8},{24,16},{9,1},{17,9},{25,17},{10,2},{18,10},{26,18},{... | collective-permute-start | bytes 569864 | tf_op jit(solution)/shard_map/ppermute | solution.py:160
  15.2 3.8 %copy-start.8 = (f32[1,16]{1,0:T(1,128)S(1)}, f32[1,16]{1,0:T(1,128)}, u32[]{:S(2)}) copy-start(f32[1,16]{1,0:T(1,128)} %param.11) | copy-start | bytes 196
  15.5 17.5 %copy-start.2 = (f32[53,7,128]{2,1,0:T(8,128)}, f32[53,7,128]{2,1,0:T(8,128)S(1)}, u32[]{:S(2)}) copy-start(f32[53,7,128]{2,1,0:T(8,128)S(1)} %collective-permute-done) | copy-start | bytes 569860
  19.0 14.0 %copy-start.3 = (f32[53,7,128]{2,1,0:T(8,128)}, f32[53,7,128]{2,1,0:T(8,128)S(1)}, u32[]{:S(2)}) copy-start(f32[53,7,128]{2,1,0:T(8,128)S(1)} %collective-permute-done.1) | copy-start | bytes 569860
  28.5 4.5 %collective-permute-start.3 = (f32[52,30,7]{0,1,2:T(8,128)S(1)}, f32[52,30,7]{0,1,2:T(8,128)S(1)}, u32[]{:S(2)}, u32[]{:S(2)}) collective-permute-start(f32[52,30,7]{0,1,2:T(8,128)S(1)} %pad_maximum_fusion.6), channel_id=1, source_target_pairs={{1,0},{2,1},{3,2},{4,3},{5,4},{6,5},{7,6},{9,8},{10,9},{11,10},{12... | collective-permute-start | bytes 131048 | tf_op jit(solution)/shard_map/ppermute | solution.py:160
  29.9 4.0 %collective-permute-start.2 = (f32[52,30,7]{0,1,2:T(8,128)S(1)}, f32[52,30,7]{0,1,2:T(8,128)S(1)}, u32[]{:S(2)}, u32[]{:S(2)}) collective-permute-start(f32[52,30,7]{0,1,2:T(8,128)S(1)} %pad_maximum_fusion.5), channel_id=1, source_target_pairs={{0,1},{1,2},{2,3},{3,4},{4,5},{5,6},{6,7},{8,9},{9,10},{10,11},{11... | collective-permute-start | bytes 131048 | tf_op jit(solution)/shard_map/ppermute | solution.py:160
  32.9 1.3 %copy-start.4 = (f32[2,16,128]{2,1,0:T(8,128)S(1)}, f32[2,16,128]{2,1,0:T(8,128)}, u32[]{:S(2)}) copy-start(f32[2,16,128]{2,1,0:T(8,128)} %param.10) | copy-start | bytes 49156
  38.1 1.4 %slice-start = ((f32[53,7,128]{2,1,0:T(8,128)}), f32[32,7,128]{2,1,0:T(8,128)S(1)}, s32[]{:S(2)}) async-start(f32[53,7,128]{2,1,0:T(8,128)} %copy-done.2), calls=%async_computation | async-start | bytes 262144 | tf_op jit(solution)/shard_map/slice | solution.py:202
  38.1 1.5 %slice-start.1 = ((f32[53,7,128]{2,1,0:T(8,128)}), f32[32,7,128]{2,1,0:T(8,128)S(1)}, s32[]{:S(2)}) async-start(f32[53,7,128]{2,1,0:T(8,128)} %copy-done.3), calls=%async_computation.1 | async-start | bytes 262144 | tf_op jit(solution)/shard_map/slice | solution.py:202
  41.2 0.7 copy-start.5
  41.2 0.7 copy-start.6
  54.3 1.7 %copy-start.7 = (s32[16,128]{1,0:T(8,128)S(1)}, s32[16,128]{1,0:T(8,128)}, u32[]{:S(2)}) copy-start(s32[16,128]{1,0:T(8,128)} %param.13) | copy-start | bytes 24580

commit v10 on v6

--- a/solution.py
+++ b/solution.py
@@ -254,7 +254,7 @@
     velocity = split(velocity)
     adjoint = split(adjoint)
     grad_col = -ice_cover[inner] * beta_col[inner] * jnp.sum(adjoint[:, -1] * velocity[:, -1], axis=0)
-    block_match = owner_match[:, inner[0], inner[1]]
+    block_match = tile_owner[None] == lax.broadcasted_iota(jnp.int32, (tile_count, 1, 1), 0)
     partial_sum = jnp.sum(jnp.where(block_match, grad_col[None], 0.0), axis=(1, 2))
     owners = lax.axis_size("gy")
     chunk = tile_count // owners

time: 62.7 us -> 62.5 us (level)
    eq x1 -> x0, other arithmetic: 0.88 us -> none  [local(): owner_match = owner_ext[None] == tiles]
    reduce_sum x1, other arithmetic: 0.35 us -> 1.03 us  [local(): jnp.sum(jnp.where(block_match, grad_col[None], 0.0), axis=(1, 2))]
where the time goes in v10:
time: 62.5 us; the launch traced here: 62 us
  other arithmetic  19.6 us (31%)
  blocking collectives  18.3 us (29%)
  starting transfers between devices  11.2 us (18%)
  local copies, waits for them, and re-layouts  10.7 us (17%)
  between operations  2.09 us (3%)
    ppermute x4, starting transfers between devices, shifted(): return lax.ppermute(piece, axis, pairs)  11.2 us
    all_gather x1, blocking collectives, local(): friction_rows = lax.all_gather(strips_near, 'gy', axis=1, tiled=True)  9.22 us
    all_gather x1, blocking collectives, local(): gathered = lax.all_gather(partial_sum.reshape(owners, chunk), 'gy')  9.04 us
    unnamed x85, local copies, waits for them, and re-layouts  4 us
    add x4, other arithmetic, relax_lanes(): right_side = rhs_field + lateral  3.52 us
    slice x11, local copies, waits for them, and re-layouts, stack_rows(): p[:, :, lo:hi]  2.73 us
    add x3, other arithmetic, relax_lanes(): lateral + along_y * (south_face * vel_pad[:, 1:-1, :-2] + north_face * ve...  2.35 us
    reduce_sum x1, other arithmetic, local(): jnp.sum(jnp.where(owner_match, row_strip[:, :, None], 0.0), axis=0)  2.23 us
  transfers between devices with their start and end apart: 4, of which 1 were waited for; matrix products, arithmetic and copies ran while one was open for 9% of the time, Pallas kernels for 0%

profile of v10, /device:TPU:0, one launch (start us, length us, event | category | flops | bytes accessed | tf_op | source)
XLA Modules:
  0.0 62.0 jit_solution(9759067864470537552)
XLA Ops:
  0.7 1.0 %constant_dynamic-update-slice_fusion.5 = (f32[53,7,128]{2,1,0:T(8,128)S(1)}, f32[53,7,128]{2,1,0:T(8,128)S(1)}) fusion(f32[32,16,128]{2,1,0:T(8,128)} %bitcast.44), kind=kLoop, calls=%fused_computation.46 | loop fusion | bytes 491520
  1.7 0.7 %convert_bitcast_fusion.1 = f32[1,16,128]{2,1,0:T(8,128)S(1)} fusion(s32[16,128]{1,0:T(8,128)} %param.12), kind=kLoop, calls=%fused_computation.636 | loop fusion | flops 2048 | bytes 16384 | tf_op jit(solution)/shard_map/broadcast_in_dim | solution.py:170
  2.4 0.7 %convert_bitcast_fusion = f32[1,16,128]{2,1,0:T(8,128)S(1)} fusion(s32[16,128]{1,0:T(8,128)} %param.13), kind=kLoop, calls=%fused_computation.635 | loop fusion | flops 2048 | bytes 16384 | tf_op jit(solution)/shard_map/broadcast_in_dim | solution.py:171
  3.1 0.9 %constant_dynamic-update-slice_fusion.4 = (f32[53,7,128]{2,1,0:T(8,128)S(1)}, f32[53,7,128]{2,1,0:T(8,128)S(1)}) fusion(f32[53,7,128]{2,1,0:T(8,128)S(1)} %get-tuple-element.250, f32[16,16,128]{2,1,0:T(8,128)} %param.9, f32[53,7,128]{2,1,0:T(8,128)S(1)} %get-tuple-element.251), kind=kLoop, calls=%fused_computation.45 | loop fusion | bytes 245760
  4.0 0.7 %constant_dynamic-update-slice_fusion.3 = (f32[53,7,128]{2,1,0:T(8,128)S(1)}, f32[53,7,128]{2,1,0:T(8,128)S(1)}) fusion(f32[53,7,128]{2,1,0:T(8,128)S(1)} %get-tuple-element.258, f32[2,16,128]{2,1,0:T(8,128)} %param.10, f32[53,7,128]{2,1,0:T(8,128)S(1)} %get-tuple-element.259), kind=kLoop, calls=%fused_computation.44 | loop fusion | bytes 30720
  4.7 0.7 %constant_dynamic-update-slice_fusion = (f32[53,7,128]{2,1,0:T(8,128)S(1)}, f32[53,7,128]{2,1,0:T(8,128)S(1)}) fusion(f32[53,7,128]{2,1,0:T(8,128)S(1)} %get-tuple-element.275, f32[1,16]{1,0:T(1,128)} %param.11, f32[53,7,128]{2,1,0:T(8,128)S(1)} %get-tuple-element.276), kind=kLoop, calls=%fused_computation.41 | loop fusion | bytes 8256 | tf_op jit(solution)/shard_map/concatenate | solution.py:177
  5.4 1.3 %collective-permute-start.1 = (f32[53,7,128]{2,1,0:T(8,128)S(1)}, f32[53,7,128]{2,1,0:T(8,128)S(1)}, u32[]{:S(2)}, u32[]{:S(2)}) collective-permute-start(f32[53,7,128]{2,1,0:T(8,128)S(1)} %get-tuple-element.283), channel_id=1, source_target_pairs={{8,0},{16,8},{24,16},{9,1},{17,9},{25,17},{10,2},{18,10},{26,18},{... | collective-permute-start | bytes 569864 | tf_op jit(solution)/shard_map/ppermute | solution.py:160
  6.7 5.6 %collective-permute-start = (f32[53,7,128]{2,1,0:T(8,128)S(1)}, f32[53,7,128]{2,1,0:T(8,128)S(1)}, u32[]{:S(2)}, u32[]{:S(2)}) collective-permute-start(f32[53,7,128]{2,1,0:T(8,128)S(1)} %get-tuple-element.282), channel_id=1, source_target_pairs={{0,8},{8,16},{16,24},{1,9},{9,17},{17,25},{2,10},{10,18},{18,26},{... | collective-permute-start | bytes 569864 | tf_op jit(solution)/shard_map/ppermute | solution.py:160
  12.3 1.2 %fusion.285 = (f32[32,16,7]{2,1,0:T(8,128)S(1)}, f32[32,16,7]{2,1,0:T(8,128)S(1)}) fusion(f32[32,16,128]{2,1,0:T(8,128)} %bitcast.45), kind=kLoop, calls=%fused_computation.646 | loop fusion | bytes 57344 | tf_op jit(solution)/shard_map/slice | solution.py:184
  13.8 0.2 copy.58
  14.0 0.2 copy.68
  14.2 0.2 copy.69
  14.4 0.2 copy.59
  14.6 0.2 copy.60
  14.9 0.2 copy.51
  15.1 0.2 copy.66
  15.3 0.2 copy.67
  15.5 0.2 copy.52
  15.7 0.2 copy.53
  17.1 1.3 %collective-permute-start.3 = (f32[52,30,7]{0,1,2:T(8,128)S(1)}, f32[52,30,7]{0,1,2:T(8,128)S(1)}, u32[]{:S(2)}, u32[]{:S(2)}) collective-permute-start(f32[52,30,7]{0,1,2:T(8,128)S(1)} %pad_maximum_fusion.6), channel_id=1, source_target_pairs={{1,0},{2,1},{3,2},{4,3},{5,4},{6,5},{7,6},{9,8},{10,9},{11,10},{12... | collective-permute-start | bytes 131048 | tf_op jit(solution)/shard_map/ppermute | solution.py:160
  18.6 0.2 copy.54
  18.8 3.0 %collective-permute-start.2 = (f32[52,30,7]{0,1,2:T(8,128)S(1)}, f32[52,30,7]{0,1,2:T(8,128)S(1)}, u32[]{:S(2)}, u32[]{:S(2)}) collective-permute-start(f32[52,30,7]{0,1,2:T(8,128)S(1)} %pad_maximum_fusion.5), channel_id=1, source_target_pairs={{0,1},{1,2},{2,3},{3,4},{4,5},{5,6},{6,7},{8,9},{9,10},{10,11},{11... | collective-permute-start | bytes 131048 | tf_op jit(solution)/shard_map/ppermute | solution.py:160
  21.9 9.2 %all-gather = f32[8,16,3]{1,2,0:T(4,128)S(1)} all-gather(f32[1,16,3]{1,2,0:T(4,128)S(1)} %maximum_bitcast_fusion.2), channel_id=1, replica_groups=mesh['gx'=4,'gy'=8] {'gy'}, dimensions={0}, use_global_device_ids=true | all-gather | bytes 1728 | tf_op jit(solution)/shard_map/all_gather | solution.py:195
  31.3 0.8 %copy.64 = f32[52,30,7]{2,1,0:T(8,128)S(1)} copy(f32[52,30,7]{0,1,2:T(8,128)S(1)} %collective-permute-done.3) | data formatting | bytes 87360 | tf_op jit(solution)/shard_map/ppermute | solution.py:160
  32.2 0.9 %copy.63 = f32[52,30,7]{2,1,0:T(8,128)S(1)} copy(f32[52,30,7]{0,1,2:T(8,128)S(1)} %collective-permute-done.2) | data formatting | bytes 87360 | tf_op jit(solution)/shard_map/ppermute | solution.py:160
  33.0 1.0 %pad_maximum_fusion = f32[52,30,142]{2,1,0:T(8,128)S(1)} fusion(f32[52,30,7]{2,1,0:T(8,128)S(1)} %copy.64, f32[52,7,128]{2,1,0:T(8,128)S(1)} %slice.1147, f32[52,16,128]{2,1,0:T(8,128)S(1)} %constant_dynamic-update-slice_fusion.12, f32[52,7,128]{2,1,0:T(8,128)S(1)} %slice.1146, f32[52,30,7]{2,1,0:T(8,128)S(1)} %copy.63), kind=kLoop, calls=%fused_computation.2 | loop fusion | flops 886080 | bytes 1772160 | tf_op jit(solution)/shard_map/concatenate | solution.py:198
  34.1 0.2 pad_maximum_fusion.1
  34.3 0.3 fusion.2
  34.8 2.2 %select_reduce_fusion = f32[30,142]{1,0:T(8,128)S(1)} fusion(f32[128,30]{0,1:T(8,128)S(1)} %pad_maximum_fusion.16, s32[30,142]{1,0:T(8,128)S(1)} %get-tuple-element.240), kind=kLoop, calls=%fused_computation | loop fusion | flops 1631580 | bytes 49440 | tf_op jit(solution)/shard_map/reduce_sum | solution.py:220
  37.2 0.8 %fusion.155 = (f32[16,30,284]{2,1,0:T(8,128)S(1)}, f32[16,30,284]{2,1,0:T(8,128)S(1)}, f32[16,30,284]{2,1,0:T(8,128)S(1)}, f32[16,30,284]{2,1,0:T(8,128)S(1)}, f...) fusion(f32[16,30,142]{2,1,0:T(8,128)S(1)} %get-tuple-element.242, f32[16,30,142]{2,1,0:T(8,128)S(1)} %get-tuple-element.243, ...), kind=kLoop, calls=%fused_computation.644 | loop fusion | flops 2044800 | bytes 4500832 | tf_op jit(solution)/shard_map/add | solution.py:133
  38.0 0.4 add_add_fusion.3
  38.5 0.3 fusion.124
  39.3 0.9 %add_add_fusion.2 = f32[16,30,284]{2,1,0:T(8,128)S(1)} fusion(f32[16,30,284]{2,1,0:T(8,128)S(1)} %broadcast_multiply_fusion.1, f32[16,30,284]{2,1,0:T(8,128)S(1)} %get-tuple-element.238, f32[16,30,284]{2,1,0:T(8,128)S(1)} %get-tuple-element.237, f32[16,30,284]{2,1,0:T(8,128)S(1)} %get-tuple-element.236, f32[16,30,284]{2,1,0:T(8,128)S(1)} %get-tuple-element.235, ...), kind=kLoop, calls=%fused_computation.22 | loop fusion | flops 2044800 | bytes 3819232 | tf_op jit(solution)/shard_map/add | solution.py:133
  40.2 0.2 fusion.106
  40.3 0.2 constant_dynamic-update-slice_fusion.48
  40.7 0.2 add_multiply_fusion.5
  40.9 0.9 %add_add_fusion.1 = f32[16,30,284]{2,1,0:T(8,128)S(1)} fusion(f32[16,30,284]{2,1,0:T(8,128)S(1)} %add_multiply_fusion.5, f32[16,30,284]{2,1,0:T(8,128)S(1)} %get-tuple-element.238, f32[16,30,284]{2,1,0:T(8,128)S(1)} %get-tuple-element.237, f32[16,30,284]{2,1,0:T(8,128)S(1)} %get-tuple-element.236, f32[16,30,284]{2,1,0:T(8,128)S(1)} %get-tuple-element.235, ...), kind=kLoop, calls=%fused_computation.20 | loop fusion | flops 2044800 | bytes 3819232 | tf_op jit(solution)/shard_map/add | solution.py:133
  41.8 0.2 fusion.91
  42.0 0.2 constant_dynamic-update-slice_fusion.64
  42.4 0.2 add_multiply_fusion.4
  42.6 0.9 %add_add_fusion = f32[16,30,284]{2,1,0:T(8,128)S(1)} fusion(f32[16,30,284]{2,1,0:T(8,128)S(1)} %add_multiply_fusion.4, f32[16,30,284]{2,1,0:T(8,128)S(1)} %get-tuple-element.238, f32[16,30,284]{2,1,0:T(8,128)S(1)} %get-tuple-element.237, f32[16,30,284]{2,1,0:T(8,128)S(1)} %get-tuple-element.236, f32[16,30,284]{2,1,0:T(8,128)S(1)} %get-tuple-element.235, ...), kind=kLoop, calls=%fused_computation.18 | loop fusion | flops 2044800 | bytes 3819232 | tf_op jit(solution)/shard_map/add | solution.py:133
  43.5 0.2 fusion.76
  43.6 0.2 constant_dynamic-update-slice_fusion.80
  44.0 0.2 add_multiply_fusion.3
  44.2 0.2 fusion.58
  44.4 0.2 constant_dynamic-update-slice_fusion.96
  44.9 0.8 %multiply_add_fusion.2 = f32[16,30,284]{2,1,0:T(8,128)S(1)} fusion(f32[16,30,284]{2,1,0:T(8,128)S(1)} %broadcast_multiply_fusion, f32[16,30,284]{2,1,0:T(8,128)S(1)} %get-tuple-element.238, f32[16,30,284]{2,1,0:T(8,128)S(1)} %get-tuple-element.237, f32[16,30,284]{2,1,0:T(8,128)S(1)} %get-tuple-element.236, f32[16,30,284]{2,1,0:T(8,128)S(1)} %get-tuple-element.235, ...), kind=kLoop, calls=%fused_computation.16 | loop fusion | flops 1772160 | bytes 3273952 | tf_op jit(solution)/shard_map/add | solution.py:130
  45.7 0.2 fusion.42
  45.9 0.2 constant_dynamic-update-slice_fusion.112
  46.3 0.2 add_multiply_fusion.2
  46.5 0.8 %multiply_add_fusion.1 = f32[16,30,284]{2,1,0:T(8,128)S(1)} fusion(f32[16,30,284]{2,1,0:T(8,128)S(1)} %add_multiply_fusion.2, f32[16,30,284]{2,1,0:T(8,128)S(1)} %get-tuple-element.238, f32[16,30,284]{2,1,0:T(8,128)S(1)} %get-tuple-element.237, f32[16,30,284]{2,1,0:T(8,128)S(1)} %get-tuple-element.236, f32[16,30,284]{2,1,0:T(8,128)S(1)} %get-tuple-element.235, ...), kind=kLoop, calls=%fused_computation.14 | loop fusion | flops 1772160 | bytes 3273952 | tf_op jit(solution)/shard_map/add | solution.py:130
  47.3 0.2 fusion.26
  47.4 0.2 constant_dynamic-update-slice_fusion.128
  47.8 0.2 add_multiply_fusion.1
  48.0 0.8 %multiply_add_fusion = f32[16,30,284]{2,1,0:T(8,128)S(1)} fusion(f32[16,30,284]{2,1,0:T(8,128)S(1)} %add_multiply_fusion.1, f32[16,30,284]{2,1,0:T(8,128)S(1)} %get-tuple-element.238, f32[16,30,284]{2,1,0:T(8,128)S(1)} %get-tuple-element.237, f32[16,30,284]{2,1,0:T(8,128)S(1)} %get-tuple-element.236, f32[16,30,284]{2,1,0:T(8,128)S(1)} %get-tuple-element.235, ...), kind=kLoop, calls=%fused_computation.12 | loop fusion | flops 1772160 | bytes 3273952 | tf_op jit(solution)/shard_map/add | solution.py:130
  48.8 0.2 fusion.10
  49.0 0.2 constant_dynamic-update-slice_fusion.144
  49.4 0.2 add_multiply_fusion
  49.6 0.2 slice_bitcast_fusion.1
  49.8 0.7 %pad_maximum_fusion.3 = f32[2,16,16,128]{3,2,1,0:T(8,128)} fusion(f32[1,16,16,128]{3,2,1,0:T(8,128)S(1)} %get-tuple-element.284, f32[1,16,16,128]{3,2,1,0:T(8,128)S(1)} %get-tuple-element.285), kind=kLoop, calls=%fused_computation.36 | loop fusion | flops 65536 | bytes 524288 | tf_op jit(solution)/shard_map/stack | solution.py:250
  50.5 0.7 %pad_maximum_fusion.4 = f32[2,16,16,128]{3,2,1,0:T(8,128)} fusion(f32[1,16,16,128]{3,2,1,0:T(8,128)S(1)} %get-tuple-element.245, f32[1,16,16,128]{3,2,1,0:T(8,128)S(1)} %get-tuple-element.244), kind=kLoop, calls=%fused_computation.39 | loop fusion | flops 65536 | bytes 524288 | tf_op jit(solution)/shard_map/stack | solution.py:250
  51.3 1.0 %select_reduce_fusion.1 = f32[128]{0:T(128)S(1)} fusion(f32[16,128]{1,0:T(8,128)S(1)} %fusion.154, s32[16,128]{1,0:T(8,128)S(1)} %copy-done.5), kind=kLoop, calls=%fused_computation.3 | loop fusion | flops 786304 | bytes 16896 | tf_op jit(solution)/shard_map/reduce_sum | solution.py:258
  52.4 9.0 %all_gather.7 = f32[8,8,16]{2,1,0:T(8,128)S(1)} all-gather(f32[1,8,16]{2,1,0:T(8,128)S(1)} %all_gather_reshape.3), channel_id=1, replica_groups=mesh['gx'=4,'gy'=8] {'gy'}, dimensions={0}, use_global_device_ids=true | all-gather | bytes 4608 | tf_op jit(solution)/shard_map/all_gather | solution.py:261
  61.5 0.5 dynamic-slice_reduce_fusion
  (184 shorter events, 3.7 us)
Async XLA Ops:
  0.6 13.1 %copy-start = (f32[2,16,16,128]{3,2,1,0:T(8,128)S(1)}, f32[2,16,16,128]{3,2,1,0:T(8,128)}, u32[]{:S(2)}) copy-start(f32[2,16,16,128]{3,2,1,0:T(8,128)} %param.8) | copy-start | bytes 786436
  0.6 12.8 %copy-start.1 = (f32[16,16,128]{2,1,0:T(8,128)S(1)}, f32[16,16,128]{2,1,0:T(8,128)}, u32[]{:S(2)}) copy-start(f32[16,16,128]{2,1,0:T(8,128)} %param.9) | copy-start | bytes 393220
  0.7 12.9 %copy-start.2 = (f32[2,16,128]{2,1,0:T(8,128)S(1)}, f32[2,16,128]{2,1,0:T(8,128)}, u32[]{:S(2)}) copy-start(f32[2,16,128]{2,1,0:T(8,128)} %param.10) | copy-start | bytes 49156
  4.0 10.9 %copy-start.6 = (s32[16,128]{1,0:T(8,128)S(1)}, s32[16,128]{1,0:T(8,128)}, u32[]{:S(2)}) copy-start(s32[16,128]{1,0:T(8,128)} %param.12) | copy-start | bytes 24580
  5.4 11.0 %collective-permute-start.1 = (f32[53,7,128]{2,1,0:T(8,128)S(1)}, f32[53,7,128]{2,1,0:T(8,128)S(1)}, u32[]{:S(2)}, u32[]{:S(2)}) collective-permute-start(f32[53,7,128]{2,1,0:T(8,128)S(1)} %get-tuple-element.283), channel_id=1, source_target_pairs={{8,0},{16,8},{24,16},{9,1},{17,9},{25,17},{10,2},{18,10},{26,18},{... | collective-permute-start | bytes 569864 | tf_op jit(solution)/shard_map/ppermute | solution.py:160
  6.7 10.1 %collective-permute-start = (f32[53,7,128]{2,1,0:T(8,128)S(1)}, f32[53,7,128]{2,1,0:T(8,128)S(1)}, u32[]{:S(2)}, u32[]{:S(2)}) collective-permute-start(f32[53,7,128]{2,1,0:T(8,128)S(1)} %get-tuple-element.282), channel_id=1, source_target_pairs={{0,8},{8,16},{16,24},{1,9},{9,17},{17,25},{2,10},{10,18},{18,26},{... | collective-permute-start | bytes 569864 | tf_op jit(solution)/shard_map/ppermute | solution.py:160
  13.5 2.8 %copy-start.5 = (s32[16,128]{1,0:T(8,128)S(1)}, s32[16,128]{1,0:T(8,128)}, u32[]{:S(2)}) copy-start(s32[16,128]{1,0:T(8,128)} %param.13) | copy-start | bytes 24580
  16.2 5.6 %copy-start.7 = (f32[1,16]{1,0:T(1,128)S(1)}, f32[1,16]{1,0:T(1,128)}, u32[]{:S(2)}) copy-start(f32[1,16]{1,0:T(1,128)} %param.11) | copy-start | bytes 196
  17.1 14.2 %collective-permute-start.3 = (f32[52,30,7]{0,1,2:T(8,128)S(1)}, f32[52,30,7]{0,1,2:T(8,128)S(1)}, u32[]{:S(2)}, u32[]{:S(2)}) collective-permute-start(f32[52,30,7]{0,1,2:T(8,128)S(1)} %pad_maximum_fusion.6), channel_id=1, source_target_pairs={{1,0},{2,1},{3,2},{4,3},{5,4},{6,5},{7,6},{9,8},{10,9},{11,10},{12... | collective-permute-start | bytes 131048 | tf_op jit(solution)/shard_map/ppermute | solution.py:160
  18.8 13.4 %collective-permute-start.2 = (f32[52,30,7]{0,1,2:T(8,128)S(1)}, f32[52,30,7]{0,1,2:T(8,128)S(1)}, u32[]{:S(2)}, u32[]{:S(2)}) collective-permute-start(f32[52,30,7]{0,1,2:T(8,128)S(1)} %pad_maximum_fusion.5), channel_id=1, source_target_pairs={{0,1},{1,2},{2,3},{3,4},{4,5},{5,6},{6,7},{8,9},{9,10},{10,11},{11... | collective-permute-start | bytes 131048 | tf_op jit(solution)/shard_map/ppermute | solution.py:160
  34.7 2.5 %copy-start.3 = (f32[284]{0:T(512)S(1)}, f32[284]{0:T(512)}, u32[]{:S(2)}) copy-start(f32[284]{0:T(512)} %constant.51.clone.1) | copy-start | bytes 3412
  34.7 2.5 %copy-start.4 = (f32[284]{0:T(512)S(1)}, f32[284]{0:T(512)}, u32[]{:S(2)}) copy-start(f32[284]{0:T(512)} %constant.49.clone.1) | copy-start | bytes 3412

commit v11 on v10

--- a/solution.py
+++ b/solution.py
@@ -254,8 +254,17 @@
     velocity = split(velocity)
     adjoint = split(adjoint)
     grad_col = -ice_cover[inner] * beta_col[inner] * jnp.sum(adjoint[:, -1] * velocity[:, -1], axis=0)
-    block_match = tile_owner[None] == lax.broadcasted_iota(jnp.int32, (tile_count, 1, 1), 0)
-    partial_sum = jnp.sum(jnp.where(block_match, grad_col[None], 0.0), axis=(1, 2))
+    high = lax.reduce_precision(grad_col, exponent_bits=8, mantissa_bits=7)
+    rest = grad_col - high
+    middle = lax.reduce_precision(rest, exponent_bits=8, mantissa_bits=7)
+    low = rest - middle
+    parts = jnp.stack([high, middle, low], axis=-1).reshape(rows * cols, 3).astype(jnp.bfloat16)
+    block_match = tile_owner.reshape(rows * cols, 1) == lax.broadcasted_iota(jnp.int32, (1, tile_count), 1)
+    per_part = lax.dot_general(
+        block_match.astype(jnp.bfloat16), parts, (((0,), (0,)), ((), ())),
+        preferred_element_type=jnp.float32,
+    )
+    partial_sum = per_part[:, 0] + per_part[:, 1] + per_part[:, 2]
     owners = lax.axis_size("gy")
     chunk = tile_count // owners
     gathered = lax.all_gather(partial_sum.reshape(owners, chunk), "gy")

time: 62.5 us -> 62 us (level)
  other arithmetic: 19.6 us -> 18.6 us
    reduce_sum x1 -> x0, other arithmetic: 1.03 us -> none  [local(): jnp.sum(jnp.where(block_match, grad_col[None], 0.0), axis=(1, 2))]
    unnamed x66 -> x68, other arithmetic: 1.96 us -> 2.05 us
    unnamed x85 -> x88, local copies, waits for them, and re-layouts: 4 us -> 4.03 us
where the time goes in v11:
time: 62 us; the launch traced here: 61.5 us
  other arithmetic  18.6 us (30%)
  blocking collectives  18.3 us (30%)
  starting transfers between devices  11.2 us (18%)
  local copies, waits for them, and re-layouts  10.7 us (17%)
  between operations  2.11 us (3%)
    ppermute x4, starting transfers between devices, shifted(): return lax.ppermute(piece, axis, pairs)  11.2 us
    all_gather x1, blocking collectives, local(): friction_rows = lax.all_gather(strips_near, 'gy', axis=1, tiled=True)  9.22 us
    all_gather x1, blocking collectives, local(): gathered = lax.all_gather(partial_sum.reshape(owners, chunk), 'gy')  9.05 us
    unnamed x88, local copies, waits for them, and re-layouts  4.03 us
    add x4, other arithmetic, relax_lanes(): right_side = rhs_field + lateral  3.52 us
    slice x11, local copies, waits for them, and re-layouts, stack_rows(): p[:, :, lo:hi]  2.73 us
    add x3, other arithmetic, relax_lanes(): lateral + along_y * (south_face * vel_pad[:, 1:-1, :-2] + north_face * ve...  2.35 us
    reduce_sum x1, other arithmetic, local(): jnp.sum(jnp.where(owner_match, row_strip[:, :, None], 0.0), axis=0)  2.23 us
  transfers between devices with their start and end apart: 4, of which 1 were waited for; matrix products, arithmetic and copies ran while one was open for 9% of the time, Pallas kernels for 0%

profile of v11, /device:TPU:0, one launch (start us, length us, event | category | flops | bytes accessed | tf_op | source)
XLA Modules:
  0.0 61.5 jit_solution(18409877884954222536)
XLA Ops:
  0.7 1.0 %constant_dynamic-update-slice_fusion.5 = (f32[53,7,128]{2,1,0:T(8,128)S(1)}, f32[53,7,128]{2,1,0:T(8,128)S(1)}) fusion(f32[32,16,128]{2,1,0:T(8,128)} %bitcast.66), kind=kLoop, calls=%fused_computation.47 | loop fusion | bytes 491520
  1.7 0.7 %convert_bitcast_fusion.1 = f32[1,16,128]{2,1,0:T(8,128)S(1)} fusion(s32[16,128]{1,0:T(8,128)} %param.12), kind=kLoop, calls=%fused_computation.650 | loop fusion | flops 2048 | bytes 16384 | tf_op jit(solution)/shard_map/broadcast_in_dim | solution.py:170
  2.4 0.7 %convert_bitcast_fusion = f32[1,16,128]{2,1,0:T(8,128)S(1)} fusion(s32[16,128]{1,0:T(8,128)} %param.13), kind=kLoop, calls=%fused_computation.649 | loop fusion | flops 2048 | bytes 16384 | tf_op jit(solution)/shard_map/broadcast_in_dim | solution.py:171
  3.1 0.9 %constant_dynamic-update-slice_fusion.4 = (f32[53,7,128]{2,1,0:T(8,128)S(1)}, f32[53,7,128]{2,1,0:T(8,128)S(1)}) fusion(f32[53,7,128]{2,1,0:T(8,128)S(1)} %get-tuple-element.252, f32[16,16,128]{2,1,0:T(8,128)} %param.9, f32[53,7,128]{2,1,0:T(8,128)S(1)} %get-tuple-element.253), kind=kLoop, calls=%fused_computation.46 | loop fusion | bytes 245760
  4.0 0.7 %constant_dynamic-update-slice_fusion.3 = (f32[53,7,128]{2,1,0:T(8,128)S(1)}, f32[53,7,128]{2,1,0:T(8,128)S(1)}) fusion(f32[53,7,128]{2,1,0:T(8,128)S(1)} %get-tuple-element.260, f32[2,16,128]{2,1,0:T(8,128)} %param.10, f32[53,7,128]{2,1,0:T(8,128)S(1)} %get-tuple-element.261), kind=kLoop, calls=%fused_computation.45 | loop fusion | bytes 30720
  4.7 0.7 %constant_dynamic-update-slice_fusion = (f32[53,7,128]{2,1,0:T(8,128)S(1)}, f32[53,7,128]{2,1,0:T(8,128)S(1)}) fusion(f32[53,7,128]{2,1,0:T(8,128)S(1)} %get-tuple-element.279, f32[1,16]{1,0:T(1,128)} %param.11, f32[53,7,128]{2,1,0:T(8,128)S(1)} %get-tuple-element.280), kind=kLoop, calls=%fused_computation.42 | loop fusion | bytes 8256 | tf_op jit(solution)/shard_map/concatenate | solution.py:177
  5.4 1.3 %collective-permute-start.1 = (f32[53,7,128]{2,1,0:T(8,128)S(1)}, f32[53,7,128]{2,1,0:T(8,128)S(1)}, u32[]{:S(2)}, u32[]{:S(2)}) collective-permute-start(f32[53,7,128]{2,1,0:T(8,128)S(1)} %get-tuple-element.287), channel_id=1, source_target_pairs={{8,0},{16,8},{24,16},{9,1},{17,9},{25,17},{10,2},{18,10},{26,18},{... | collective-permute-start | bytes 569864 | tf_op jit(solution)/shard_map/ppermute | solution.py:160
  6.7 5.6 %collective-permute-start = (f32[53,7,128]{2,1,0:T(8,128)S(1)}, f32[53,7,128]{2,1,0:T(8,128)S(1)}, u32[]{:S(2)}, u32[]{:S(2)}) collective-permute-start(f32[53,7,128]{2,1,0:T(8,128)S(1)} %get-tuple-element.286), channel_id=1, source_target_pairs={{0,8},{8,16},{16,24},{1,9},{9,17},{17,25},{2,10},{10,18},{18,26},{... | collective-permute-start | bytes 569864 | tf_op jit(solution)/shard_map/ppermute | solution.py:160
  12.3 1.2 %fusion.298 = (f32[32,16,7]{2,1,0:T(8,128)S(1)}, f32[32,16,7]{2,1,0:T(8,128)S(1)}) fusion(f32[32,16,128]{2,1,0:T(8,128)} %bitcast.67), kind=kLoop, calls=%fused_computation.665 | loop fusion | bytes 57344 | tf_op jit(solution)/shard_map/slice | solution.py:184
  13.8 0.2 copy.57
  14.0 0.2 copy.67
  14.2 0.2 copy.68
  14.4 0.2 copy.58
  14.6 0.2 copy.59
  14.9 0.2 copy.50
  15.1 0.2 copy.65
  15.3 0.2 copy.66
  15.5 0.2 copy.51
  15.7 0.2 copy.52
  17.1 1.3 %collective-permute-start.3 = (f32[52,30,7]{0,1,2:T(8,128)S(1)}, f32[52,30,7]{0,1,2:T(8,128)S(1)}, u32[]{:S(2)}, u32[]{:S(2)}) collective-permute-start(f32[52,30,7]{0,1,2:T(8,128)S(1)} %pad_maximum_fusion.6), channel_id=1, source_target_pairs={{1,0},{2,1},{3,2},{4,3},{5,4},{6,5},{7,6},{9,8},{10,9},{11,10},{12... | collective-permute-start | bytes 131048 | tf_op jit(solution)/shard_map/ppermute | solution.py:160
  18.6 0.2 copy.53
  18.8 3.0 %collective-permute-start.2 = (f32[52,30,7]{0,1,2:T(8,128)S(1)}, f32[52,30,7]{0,1,2:T(8,128)S(1)}, u32[]{:S(2)}, u32[]{:S(2)}) collective-permute-start(f32[52,30,7]{0,1,2:T(8,128)S(1)} %pad_maximum_fusion.5), channel_id=1, source_target_pairs={{0,1},{1,2},{2,3},{3,4},{4,5},{5,6},{6,7},{8,9},{9,10},{10,11},{11... | collective-permute-start | bytes 131048 | tf_op jit(solution)/shard_map/ppermute | solution.py:160
  21.9 9.2 %all-gather = f32[8,16,3]{1,2,0:T(4,128)S(1)} all-gather(f32[1,16,3]{1,2,0:T(4,128)S(1)} %maximum_bitcast_fusion.2), channel_id=1, replica_groups=mesh['gx'=4,'gy'=8] {'gy'}, dimensions={0}, use_global_device_ids=true | all-gather | bytes 1728 | tf_op jit(solution)/shard_map/all_gather | solution.py:195
  31.3 0.8 %copy.63 = f32[52,30,7]{2,1,0:T(8,128)S(1)} copy(f32[52,30,7]{0,1,2:T(8,128)S(1)} %collective-permute-done.3) | data formatting | bytes 87360 | tf_op jit(solution)/shard_map/ppermute | solution.py:160
  32.2 0.9 %copy.62 = f32[52,30,7]{2,1,0:T(8,128)S(1)} copy(f32[52,30,7]{0,1,2:T(8,128)S(1)} %collective-permute-done.2) | data formatting | bytes 87360 | tf_op jit(solution)/shard_map/ppermute | solution.py:160
  33.0 1.0 %pad_maximum_fusion = f32[52,30,142]{2,1,0:T(8,128)S(1)} fusion(f32[52,30,7]{2,1,0:T(8,128)S(1)} %copy.63, f32[52,7,128]{2,1,0:T(8,128)S(1)} %slice.1159, f32[52,16,128]{2,1,0:T(8,128)S(1)} %constant_dynamic-update-slice_fusion.12, f32[52,7,128]{2,1,0:T(8,128)S(1)} %slice.1158, f32[52,30,7]{2,1,0:T(8,128)S(1)} %copy.62), kind=kLoop, calls=%fused_computation.2 | loop fusion | flops 886080 | bytes 1772160 | tf_op jit(solution)/shard_map/concatenate | solution.py:198
  34.1 0.2 pad_maximum_fusion.1
  34.3 0.3 fusion.3
  34.8 2.2 %select_reduce_fusion = f32[30,142]{1,0:T(8,128)S(1)} fusion(f32[128,30]{0,1:T(8,128)S(1)} %pad_maximum_fusion.16, s32[30,142]{1,0:T(8,128)S(1)} %get-tuple-element.242), kind=kLoop, calls=%fused_computation | loop fusion | flops 1631580 | bytes 49440 | tf_op jit(solution)/shard_map/reduce_sum | solution.py:220
  37.2 0.8 %fusion.167 = (f32[16,30,284]{2,1,0:T(8,128)S(1)}, f32[16,30,284]{2,1,0:T(8,128)S(1)}, f32[16,30,284]{2,1,0:T(8,128)S(1)}, f32[16,30,284]{2,1,0:T(8,128)S(1)}, f...) fusion(f32[16,30,142]{2,1,0:T(8,128)S(1)} %get-tuple-element.244, f32[16,30,142]{2,1,0:T(8,128)S(1)} %get-tuple-element.245, ...), kind=kLoop, calls=%fused_computation.663 | loop fusion | flops 2044800 | bytes 4500832 | tf_op jit(solution)/shard_map/add | solution.py:133
  38.0 0.4 add_add_fusion.3
  38.5 0.3 fusion.126
  39.3 0.9 %add_add_fusion.2 = f32[16,30,284]{2,1,0:T(8,128)S(1)} fusion(f32[16,30,284]{2,1,0:T(8,128)S(1)} %broadcast_multiply_fusion.1, f32[16,30,284]{2,1,0:T(8,128)S(1)} %get-tuple-element.240, f32[16,30,284]{2,1,0:T(8,128)S(1)} %get-tuple-element.239, f32[16,30,284]{2,1,0:T(8,128)S(1)} %get-tuple-element.238, f32[16,30,284]{2,1,0:T(8,128)S(1)} %get-tuple-element.237, ...), kind=kLoop, calls=%fused_computation.22 | loop fusion | flops 2044800 | bytes 3819232 | tf_op jit(solution)/shard_map/add | solution.py:133
  40.2 0.2 fusion.108
  40.3 0.2 constant_dynamic-update-slice_fusion.48
  40.7 0.2 add_multiply_fusion.5
  40.9 0.9 %add_add_fusion.1 = f32[16,30,284]{2,1,0:T(8,128)S(1)} fusion(f32[16,30,284]{2,1,0:T(8,128)S(1)} %add_multiply_fusion.5, f32[16,30,284]{2,1,0:T(8,128)S(1)} %get-tuple-element.240, f32[16,30,284]{2,1,0:T(8,128)S(1)} %get-tuple-element.239, f32[16,30,284]{2,1,0:T(8,128)S(1)} %get-tuple-element.238, f32[16,30,284]{2,1,0:T(8,128)S(1)} %get-tuple-element.237, ...), kind=kLoop, calls=%fused_computation.20 | loop fusion | flops 2044800 | bytes 3819232 | tf_op jit(solution)/shard_map/add | solution.py:133
  41.8 0.2 fusion.93
  42.0 0.2 constant_dynamic-update-slice_fusion.64
  42.4 0.2 add_multiply_fusion.4
  42.6 0.9 %add_add_fusion = f32[16,30,284]{2,1,0:T(8,128)S(1)} fusion(f32[16,30,284]{2,1,0:T(8,128)S(1)} %add_multiply_fusion.4, f32[16,30,284]{2,1,0:T(8,128)S(1)} %get-tuple-element.240, f32[16,30,284]{2,1,0:T(8,128)S(1)} %get-tuple-element.239, f32[16,30,284]{2,1,0:T(8,128)S(1)} %get-tuple-element.238, f32[16,30,284]{2,1,0:T(8,128)S(1)} %get-tuple-element.237, ...), kind=kLoop, calls=%fused_computation.18 | loop fusion | flops 2044800 | bytes 3819232 | tf_op jit(solution)/shard_map/add | solution.py:133
  43.5 0.2 fusion.78
  43.6 0.2 constant_dynamic-update-slice_fusion.80
  44.0 0.2 add_multiply_fusion.3
  44.2 0.2 fusion.60
  44.4 0.2 constant_dynamic-update-slice_fusion.96
  44.9 0.8 %multiply_add_fusion.2 = f32[16,30,284]{2,1,0:T(8,128)S(1)} fusion(f32[16,30,284]{2,1,0:T(8,128)S(1)} %broadcast_multiply_fusion, f32[16,30,284]{2,1,0:T(8,128)S(1)} %get-tuple-element.240, f32[16,30,284]{2,1,0:T(8,128)S(1)} %get-tuple-element.239, f32[16,30,284]{2,1,0:T(8,128)S(1)} %get-tuple-element.238, f32[16,30,284]{2,1,0:T(8,128)S(1)} %get-tuple-element.237, ...), kind=kLoop, calls=%fused_computation.16 | loop fusion | flops 1772160 | bytes 3273952 | tf_op jit(solution)/shard_map/add | solution.py:130
  45.7 0.2 fusion.44
  45.9 0.2 constant_dynamic-update-slice_fusion.112
  46.3 0.2 add_multiply_fusion.2
  46.5 0.8 %multiply_add_fusion.1 = f32[16,30,284]{2,1,0:T(8,128)S(1)} fusion(f32[16,30,284]{2,1,0:T(8,128)S(1)} %add_multiply_fusion.2, f32[16,30,284]{2,1,0:T(8,128)S(1)} %get-tuple-element.240, f32[16,30,284]{2,1,0:T(8,128)S(1)} %get-tuple-element.239, f32[16,30,284]{2,1,0:T(8,128)S(1)} %get-tuple-element.238, f32[16,30,284]{2,1,0:T(8,128)S(1)} %get-tuple-element.237, ...), kind=kLoop, calls=%fused_computation.14 | loop fusion | flops 1772160 | bytes 3273952 | tf_op jit(solution)/shard_map/add | solution.py:130
  47.3 0.2 fusion.28
  47.4 0.2 constant_dynamic-update-slice_fusion.128
  47.8 0.2 add_multiply_fusion.1
  48.0 0.8 %multiply_add_fusion = f32[16,30,284]{2,1,0:T(8,128)S(1)} fusion(f32[16,30,284]{2,1,0:T(8,128)S(1)} %add_multiply_fusion.1, f32[16,30,284]{2,1,0:T(8,128)S(1)} %get-tuple-element.240, f32[16,30,284]{2,1,0:T(8,128)S(1)} %get-tuple-element.239, f32[16,30,284]{2,1,0:T(8,128)S(1)} %get-tuple-element.238, f32[16,30,284]{2,1,0:T(8,128)S(1)} %get-tuple-element.237, ...), kind=kLoop, calls=%fused_computation.12 | loop fusion | flops 1772160 | bytes 3273952 | tf_op jit(solution)/shard_map/add | solution.py:130
  48.8 0.2 fusion.12
  49.0 0.2 constant_dynamic-update-slice_fusion.144
  49.4 0.2 add_multiply_fusion
  49.6 0.2 slice_bitcast_fusion.1
  49.8 0.7 %pad_maximum_fusion.3 = f32[2,16,16,128]{3,2,1,0:T(8,128)} fusion(f32[1,16,16,128]{3,2,1,0:T(8,128)S(1)} %get-tuple-element.288, f32[1,16,16,128]{3,2,1,0:T(8,128)S(1)} %get-tuple-element.289), kind=kLoop, calls=%fused_computation.37 | loop fusion | flops 65536 | bytes 524288 | tf_op jit(solution)/shard_map/stack | solution.py:250
  50.5 0.7 %pad_maximum_fusion.4 = f32[2,16,16,128]{3,2,1,0:T(8,128)} fusion(f32[1,16,16,128]{3,2,1,0:T(8,128)S(1)} %get-tuple-element.247, f32[1,16,16,128]{3,2,1,0:T(8,128)S(1)} %get-tuple-element.246), kind=kLoop, calls=%fused_computation.40 | loop fusion | flops 65536 | bytes 524288 | tf_op jit(solution)/shard_map/stack | solution.py:250
  51.4 0.5 fusion
  51.9 9.1 %all_gather.7 = f32[8,8,16]{2,1,0:T(8,128)S(1)} all-gather(f32[1,8,16]{2,1,0:T(8,128)S(1)} %add.4639), channel_id=1, replica_groups=mesh['gx'=4,'gy'=8] {'gy'}, dimensions={0}, use_global_device_ids=true | all-gather | bytes 4608 | tf_op jit(solution)/shard_map/all_gather | solution.py:270
  61.0 0.5 dynamic-slice_reduce_fusion
  (189 shorter events, 3.8 us)
Async XLA Ops:
  0.6 13.1 %copy-start = (f32[2,16,16,128]{3,2,1,0:T(8,128)S(1)}, f32[2,16,16,128]{3,2,1,0:T(8,128)}, u32[]{:S(2)}) copy-start(f32[2,16,16,128]{3,2,1,0:T(8,128)} %param.8) | copy-start | bytes 786436
  0.6 12.8 %copy-start.1 = (f32[16,16,128]{2,1,0:T(8,128)S(1)}, f32[16,16,128]{2,1,0:T(8,128)}, u32[]{:S(2)}) copy-start(f32[16,16,128]{2,1,0:T(8,128)} %param.9) | copy-start | bytes 393220
  0.7 12.9 %copy-start.2 = (f32[2,16,128]{2,1,0:T(8,128)S(1)}, f32[2,16,128]{2,1,0:T(8,128)}, u32[]{:S(2)}) copy-start(f32[2,16,128]{2,1,0:T(8,128)} %param.10) | copy-start | bytes 49156
  4.0 10.9 %copy-start.5 = (s32[16,128]{1,0:T(8,128)S(1)}, s32[16,128]{1,0:T(8,128)}, u32[]{:S(2)}) copy-start(s32[16,128]{1,0:T(8,128)} %param.12) | copy-start | bytes 24580
  5.4 11.0 %collective-permute-start.1 = (f32[53,7,128]{2,1,0:T(8,128)S(1)}, f32[53,7,128]{2,1,0:T(8,128)S(1)}, u32[]{:S(2)}, u32[]{:S(2)}) collective-permute-start(f32[53,7,128]{2,1,0:T(8,128)S(1)} %get-tuple-element.287), channel_id=1, source_target_pairs={{8,0},{16,8},{24,16},{9,1},{17,9},{25,17},{10,2},{18,10},{26,18},{... | collective-permute-start | bytes 569864 | tf_op jit(solution)/shard_map/ppermute | solution.py:160
  6.7 10.1 %collective-permute-start = (f32[53,7,128]{2,1,0:T(8,128)S(1)}, f32[53,7,128]{2,1,0:T(8,128)S(1)}, u32[]{:S(2)}, u32[]{:S(2)}) collective-permute-start(f32[53,7,128]{2,1,0:T(8,128)S(1)} %get-tuple-element.286), channel_id=1, source_target_pairs={{0,8},{8,16},{16,24},{1,9},{9,17},{17,25},{2,10},{10,18},{18,26},{... | collective-permute-start | bytes 569864 | tf_op jit(solution)/shard_map/ppermute | solution.py:160
  13.5 2.8 %copy-start.6 = (s32[16,128]{1,0:T(8,128)S(1)}, s32[16,128]{1,0:T(8,128)}, u32[]{:S(2)}) copy-start(s32[16,128]{1,0:T(8,128)} %param.13) | copy-start | bytes 24580
  16.2 5.6 %copy-start.7 = (f32[1,16]{1,0:T(1,128)S(1)}, f32[1,16]{1,0:T(1,128)}, u32[]{:S(2)}) copy-start(f32[1,16]{1,0:T(1,128)} %param.11) | copy-start | bytes 196
  17.1 14.2 %collective-permute-start.3 = (f32[52,30,7]{0,1,2:T(8,128)S(1)}, f32[52,30,7]{0,1,2:T(8,128)S(1)}, u32[]{:S(2)}, u32[]{:S(2)}) collective-permute-start(f32[52,30,7]{0,1,2:T(8,128)S(1)} %pad_maximum_fusion.6), channel_id=1, source_target_pairs={{1,0},{2,1},{3,2},{4,3},{5,4},{6,5},{7,6},{9,8},{10,9},{11,10},{12... | collective-permute-start | bytes 131048 | tf_op jit(solution)/shard_map/ppermute | solution.py:160
  18.8 13.4 %collective-permute-start.2 = (f32[52,30,7]{0,1,2:T(8,128)S(1)}, f32[52,30,7]{0,1,2:T(8,128)S(1)}, u32[]{:S(2)}, u32[]{:S(2)}) collective-permute-start(f32[52,30,7]{0,1,2:T(8,128)S(1)} %pad_maximum_fusion.5), channel_id=1, source_target_pairs={{0,1},{1,2},{2,3},{3,4},{4,5},{5,6},{6,7},{8,9},{9,10},{10,11},{11... | collective-permute-start | bytes 131048 | tf_op jit(solution)/shard_map/ppermute | solution.py:160
  34.7 2.5 %copy-start.3 = (f32[284]{0:T(512)S(1)}, f32[284]{0:T(512)}, u32[]{:S(2)}) copy-start(f32[284]{0:T(512)} %constant.51.clone.1) | copy-start | bytes 3412
  34.7 2.5 %copy-start.4 = (f32[284]{0:T(512)S(1)}, f32[284]{0:T(512)}, u32[]{:S(2)}) copy-start(f32[284]{0:T(512)} %constant.49.clone.1) | copy-start | bytes 3412

commit v12 on v7

--- a/solution.py
+++ b/solution.py
@@ -261,8 +261,17 @@
     velocity = split(velocity)
     adjoint = split(adjoint)
     grad_col = -ice_cover[inner] * beta_col[inner] * jnp.sum(adjoint[:, -1] * velocity[:, -1], axis=0)
-    block_match = tile_owner[None] == lax.broadcasted_iota(jnp.int32, (tile_count, 1, 1), 0)
-    partial_sum = jnp.sum(jnp.where(block_match, grad_col[None], 0.0), axis=(1, 2))
+    high = lax.reduce_precision(grad_col, exponent_bits=8, mantissa_bits=7)
+    rest = grad_col - high
+    middle = lax.reduce_precision(rest, exponent_bits=8, mantissa_bits=7)
+    low = rest - middle
+    parts = jnp.stack([high, middle, low], axis=-1).reshape(rows * cols, 3).astype(jnp.bfloat16)
+    block_match = tile_owner.reshape(rows * cols, 1) == lax.broadcasted_iota(jnp.int32, (1, tile_count), 1)
+    per_part = lax.dot_general(
+        block_match.astype(jnp.bfloat16), parts, (((0,), (0,)), ((), ())),
+        preferred_element_type=jnp.float32,
+    )
+    partial_sum = per_part[:, 0] + per_part[:, 1] + per_part[:, 2]
     owners = lax.axis_size("gy")
     chunk = tile_count // owners
     gathered = lax.all_gather(partial_sum.reshape(owners, chunk), "gy")

time: 64.8 us -> 64.3 us (level)
  other arithmetic: 17.7 us -> 16.7 us
    reduce_sum x1 -> x0, other arithmetic: 1.03 us -> none  [local(): jnp.sum(jnp.where(block_match, grad_col[None], 0.0), axis=(1, 2))]
    unnamed x66 -> x68, other arithmetic: 1.96 us -> 2.05 us
    unnamed x84 -> x87, local copies, waits for them, and re-layouts: 3.93 us -> 3.96 us
where the time goes in v12:
time: 64.3 us; the launch traced here: 63.8 us
  blocking collectives  20.9 us (33%)
  other arithmetic  16.7 us (26%)
  local copies, waits for them, and re-layouts  10.8 us (17%)
  starting transfers between devices  8.81 us (14%)
  waiting for transfers between devices  2.94 us (5%)
  between operations  2.1 us (3%)
  matrix products  1.61 us (3%)
    all_gather x1, blocking collectives, local(): friction_rows = lax.all_gather(strips_near, 'gy', axis=1, tiled=True)  12.8 us
    ppermute x4, starting transfers between devices, shifted(): return lax.ppermute(piece, axis, pairs)  8.81 us
    all_gather x1, blocking collectives, local(): gathered = lax.all_gather(partial_sum.reshape(owners, chunk), 'gy')  8.15 us
    unnamed x87, local copies, waits for them, and re-layouts  3.96 us
    add x4, other arithmetic, relax_lanes(): right_side = rhs_field + lateral  3.53 us
    ppermute x4, waiting for transfers between devices, shifted(): return lax.ppermute(piece, axis, pairs)  2.94 us
    slice x11, local copies, waits for them, and re-layouts, stack_rows(): p[:, :, lo:hi]  2.74 us
    add x3, other arithmetic, relax_lanes(): lateral + along_y * (south_face * vel_pad[:, 1:-1, :-2] + north_face * ve...  2.36 us
  transfers between devices with their start and end apart: 4, of which 1 were waited for; matrix products, arithmetic and copies ran while one was open for 9% of the time, Pallas kernels for 0%

profile of v12, /device:TPU:0, one launch (start us, length us, event | category | flops | bytes accessed | tf_op | source)
XLA Modules:
  0.0 63.8 jit_solution(2702452188292389744)
XLA Ops:
  0.7 1.0 %constant_dynamic-update-slice_fusion.5 = (f32[53,7,128]{2,1,0:T(8,128)S(1)}, f32[53,7,128]{2,1,0:T(8,128)S(1)}) fusion(f32[32,16,128]{2,1,0:T(8,128)} %bitcast.80), kind=kLoop, calls=%fused_computation.48 | loop fusion | bytes 491520
  1.7 0.7 %convert_bitcast_fusion.1 = f32[1,16,128]{2,1,0:T(8,128)S(1)} fusion(s32[16,128]{1,0:T(8,128)} %param.12), kind=kLoop, calls=%fused_computation.663 | loop fusion | flops 2048 | bytes 16384 | tf_op jit(solution)/shard_map/broadcast_in_dim | solution.py:170
  2.4 0.7 %convert_bitcast_fusion = f32[1,16,128]{2,1,0:T(8,128)S(1)} fusion(s32[16,128]{1,0:T(8,128)} %param.13), kind=kLoop, calls=%fused_computation.662 | loop fusion | flops 2048 | bytes 16384 | tf_op jit(solution)/shard_map/broadcast_in_dim | solution.py:171
  3.1 0.9 %constant_dynamic-update-slice_fusion.4 = (f32[53,7,128]{2,1,0:T(8,128)S(1)}, f32[53,7,128]{2,1,0:T(8,128)S(1)}) fusion(f32[53,7,128]{2,1,0:T(8,128)S(1)} %get-tuple-element.256, f32[16,16,128]{2,1,0:T(8,128)} %param.9, f32[53,7,128]{2,1,0:T(8,128)S(1)} %get-tuple-element.257), kind=kLoop, calls=%fused_computation.47 | loop fusion | bytes 245760
  4.0 0.7 %constant_dynamic-update-slice_fusion.3 = (f32[53,7,128]{2,1,0:T(8,128)S(1)}, f32[53,7,128]{2,1,0:T(8,128)S(1)}) fusion(f32[53,7,128]{2,1,0:T(8,128)S(1)} %get-tuple-element.264, f32[2,16,128]{2,1,0:T(8,128)} %param.10, f32[53,7,128]{2,1,0:T(8,128)S(1)} %get-tuple-element.265), kind=kLoop, calls=%fused_computation.46 | loop fusion | bytes 30720
  4.7 0.7 %constant_dynamic-update-slice_fusion = (f32[53,7,128]{2,1,0:T(8,128)S(1)}, f32[53,7,128]{2,1,0:T(8,128)S(1)}) fusion(f32[53,7,128]{2,1,0:T(8,128)S(1)} %get-tuple-element.283, f32[1,16]{1,0:T(1,128)} %param.11, f32[53,7,128]{2,1,0:T(8,128)S(1)} %get-tuple-element.284), kind=kLoop, calls=%fused_computation.43 | loop fusion | bytes 8256 | tf_op jit(solution)/shard_map/concatenate | solution.py:177
  5.4 4.9 %collective-permute-start = (f32[53,7,128]{2,1,0:T(8,128)S(1)}, f32[53,7,128]{2,1,0:T(8,128)S(1)}, u32[]{:S(2)}, u32[]{:S(2)}) collective-permute-start(f32[53,7,128]{2,1,0:T(8,128)S(1)} %get-tuple-element.290), channel_id=1, source_target_pairs={{0,8},{8,16},{16,24},{1,9},{9,17},{17,25},{2,10},{10,18},{18,26},{... | collective-permute-start | bytes 569864 | tf_op jit(solution)/shard_map/ppermute | solution.py:160
  10.3 1.3 %collective-permute-start.1 = (f32[53,7,128]{2,1,0:T(8,128)S(1)}, f32[53,7,128]{2,1,0:T(8,128)S(1)}, u32[]{:S(2)}, u32[]{:S(2)}) collective-permute-start(f32[53,7,128]{2,1,0:T(8,128)S(1)} %get-tuple-element.291), channel_id=1, source_target_pairs={{8,0},{16,8},{24,16},{9,1},{17,9},{25,17},{10,2},{18,10},{26,18},{... | collective-permute-start | bytes 569864 | tf_op jit(solution)/shard_map/ppermute | solution.py:160
  11.6 1.2 %fusion.312 = (f32[32,16,7]{2,1,0:T(8,128)S(1)}, f32[32,16,7]{2,1,0:T(8,128)S(1)}) fusion(f32[32,16,128]{2,1,0:T(8,128)} %bitcast.81), kind=kLoop, calls=%fused_computation.691 | loop fusion | bytes 57344 | tf_op jit(solution)/shard_map/slice | solution.py:184
  13.2 0.2 copy.18
  13.4 0.2 copy.19
  13.6 0.2 copy.20
  13.8 0.2 copy.40
  14.0 0.2 copy.41
  14.3 0.2 copy.25
  14.5 0.2 copy.26
  14.7 0.2 copy.27
  14.9 0.2 copy.42
  15.1 0.2 copy.43
  16.1 2.9 %collective-permute-done.1 = f32[53,7,128]{2,1,0:T(8,128)S(1)} collective-permute-done((f32[53,7,128]{2,1,0:T(8,128)S(1)}, f32[53,7,128]{2,1,0:T(8,128)S(1)}, u32[]{:S(2)}, u32[]{:S(2)}) %collective-permute-start.1) | collective-permute-done | bytes 189984 | tf_op jit(solution)/shard_map/ppermute | solution.py:160
  19.3 1.3 %collective-permute-start.2 = (f32[52,30,7]{0,1,2:T(8,128)S(1)}, f32[52,30,7]{0,1,2:T(8,128)S(1)}, u32[]{:S(2)}, u32[]{:S(2)}) collective-permute-start(f32[52,30,7]{0,1,2:T(8,128)S(1)} %pad_maximum_fusion.5), channel_id=1, source_target_pairs={{0,1},{1,2},{2,3},{3,4},{4,5},{5,6},{6,7},{8,9},{9,10},{10,11},{11... | collective-permute-start | bytes 131048 | tf_op jit(solution)/shard_map/ppermute | solution.py:160
  20.8 0.2 copy.29
  21.0 1.3 %collective-permute-start.3 = (f32[52,30,7]{0,1,2:T(8,128)S(1)}, f32[52,30,7]{0,1,2:T(8,128)S(1)}, u32[]{:S(2)}, u32[]{:S(2)}) collective-permute-start(f32[52,30,7]{0,1,2:T(8,128)S(1)} %pad_maximum_fusion.6), channel_id=1, source_target_pairs={{1,0},{2,1},{3,2},{4,3},{5,4},{6,5},{7,6},{9,8},{10,9},{11,10},{12... | collective-permute-start | bytes 131048 | tf_op jit(solution)/shard_map/ppermute | solution.py:160
  22.3 12.8 %all-gather = f32[8,16,3]{1,2,0:T(4,128)S(1)} all-gather(f32[1,16,3]{1,2,0:T(4,128)S(1)} %maximum_bitcast_fusion.4), channel_id=1, replica_groups=mesh['gx'=4,'gy'=8] {'gy'}, dimensions={0}, use_global_device_ids=true | all-gather | bytes 1728 | tf_op jit(solution)/shard_map/all_gather | solution.py:195
  35.3 0.8 %copy.30 = f32[52,30,7]{2,1,0:T(8,128)S(1)} copy(f32[52,30,7]{0,1,2:T(8,128)S(1)} %collective-permute-done.2) | data formatting | bytes 87360 | tf_op jit(solution)/shard_map/ppermute | solution.py:160
  36.1 0.9 %copy.31 = f32[52,30,7]{2,1,0:T(8,128)S(1)} copy(f32[52,30,7]{0,1,2:T(8,128)S(1)} %collective-permute-done.3) | data formatting | bytes 87360 | tf_op jit(solution)/shard_map/ppermute | solution.py:160
  37.1 1.0 %pad_maximum_fusion = f32[52,30,142]{2,1,0:T(8,128)S(1)} fusion(f32[52,30,7]{2,1,0:T(8,128)S(1)} %copy.31, f32[52,7,128]{2,1,0:T(8,128)S(1)} %slice.1183, f32[52,16,128]{2,1,0:T(8,128)S(1)} %constant_dynamic-update-slice_fusion.12, f32[52,7,128]{2,1,0:T(8,128)S(1)} %slice.1182, f32[52,30,7]{2,1,0:T(8,128)S(1)} %copy.30), kind=kLoop, calls=%fused_computation.2 | loop fusion | flops 886080 | bytes 1772160 | tf_op jit(solution)/shard_map/concatenate | solution.py:198
  38.2 0.2 pad_maximum_fusion.1
  38.4 0.3 fusion.5
  38.8 1.2 %fusion = f32[30,142,9]{1,2,0:T(8,128)S(1)} fusion(s32[30,142]{1,0:T(8,128)S(1)} %get-tuple-element.239, bf16[128,3]{0,1:T(4,128)(2,1)S(1)} %get-tuple-element.288, bf16[128,3]{0,1:T(4,128)(2,1)S(1)} %get-tuple-element.289, bf16[128,3]{0,1:T(4,128)(2,1)S(1)} %get-tuple-element.287), kind=kOutput, calls=%fused_computation.1 | convolution fusion | flops 10367232 | bytes 172704 | tf_op jit(solution)/shard_map/dot_general | solution.py:218
  39.9 0.2 slice_add_fusion.143
  40.4 0.8 %fusion.181 = (f32[16,30,284]{2,1,0:T(8,128)S(1)}, f32[16,30,284]{2,1,0:T(8,128)S(1)}, f32[16,30,284]{2,1,0:T(8,128)S(1)}, f32[16,30,284]{2,1,0:T(8,128)S(1)}, f...) fusion(f32[16,30,142]{2,1,0:T(8,128)S(1)} %get-tuple-element.241, f32[16,30,142]{2,1,0:T(8,128)S(1)} %get-tuple-element.242, ...), kind=kLoop, calls=%fused_computation.689 | loop fusion | flops 2044800 | bytes 4500832 | tf_op jit(solution)/shard_map/add | solution.py:133
  41.2 0.4 add_add_fusion.3
  41.6 0.3 fusion.128
  42.4 0.9 %add_add_fusion.2 = f32[16,30,284]{2,1,0:T(8,128)S(1)} fusion(f32[16,30,284]{2,1,0:T(8,128)S(1)} %broadcast_multiply_fusion.1, f32[16,30,284]{2,1,0:T(8,128)S(1)} %get-tuple-element.237, f32[16,30,284]{2,1,0:T(8,128)S(1)} %get-tuple-element.236, f32[16,30,284]{2,1,0:T(8,128)S(1)} %get-tuple-element.235, f32[16,30,284]{2,1,0:T(8,128)S(1)} %get-tuple-element.234, ...), kind=kLoop, calls=%fused_computation.23 | loop fusion | flops 2044800 | bytes 3819232 | tf_op jit(solution)/shard_map/add | solution.py:133
  43.3 0.2 fusion.110
  43.9 0.2 add_multiply_fusion.5
  44.1 0.9 %add_add_fusion.1 = f32[16,30,284]{2,1,0:T(8,128)S(1)} fusion(f32[16,30,284]{2,1,0:T(8,128)S(1)} %add_multiply_fusion.5, f32[16,30,284]{2,1,0:T(8,128)S(1)} %get-tuple-element.237, f32[16,30,284]{2,1,0:T(8,128)S(1)} %get-tuple-element.236, f32[16,30,284]{2,1,0:T(8,128)S(1)} %get-tuple-element.235, f32[16,30,284]{2,1,0:T(8,128)S(1)} %get-tuple-element.234, ...), kind=kLoop, calls=%fused_computation.21 | loop fusion | flops 2044800 | bytes 3819232 | tf_op jit(solution)/shard_map/add | solution.py:133
  45.0 0.2 fusion.95
  45.1 0.2 constant_dynamic-update-slice_fusion.64
  45.5 0.2 add_multiply_fusion.4
  45.7 0.9 %add_add_fusion = f32[16,30,284]{2,1,0:T(8,128)S(1)} fusion(f32[16,30,284]{2,1,0:T(8,128)S(1)} %add_multiply_fusion.4, f32[16,30,284]{2,1,0:T(8,128)S(1)} %get-tuple-element.237, f32[16,30,284]{2,1,0:T(8,128)S(1)} %get-tuple-element.236, f32[16,30,284]{2,1,0:T(8,128)S(1)} %get-tuple-element.235, f32[16,30,284]{2,1,0:T(8,128)S(1)} %get-tuple-element.234, ...), kind=kLoop, calls=%fused_computation.19 | loop fusion | flops 2044800 | bytes 3819232 | tf_op jit(solution)/shard_map/add | solution.py:133
  46.6 0.2 fusion.80
  46.8 0.2 constant_dynamic-update-slice_fusion.80
  47.2 0.2 add_multiply_fusion.3
  47.5 0.2 fusion.62
  47.7 0.2 constant_dynamic-update-slice_fusion.96
  48.2 0.8 %multiply_add_fusion.2 = f32[16,30,284]{2,1,0:T(8,128)S(1)} fusion(f32[16,30,284]{2,1,0:T(8,128)S(1)} %broadcast_multiply_fusion, f32[16,30,284]{2,1,0:T(8,128)S(1)} %get-tuple-element.237, f32[16,30,284]{2,1,0:T(8,128)S(1)} %get-tuple-element.236, f32[16,30,284]{2,1,0:T(8,128)S(1)} %get-tuple-element.235, f32[16,30,284]{2,1,0:T(8,128)S(1)} %get-tuple-element.234, ...), kind=kLoop, calls=%fused_computation.17 | loop fusion | flops 1772160 | bytes 3273952 | tf_op jit(solution)/shard_map/add | solution.py:130
  49.0 0.2 fusion.46
  49.2 0.2 constant_dynamic-update-slice_fusion.112
  49.6 0.2 add_multiply_fusion.2
  49.8 0.8 %multiply_add_fusion.1 = f32[16,30,284]{2,1,0:T(8,128)S(1)} fusion(f32[16,30,284]{2,1,0:T(8,128)S(1)} %add_multiply_fusion.2, f32[16,30,284]{2,1,0:T(8,128)S(1)} %get-tuple-element.237, f32[16,30,284]{2,1,0:T(8,128)S(1)} %get-tuple-element.236, f32[16,30,284]{2,1,0:T(8,128)S(1)} %get-tuple-element.235, f32[16,30,284]{2,1,0:T(8,128)S(1)} %get-tuple-element.234, ...), kind=kLoop, calls=%fused_computation.15 | loop fusion | flops 1772160 | bytes 3273952 | tf_op jit(solution)/shard_map/add | solution.py:130
  50.6 0.2 fusion.30
  50.7 0.2 constant_dynamic-update-slice_fusion.128
  51.1 0.2 add_multiply_fusion.1
  51.3 0.8 %multiply_add_fusion = f32[16,30,284]{2,1,0:T(8,128)S(1)} fusion(f32[16,30,284]{2,1,0:T(8,128)S(1)} %add_multiply_fusion.1, f32[16,30,284]{2,1,0:T(8,128)S(1)} %get-tuple-element.237, f32[16,30,284]{2,1,0:T(8,128)S(1)} %get-tuple-element.236, f32[16,30,284]{2,1,0:T(8,128)S(1)} %get-tuple-element.235, f32[16,30,284]{2,1,0:T(8,128)S(1)} %get-tuple-element.234, ...), kind=kLoop, calls=%fused_computation.13 | loop fusion | flops 1772160 | bytes 3273952 | tf_op jit(solution)/shard_map/add | solution.py:130
  52.1 0.2 fusion.14
  52.3 0.2 constant_dynamic-update-slice_fusion.144
  52.7 0.2 add_multiply_fusion
  53.0 0.7 %pad_maximum_fusion.4 = f32[2,16,16,128]{3,2,1,0:T(8,128)} fusion(f32[1,16,16,128]{3,2,1,0:T(8,128)S(1)} %get-tuple-element.244, f32[1,16,16,128]{3,2,1,0:T(8,128)S(1)} %get-tuple-element.243), kind=kLoop, calls=%fused_computation.41 | loop fusion | flops 65536 | bytes 524288 | tf_op jit(solution)/shard_map/stack | solution.py:257
  53.7 0.7 %pad_maximum_fusion.3 = f32[2,16,16,128]{3,2,1,0:T(8,128)} fusion(f32[1,16,16,128]{3,2,1,0:T(8,128)S(1)} %get-tuple-element.246, f32[1,16,16,128]{3,2,1,0:T(8,128)S(1)} %get-tuple-element.245), kind=kLoop, calls=%fused_computation.38 | loop fusion | flops 65536 | bytes 524288 | tf_op jit(solution)/shard_map/stack | solution.py:257
  54.6 0.5 fusion.2
  55.2 8.2 %all_gather.7 = f32[8,8,16]{2,1,0:T(8,128)S(1)} all-gather(f32[1,8,16]{2,1,0:T(8,128)S(1)} %add.4686), channel_id=1, replica_groups=mesh['gx'=4,'gy'=8] {'gy'}, dimensions={0}, use_global_device_ids=true | all-gather | bytes 4608 | tf_op jit(solution)/shard_map/all_gather | solution.py:277
  63.3 0.5 dynamic-slice_reduce_fusion
  (190 shorter events, 4.2 us)
Async XLA Ops:
  0.6 12.5 %copy-start = (f32[2,16,16,128]{3,2,1,0:T(8,128)S(1)}, f32[2,16,16,128]{3,2,1,0:T(8,128)}, u32[]{:S(2)}) copy-start(f32[2,16,16,128]{3,2,1,0:T(8,128)} %param.8) | copy-start | bytes 786436
  0.6 12.3 %copy-start.1 = (f32[16,16,128]{2,1,0:T(8,128)S(1)}, f32[16,16,128]{2,1,0:T(8,128)}, u32[]{:S(2)}) copy-start(f32[16,16,128]{2,1,0:T(8,128)} %param.9) | copy-start | bytes 393220
  0.7 12.4 %copy-start.2 = (f32[2,16,128]{2,1,0:T(8,128)S(1)}, f32[2,16,128]{2,1,0:T(8,128)}, u32[]{:S(2)}) copy-start(f32[2,16,128]{2,1,0:T(8,128)} %param.10) | copy-start | bytes 49156
  5.4 10.4 %collective-permute-start = (f32[53,7,128]{2,1,0:T(8,128)S(1)}, f32[53,7,128]{2,1,0:T(8,128)S(1)}, u32[]{:S(2)}, u32[]{:S(2)}) collective-permute-start(f32[53,7,128]{2,1,0:T(8,128)S(1)} %get-tuple-element.290), channel_id=1, source_target_pairs={{0,8},{8,16},{16,24},{1,9},{9,17},{17,25},{2,10},{10,18},{18,26},{... | collective-permute-start | bytes 569864 | tf_op jit(solution)/shard_map/ppermute | solution.py:160
  10.3 8.7 %collective-permute-start.1 = (f32[53,7,128]{2,1,0:T(8,128)S(1)}, f32[53,7,128]{2,1,0:T(8,128)S(1)}, u32[]{:S(2)}, u32[]{:S(2)}) collective-permute-start(f32[53,7,128]{2,1,0:T(8,128)S(1)} %get-tuple-element.291), channel_id=1, source_target_pairs={{8,0},{16,8},{24,16},{9,1},{17,9},{25,17},{10,2},{18,10},{26,18},{... | collective-permute-start | bytes 569864 | tf_op jit(solution)/shard_map/ppermute | solution.py:160
  12.8 2.6 %copy-start.5 = (s32[16,128]{1,0:T(8,128)S(1)}, s32[16,128]{1,0:T(8,128)}, u32[]{:S(2)}) copy-start(s32[16,128]{1,0:T(8,128)} %param.12) | copy-start | bytes 24580
  13.1 2.7 %copy-start.6 = (s32[16,128]{1,0:T(8,128)S(1)}, s32[16,128]{1,0:T(8,128)}, u32[]{:S(2)}) copy-start(s32[16,128]{1,0:T(8,128)} %param.13) | copy-start | bytes 24580
  15.6 6.7 %copy-start.7 = (f32[1,16]{1,0:T(1,128)S(1)}, f32[1,16]{1,0:T(1,128)}, u32[]{:S(2)}) copy-start(f32[1,16]{1,0:T(1,128)} %param.11) | copy-start | bytes 196
  19.3 15.9 %collective-permute-start.2 = (f32[52,30,7]{0,1,2:T(8,128)S(1)}, f32[52,30,7]{0,1,2:T(8,128)S(1)}, u32[]{:S(2)}, u32[]{:S(2)}) collective-permute-start(f32[52,30,7]{0,1,2:T(8,128)S(1)} %pad_maximum_fusion.5), channel_id=1, source_target_pairs={{0,1},{1,2},{2,3},{3,4},{4,5},{5,6},{6,7},{8,9},{9,10},{10,11},{11... | collective-permute-start | bytes 131048 | tf_op jit(solution)/shard_map/ppermute | solution.py:160
  21.0 15.1 %collective-permute-start.3 = (f32[52,30,7]{0,1,2:T(8,128)S(1)}, f32[52,30,7]{0,1,2:T(8,128)S(1)}, u32[]{:S(2)}, u32[]{:S(2)}) collective-permute-start(f32[52,30,7]{0,1,2:T(8,128)S(1)} %pad_maximum_fusion.6), channel_id=1, source_target_pairs={{1,0},{2,1},{3,2},{4,3},{5,4},{6,5},{7,6},{9,8},{10,9},{11,10},{12... | collective-permute-start | bytes 131048 | tf_op jit(solution)/shard_map/ppermute | solution.py:160
  38.4 1.9 %copy-start.3 = (f32[284]{0:T(512)S(1)}, f32[284]{0:T(512)}, u32[]{:S(2)}) copy-start(f32[284]{0:T(512)} %constant.56.clone.1) | copy-start | bytes 3412
  38.4 1.9 %copy-start.4 = (f32[284]{0:T(512)S(1)}, f32[284]{0:T(512)}, u32[]{:S(2)}) copy-start(f32[284]{0:T(512)} %constant.58.clone.1) | copy-start | bytes 3412

commit v13 on v11

--- a/solution.py
+++ b/solution.py
@@ -266,10 +266,8 @@
     )
     partial_sum = per_part[:, 0] + per_part[:, 1] + per_part[:, 2]
     owners = lax.axis_size("gy")
-    chunk = tile_count // owners
-    gathered = lax.all_gather(partial_sum.reshape(owners, chunk), "gy")
-    mine = lax.dynamic_index_in_dim(gathered, lax.axis_index("gy"), axis=1, keepdims=False)
-    grad_tiles = jnp.sum(mine, axis=0)[None]
+    received = lax.all_to_all(partial_sum.reshape(owners, -1), "gy", 0, 0, tiled=True)
+    grad_tiles = jnp.sum(received, axis=0)[None]
     return (velocity, adjoint, grad_tiles)
 
 

time: 62 us -> 67.9 us (1.095)
  blocking collectives: 18.3 us -> 8.91 us
  starting transfers between devices: 11.2 us -> 18.4 us
  waiting for transfers between devices: 0.15 us -> 6.82 us
  local copies, waits for them, and re-layouts: 10.7 us -> 12.1 us
    all_gather x1 -> x0, blocking collectives: 9.05 us -> none  [local(): gathered = lax.all_gather(partial_sum.reshape(owners, chunk), 'gy')]
    all_to_all x0 -> x1, starting transfers between devices: none -> 7.8 us  [local(): lax.all_to_all(partial_sum.reshape(owners, -1), 'gy', 0, 0, tiled=True)]
    all_to_all x0 -> x1, waiting for transfers between devices: none -> 3.94 us  [local(): lax.all_to_all(partial_sum.reshape(owners, -1), 'gy', 0, 0, tiled=True)]
    ppermute x4, waiting for transfers between devices: 0.15 us -> 2.89 us  [shifted(): return lax.ppermute(piece, axis, pairs)]
    slice x11, local copies, waits for them, and re-layouts: 2.73 us -> 3.49 us  [stack_rows(): p[:, :, lo:hi]]
  transfers between devices with their start and end apart: 4 -> 5, of which waited for: 1 -> 3; matrix products, arithmetic and copies ran while one was open for 9% -> 10% of each run, Pallas kernels for 0% -> 0%
where the time goes in v13:
time: 67.9 us; the launch traced here: 67.4 us
  other arithmetic  18.6 us (27%)
  starting transfers between devices  18.4 us (27%)
  local copies, waits for them, and re-layouts  12.1 us (18%)
  blocking collectives  8.91 us (13%)
  waiting for transfers between devices  6.82 us (10%)
  between operations  2.07 us (3%)
    ppermute x4, starting transfers between devices, shifted(): return lax.ppermute(piece, axis, pairs)  10.5 us
    all_gather x1, blocking collectives, local(): friction_rows = lax.all_gather(strips_near, 'gy', axis=1, tiled=True)  8.91 us
    all_to_all x1, starting transfers between devices, local(): lax.all_to_all(partial_sum.reshape(owners, -1), 'gy', 0, 0, tiled=True)  7.8 us
    unnamed x88, local copies, waits for them, and re-layouts  4.01 us
    all_to_all x1, waiting for transfers between devices, local(): lax.all_to_all(partial_sum.reshape(owners, -1), 'gy', 0, 0, tiled=True)  3.94 us
    add x4, other arithmetic, relax_lanes(): right_side = rhs_field + lateral  3.52 us
    slice x11, local copies, waits for them, and re-layouts, stack_rows(): p[:, :, lo:hi]  3.49 us
    ppermute x4, waiting for transfers between devices, shifted(): return lax.ppermute(piece, axis, pairs)  2.89 us
  transfers between devices with their start and end apart: 5, of which 3 were waited for; matrix products, arithmetic and copies ran while one was open for 10% of the time, Pallas kernels for 0%

profile of v13, /device:TPU:0, one launch (start us, length us, event | category | flops | bytes accessed | tf_op | source)
XLA Modules:
  0.0 67.4 jit_solution(16487727154402167970)
XLA Ops:
  0.6 0.7 %convert_bitcast_fusion.1 = f32[1,16,128]{2,1,0:T(8,128)S(1)} fusion(s32[16,128]{1,0:T(8,128)} %param.12), kind=kLoop, calls=%fused_computation.650 | loop fusion | flops 2048 | bytes 16384 | tf_op jit(solution)/shard_map/broadcast_in_dim | solution.py:170
  1.4 0.7 %convert_bitcast_fusion = f32[1,16,128]{2,1,0:T(8,128)S(1)} fusion(s32[16,128]{1,0:T(8,128)} %param.13), kind=kLoop, calls=%fused_computation.649 | loop fusion | flops 2048 | bytes 16384 | tf_op jit(solution)/shard_map/broadcast_in_dim | solution.py:171
  2.1 1.0 %constant_dynamic-update-slice_fusion.5 = (f32[53,7,128]{2,1,0:T(8,128)S(1)}, f32[53,7,128]{2,1,0:T(8,128)S(1)}) fusion(f32[32,16,128]{2,1,0:T(8,128)} %bitcast.67), kind=kLoop, calls=%fused_computation.47 | loop fusion | bytes 491520
  3.1 0.9 %constant_dynamic-update-slice_fusion.4 = (f32[53,7,128]{2,1,0:T(8,128)S(1)}, f32[53,7,128]{2,1,0:T(8,128)S(1)}) fusion(f32[53,7,128]{2,1,0:T(8,128)S(1)} %get-tuple-element.252, f32[16,16,128]{2,1,0:T(8,128)} %param.9, f32[53,7,128]{2,1,0:T(8,128)S(1)} %get-tuple-element.253), kind=kLoop, calls=%fused_computation.46 | loop fusion | bytes 245760
  4.0 0.8 %constant_dynamic-update-slice_fusion.3 = (f32[53,7,128]{2,1,0:T(8,128)S(1)}, f32[53,7,128]{2,1,0:T(8,128)S(1)}) fusion(f32[53,7,128]{2,1,0:T(8,128)S(1)} %get-tuple-element.260, f32[2,16,128]{2,1,0:T(8,128)} %param.10, f32[53,7,128]{2,1,0:T(8,128)S(1)} %get-tuple-element.261), kind=kLoop, calls=%fused_computation.45 | loop fusion | bytes 30720
  4.7 0.7 constant_dynamic-update-slice_fusion
  5.4 4.9 %collective-permute-start = (f32[53,7,128]{2,1,0:T(8,128)S(1)}, f32[53,7,128]{2,1,0:T(8,128)S(1)}, u32[]{:S(2)}, u32[]{:S(2)}) collective-permute-start(f32[53,7,128]{2,1,0:T(8,128)S(1)} %get-tuple-element.286), channel_id=1, source_target_pairs={{0,8},{8,16},{16,24},{1,9},{9,17},{17,25},{2,10},{10,18},{18,26},{... | collective-permute-start | bytes 569864 | tf_op jit(solution)/shard_map/ppermute | solution.py:160
  10.3 1.3 %collective-permute-start.1 = (f32[53,7,128]{2,1,0:T(8,128)S(1)}, f32[53,7,128]{2,1,0:T(8,128)S(1)}, u32[]{:S(2)}, u32[]{:S(2)}) collective-permute-start(f32[53,7,128]{2,1,0:T(8,128)S(1)} %get-tuple-element.287), channel_id=1, source_target_pairs={{8,0},{16,8},{24,16},{9,1},{17,9},{25,17},{10,2},{18,10},{26,18},{... | collective-permute-start | bytes 569864 | tf_op jit(solution)/shard_map/ppermute | solution.py:160
  11.8 0.9 %fusion.302 = (f32[2,16,7]{2,1,0:T(8,128)S(1)}, f32[2,16,7]{2,1,0:T(8,128)S(1)}) fusion(f32[2,16,128]{2,1,0:T(8,128)} %param.10), kind=kLoop, calls=%fused_computation.668 | loop fusion | bytes 3584 | tf_op jit(solution)/shard_map/slice | solution.py:184
  12.7 1.1 %fusion.301 = (f32[16,16,7]{2,1,0:T(8,128)S(1)}, f32[16,16,7]{2,1,0:T(8,128)S(1)}) fusion(f32[16,16,128]{2,1,0:T(8,128)} %param.9), kind=kLoop, calls=%fused_computation.667 | loop fusion | bytes 28672 | tf_op jit(solution)/shard_map/slice | solution.py:184
  13.9 0.2 copy.69
  14.2 0.2 copy.53
  14.4 0.2 copy.54
  14.6 0.2 copy.71
  14.8 0.2 copy.60
  15.0 0.2 copy.61
  15.4 0.2 copy.68
  15.6 0.2 copy.70
  15.9 0.2 copy.52
  16.0 0.2 copy.59
  16.8 0.2 copy.62
  17.0 2.0 %collective-permute-done.1 = f32[53,7,128]{2,1,0:T(8,128)S(1)} collective-permute-done((f32[53,7,128]{2,1,0:T(8,128)S(1)}, f32[53,7,128]{2,1,0:T(8,128)S(1)}, u32[]{:S(2)}, u32[]{:S(2)}) %collective-permute-start.1) | collective-permute-done | bytes 189984 | tf_op jit(solution)/shard_map/ppermute | solution.py:160
  19.1 8.9 %all-gather = f32[8,16,3]{1,2,0:T(4,128)S(1)} all-gather(f32[1,16,3]{1,2,0:T(4,128)S(1)} %maximum_bitcast_fusion.2), channel_id=1, replica_groups=mesh['gx'=4,'gy'=8] {'gy'}, dimensions={0}, use_global_device_ids=true | all-gather | bytes 1728 | tf_op jit(solution)/shard_map/all_gather | solution.py:195
  28.3 0.2 copy.63
  28.5 1.3 %collective-permute-start.3 = (f32[52,30,7]{0,1,2:T(8,128)S(1)}, f32[52,30,7]{0,1,2:T(8,128)S(1)}, u32[]{:S(2)}, u32[]{:S(2)}) collective-permute-start(f32[52,30,7]{0,1,2:T(8,128)S(1)} %pad_maximum_fusion.6), channel_id=1, source_target_pairs={{1,0},{2,1},{3,2},{4,3},{5,4},{6,5},{7,6},{9,8},{10,9},{11,10},{12... | collective-permute-start | bytes 131048 | tf_op jit(solution)/shard_map/ppermute | solution.py:160
  29.9 3.0 %collective-permute-start.2 = (f32[52,30,7]{0,1,2:T(8,128)S(1)}, f32[52,30,7]{0,1,2:T(8,128)S(1)}, u32[]{:S(2)}, u32[]{:S(2)}) collective-permute-start(f32[52,30,7]{0,1,2:T(8,128)S(1)} %pad_maximum_fusion.5), channel_id=1, source_target_pairs={{0,1},{1,2},{2,3},{3,4},{4,5},{5,6},{6,7},{8,9},{9,10},{10,11},{11... | collective-permute-start | bytes 131048 | tf_op jit(solution)/shard_map/ppermute | solution.py:160
  33.0 0.8 %collective-permute-done.2 = f32[52,30,7]{0,1,2:T(8,128)S(1)} collective-permute-done((f32[52,30,7]{0,1,2:T(8,128)S(1)}, f32[52,30,7]{0,1,2:T(8,128)S(1)}, u32[]{:S(2)}, u32[]{:S(2)}) %collective-permute-start.2) | collective-permute-done | bytes 43712 | tf_op jit(solution)/shard_map/ppermute | solution.py:160
  33.9 0.8 %copy.64 = f32[52,30,7]{2,1,0:T(8,128)S(1)} copy(f32[52,30,7]{0,1,2:T(8,128)S(1)} %collective-permute-done.2) | data formatting | bytes 87360 | tf_op jit(solution)/shard_map/ppermute | solution.py:160
  34.7 0.9 %copy.65 = f32[52,30,7]{2,1,0:T(8,128)S(1)} copy(f32[52,30,7]{0,1,2:T(8,128)S(1)} %collective-permute-done.3) | data formatting | bytes 87360 | tf_op jit(solution)/shard_map/ppermute | solution.py:160
  35.7 1.0 %pad_maximum_fusion = f32[52,30,142]{2,1,0:T(8,128)S(1)} fusion(f32[52,30,7]{2,1,0:T(8,128)S(1)} %copy.65, f32[52,7,128]{2,1,0:T(8,128)S(1)} %slice.1159, f32[52,16,128]{2,1,0:T(8,128)S(1)} %constant_dynamic-update-slice_fusion.12, f32[52,7,128]{2,1,0:T(8,128)S(1)} %slice.1158, f32[52,30,7]{2,1,0:T(8,128)S(1)} %copy.64), kind=kLoop, calls=%fused_computation.2 | loop fusion | flops 886080 | bytes 1772160 | tf_op jit(solution)/shard_map/concatenate | solution.py:198
  36.8 0.3 fusion.3
  37.1 0.2 pad_maximum_fusion.1
  37.3 2.2 %select_reduce_fusion = f32[30,142]{1,0:T(8,128)S(1)} fusion(f32[128,30]{0,1:T(8,128)S(1)} %pad_maximum_fusion.16, s32[30,142]{1,0:T(8,128)S(1)} %get-tuple-element.242), kind=kLoop, calls=%fused_computation | loop fusion | flops 1631580 | bytes 49440 | tf_op jit(solution)/shard_map/reduce_sum | solution.py:220
  39.8 0.8 %fusion.167 = (f32[16,30,284]{2,1,0:T(8,128)S(1)}, f32[16,30,284]{2,1,0:T(8,128)S(1)}, f32[16,30,284]{2,1,0:T(8,128)S(1)}, f32[16,30,284]{2,1,0:T(8,128)S(1)}, f...) fusion(f32[16,30,142]{2,1,0:T(8,128)S(1)} %get-tuple-element.244, f32[16,30,142]{2,1,0:T(8,128)S(1)} %get-tuple-element.245, ...), kind=kLoop, calls=%fused_computation.662 | loop fusion | flops 2044800 | bytes 4500832 | tf_op jit(solution)/shard_map/add | solution.py:133
  40.6 0.4 add_add_fusion.3
  41.0 0.3 fusion.126
  41.8 0.9 %add_add_fusion.2 = f32[16,30,284]{2,1,0:T(8,128)S(1)} fusion(f32[16,30,284]{2,1,0:T(8,128)S(1)} %broadcast_multiply_fusion.1, f32[16,30,284]{2,1,0:T(8,128)S(1)} %get-tuple-element.240, f32[16,30,284]{2,1,0:T(8,128)S(1)} %get-tuple-element.239, f32[16,30,284]{2,1,0:T(8,128)S(1)} %get-tuple-element.238, f32[16,30,284]{2,1,0:T(8,128)S(1)} %get-tuple-element.237, ...), kind=kLoop, calls=%fused_computation.22 | loop fusion | flops 2044800 | bytes 3819232 | tf_op jit(solution)/shard_map/add | solution.py:133
  42.7 0.2 fusion.108
  43.4 0.9 %add_add_fusion.1 = f32[16,30,284]{2,1,0:T(8,128)S(1)} fusion(f32[16,30,284]{2,1,0:T(8,128)S(1)} %add_multiply_fusion.5, f32[16,30,284]{2,1,0:T(8,128)S(1)} %get-tuple-element.240, f32[16,30,284]{2,1,0:T(8,128)S(1)} %get-tuple-element.239, f32[16,30,284]{2,1,0:T(8,128)S(1)} %get-tuple-element.238, f32[16,30,284]{2,1,0:T(8,128)S(1)} %get-tuple-element.237, ...), kind=kLoop, calls=%fused_computation.20 | loop fusion | flops 2044800 | bytes 3819232 | tf_op jit(solution)/shard_map/add | solution.py:133
  44.4 0.2 fusion.93
  44.5 0.2 constant_dynamic-update-slice_fusion.64
  44.9 0.2 add_multiply_fusion.4
  45.1 0.9 %add_add_fusion = f32[16,30,284]{2,1,0:T(8,128)S(1)} fusion(f32[16,30,284]{2,1,0:T(8,128)S(1)} %add_multiply_fusion.4, f32[16,30,284]{2,1,0:T(8,128)S(1)} %get-tuple-element.240, f32[16,30,284]{2,1,0:T(8,128)S(1)} %get-tuple-element.239, f32[16,30,284]{2,1,0:T(8,128)S(1)} %get-tuple-element.238, f32[16,30,284]{2,1,0:T(8,128)S(1)} %get-tuple-element.237, ...), kind=kLoop, calls=%fused_computation.18 | loop fusion | flops 2044800 | bytes 3819232 | tf_op jit(solution)/shard_map/add | solution.py:133
  46.0 0.2 fusion.78
  46.6 0.2 add_multiply_fusion.3
  46.8 0.2 fusion.60
  47.0 0.2 constant_dynamic-update-slice_fusion.96
  47.5 0.8 %multiply_add_fusion.2 = f32[16,30,284]{2,1,0:T(8,128)S(1)} fusion(f32[16,30,284]{2,1,0:T(8,128)S(1)} %broadcast_multiply_fusion, f32[16,30,284]{2,1,0:T(8,128)S(1)} %get-tuple-element.240, f32[16,30,284]{2,1,0:T(8,128)S(1)} %get-tuple-element.239, f32[16,30,284]{2,1,0:T(8,128)S(1)} %get-tuple-element.238, f32[16,30,284]{2,1,0:T(8,128)S(1)} %get-tuple-element.237, ...), kind=kLoop, calls=%fused_computation.16 | loop fusion | flops 1772160 | bytes 3273952 | tf_op jit(solution)/shard_map/add | solution.py:130
  48.2 0.2 fusion.44
  48.8 0.2 add_multiply_fusion.2
  49.0 0.8 %multiply_add_fusion.1 = f32[16,30,284]{2,1,0:T(8,128)S(1)} fusion(f32[16,30,284]{2,1,0:T(8,128)S(1)} %add_multiply_fusion.2, f32[16,30,284]{2,1,0:T(8,128)S(1)} %get-tuple-element.240, f32[16,30,284]{2,1,0:T(8,128)S(1)} %get-tuple-element.239, f32[16,30,284]{2,1,0:T(8,128)S(1)} %get-tuple-element.238, f32[16,30,284]{2,1,0:T(8,128)S(1)} %get-tuple-element.237, ...), kind=kLoop, calls=%fused_computation.14 | loop fusion | flops 1772160 | bytes 3273952 | tf_op jit(solution)/shard_map/add | solution.py:130
  49.8 0.2 fusion.28
  50.4 0.2 add_multiply_fusion.1
  50.6 0.8 %multiply_add_fusion = f32[16,30,284]{2,1,0:T(8,128)S(1)} fusion(f32[16,30,284]{2,1,0:T(8,128)S(1)} %add_multiply_fusion.1, f32[16,30,284]{2,1,0:T(8,128)S(1)} %get-tuple-element.240, f32[16,30,284]{2,1,0:T(8,128)S(1)} %get-tuple-element.239, f32[16,30,284]{2,1,0:T(8,128)S(1)} %get-tuple-element.238, f32[16,30,284]{2,1,0:T(8,128)S(1)} %get-tuple-element.237, ...), kind=kLoop, calls=%fused_computation.12 | loop fusion | flops 1772160 | bytes 3273952 | tf_op jit(solution)/shard_map/add | solution.py:130
  51.4 0.2 fusion.12
  51.9 0.2 add_multiply_fusion
  52.1 0.2 slice_bitcast_fusion.1
  52.3 0.7 %pad_maximum_fusion.4 = f32[2,16,16,128]{3,2,1,0:T(8,128)} fusion(f32[1,16,16,128]{3,2,1,0:T(8,128)S(1)} %get-tuple-element.247, f32[1,16,16,128]{3,2,1,0:T(8,128)S(1)} %get-tuple-element.246), kind=kLoop, calls=%fused_computation.40 | loop fusion | flops 65536 | bytes 524288 | tf_op jit(solution)/shard_map/stack | solution.py:250
  53.2 0.5 fusion
  53.7 0.7 %add.4637 = f32[8,1,16]{2,0,1:T(8,128)} reshape(f32[128]{0:T(128)S(1)} %add_reduce_fusion) | data formatting | bytes 1024 | tf_op jit(solution)/shard_map/add | solution.py:267
  54.4 7.8 %all-to-all-start = ((f32[8,1,16]{2,1,0:T(1,128)}), f32[8,1,16]{2,1,0:T(1,128)S(1)}, u32[]{:S(2)}, u32[]{:S(2)}) async-start(f32[8,1,16]{2,1,0:T(1,128)} %bitcast.20), calls=%async_computation | async-start | bytes 8192 | tf_op jit(solution)/shard_map/all_to_all | solution.py:269
  62.2 0.7 %pad_maximum_fusion.3 = f32[2,16,16,128]{3,2,1,0:T(8,128)} fusion(f32[1,16,16,128]{3,2,1,0:T(8,128)S(1)} %get-tuple-element.288, f32[1,16,16,128]{3,2,1,0:T(8,128)S(1)} %get-tuple-element.289), kind=kLoop, calls=%fused_computation.37 | loop fusion | flops 65536 | bytes 524288 | tf_op jit(solution)/shard_map/stack | solution.py:250
  62.9 3.9 %all-to-all-done = f32[8,1,16]{2,1,0:T(1,128)S(1)} async-done(((f32[8,1,16]{2,1,0:T(1,128)}), f32[8,1,16]{2,1,0:T(1,128)S(1)}, u32[]{:S(2)}, u32[]{:S(2)}) %all-to-all-start) | async-done | bytes 544 | tf_op jit(solution)/shard_map/all_to_all | solution.py:269
  66.8 0.5 reduce_sum.29
  (190 shorter events, 4.3 us)
Async XLA Ops:
  0.6 13.1 %copy-start = (f32[2,16,16,128]{3,2,1,0:T(8,128)S(1)}, f32[2,16,16,128]{3,2,1,0:T(8,128)}, u32[]{:S(2)}) copy-start(f32[2,16,16,128]{3,2,1,0:T(8,128)} %param.8) | copy-start | bytes 786436
  4.0 11.8 %copy-start.1 = (f32[16,16,128]{2,1,0:T(8,128)S(1)}, f32[16,16,128]{2,1,0:T(8,128)}, u32[]{:S(2)}) copy-start(f32[16,16,128]{2,1,0:T(8,128)} %param.9) | copy-start | bytes 393220
  5.4 11.1 %collective-permute-start = (f32[53,7,128]{2,1,0:T(8,128)S(1)}, f32[53,7,128]{2,1,0:T(8,128)S(1)}, u32[]{:S(2)}, u32[]{:S(2)}) collective-permute-start(f32[53,7,128]{2,1,0:T(8,128)S(1)} %get-tuple-element.286), channel_id=1, source_target_pairs={{0,8},{8,16},{16,24},{1,9},{9,17},{17,25},{2,10},{10,18},{18,26},{... | collective-permute-start | bytes 569864 | tf_op jit(solution)/shard_map/ppermute | solution.py:160
  10.3 8.7 %collective-permute-start.1 = (f32[53,7,128]{2,1,0:T(8,128)S(1)}, f32[53,7,128]{2,1,0:T(8,128)S(1)}, u32[]{:S(2)}, u32[]{:S(2)}) collective-permute-start(f32[53,7,128]{2,1,0:T(8,128)S(1)} %get-tuple-element.287), channel_id=1, source_target_pairs={{8,0},{16,8},{24,16},{9,1},{17,9},{25,17},{10,2},{18,10},{26,18},{... | collective-permute-start | bytes 569864 | tf_op jit(solution)/shard_map/ppermute | solution.py:160
  12.7 3.2 %copy-start.2 = (f32[2,16,128]{2,1,0:T(8,128)S(1)}, f32[2,16,128]{2,1,0:T(8,128)}, u32[]{:S(2)}) copy-start(f32[2,16,128]{2,1,0:T(8,128)} %param.10) | copy-start | bytes 49156
  12.7 3.2 %copy-start.5 = (s32[16,128]{1,0:T(8,128)S(1)}, s32[16,128]{1,0:T(8,128)}, u32[]{:S(2)}) copy-start(s32[16,128]{1,0:T(8,128)} %param.12) | copy-start | bytes 24580
  13.8 2.7 %copy-start.6 = (s32[16,128]{1,0:T(8,128)S(1)}, s32[16,128]{1,0:T(8,128)}, u32[]{:S(2)}) copy-start(s32[16,128]{1,0:T(8,128)} %param.13) | copy-start | bytes 24580
  15.4 3.7 %copy-start.7 = (f32[1,16]{1,0:T(1,128)S(1)}, f32[1,16]{1,0:T(1,128)}, u32[]{:S(2)}) copy-start(f32[1,16]{1,0:T(1,128)} %param.11) | copy-start | bytes 196
  28.5 6.2 %collective-permute-start.3 = (f32[52,30,7]{0,1,2:T(8,128)S(1)}, f32[52,30,7]{0,1,2:T(8,128)S(1)}, u32[]{:S(2)}, u32[]{:S(2)}) collective-permute-start(f32[52,30,7]{0,1,2:T(8,128)S(1)} %pad_maximum_fusion.6), channel_id=1, source_target_pairs={{1,0},{2,1},{3,2},{4,3},{5,4},{6,5},{7,6},{9,8},{10,9},{11,10},{12... | collective-permute-start | bytes 131048 | tf_op jit(solution)/shard_map/ppermute | solution.py:160
  29.9 4.0 %collective-permute-start.2 = (f32[52,30,7]{0,1,2:T(8,128)S(1)}, f32[52,30,7]{0,1,2:T(8,128)S(1)}, u32[]{:S(2)}, u32[]{:S(2)}) collective-permute-start(f32[52,30,7]{0,1,2:T(8,128)S(1)} %pad_maximum_fusion.5), channel_id=1, source_target_pairs={{0,1},{1,2},{2,3},{3,4},{4,5},{5,6},{6,7},{8,9},{9,10},{10,11},{11... | collective-permute-start | bytes 131048 | tf_op jit(solution)/shard_map/ppermute | solution.py:160
  36.8 3.0 %copy-start.3 = (f32[284]{0:T(512)S(1)}, f32[284]{0:T(512)}, u32[]{:S(2)}) copy-start(f32[284]{0:T(512)} %constant.44.clone.1) | copy-start | bytes 3412
  36.8 3.0 %copy-start.4 = (f32[284]{0:T(512)S(1)}, f32[284]{0:T(512)}, u32[]{:S(2)}) copy-start(f32[284]{0:T(512)} %constant.42.clone.1) | copy-start | bytes 3412
  54.4 12.5 %all-to-all-start = ((f32[8,1,16]{2,1,0:T(1,128)}), f32[8,1,16]{2,1,0:T(1,128)S(1)}, u32[]{:S(2)}, u32[]{:S(2)}) async-start(f32[8,1,16]{2,1,0:T(1,128)} %bitcast.20), calls=%async_computation | async-start | bytes 8192 | tf_op jit(solution)/shard_map/all_to_all | solution.py:269

commit v14 on v11

--- a/solution.py
+++ b/solution.py
@@ -163,25 +163,27 @@
 def local(forcing, viscosity, observed, beta_tiles, ice_mask, tile_owner):
     comps, layers, rows, cols = forcing.shape
     tiles_here = beta_tiles.shape[1]
-    planes = [
-        forcing.reshape(comps * layers, rows, cols),
-        viscosity,
-        observed,
-        ice_mask.astype(jnp.float32)[None],
-        tile_owner.astype(jnp.float32)[None],
-    ]
-    plane_count = sum(p.shape[0] for p in planes)
+    float_planes = [forcing.reshape(comps * layers, rows, cols), viscosity, observed]
+    int_planes = [ice_mask[None], tile_owner[None]]
+
+    def pieces(rows_at, cols_at):
+        return [p[:, rows_at, cols_at] for p in float_planes] + [
+            p[:, rows_at, cols_at].astype(jnp.float32) for p in int_planes
+        ]
+
+    plane_count = sum(p.shape[0] for p in float_planes + int_planes)
+    every = slice(None)
 
     beta_plane = jnp.pad(beta_tiles, ((0, HALO - 1), (0, cols - tiles_here)))[None]
-    head = jnp.concatenate([p[:, :HALO] for p in planes] + [beta_plane], axis=0)
-    tail = jnp.concatenate([p[:, rows - HALO:] for p in planes] + [beta_plane], axis=0)
+    head = jnp.concatenate(pieces(slice(0, HALO), every) + [beta_plane], axis=0)
+    tail = jnp.concatenate(pieces(slice(rows - HALO, rows), every) + [beta_plane], axis=0)
     from_above = shifted(tail, "gx", True)
     from_below = shifted(head, "gx", False)
 
     def stack_rows(lo, hi):
         return jnp.concatenate(
             [from_above[:plane_count, :, lo:hi]]
-            + [jnp.concatenate([p[:, :, lo:hi] for p in planes], axis=0)]
+            + [jnp.concatenate(pieces(every, slice(lo, hi)), axis=0)]
             + [from_below[:plane_count, :, lo:hi]],
             axis=1,
         )

time: 62 us -> 62 us (level)
    unnamed x68 -> x70, other arithmetic: 2.05 us -> 3.46 us
    broadcast_in_dim x2 -> x0, other arithmetic: 1.4 us -> none  [the longest x1 0.7 us: local(): ice_mask.astype(jnp.float32)[None]]
    slice x11 -> x5, local copies, waits for them, and re-layouts: 2.73 us -> 1.71 us  [pieces(): p[:, rows_at, cols_at]]
    convert_element_type x0 -> x4, local copies, waits for them, and re-layouts: none -> 0.87 us  [pieces(): p[:, rows_at, cols_at].astype(jnp.float32)]
    unnamed x88 -> x86, local copies, waits for them, and re-layouts: 4.03 us -> 4.03 us
where the time goes in v14:
time: 62 us; the launch traced here: 61.5 us
  other arithmetic  18.8 us (30%)
  blocking collectives  18.3 us (30%)
  starting transfers between devices  11.2 us (18%)
  local copies, waits for them, and re-layouts  10.6 us (17%)
  between operations  2.09 us (3%)
    ppermute x4, starting transfers between devices, shifted(): return lax.ppermute(piece, axis, pairs)  11.2 us
    all_gather x1, blocking collectives, local(): friction_rows = lax.all_gather(strips_near, 'gy', axis=1, tiled=True)  9.2 us
    all_gather x1, blocking collectives, local(): gathered = lax.all_gather(partial_sum.reshape(owners, chunk), 'gy')  9.05 us
    unnamed x86, local copies, waits for them, and re-layouts  4.03 us
    add x4, other arithmetic, relax_lanes(): right_side = rhs_field + lateral  3.52 us
    unnamed x70, other arithmetic  3.46 us
    add x3, other arithmetic, relax_lanes(): lateral + along_y * (south_face * vel_pad[:, 1:-1, :-2] + north_face * ve...  2.35 us
    reduce_sum x1, other arithmetic, local(): jnp.sum(jnp.where(owner_match, row_strip[:, :, None], 0.0), axis=0)  2.23 us
  transfers between devices with their start and end apart: 4, of which 1 were waited for; matrix products, arithmetic and copies ran while one was open for 9% of the time, Pallas kernels for 0%

profile of v14, /device:TPU:0, one launch (start us, length us, event | category | flops | bytes accessed | tf_op | source)
XLA Modules:
  0.0 61.5 jit_solution(2362320991496488223)
XLA Ops:
  0.7 1.0 %constant_dynamic-update-slice_fusion.5 = (f32[53,7,128]{2,1,0:T(8,128)S(1)}, f32[53,7,128]{2,1,0:T(8,128)S(1)}) fusion(f32[32,16,128]{2,1,0:T(8,128)} %bitcast.64), kind=kLoop, calls=%fused_computation.47 | loop fusion | bytes 491520
  1.7 0.9 %constant_dynamic-update-slice_fusion.4 = (f32[53,7,128]{2,1,0:T(8,128)S(1)}, f32[53,7,128]{2,1,0:T(8,128)S(1)}) fusion(f32[53,7,128]{2,1,0:T(8,128)S(1)} %get-tuple-element.252, f32[16,16,128]{2,1,0:T(8,128)} %param.9, f32[53,7,128]{2,1,0:T(8,128)S(1)} %get-tuple-element.253), kind=kLoop, calls=%fused_computation.46 | loop fusion | bytes 245760
  2.6 0.7 %constant_dynamic-update-slice_fusion.3 = (f32[53,7,128]{2,1,0:T(8,128)S(1)}, f32[53,7,128]{2,1,0:T(8,128)S(1)}) fusion(f32[53,7,128]{2,1,0:T(8,128)S(1)} %get-tuple-element.260, f32[2,16,128]{2,1,0:T(8,128)} %param.10, f32[53,7,128]{2,1,0:T(8,128)S(1)} %get-tuple-element.261), kind=kLoop, calls=%fused_computation.45 | loop fusion | bytes 30720
  3.3 0.7 %constant_dynamic-update-slice_fusion.2 = (f32[53,7,128]{2,1,0:T(8,128)S(1)}, f32[53,7,128]{2,1,0:T(8,128)S(1)}) fusion(f32[53,7,128]{2,1,0:T(8,128)S(1)} %get-tuple-element.271, s32[1,16,128]{2,1,0:T(8,128)} %bitcast.67, f32[53,7,128]{2,1,0:T(8,128)S(1)} %get-tuple-element.272), kind=kLoop, calls=%fused_computation.44 | loop fusion | flops 1792 | bytes 15360
  4.1 0.7 %constant_dynamic-update-slice_fusion.1 = (f32[53,7,128]{2,1,0:T(8,128)S(1)}, f32[53,7,128]{2,1,0:T(8,128)S(1)}) fusion(f32[53,7,128]{2,1,0:T(8,128)S(1)} %get-tuple-element.281, s32[1,16,128]{2,1,0:T(8,128)} %bitcast.69, f32[53,7,128]{2,1,0:T(8,128)S(1)} %get-tuple-element.282), kind=kLoop, calls=%fused_computation.43 | loop fusion | flops 1792 | bytes 15360
  4.8 0.7 %constant_dynamic-update-slice_fusion = (f32[53,7,128]{2,1,0:T(8,128)S(1)}, f32[53,7,128]{2,1,0:T(8,128)S(1)}) fusion(f32[53,7,128]{2,1,0:T(8,128)S(1)} %get-tuple-element.279, f32[1,16]{1,0:T(1,128)} %param.11, f32[53,7,128]{2,1,0:T(8,128)S(1)} %get-tuple-element.280), kind=kLoop, calls=%fused_computation.42 | loop fusion | bytes 8256 | tf_op jit(solution)/shard_map/concatenate | solution.py:179
  5.4 1.3 %collective-permute-start.1 = (f32[53,7,128]{2,1,0:T(8,128)S(1)}, f32[53,7,128]{2,1,0:T(8,128)S(1)}, u32[]{:S(2)}, u32[]{:S(2)}) collective-permute-start(f32[53,7,128]{2,1,0:T(8,128)S(1)} %get-tuple-element.287), channel_id=1, source_target_pairs={{8,0},{16,8},{24,16},{9,1},{17,9},{25,17},{10,2},{18,10},{26,18},{... | collective-permute-start | bytes 569864 | tf_op jit(solution)/shard_map/ppermute | solution.py:160
  6.7 5.6 %collective-permute-start = (f32[53,7,128]{2,1,0:T(8,128)S(1)}, f32[53,7,128]{2,1,0:T(8,128)S(1)}, u32[]{:S(2)}, u32[]{:S(2)}) collective-permute-start(f32[53,7,128]{2,1,0:T(8,128)S(1)} %get-tuple-element.286), channel_id=1, source_target_pairs={{0,8},{8,16},{16,24},{1,9},{9,17},{17,25},{2,10},{10,18},{18,26},{... | collective-permute-start | bytes 569864 | tf_op jit(solution)/shard_map/ppermute | solution.py:160
  12.3 1.2 %fusion.298 = (f32[32,16,7]{2,1,0:T(8,128)S(1)}, f32[32,16,7]{2,1,0:T(8,128)S(1)}) fusion(f32[32,16,128]{2,1,0:T(8,128)} %bitcast.65), kind=kLoop, calls=%fused_computation.671 | loop fusion | bytes 57344 | tf_op jit(solution)/shard_map/slice | solution.py:170
  13.8 0.2 copy.59
  14.0 0.2 copy.69
  14.2 0.2 copy.70
  14.4 0.2 copy.60
  14.7 0.2 copy.61
  14.9 0.2 copy.52
  15.1 0.2 copy.67
  15.3 0.2 copy.68
  15.5 0.2 copy.53
  15.8 0.2 copy.54
  16.7 0.2 collective-permute-done
  17.2 1.3 %collective-permute-start.3 = (f32[52,30,7]{0,1,2:T(8,128)S(1)}, f32[52,30,7]{0,1,2:T(8,128)S(1)}, u32[]{:S(2)}, u32[]{:S(2)}) collective-permute-start(f32[52,30,7]{0,1,2:T(8,128)S(1)} %pad_maximum_fusion.6), channel_id=1, source_target_pairs={{1,0},{2,1},{3,2},{4,3},{5,4},{6,5},{7,6},{9,8},{10,9},{11,10},{12... | collective-permute-start | bytes 131048 | tf_op jit(solution)/shard_map/ppermute | solution.py:160
  18.6 0.2 copy.55
  18.8 3.0 %collective-permute-start.2 = (f32[52,30,7]{0,1,2:T(8,128)S(1)}, f32[52,30,7]{0,1,2:T(8,128)S(1)}, u32[]{:S(2)}, u32[]{:S(2)}) collective-permute-start(f32[52,30,7]{0,1,2:T(8,128)S(1)} %pad_maximum_fusion.5), channel_id=1, source_target_pairs={{0,1},{1,2},{2,3},{3,4},{4,5},{5,6},{6,7},{8,9},{9,10},{10,11},{11... | collective-permute-start | bytes 131048 | tf_op jit(solution)/shard_map/ppermute | solution.py:160
  21.9 9.2 %all-gather = f32[8,16,3]{1,2,0:T(4,128)S(1)} all-gather(f32[1,16,3]{1,2,0:T(4,128)S(1)} %maximum_bitcast_fusion.2), channel_id=1, replica_groups=mesh['gx'=4,'gy'=8] {'gy'}, dimensions={0}, use_global_device_ids=true | all-gather | bytes 1728 | tf_op jit(solution)/shard_map/all_gather | solution.py:197
  31.3 0.8 %copy.65 = f32[52,30,7]{2,1,0:T(8,128)S(1)} copy(f32[52,30,7]{0,1,2:T(8,128)S(1)} %collective-permute-done.3) | data formatting | bytes 87360 | tf_op jit(solution)/shard_map/ppermute | solution.py:160
  32.2 0.9 %copy.64 = f32[52,30,7]{2,1,0:T(8,128)S(1)} copy(f32[52,30,7]{0,1,2:T(8,128)S(1)} %collective-permute-done.2) | data formatting | bytes 87360 | tf_op jit(solution)/shard_map/ppermute | solution.py:160
  33.0 1.0 %pad_maximum_fusion = f32[52,30,142]{2,1,0:T(8,128)S(1)} fusion(f32[52,30,7]{2,1,0:T(8,128)S(1)} %copy.65, f32[52,7,128]{2,1,0:T(8,128)S(1)} %slice.1159, f32[52,16,128]{2,1,0:T(8,128)S(1)} %constant_dynamic-update-slice_fusion.12, f32[52,7,128]{2,1,0:T(8,128)S(1)} %slice.1158, f32[52,30,7]{2,1,0:T(8,128)S(1)} %copy.64), kind=kLoop, calls=%fused_computation.2 | loop fusion | flops 886080 | bytes 1772160 | tf_op jit(solution)/shard_map/concatenate | solution.py:200
  34.1 0.2 pad_maximum_fusion.1
  34.3 0.3 fusion.3
  34.8 2.2 %select_reduce_fusion = f32[30,142]{1,0:T(8,128)S(1)} fusion(f32[128,30]{0,1:T(8,128)S(1)} %pad_maximum_fusion.16, s32[30,142]{1,0:T(8,128)S(1)} %get-tuple-element.242), kind=kLoop, calls=%fused_computation | loop fusion | flops 1631580 | bytes 49440 | tf_op jit(solution)/shard_map/reduce_sum | solution.py:222
  37.2 0.8 %fusion.167 = (f32[16,30,284]{2,1,0:T(8,128)S(1)}, f32[16,30,284]{2,1,0:T(8,128)S(1)}, f32[16,30,284]{2,1,0:T(8,128)S(1)}, f32[16,30,284]{2,1,0:T(8,128)S(1)}, f...) fusion(f32[16,30,142]{2,1,0:T(8,128)S(1)} %get-tuple-element.244, f32[16,30,142]{2,1,0:T(8,128)S(1)} %get-tuple-element.245, ...), kind=kLoop, calls=%fused_computation.669 | loop fusion | flops 2044800 | bytes 4500832 | tf_op jit(solution)/shard_map/add | solution.py:133
  38.0 0.4 add_add_fusion.3
  38.5 0.3 fusion.126
  39.3 0.9 %add_add_fusion.2 = f32[16,30,284]{2,1,0:T(8,128)S(1)} fusion(f32[16,30,284]{2,1,0:T(8,128)S(1)} %broadcast_multiply_fusion.1, f32[16,30,284]{2,1,0:T(8,128)S(1)} %get-tuple-element.240, f32[16,30,284]{2,1,0:T(8,128)S(1)} %get-tuple-element.239, f32[16,30,284]{2,1,0:T(8,128)S(1)} %get-tuple-element.238, f32[16,30,284]{2,1,0:T(8,128)S(1)} %get-tuple-element.237, ...), kind=kLoop, calls=%fused_computation.22 | loop fusion | flops 2044800 | bytes 3819232 | tf_op jit(solution)/shard_map/add | solution.py:133
  40.2 0.2 fusion.108
  40.7 0.2 add_multiply_fusion.5
  40.9 0.9 %add_add_fusion.1 = f32[16,30,284]{2,1,0:T(8,128)S(1)} fusion(f32[16,30,284]{2,1,0:T(8,128)S(1)} %add_multiply_fusion.5, f32[16,30,284]{2,1,0:T(8,128)S(1)} %get-tuple-element.240, f32[16,30,284]{2,1,0:T(8,128)S(1)} %get-tuple-element.239, f32[16,30,284]{2,1,0:T(8,128)S(1)} %get-tuple-element.238, f32[16,30,284]{2,1,0:T(8,128)S(1)} %get-tuple-element.237, ...), kind=kLoop, calls=%fused_computation.20 | loop fusion | flops 2044800 | bytes 3819232 | tf_op jit(solution)/shard_map/add | solution.py:133
  41.8 0.2 fusion.93
  42.0 0.2 constant_dynamic-update-slice_fusion.64
  42.4 0.2 add_multiply_fusion.4
  42.6 0.9 %add_add_fusion = f32[16,30,284]{2,1,0:T(8,128)S(1)} fusion(f32[16,30,284]{2,1,0:T(8,128)S(1)} %add_multiply_fusion.4, f32[16,30,284]{2,1,0:T(8,128)S(1)} %get-tuple-element.240, f32[16,30,284]{2,1,0:T(8,128)S(1)} %get-tuple-element.239, f32[16,30,284]{2,1,0:T(8,128)S(1)} %get-tuple-element.238, f32[16,30,284]{2,1,0:T(8,128)S(1)} %get-tuple-element.237, ...), kind=kLoop, calls=%fused_computation.18 | loop fusion | flops 2044800 | bytes 3819232 | tf_op jit(solution)/shard_map/add | solution.py:133
  43.5 0.2 fusion.78
  43.6 0.2 constant_dynamic-update-slice_fusion.80
  44.0 0.2 add_multiply_fusion.3
  44.2 0.2 fusion.60
  44.4 0.2 constant_dynamic-update-slice_fusion.96
  44.9 0.8 %multiply_add_fusion.2 = f32[16,30,284]{2,1,0:T(8,128)S(1)} fusion(f32[16,30,284]{2,1,0:T(8,128)S(1)} %broadcast_multiply_fusion, f32[16,30,284]{2,1,0:T(8,128)S(1)} %get-tuple-element.240, f32[16,30,284]{2,1,0:T(8,128)S(1)} %get-tuple-element.239, f32[16,30,284]{2,1,0:T(8,128)S(1)} %get-tuple-element.238, f32[16,30,284]{2,1,0:T(8,128)S(1)} %get-tuple-element.237, ...), kind=kLoop, calls=%fused_computation.16 | loop fusion | flops 1772160 | bytes 3273952 | tf_op jit(solution)/shard_map/add | solution.py:130
  45.7 0.2 fusion.44
  45.9 0.2 constant_dynamic-update-slice_fusion.112
  46.3 0.2 add_multiply_fusion.2
  46.5 0.8 %multiply_add_fusion.1 = f32[16,30,284]{2,1,0:T(8,128)S(1)} fusion(f32[16,30,284]{2,1,0:T(8,128)S(1)} %add_multiply_fusion.2, f32[16,30,284]{2,1,0:T(8,128)S(1)} %get-tuple-element.240, f32[16,30,284]{2,1,0:T(8,128)S(1)} %get-tuple-element.239, f32[16,30,284]{2,1,0:T(8,128)S(1)} %get-tuple-element.238, f32[16,30,284]{2,1,0:T(8,128)S(1)} %get-tuple-element.237, ...), kind=kLoop, calls=%fused_computation.14 | loop fusion | flops 1772160 | bytes 3273952 | tf_op jit(solution)/shard_map/add | solution.py:130
  47.3 0.2 fusion.28
  47.4 0.2 constant_dynamic-update-slice_fusion.128
  47.8 0.2 add_multiply_fusion.1
  48.0 0.8 %multiply_add_fusion = f32[16,30,284]{2,1,0:T(8,128)S(1)} fusion(f32[16,30,284]{2,1,0:T(8,128)S(1)} %add_multiply_fusion.1, f32[16,30,284]{2,1,0:T(8,128)S(1)} %get-tuple-element.240, f32[16,30,284]{2,1,0:T(8,128)S(1)} %get-tuple-element.239, f32[16,30,284]{2,1,0:T(8,128)S(1)} %get-tuple-element.238, f32[16,30,284]{2,1,0:T(8,128)S(1)} %get-tuple-element.237, ...), kind=kLoop, calls=%fused_computation.12 | loop fusion | flops 1772160 | bytes 3273952 | tf_op jit(solution)/shard_map/add | solution.py:130
  48.8 0.2 fusion.12
  49.0 0.2 constant_dynamic-update-slice_fusion.144
  49.4 0.2 add_multiply_fusion
  49.6 0.2 slice_bitcast_fusion.1
  49.8 0.7 %pad_maximum_fusion.3 = f32[2,16,16,128]{3,2,1,0:T(8,128)} fusion(f32[1,16,16,128]{3,2,1,0:T(8,128)S(1)} %get-tuple-element.288, f32[1,16,16,128]{3,2,1,0:T(8,128)S(1)} %get-tuple-element.289), kind=kLoop, calls=%fused_computation.37 | loop fusion | flops 65536 | bytes 524288 | tf_op jit(solution)/shard_map/stack | solution.py:252
  50.5 0.7 %pad_maximum_fusion.4 = f32[2,16,16,128]{3,2,1,0:T(8,128)} fusion(f32[1,16,16,128]{3,2,1,0:T(8,128)S(1)} %get-tuple-element.247, f32[1,16,16,128]{3,2,1,0:T(8,128)S(1)} %get-tuple-element.246), kind=kLoop, calls=%fused_computation.40 | loop fusion | flops 65536 | bytes 524288 | tf_op jit(solution)/shard_map/stack | solution.py:252
  51.4 0.5 fusion
  51.9 9.1 %all_gather.7 = f32[8,8,16]{2,1,0:T(8,128)S(1)} all-gather(f32[1,8,16]{2,1,0:T(8,128)S(1)} %add.4639), channel_id=1, replica_groups=mesh['gx'=4,'gy'=8] {'gy'}, dimensions={0}, use_global_device_ids=true | all-gather | bytes 4608 | tf_op jit(solution)/shard_map/all_gather | solution.py:272
  61.0 0.5 dynamic-slice_reduce_fusion
  (187 shorter events, 3.8 us)
Async XLA Ops:
  0.6 13.2 %copy-start = (f32[2,16,16,128]{3,2,1,0:T(8,128)S(1)}, f32[2,16,16,128]{3,2,1,0:T(8,128)}, u32[]{:S(2)}) copy-start(f32[2,16,16,128]{3,2,1,0:T(8,128)} %param.8) | copy-start | bytes 786436
  0.6 12.8 %copy-start.1 = (f32[16,16,128]{2,1,0:T(8,128)S(1)}, f32[16,16,128]{2,1,0:T(8,128)}, u32[]{:S(2)}) copy-start(f32[16,16,128]{2,1,0:T(8,128)} %param.9) | copy-start | bytes 393220
  0.7 12.9 %copy-start.2 = (f32[2,16,128]{2,1,0:T(8,128)S(1)}, f32[2,16,128]{2,1,0:T(8,128)}, u32[]{:S(2)}) copy-start(f32[2,16,128]{2,1,0:T(8,128)} %param.10) | copy-start | bytes 49156
  0.7 13.0 %copy-start.5 = (s32[16,128]{1,0:T(8,128)S(1)}, s32[16,128]{1,0:T(8,128)}, u32[]{:S(2)}) copy-start(s32[16,128]{1,0:T(8,128)} %param.12) | copy-start | bytes 24580
  0.7 13.0 %copy-start.6 = (s32[16,128]{1,0:T(8,128)S(1)}, s32[16,128]{1,0:T(8,128)}, u32[]{:S(2)}) copy-start(s32[16,128]{1,0:T(8,128)} %param.13) | copy-start | bytes 24580
  5.4 11.0 %collective-permute-start.1 = (f32[53,7,128]{2,1,0:T(8,128)S(1)}, f32[53,7,128]{2,1,0:T(8,128)S(1)}, u32[]{:S(2)}, u32[]{:S(2)}) collective-permute-start(f32[53,7,128]{2,1,0:T(8,128)S(1)} %get-tuple-element.287), channel_id=1, source_target_pairs={{8,0},{16,8},{24,16},{9,1},{17,9},{25,17},{10,2},{18,10},{26,18},{... | collective-permute-start | bytes 569864 | tf_op jit(solution)/shard_map/ppermute | solution.py:160
  6.7 10.1 %collective-permute-start = (f32[53,7,128]{2,1,0:T(8,128)S(1)}, f32[53,7,128]{2,1,0:T(8,128)S(1)}, u32[]{:S(2)}, u32[]{:S(2)}) collective-permute-start(f32[53,7,128]{2,1,0:T(8,128)S(1)} %get-tuple-element.286), channel_id=1, source_target_pairs={{0,8},{8,16},{16,24},{1,9},{9,17},{17,25},{2,10},{10,18},{18,26},{... | collective-permute-start | bytes 569864 | tf_op jit(solution)/shard_map/ppermute | solution.py:160
  16.2 5.7 %copy-start.7 = (f32[1,16]{1,0:T(1,128)S(1)}, f32[1,16]{1,0:T(1,128)}, u32[]{:S(2)}) copy-start(f32[1,16]{1,0:T(1,128)} %param.11) | copy-start | bytes 196
  17.2 14.1 %collective-permute-start.3 = (f32[52,30,7]{0,1,2:T(8,128)S(1)}, f32[52,30,7]{0,1,2:T(8,128)S(1)}, u32[]{:S(2)}, u32[]{:S(2)}) collective-permute-start(f32[52,30,7]{0,1,2:T(8,128)S(1)} %pad_maximum_fusion.6), channel_id=1, source_target_pairs={{1,0},{2,1},{3,2},{4,3},{5,4},{6,5},{7,6},{9,8},{10,9},{11,10},{12... | collective-permute-start | bytes 131048 | tf_op jit(solution)/shard_map/ppermute | solution.py:160
  18.8 13.3 %collective-permute-start.2 = (f32[52,30,7]{0,1,2:T(8,128)S(1)}, f32[52,30,7]{0,1,2:T(8,128)S(1)}, u32[]{:S(2)}, u32[]{:S(2)}) collective-permute-start(f32[52,30,7]{0,1,2:T(8,128)S(1)} %pad_maximum_fusion.5), channel_id=1, source_target_pairs={{0,1},{1,2},{2,3},{3,4},{4,5},{5,6},{6,7},{8,9},{9,10},{10,11},{11... | collective-permute-start | bytes 131048 | tf_op jit(solution)/shard_map/ppermute | solution.py:160
  34.7 2.5 %copy-start.3 = (f32[284]{0:T(512)S(1)}, f32[284]{0:T(512)}, u32[]{:S(2)}) copy-start(f32[284]{0:T(512)} %constant.51.clone.1) | copy-start | bytes 3412
  34.7 2.5 %copy-start.4 = (f32[284]{0:T(512)S(1)}, f32[284]{0:T(512)}, u32[]{:S(2)}) copy-start(f32[284]{0:T(512)} %constant.49.clone.1) | copy-start | bytes 3412

commit v15 on v14

--- a/solution.py
+++ b/solution.py
@@ -160,6 +160,22 @@
     return lax.ppermute(piece, axis, pairs)
 
 
+def stack_planes(parts):
+    total = sum(p.shape[0] for p in parts)
+    index = lax.broadcasted_iota(jnp.int32, (total,) + parts[0].shape[1:], 0)
+    stacked = None
+    start = 0
+    for part in parts:
+        count = part.shape[0]
+        placed = jnp.pad(part, [(start, total - start - count)] + [(0, 0)] * (part.ndim - 1))
+        if stacked is None:
+            stacked = placed
+        else:
+            stacked = jnp.where(index >= start, placed, stacked)
+        start += count
+    return stacked
+
+
 def local(forcing, viscosity, observed, beta_tiles, ice_mask, tile_owner):
     comps, layers, rows, cols = forcing.shape
     tiles_here = beta_tiles.shape[1]
@@ -175,8 +191,8 @@
     every = slice(None)
 
     beta_plane = jnp.pad(beta_tiles, ((0, HALO - 1), (0, cols - tiles_here)))[None]
-    head = jnp.concatenate(pieces(slice(0, HALO), every) + [beta_plane], axis=0)
-    tail = jnp.concatenate(pieces(slice(rows - HALO, rows), every) + [beta_plane], axis=0)
+    head = stack_planes(pieces(slice(0, HALO), every) + [beta_plane])
+    tail = stack_planes(pieces(slice(rows - HALO, rows), every) + [beta_plane])
     from_above = shifted(tail, "gx", True)
     from_below = shifted(head, "gx", False)
 

time: 62 us -> 64.9 us (1.047)
  waiting for transfers between devices: 0.18 us -> 4.02 us
  blocking collectives: 18.3 us -> 20.9 us
  starting transfers between devices: 11.2 us -> 8.82 us
  local copies, waits for them, and re-layouts: 10.6 us -> 9.67 us
    ppermute x4, waiting for transfers between devices: 0.18 us -> 4.02 us  [shifted(): return lax.ppermute(piece, axis, pairs)]
    all_gather x1, blocking collectives: 9.2 us -> 12.8 us  [local(): friction_rows = lax.all_gather(strips_near, 'gy', axis=1, tiled=True)]
    unnamed x86 -> x83, local copies, waits for them, and re-layouts: 4.03 us -> 1.4 us
    ppermute x4, starting transfers between devices: 11.2 us -> 8.82 us  [shifted(): return lax.ppermute(piece, axis, pairs)]
    slice x5 -> x8, local copies, waits for them, and re-layouts: 1.71 us -> 3.38 us  [pieces(): p[:, rows_at, cols_at]]
    unnamed x70 -> x68, other arithmetic: 3.46 us -> 2.05 us
    all_gather x1, blocking collectives: 9.05 us -> 8.15 us  [local(): gathered = lax.all_gather(partial_sum.reshape(owners, chunk), 'gy')]
    convert_element_type x2 -> x3, other arithmetic: 0.15 us -> 0.89 us  [pieces(): p[:, rows_at, cols_at].astype(jnp.float32)]
  transfers between devices with their start and end apart: 4 -> 4, of which waited for: 1 -> 2; matrix products, arithmetic and copies ran while one was open for 9% -> 7% of each run, Pallas kernels for 0% -> 0%
where the time goes in v15:
time: 64.9 us; the launch traced here: 64.5 us
  blocking collectives  20.9 us (32%)
  other arithmetic  18.5 us (29%)
  local copies, waits for them, and re-layouts  9.67 us (15%)
  starting transfers between devices  8.82 us (14%)
  waiting for transfers between devices  4.02 us (6%)
  between operations  2.12 us (3%)
    all_gather x1, blocking collectives, local(): friction_rows = lax.all_gather(strips_near, 'gy', axis=1, tiled=True)  12.8 us
    ppermute x4, starting transfers between devices, shifted(): return lax.ppermute(piece, axis, pairs)  8.82 us
    all_gather x1, blocking collectives, local(): gathered = lax.all_gather(partial_sum.reshape(owners, chunk), 'gy')  8.15 us
    ppermute x4, waiting for transfers between devices, shifted(): return lax.ppermute(piece, axis, pairs)  4.02 us
    add x4, other arithmetic, relax_lanes(): right_side = rhs_field + lateral  3.53 us
    slice x8, local copies, waits for them, and re-layouts, pieces(): p[:, rows_at, cols_at]  3.38 us
    add x3, other arithmetic, relax_lanes(): lateral + along_y * (south_face * vel_pad[:, 1:-1, :-2] + north_face * ve...  2.36 us
    reduce_sum x1, other arithmetic, local(): jnp.sum(jnp.where(owner_match, row_strip[:, :, None], 0.0), axis=0)  2.23 us
  transfers between devices with their start and end apart: 4, of which 2 were waited for; matrix products, arithmetic and copies ran while one was open for 7% of the time, Pallas kernels for 0%

profile of v15, /device:TPU:0, one launch (start us, length us, event | category | flops | bytes accessed | tf_op | source)
XLA Modules:
  0.0 64.5 jit_solution(14737075941638746580)
XLA Ops:
  0.7 1.1 %fusion.299 = (f32[32,7,128]{2,1,0:T(8,128)S(1)}, f32[32,7,128]{2,1,0:T(8,128)S(1)}) fusion(f32[32,16,128]{2,1,0:T(8,128)} %bitcast.63), kind=kLoop, calls=%fused_computation.668 | loop fusion | bytes 458752 | tf_op jit(solution)/shard_map/slice | solution.py:186
  1.8 0.9 %fusion.303 = (f32[16,7,128]{2,1,0:T(8,128)S(1)}, f32[16,7,128]{2,1,0:T(8,128)S(1)}) fusion(f32[16,16,128]{2,1,0:T(8,128)} %param.9), kind=kLoop, calls=%fused_computation.672 | loop fusion | bytes 229376 | tf_op jit(solution)/shard_map/slice | solution.py:186
  2.7 0.7 %fusion.305 = (f32[2,7,128]{2,1,0:T(8,128)S(1)}, f32[2,7,128]{2,1,0:T(8,128)S(1)}) fusion(f32[2,16,128]{2,1,0:T(8,128)} %param.10), kind=kLoop, calls=%fused_computation.674 | loop fusion | bytes 28672 | tf_op jit(solution)/shard_map/slice | solution.py:186
  3.4 0.7 %pad_bitcast_fusion = f32[1,7,128]{2,1,0:T(8,128)S(1)} fusion(f32[1,16]{1,0:T(1,128)} %param.11), kind=kLoop, calls=%fused_computation.651 | loop fusion | bytes 3648 | tf_op jit(solution)/shard_map/broadcast_in_dim | solution.py:193
  4.1 0.7 %slice_convert_fusion.6 = (f32[1,7,128]{2,1,0:T(8,128)S(1)}, f32[1,7,128]{2,1,0:T(8,128)S(1)}, f32[1,7,128]{2,1,0:T(8,128)S(1)}, f32[1,7,128]{2,1,0:T(8,128)S(1)}) fusion(s32[1,16,128]{2,1,0:T(8,128)} %bitcast.66, s32[1,16,128]{2,1,0:T(8,128)} %bitcast.68), kind=kLoop, calls=%fused_computation.648 | loop fusion | flops 3584 | bytes 28672 | tf_op jit(solution)/shard_map/convert_element_type | solution.py:187
  4.8 0.3 pad_select_fusion.1
  5.2 4.9 %collective-permute-start = (f32[53,7,128]{2,1,0:T(8,128)S(1)}, f32[53,7,128]{2,1,0:T(8,128)S(1)}, u32[]{:S(2)}, u32[]{:S(2)}) collective-permute-start(f32[53,7,128]{2,1,0:T(8,128)S(1)} %get-tuple-element.283), channel_id=1, source_target_pairs={{0,8},{8,16},{16,24},{1,9},{9,17},{17,25},{2,10},{10,18},{18,26},{... | collective-permute-start | bytes 569864 | tf_op jit(solution)/shard_map/ppermute | solution.py:160
  10.1 1.3 %collective-permute-start.1 = (f32[53,7,128]{2,1,0:T(8,128)S(1)}, f32[53,7,128]{2,1,0:T(8,128)S(1)}, u32[]{:S(2)}, u32[]{:S(2)}) collective-permute-start(f32[53,7,128]{2,1,0:T(8,128)S(1)} %get-tuple-element.284), channel_id=1, source_target_pairs={{8,0},{16,8},{24,16},{9,1},{17,9},{25,17},{10,2},{18,10},{26,18},{... | collective-permute-start | bytes 569864 | tf_op jit(solution)/shard_map/ppermute | solution.py:160
  11.9 0.2 copy.52
  12.1 0.2 copy.53
  12.3 0.2 copy.54
  12.6 0.2 copy.67
  12.8 0.2 copy.68
  13.0 0.2 copy.59
  13.2 0.2 copy.60
  13.4 0.2 copy.61
  13.6 0.2 copy.69
  13.8 0.2 copy.70
  14.5 0.2 collective-permute-done
  14.9 3.9 %collective-permute-done.1 = f32[53,7,128]{2,1,0:T(8,128)S(1)} collective-permute-done((f32[53,7,128]{2,1,0:T(8,128)S(1)}, f32[53,7,128]{2,1,0:T(8,128)S(1)}, u32[]{:S(2)}, u32[]{:S(2)}) %collective-permute-start.1) | collective-permute-done | bytes 189984 | tf_op jit(solution)/shard_map/ppermute | solution.py:160
  19.1 1.3 %collective-permute-start.2 = (f32[52,30,7]{0,1,2:T(8,128)S(1)}, f32[52,30,7]{0,1,2:T(8,128)S(1)}, u32[]{:S(2)}, u32[]{:S(2)}) collective-permute-start(f32[52,30,7]{0,1,2:T(8,128)S(1)} %pad_maximum_fusion.5), channel_id=1, source_target_pairs={{0,1},{1,2},{2,3},{3,4},{4,5},{5,6},{6,7},{8,9},{9,10},{10,11},{11... | collective-permute-start | bytes 131048 | tf_op jit(solution)/shard_map/ppermute | solution.py:160
  20.6 0.2 copy.63
  20.8 1.3 %collective-permute-start.3 = (f32[52,30,7]{0,1,2:T(8,128)S(1)}, f32[52,30,7]{0,1,2:T(8,128)S(1)}, u32[]{:S(2)}, u32[]{:S(2)}) collective-permute-start(f32[52,30,7]{0,1,2:T(8,128)S(1)} %pad_maximum_fusion.6), channel_id=1, source_target_pairs={{1,0},{2,1},{3,2},{4,3},{5,4},{6,5},{7,6},{9,8},{10,9},{11,10},{12... | collective-permute-start | bytes 131048 | tf_op jit(solution)/shard_map/ppermute | solution.py:160
  22.1 12.8 %all-gather = f32[8,16,3]{1,2,0:T(4,128)S(1)} all-gather(f32[1,16,3]{1,2,0:T(4,128)S(1)} %maximum_bitcast_fusion.2), channel_id=1, replica_groups=mesh['gx'=4,'gy'=8] {'gy'}, dimensions={0}, use_global_device_ids=true | all-gather | bytes 1728 | tf_op jit(solution)/shard_map/all_gather | solution.py:213
  35.1 0.8 %copy.64 = f32[52,30,7]{2,1,0:T(8,128)S(1)} copy(f32[52,30,7]{0,1,2:T(8,128)S(1)} %collective-permute-done.2) | data formatting | bytes 87360 | tf_op jit(solution)/shard_map/ppermute | solution.py:160
  36.0 0.9 %copy.65 = f32[52,30,7]{2,1,0:T(8,128)S(1)} copy(f32[52,30,7]{0,1,2:T(8,128)S(1)} %collective-permute-done.3) | data formatting | bytes 87360 | tf_op jit(solution)/shard_map/ppermute | solution.py:160
  36.8 1.0 %pad_maximum_fusion = f32[52,30,142]{2,1,0:T(8,128)S(1)} fusion(f32[52,30,7]{2,1,0:T(8,128)S(1)} %copy.65, f32[52,7,128]{2,1,0:T(8,128)S(1)} %slice.1159, f32[52,16,128]{2,1,0:T(8,128)S(1)} %constant_dynamic-update-slice_fusion, f32[52,7,128]{2,1,0:T(8,128)S(1)} %slice.1158, f32[52,30,7]{2,1,0:T(8,128)S(1)} %copy.64), kind=kLoop, calls=%fused_computation.2 | loop fusion | flops 886080 | bytes 1772160 | tf_op jit(solution)/shard_map/concatenate | solution.py:216
  38.1 0.2 pad_maximum_fusion.1
  38.3 0.3 fusion.3
  38.6 2.2 %select_reduce_fusion = f32[30,142]{1,0:T(8,128)S(1)} fusion(f32[128,30]{0,1:T(8,128)S(1)} %pad_maximum_fusion.16, s32[30,142]{1,0:T(8,128)S(1)} %get-tuple-element.242), kind=kLoop, calls=%fused_computation | loop fusion | flops 1631580 | bytes 49440 | tf_op jit(solution)/shard_map/reduce_sum | solution.py:238
  41.0 0.8 %fusion.167 = (f32[16,30,284]{2,1,0:T(8,128)S(1)}, f32[16,30,284]{2,1,0:T(8,128)S(1)}, f32[16,30,284]{2,1,0:T(8,128)S(1)}, f32[16,30,284]{2,1,0:T(8,128)S(1)}, f...) fusion(f32[16,30,142]{2,1,0:T(8,128)S(1)} %get-tuple-element.244, f32[16,30,142]{2,1,0:T(8,128)S(1)} %get-tuple-element.245, ...), kind=kLoop, calls=%fused_computation.665 | loop fusion | flops 2044800 | bytes 4500832 | tf_op jit(solution)/shard_map/add | solution.py:133
  41.8 0.4 add_add_fusion.3
  42.3 0.3 fusion.126
  43.1 0.9 %add_add_fusion.2 = f32[16,30,284]{2,1,0:T(8,128)S(1)} fusion(f32[16,30,284]{2,1,0:T(8,128)S(1)} %broadcast_multiply_fusion.1, f32[16,30,284]{2,1,0:T(8,128)S(1)} %get-tuple-element.240, f32[16,30,284]{2,1,0:T(8,128)S(1)} %get-tuple-element.239, f32[16,30,284]{2,1,0:T(8,128)S(1)} %get-tuple-element.238, f32[16,30,284]{2,1,0:T(8,128)S(1)} %get-tuple-element.237, ...), kind=kLoop, calls=%fused_computation.22 | loop fusion | flops 2044800 | bytes 3819232 | tf_op jit(solution)/shard_map/add | solution.py:133
  44.0 0.2 fusion.108
  44.1 0.2 constant_dynamic-update-slice_fusion.36
  44.5 0.2 add_multiply_fusion.5
  44.7 0.9 %add_add_fusion.1 = f32[16,30,284]{2,1,0:T(8,128)S(1)} fusion(f32[16,30,284]{2,1,0:T(8,128)S(1)} %add_multiply_fusion.5, f32[16,30,284]{2,1,0:T(8,128)S(1)} %get-tuple-element.240, f32[16,30,284]{2,1,0:T(8,128)S(1)} %get-tuple-element.239, f32[16,30,284]{2,1,0:T(8,128)S(1)} %get-tuple-element.238, f32[16,30,284]{2,1,0:T(8,128)S(1)} %get-tuple-element.237, ...), kind=kLoop, calls=%fused_computation.20 | loop fusion | flops 2044800 | bytes 3819232 | tf_op jit(solution)/shard_map/add | solution.py:133
  45.6 0.2 fusion.93
  45.8 0.2 constant_dynamic-update-slice_fusion.52
  46.2 0.2 add_multiply_fusion.4
  46.4 0.9 %add_add_fusion = f32[16,30,284]{2,1,0:T(8,128)S(1)} fusion(f32[16,30,284]{2,1,0:T(8,128)S(1)} %add_multiply_fusion.4, f32[16,30,284]{2,1,0:T(8,128)S(1)} %get-tuple-element.240, f32[16,30,284]{2,1,0:T(8,128)S(1)} %get-tuple-element.239, f32[16,30,284]{2,1,0:T(8,128)S(1)} %get-tuple-element.238, f32[16,30,284]{2,1,0:T(8,128)S(1)} %get-tuple-element.237, ...), kind=kLoop, calls=%fused_computation.18 | loop fusion | flops 2044800 | bytes 3819232 | tf_op jit(solution)/shard_map/add | solution.py:133
  47.3 0.2 fusion.78
  47.4 0.2 constant_dynamic-update-slice_fusion.68
  47.8 0.2 add_multiply_fusion.3
  48.1 0.2 fusion.60
  48.4 0.2 constant_dynamic-update-slice_fusion.84
  48.9 0.8 %multiply_add_fusion.2 = f32[16,30,284]{2,1,0:T(8,128)S(1)} fusion(f32[16,30,284]{2,1,0:T(8,128)S(1)} %broadcast_multiply_fusion, f32[16,30,284]{2,1,0:T(8,128)S(1)} %get-tuple-element.240, f32[16,30,284]{2,1,0:T(8,128)S(1)} %get-tuple-element.239, f32[16,30,284]{2,1,0:T(8,128)S(1)} %get-tuple-element.238, f32[16,30,284]{2,1,0:T(8,128)S(1)} %get-tuple-element.237, ...), kind=kLoop, calls=%fused_computation.16 | loop fusion | flops 1772160 | bytes 3273952 | tf_op jit(solution)/shard_map/add | solution.py:130
  49.6 0.2 fusion.44
  49.8 0.2 constant_dynamic-update-slice_fusion.100
  50.2 0.2 add_multiply_fusion.2
  50.4 0.8 %multiply_add_fusion.1 = f32[16,30,284]{2,1,0:T(8,128)S(1)} fusion(f32[16,30,284]{2,1,0:T(8,128)S(1)} %add_multiply_fusion.2, f32[16,30,284]{2,1,0:T(8,128)S(1)} %get-tuple-element.240, f32[16,30,284]{2,1,0:T(8,128)S(1)} %get-tuple-element.239, f32[16,30,284]{2,1,0:T(8,128)S(1)} %get-tuple-element.238, f32[16,30,284]{2,1,0:T(8,128)S(1)} %get-tuple-element.237, ...), kind=kLoop, calls=%fused_computation.14 | loop fusion | flops 1772160 | bytes 3273952 | tf_op jit(solution)/shard_map/add | solution.py:130
  51.2 0.2 fusion.28
  51.4 0.2 constant_dynamic-update-slice_fusion.116
  51.8 0.2 add_multiply_fusion.1
  52.0 0.8 %multiply_add_fusion = f32[16,30,284]{2,1,0:T(8,128)S(1)} fusion(f32[16,30,284]{2,1,0:T(8,128)S(1)} %add_multiply_fusion.1, f32[16,30,284]{2,1,0:T(8,128)S(1)} %get-tuple-element.240, f32[16,30,284]{2,1,0:T(8,128)S(1)} %get-tuple-element.239, f32[16,30,284]{2,1,0:T(8,128)S(1)} %get-tuple-element.238, f32[16,30,284]{2,1,0:T(8,128)S(1)} %get-tuple-element.237, ...), kind=kLoop, calls=%fused_computation.12 | loop fusion | flops 1772160 | bytes 3273952 | tf_op jit(solution)/shard_map/add | solution.py:130
  52.8 0.2 fusion.12
  52.9 0.2 constant_dynamic-update-slice_fusion.132
  53.3 0.2 add_multiply_fusion
  53.7 0.7 %pad_maximum_fusion.4 = f32[2,16,16,128]{3,2,1,0:T(8,128)} fusion(f32[1,16,16,128]{3,2,1,0:T(8,128)S(1)} %get-tuple-element.247, f32[1,16,16,128]{3,2,1,0:T(8,128)S(1)} %get-tuple-element.246), kind=kLoop, calls=%fused_computation.40 | loop fusion | flops 65536 | bytes 524288 | tf_op jit(solution)/shard_map/stack | solution.py:268
  54.4 0.7 %pad_maximum_fusion.3 = f32[2,16,16,128]{3,2,1,0:T(8,128)} fusion(f32[1,16,16,128]{3,2,1,0:T(8,128)S(1)} %get-tuple-element.249, f32[1,16,16,128]{3,2,1,0:T(8,128)S(1)} %get-tuple-element.248), kind=kLoop, calls=%fused_computation.37 | loop fusion | flops 65536 | bytes 524288 | tf_op jit(solution)/shard_map/stack | solution.py:268
  55.2 0.5 fusion
  55.8 8.2 %all_gather.7 = f32[8,8,16]{2,1,0:T(8,128)S(1)} all-gather(f32[1,8,16]{2,1,0:T(8,128)S(1)} %add.4661), channel_id=1, replica_groups=mesh['gx'=4,'gy'=8] {'gy'}, dimensions={0}, use_global_device_ids=true | all-gather | bytes 4608 | tf_op jit(solution)/shard_map/all_gather | solution.py:288
  63.9 0.5 dynamic-slice_reduce_fusion
  (191 shorter events, 4.0 us)
Async XLA Ops:
  0.6 10.8 %copy-start = (f32[2,16,16,128]{3,2,1,0:T(8,128)S(1)}, f32[2,16,16,128]{3,2,1,0:T(8,128)}, u32[]{:S(2)}) copy-start(f32[2,16,16,128]{3,2,1,0:T(8,128)} %param.8) | copy-start | bytes 786436
  0.6 11.1 %copy-start.1 = (f32[16,16,128]{2,1,0:T(8,128)S(1)}, f32[16,16,128]{2,1,0:T(8,128)}, u32[]{:S(2)}) copy-start(f32[16,16,128]{2,1,0:T(8,128)} %param.9) | copy-start | bytes 393220
  0.7 11.2 %copy-start.2 = (f32[2,16,128]{2,1,0:T(8,128)S(1)}, f32[2,16,128]{2,1,0:T(8,128)}, u32[]{:S(2)}) copy-start(f32[2,16,128]{2,1,0:T(8,128)} %param.10) | copy-start | bytes 49156
  0.7 11.0 %copy-start.6 = (s32[16,128]{1,0:T(8,128)S(1)}, s32[16,128]{1,0:T(8,128)}, u32[]{:S(2)}) copy-start(s32[16,128]{1,0:T(8,128)} %param.13) | copy-start | bytes 24580
  0.7 10.9 %copy-start.5 = (s32[16,128]{1,0:T(8,128)S(1)}, s32[16,128]{1,0:T(8,128)}, u32[]{:S(2)}) copy-start(s32[16,128]{1,0:T(8,128)} %param.12) | copy-start | bytes 24580
  5.2 9.5 %collective-permute-start = (f32[53,7,128]{2,1,0:T(8,128)S(1)}, f32[53,7,128]{2,1,0:T(8,128)S(1)}, u32[]{:S(2)}, u32[]{:S(2)}) collective-permute-start(f32[53,7,128]{2,1,0:T(8,128)S(1)} %get-tuple-element.283), channel_id=1, source_target_pairs={{0,8},{8,16},{16,24},{1,9},{9,17},{17,25},{2,10},{10,18},{18,26},{... | collective-permute-start | bytes 569864 | tf_op jit(solution)/shard_map/ppermute | solution.py:160
  10.1 8.7 %collective-permute-start.1 = (f32[53,7,128]{2,1,0:T(8,128)S(1)}, f32[53,7,128]{2,1,0:T(8,128)S(1)}, u32[]{:S(2)}, u32[]{:S(2)}) collective-permute-start(f32[53,7,128]{2,1,0:T(8,128)S(1)} %get-tuple-element.284), channel_id=1, source_target_pairs={{8,0},{16,8},{24,16},{9,1},{17,9},{25,17},{10,2},{18,10},{26,18},{... | collective-permute-start | bytes 569864 | tf_op jit(solution)/shard_map/ppermute | solution.py:160
  14.3 7.8 %copy-start.7 = (f32[1,16]{1,0:T(1,128)S(1)}, f32[1,16]{1,0:T(1,128)}, u32[]{:S(2)}) copy-start(f32[1,16]{1,0:T(1,128)} %param.11) | copy-start | bytes 196
  19.1 16.0 %collective-permute-start.2 = (f32[52,30,7]{0,1,2:T(8,128)S(1)}, f32[52,30,7]{0,1,2:T(8,128)S(1)}, u32[]{:S(2)}, u32[]{:S(2)}) collective-permute-start(f32[52,30,7]{0,1,2:T(8,128)S(1)} %pad_maximum_fusion.5), channel_id=1, source_target_pairs={{0,1},{1,2},{2,3},{3,4},{4,5},{5,6},{6,7},{8,9},{9,10},{10,11},{11... | collective-permute-start | bytes 131048 | tf_op jit(solution)/shard_map/ppermute | solution.py:160
  20.8 15.2 %collective-permute-start.3 = (f32[52,30,7]{0,1,2:T(8,128)S(1)}, f32[52,30,7]{0,1,2:T(8,128)S(1)}, u32[]{:S(2)}, u32[]{:S(2)}) collective-permute-start(f32[52,30,7]{0,1,2:T(8,128)S(1)} %pad_maximum_fusion.6), channel_id=1, source_target_pairs={{1,0},{2,1},{3,2},{4,3},{5,4},{6,5},{7,6},{9,8},{10,9},{11,10},{12... | collective-permute-start | bytes 131048 | tf_op jit(solution)/shard_map/ppermute | solution.py:160
  38.0 3.0 %copy-start.3 = (f32[284]{0:T(512)S(1)}, f32[284]{0:T(512)}, u32[]{:S(2)}) copy-start(f32[284]{0:T(512)} %constant.59.clone.1) | copy-start | bytes 3412
  38.0 3.0 %copy-start.4 = (f32[284]{0:T(512)S(1)}, f32[284]{0:T(512)}, u32[]{:S(2)}) copy-start(f32[284]{0:T(512)} %constant.61.clone.1) | copy-start | bytes 3412

commit v16 on v14

--- a/solution.py
+++ b/solution.py
@@ -174,30 +174,25 @@
     plane_count = sum(p.shape[0] for p in float_planes + int_planes)
     every = slice(None)
 
-    beta_plane = jnp.pad(beta_tiles, ((0, HALO - 1), (0, cols - tiles_here)))[None]
-    head = jnp.concatenate(pieces(slice(0, HALO), every) + [beta_plane], axis=0)
-    tail = jnp.concatenate(pieces(slice(rows - HALO, rows), every) + [beta_plane], axis=0)
+    from_left = shifted(jnp.concatenate(pieces(every, slice(cols - HALO, cols)), axis=0), "gy", True)
+    from_right = shifted(jnp.concatenate(pieces(every, slice(0, HALO)), axis=0), "gy", False)
+    widened = jnp.concatenate(
+        [from_left, jnp.concatenate(pieces(every, every), axis=0), from_right], axis=2
+    )
+    wide_cols = widened.shape[2]
+    beta_plane = jnp.pad(beta_tiles, ((0, HALO - 1), (0, wide_cols - tiles_here)))[None]
+    head = jnp.concatenate([widened[:, :HALO], beta_plane], axis=0)
+    tail = jnp.concatenate([widened[:, rows - HALO:], beta_plane], axis=0)
     from_above = shifted(tail, "gx", True)
     from_below = shifted(head, "gx", False)
 
-    def stack_rows(lo, hi):
-        return jnp.concatenate(
-            [from_above[:plane_count, :, lo:hi]]
-            + [jnp.concatenate(pieces(every, slice(lo, hi)), axis=0)]
-            + [from_below[:plane_count, :, lo:hi]],
-            axis=1,
-        )
-
-    from_left = shifted(stack_rows(cols - HALO, cols), "gy", True)
-    from_right = shifted(stack_rows(0, HALO), "gy", False)
-
     strips_near = jnp.stack(
         [from_above[plane_count, 0, :tiles_here], beta_tiles[0], from_below[plane_count, 0, :tiles_here]]
     )
     friction_rows = lax.all_gather(strips_near, "gy", axis=1, tiled=True)
     tile_count = friction_rows.shape[1]
 
-    packed = jnp.concatenate([from_left, stack_rows(0, cols), from_right], axis=2)
+    packed = jnp.concatenate([from_above[:plane_count], widened, from_below[:plane_count]], axis=1)
     ext_rows, ext_cols = packed.shape[1], packed.shape[2]
     at = 0
     forcing_ext = packed[at:at + comps * layers].reshape(comps, layers, ext_rows, ext_cols)

time: 62 us -> 80 us (1.29)
  blocking collectives: 18.3 us -> 27.4 us
  waiting for transfers between devices: 0.18 us -> 6.72 us
  other arithmetic: 18.8 us -> 21.3 us
    all_gather x1, blocking collectives: 9.2 us -> 19.5 us  [local(): friction_rows = lax.all_gather(strips_near, 'gy', axis=1, tiled=True)]
    ppermute x4, waiting for transfers between devices: 0.18 us -> 6.72 us  [shifted(): return lax.ppermute(piece, axis, pairs)]
    unnamed x86 -> x100, local copies, waits for them, and re-layouts: 4.03 us -> 6.49 us
    slice x13 -> x3, local copies, waits for them, and re-layouts: 2.58 us -> 0.12 us  [the longest x1 0.07 us: local(): tail = jnp.concatenate([widened[:, rows - HALO:], beta_plane], axis=0)]
    ppermute x2 -> x0, local copies, waits for them, and re-layouts: 1.7 us -> none  [shifted(): return lax.ppermute(piece, axis, pairs)]
    another operation x2, local copies, waits for them, and re-layouts: 0.01 us -> 1.35 us  [local(): jnp.stack([from_above[plane_count, 0, :tiles_here], beta_tiles[0], from_b...]
    all_gather x1, blocking collectives: 9.05 us -> 7.86 us  [local(): gathered = lax.all_gather(partial_sum.reshape(owners, chunk), 'gy')]
    concatenate x3 -> x0, local copies, waits for them, and re-layouts: 0.92 us -> none  [the longest x1 0.66 us: local(): jnp.concatenate(pieces(slice(rows - HALO, rows), every) + [beta_plane], a...]
  transfers between devices with their start and end apart: 4 -> 4, of which waited for: 1 -> 3; matrix products, arithmetic and copies ran while one was open for 9% -> 1% of each run, Pallas kernels for 0% -> 0%
where the time goes in v16:
time: 80 us; the launch traced here: 78.9 us
  blocking collectives  27.4 us (34%)
  other arithmetic  21.3 us (27%)
  starting transfers between devices  11.2 us (14%)
  local copies, waits for them, and re-layouts  9.83 us (12%)
  waiting for transfers between devices  6.72 us (8%)
  between operations  2.04 us (3%)
    all_gather x1, blocking collectives, local(): friction_rows = lax.all_gather(strips_near, 'gy', axis=1, tiled=True)  19.5 us
    ppermute x4, starting transfers between devices, shifted(): return lax.ppermute(piece, axis, pairs)  11.2 us
    all_gather x1, blocking collectives, local(): gathered = lax.all_gather(partial_sum.reshape(owners, chunk), 'gy')  7.86 us
    ppermute x4, waiting for transfers between devices, shifted(): return lax.ppermute(piece, axis, pairs)  6.72 us
    unnamed x100, local copies, waits for them, and re-layouts  6.49 us
    add x4, other arithmetic, relax_lanes(): right_side = rhs_field + lateral  3.54 us
    unnamed x69, other arithmetic  2.91 us
    add x3, other arithmetic, relax_lanes(): lateral + along_y * (south_face * vel_pad[:, 1:-1, :-2] + north_face * ve...  2.36 us
  transfers between devices with their start and end apart: 4, of which 3 were waited for; matrix products, arithmetic and copies ran while one was open for 1% of the time, Pallas kernels for 0%

profile of v16, /device:TPU:0, one launch (start us, length us, event | category | flops | bytes accessed | tf_op | source)
XLA Modules:
  0.0 78.9 jit_solution(15998533362687778499)
XLA Ops:
  0.7 1.2 %constant_dynamic-update-slice_fusion.4 = (f32[52,16,7]{2,1,0:T(8,128)S(1)}, f32[52,16,7]{2,1,0:T(8,128)S(1)}) fusion(f32[32,16,128]{2,1,0:T(8,128)} %bitcast.63), kind=kLoop, calls=%fused_computation.49 | loop fusion | bytes 552960
  1.9 1.1 %constant_dynamic-update-slice_fusion.3 = (f32[52,16,7]{2,1,0:T(8,128)S(1)}, f32[52,16,7]{2,1,0:T(8,128)S(1)}) fusion(f32[52,16,7]{2,1,0:T(8,128)S(1)} %get-tuple-element.252, f32[16,16,128]{2,1,0:T(8,128)} %param.9, f32[52,16,7]{2,1,0:T(8,128)S(1)} %get-tuple-element.253), kind=kLoop, calls=%fused_computation.48 | loop fusion | bytes 276480
  3.0 0.9 %constant_dynamic-update-slice_fusion.2 = (f32[52,16,7]{2,1,0:T(8,128)S(1)}, f32[52,16,7]{2,1,0:T(8,128)S(1)}) fusion(f32[52,16,7]{2,1,0:T(8,128)S(1)} %get-tuple-element.254, f32[2,16,128]{2,1,0:T(8,128)} %param.10, f32[52,16,7]{2,1,0:T(8,128)S(1)} %get-tuple-element.255), kind=kLoop, calls=%fused_computation.47 | loop fusion | bytes 34560
  3.9 0.8 %constant_dynamic-update-slice_fusion.1 = (f32[52,16,7]{2,1,0:T(8,128)S(1)}, f32[52,16,7]{2,1,0:T(8,128)S(1)}) fusion(f32[52,16,7]{2,1,0:T(8,128)S(1)} %get-tuple-element.263, s32[1,16,128]{2,1,0:T(8,128)} %bitcast.65, f32[52,16,7]{2,1,0:T(8,128)S(1)} %get-tuple-element.264), kind=kLoop, calls=%fused_computation.46 | loop fusion | flops 224 | bytes 17280
  4.7 0.8 %constant_dynamic-update-slice_fusion = (f32[52,16,7]{2,1,0:T(8,128)S(1)}, f32[52,16,7]{2,1,0:T(8,128)S(1)}) fusion(f32[52,16,7]{2,1,0:T(8,128)S(1)} %get-tuple-element.271, s32[1,16,128]{2,1,0:T(8,128)} %bitcast.66, f32[52,16,7]{2,1,0:T(8,128)S(1)} %get-tuple-element.272), kind=kLoop, calls=%fused_computation.45 | loop fusion | flops 224 | bytes 17280 | tf_op jit(solution)/shard_map/concatenate | solution.py:177
  5.6 1.3 %collective-permute-start.1 = (f32[52,16,7]{2,1,0:T(8,128)S(1)}, f32[52,16,7]{2,1,0:T(8,128)S(1)}, u32[]{:S(2)}, u32[]{:S(2)}) collective-permute-start(f32[52,16,7]{2,1,0:T(8,128)S(1)} %get-tuple-element.270), channel_id=1, source_target_pairs={{1,0},{2,1},{3,2},{4,3},{5,4},{6,5},{7,6},{9,8},{10,9},{11,10},{12... | collective-permute-start | bytes 69896 | tf_op jit(solution)/shard_map/ppermute | solution.py:160
  6.9 3.1 %collective-permute-start = (f32[52,16,7]{2,1,0:T(8,128)S(1)}, f32[52,16,7]{2,1,0:T(8,128)S(1)}, u32[]{:S(2)}, u32[]{:S(2)}) collective-permute-start(f32[52,16,7]{2,1,0:T(8,128)S(1)} %get-tuple-element.269), channel_id=1, source_target_pairs={{0,1},{1,2},{2,3},{3,4},{4,5},{5,6},{6,7},{8,9},{9,10},{10,11},{11... | collective-permute-start | bytes 69896 | tf_op jit(solution)/shard_map/ppermute | solution.py:160
  10.1 1.2 %collective-permute-done = f32[52,16,7]{2,1,0:T(8,128)S(1)} collective-permute-done((f32[52,16,7]{2,1,0:T(8,128)S(1)}, f32[52,16,7]{2,1,0:T(8,128)S(1)}, u32[]{:S(2)}, u32[]{:S(2)}) %collective-permute-start) | collective-permute-done | bytes 23328 | tf_op jit(solution)/shard_map/ppermute | solution.py:160
  11.3 0.4 pad_maximum_fusion.2
  11.9 1.3 %collective-permute-start.3 = (f32[53,7,142]{2,1,0:T(8,128)S(1)}, f32[53,7,142]{2,1,0:T(8,128)S(1)}, u32[]{:S(2)}, u32[]{:S(2)}) collective-permute-start(f32[53,7,142]{2,1,0:T(8,128)S(1)} %get-tuple-element.268), channel_id=1, source_target_pairs={{8,0},{16,8},{24,16},{9,1},{17,9},{25,17},{10,2},{18,10},{26,18},{... | collective-permute-start | bytes 632192 | tf_op jit(solution)/shard_map/ppermute | solution.py:160
  13.2 5.6 %collective-permute-start.2 = (f32[53,7,142]{2,1,0:T(8,128)S(1)}, f32[53,7,142]{2,1,0:T(8,128)S(1)}, u32[]{:S(2)}, u32[]{:S(2)}) collective-permute-start(f32[53,7,142]{2,1,0:T(8,128)S(1)} %get-tuple-element.267), channel_id=1, source_target_pairs={{0,8},{8,16},{16,24},{1,9},{9,17},{17,25},{2,10},{10,18},{18,26},{... | collective-permute-start | bytes 632192 | tf_op jit(solution)/shard_map/ppermute | solution.py:160
  18.8 0.7 fusion.6
  19.5 3.8 %collective-permute-done.3 = f32[53,7,142]{2,1,0:T(8,128)S(1)} collective-permute-done((f32[53,7,142]{2,1,0:T(8,128)S(1)}, f32[53,7,142]{2,1,0:T(8,128)S(1)}, u32[]{:S(2)}, u32[]{:S(2)}) %collective-permute-start.3) | collective-permute-done | bytes 210760 | tf_op jit(solution)/shard_map/ppermute | solution.py:160
  23.3 1.7 %collective-permute-done.2 = f32[53,7,142]{2,1,0:T(8,128)S(1)} collective-permute-done((f32[53,7,142]{2,1,0:T(8,128)S(1)}, f32[53,7,142]{2,1,0:T(8,128)S(1)}, u32[]{:S(2)}, u32[]{:S(2)}) %collective-permute-start.2) | collective-permute-done | bytes 210760 | tf_op jit(solution)/shard_map/ppermute | solution.py:160
  25.1 0.7 copy-done.6
  25.8 0.6 pad_maximum_fusion
  26.4 0.1 fusion.297
  26.6 1.1 %pad_maximum_fusion.1 = f32[16,30,284]{2,1,0:T(8,128)} fusion(f32[16,30,142]{2,1,0:T(8,128)S(1)} %get-tuple-element.243), kind=kLoop, calls=%fused_computation.7 | loop fusion | flops 136320 | bytes 817920 | tf_op jit(solution)/shard_map/concatenate | solution.py:220
  27.7 0.3 fusion.3
  28.0 0.7 slice_bitcast_fusion.4
  28.7 0.7 slice_bitcast_fusion.5
  29.4 19.5 %all-gather = f32[8,16,3]{1,2,0:T(4,128)S(1)} all-gather(f32[1,16,3]{1,2,0:T(4,128)S(1)} %maximum_bitcast_fusion.2), channel_id=1, replica_groups=mesh['gx'=4,'gy'=8] {'gy'}, dimensions={0}, use_global_device_ids=true | all-gather | bytes 1728 | tf_op jit(solution)/shard_map/all_gather | solution.py:192
  48.9 0.6 copy.42
  49.5 1.4 %reshape.116 = f32[128,3]{0,1:T(4,128)} reshape(f32[8,16,3]{1,0,2:T(8,128)} %copy.42) | data formatting | bytes 3072
  50.9 0.8 %slice_bitcast_fusion.8 = (f32[128]{0:T(128)S(1)}, f32[128]{0:T(128)S(1)}, f32[128]{0:T(128)S(1)}) fusion(f32[3,128]{1,0:T(4,128)} %bitcast.71), kind=kLoop, calls=%fused_computation.663 | loop fusion | bytes 3072 | tf_op jit(solution)/shard_map/broadcast_in_dim | solution.py:211
  51.7 0.8 %maximum_bitcast_fusion.1 = (f32[30,142]{1,0:T(8,128)S(1)}, s32[30,142]{1,0:T(8,128)S(1)}) fusion(f32[52,7,142]{2,1,0:T(8,128)S(1)} %slice.1108, f32[52,7,142]{2,1,0:T(8,128)} %copy-done, f32[52,16,7]{2,1,0:T(8,128)S(1)} %collective-permute-done.1, f32[52,16,128]{2,1,0:T(8,128)S(1)} %constant_dynamic-update-slice_fusion.5, ...), kind=kLoop, calls=%fused_computation.624 | loop fusion | flops 38340 | bytes 920160 | tf_op jit(solution)/shard_map/squeeze | solution.py:204
  52.5 2.2 %select_reduce_fusion = f32[30,142]{1,0:T(8,128)S(1)} fusion(f32[128,30]{0,1:T(8,128)S(1)} %pad_maximum_fusion.17, s32[30,142]{1,0:T(8,128)S(1)} %get-tuple-element.242), kind=kLoop, calls=%fused_computation | loop fusion | flops 1631580 | bytes 49440 | tf_op jit(solution)/shard_map/reduce_sum | solution.py:217
  55.0 0.8 %fusion.167 = (f32[16,30,284]{2,1,0:T(8,128)S(1)}, f32[16,30,284]{2,1,0:T(8,128)S(1)}, f32[16,30,284]{2,1,0:T(8,128)S(1)}, f32[16,30,284]{2,1,0:T(8,128)S(1)}, f...) fusion(f32[16,30,142]{2,1,0:T(8,128)S(1)} %get-tuple-element.244, f32[16,30,142]{2,1,0:T(8,128)S(1)} %get-tuple-element.245, ...), kind=kLoop, calls=%fused_computation.665 | loop fusion | flops 2044800 | bytes 4500832 | tf_op jit(solution)/shard_map/add | solution.py:133
  55.8 0.4 add_add_fusion.3
  56.3 0.3 fusion.126
  56.6 0.2 constant_dynamic-update-slice_fusion.30
  57.0 0.9 %add_add_fusion.2 = f32[16,30,284]{2,1,0:T(8,128)S(1)} fusion(f32[16,30,284]{2,1,0:T(8,128)S(1)} %broadcast_multiply_fusion.1, f32[16,30,284]{2,1,0:T(8,128)S(1)} %get-tuple-element.240, f32[16,30,284]{2,1,0:T(8,128)S(1)} %get-tuple-element.239, f32[16,30,284]{2,1,0:T(8,128)S(1)} %get-tuple-element.238, f32[16,30,284]{2,1,0:T(8,128)S(1)} %get-tuple-element.237, ...), kind=kLoop, calls=%fused_computation.23 | loop fusion | flops 2044800 | bytes 3819232 | tf_op jit(solution)/shard_map/add | solution.py:133
  57.9 0.2 fusion.108
  58.1 0.2 constant_dynamic-update-slice_fusion.46
  58.5 0.2 add_multiply_fusion.5
  58.7 0.9 %add_add_fusion.1 = f32[16,30,284]{2,1,0:T(8,128)S(1)} fusion(f32[16,30,284]{2,1,0:T(8,128)S(1)} %add_multiply_fusion.5, f32[16,30,284]{2,1,0:T(8,128)S(1)} %get-tuple-element.240, f32[16,30,284]{2,1,0:T(8,128)S(1)} %get-tuple-element.239, f32[16,30,284]{2,1,0:T(8,128)S(1)} %get-tuple-element.238, f32[16,30,284]{2,1,0:T(8,128)S(1)} %get-tuple-element.237, ...), kind=kLoop, calls=%fused_computation.21 | loop fusion | flops 2044800 | bytes 3819232 | tf_op jit(solution)/shard_map/add | solution.py:133
  59.6 0.2 fusion.93
  59.8 0.2 constant_dynamic-update-slice_fusion.62
  60.2 0.2 add_multiply_fusion.4
  60.4 0.9 %add_add_fusion = f32[16,30,284]{2,1,0:T(8,128)S(1)} fusion(f32[16,30,284]{2,1,0:T(8,128)S(1)} %add_multiply_fusion.4, f32[16,30,284]{2,1,0:T(8,128)S(1)} %get-tuple-element.240, f32[16,30,284]{2,1,0:T(8,128)S(1)} %get-tuple-element.239, f32[16,30,284]{2,1,0:T(8,128)S(1)} %get-tuple-element.238, f32[16,30,284]{2,1,0:T(8,128)S(1)} %get-tuple-element.237, ...), kind=kLoop, calls=%fused_computation.19 | loop fusion | flops 2044800 | bytes 3819232 | tf_op jit(solution)/shard_map/add | solution.py:133
  61.3 0.2 fusion.78
  61.5 0.2 constant_dynamic-update-slice_fusion.78
  61.9 0.2 add_multiply_fusion.3
  62.0 0.7 copy-done.1
  62.8 0.2 fusion.60
  63.0 0.2 constant_dynamic-update-slice_fusion.94
  63.5 0.8 multiply_add_fusion.2
  64.2 0.2 fusion.44
  64.4 0.2 constant_dynamic-update-slice_fusion.110
  64.8 0.2 add_multiply_fusion.2
  65.0 0.8 %multiply_add_fusion.1 = f32[16,30,284]{2,1,0:T(8,128)S(1)} fusion(f32[16,30,284]{2,1,0:T(8,128)S(1)} %add_multiply_fusion.2, f32[16,30,284]{2,1,0:T(8,128)S(1)} %get-tuple-element.240, f32[16,30,284]{2,1,0:T(8,128)S(1)} %get-tuple-element.239, f32[16,30,284]{2,1,0:T(8,128)S(1)} %get-tuple-element.238, f32[16,30,284]{2,1,0:T(8,128)S(1)} %get-tuple-element.237, ...), kind=kLoop, calls=%fused_computation.15 | loop fusion | flops 1772160 | bytes 3273952 | tf_op jit(solution)/shard_map/add | solution.py:130
  65.8 0.2 fusion.28
  66.0 0.2 constant_dynamic-update-slice_fusion.126
  66.4 0.2 add_multiply_fusion.1
  66.6 0.8 %multiply_add_fusion = f32[16,30,284]{2,1,0:T(8,128)S(1)} fusion(f32[16,30,284]{2,1,0:T(8,128)S(1)} %add_multiply_fusion.1, f32[16,30,284]{2,1,0:T(8,128)S(1)} %get-tuple-element.240, f32[16,30,284]{2,1,0:T(8,128)S(1)} %get-tuple-element.239, f32[16,30,284]{2,1,0:T(8,128)S(1)} %get-tuple-element.238, f32[16,30,284]{2,1,0:T(8,128)S(1)} %get-tuple-element.237, ...), kind=kLoop, calls=%fused_computation.13 | loop fusion | flops 1772160 | bytes 3273952 | tf_op jit(solution)/shard_map/add | solution.py:130
  67.4 0.2 fusion.12
  67.6 0.2 constant_dynamic-update-slice_fusion.142
  68.0 0.1 add_multiply_fusion
  68.1 0.2 slice_bitcast_fusion.1
  68.4 0.7 pad_maximum_fusion.6
  69.1 0.7 pad_maximum_fusion.7
  70.0 0.5 fusion
  70.5 7.9 %all_gather.7 = f32[8,8,16]{2,1,0:T(8,128)S(1)} all-gather(f32[1,8,16]{2,1,0:T(8,128)S(1)} %add.4639), channel_id=1, replica_groups=mesh['gx'=4,'gy'=8] {'gy'}, dimensions={0}, use_global_device_ids=true | all-gather | bytes 4608 | tf_op jit(solution)/shard_map/all_gather | solution.py:267
  78.4 0.5 dynamic-slice_reduce_fusion
  (181 shorter events, 2.0 us)
Async XLA Ops:
  0.6 9.3 %copy-start.3 = (f32[2,16,16,128]{3,2,1,0:T(8,128)S(1)}, f32[2,16,16,128]{3,2,1,0:T(8,128)}, u32[]{:S(2)}) copy-start(f32[2,16,16,128]{3,2,1,0:T(8,128)} %param.8) | copy-start | bytes 786436
  0.6 9.3 %copy-start.4 = (f32[16,16,128]{2,1,0:T(8,128)S(1)}, f32[16,16,128]{2,1,0:T(8,128)}, u32[]{:S(2)}) copy-start(f32[16,16,128]{2,1,0:T(8,128)} %param.9) | copy-start | bytes 393220
  0.7 9.3 %copy-start.10 = (f32[2,16,128]{2,1,0:T(8,128)S(1)}, f32[2,16,128]{2,1,0:T(8,128)}, u32[]{:S(2)}) copy-start(f32[2,16,128]{2,1,0:T(8,128)} %param.10) | copy-start | bytes 49156
  0.7 9.4 %copy-start.13 = (s32[16,128]{1,0:T(8,128)S(1)}, s32[16,128]{1,0:T(8,128)}, u32[]{:S(2)}) copy-start(s32[16,128]{1,0:T(8,128)} %param.12) | copy-start | bytes 24580
  0.7 9.4 %copy-start.14 = (s32[16,128]{1,0:T(8,128)S(1)}, s32[16,128]{1,0:T(8,128)}, u32[]{:S(2)}) copy-start(s32[16,128]{1,0:T(8,128)} %param.13) | copy-start | bytes 24580
  0.7 9.4 %copy-start.15 = (f32[1,16]{1,0:T(1,128)S(1)}, f32[1,16]{1,0:T(1,128)}, u32[]{:S(2)}) copy-start(f32[1,16]{1,0:T(1,128)} %param.11) | copy-start | bytes 196
  5.6 4.5 %collective-permute-start.1 = (f32[52,16,7]{2,1,0:T(8,128)S(1)}, f32[52,16,7]{2,1,0:T(8,128)S(1)}, u32[]{:S(2)}, u32[]{:S(2)}) collective-permute-start(f32[52,16,7]{2,1,0:T(8,128)S(1)} %get-tuple-element.270), channel_id=1, source_target_pairs={{1,0},{2,1},{3,2},{4,3},{5,4},{6,5},{7,6},{9,8},{10,9},{11,10},{12... | collective-permute-start | bytes 69896 | tf_op jit(solution)/shard_map/ppermute | solution.py:160
  6.9 4.4 %collective-permute-start = (f32[52,16,7]{2,1,0:T(8,128)S(1)}, f32[52,16,7]{2,1,0:T(8,128)S(1)}, u32[]{:S(2)}, u32[]{:S(2)}) collective-permute-start(f32[52,16,7]{2,1,0:T(8,128)S(1)} %get-tuple-element.269), channel_id=1, source_target_pairs={{0,1},{1,2},{2,3},{3,4},{4,5},{5,6},{6,7},{8,9},{9,10},{10,11},{11... | collective-permute-start | bytes 69896 | tf_op jit(solution)/shard_map/ppermute | solution.py:160
  11.9 11.4 %collective-permute-start.3 = (f32[53,7,142]{2,1,0:T(8,128)S(1)}, f32[53,7,142]{2,1,0:T(8,128)S(1)}, u32[]{:S(2)}, u32[]{:S(2)}) collective-permute-start(f32[53,7,142]{2,1,0:T(8,128)S(1)} %get-tuple-element.268), channel_id=1, source_target_pairs={{8,0},{16,8},{24,16},{9,1},{17,9},{25,17},{10,2},{18,10},{26,18},{... | collective-permute-start | bytes 632192 | tf_op jit(solution)/shard_map/ppermute | solution.py:160
  13.2 11.9 %collective-permute-start.2 = (f32[53,7,142]{2,1,0:T(8,128)S(1)}, f32[53,7,142]{2,1,0:T(8,128)S(1)}, u32[]{:S(2)}, u32[]{:S(2)}) collective-permute-start(f32[53,7,142]{2,1,0:T(8,128)S(1)} %get-tuple-element.267), channel_id=1, source_target_pairs={{0,8},{8,16},{16,24},{1,9},{9,17},{17,25},{2,10},{10,18},{18,26},{... | collective-permute-start | bytes 632192 | tf_op jit(solution)/shard_map/ppermute | solution.py:160
  23.3 1.8 %copy-start.5 = (f32[53,7,142]{2,1,0:T(8,128)}, f32[53,7,142]{2,1,0:T(8,128)S(1)}, u32[]{:S(2)}) copy-start(f32[53,7,142]{2,1,0:T(8,128)S(1)} %collective-permute-done.3) | copy-start | bytes 632188
  25.1 0.8 copy-start.6
  25.8 0.8 copy-start
  26.5 2.9 %copy-start.16 = (f32[1,16]{1,0:T(1,128)S(1)}, f32[1,16]{1,0:T(1,128)}, u32[]{:S(2)}) copy-start(f32[1,16]{1,0:T(1,128)} %param.11) | copy-start | bytes 196
  27.7 27.2 %copy-start.11 = (f32[284]{0:T(512)S(1)}, f32[284]{0:T(512)}, u32[]{:S(2)}) copy-start(f32[284]{0:T(512)} %constant.51.clone.1) | copy-start | bytes 3412
  27.7 27.2 %copy-start.12 = (f32[284]{0:T(512)S(1)}, f32[284]{0:T(512)}, u32[]{:S(2)}) copy-start(f32[284]{0:T(512)} %constant.49.clone.1) | copy-start | bytes 3412
  50.9 4.0 %copy-start.2 = (f32[16,30,284]{2,1,0:T(8,128)S(1)}, f32[16,30,284]{2,1,0:T(8,128)}, u32[]{:S(2)}) copy-start(f32[16,30,284]{2,1,0:T(8,128)} %pad_maximum_fusion.1) | copy-start | bytes 1635844
  50.9 4.1 %copy-start.7 = (f32[30,284]{1,0:T(8,128)S(1)}, f32[30,284]{1,0:T(8,128)}, u32[]{:S(2)}) copy-start(f32[30,284]{1,0:T(8,128)} %get-tuple-element.257) | copy-start | bytes 102244
  50.9 4.1 %copy-start.8 = (f32[30,284]{1,0:T(8,128)S(1)}, f32[30,284]{1,0:T(8,128)}, u32[]{:S(2)}) copy-start(f32[30,284]{1,0:T(8,128)} %get-tuple-element.258) | copy-start | bytes 102244
  50.9 4.1 %copy-start.9 = (f32[30,284]{1,0:T(8,128)S(1)}, f32[30,284]{1,0:T(8,128)}, u32[]{:S(2)}) copy-start(f32[30,284]{1,0:T(8,128)} %get-tuple-element.259) | copy-start | bytes 102244
  61.8 1.0 %copy-start.1 = (f32[52,7,142]{2,1,0:T(8,128)S(1)}, f32[52,7,142]{2,1,0:T(8,128)}, u32[]{:S(2)}) copy-start(f32[52,7,142]{2,1,0:T(8,128)} %copy-done) | copy-start | bytes 620260

commit v17 on v14

--- a/solution.py
+++ b/solution.py
@@ -194,7 +194,7 @@
     strips_near = jnp.stack(
         [from_above[plane_count, 0, :tiles_here], beta_tiles[0], from_below[plane_count, 0, :tiles_here]]
     )
-    friction_rows = lax.all_gather(strips_near, "gy", axis=1, tiled=True)
+    friction_rows = lax.all_gather(strips_near, "gy").transpose(1, 0, 2).reshape(strips_near.shape[0], -1)
     tile_count = friction_rows.shape[1]
 
     packed = jnp.concatenate([from_left, stack_rows(0, cols), from_right], axis=2)

time: 62 us -> 62.1 us (level)
    unnamed x86 -> x85, local copies, waits for them, and re-layouts: 4.03 us -> 3.95 us
where the time goes in v17:
time: 62.1 us; the launch traced here: 61.7 us
  other arithmetic  18.8 us (30%)
  blocking collectives  18.3 us (29%)
  starting transfers between devices  11.2 us (18%)
  local copies, waits for them, and re-layouts  10.8 us (17%)
  between operations  2.09 us (3%)
    ppermute x4, starting transfers between devices, shifted(): return lax.ppermute(piece, axis, pairs)  11.2 us
    all_gather x1, blocking collectives, local(): lax.all_gather(strips_near, 'gy').transpose(1, 0, 2)  9.2 us
    all_gather x1, blocking collectives, local(): gathered = lax.all_gather(partial_sum.reshape(owners, chunk), 'gy')  9.05 us
    unnamed x85, local copies, waits for them, and re-layouts  3.95 us
    add x4, other arithmetic, relax_lanes(): right_side = rhs_field + lateral  3.52 us
    unnamed x70, other arithmetic  3.46 us
    add x3, other arithmetic, relax_lanes(): lateral + along_y * (south_face * vel_pad[:, 1:-1, :-2] + north_face * ve...  2.35 us
    reduce_sum x1, other arithmetic, local(): jnp.sum(jnp.where(owner_match, row_strip[:, :, None], 0.0), axis=0)  2.23 us
  transfers between devices with their start and end apart: 4, of which 1 were waited for; matrix products, arithmetic and copies ran while one was open for 9% of the time, Pallas kernels for 0%

profile of v17, /device:TPU:0, one launch (start us, length us, event | category | flops | bytes accessed | tf_op | source)
XLA Modules:
  0.0 61.7 jit_solution(8327870659853190544)
XLA Ops:
  0.7 1.0 %constant_dynamic-update-slice_fusion.5 = (f32[53,7,128]{2,1,0:T(8,128)S(1)}, f32[53,7,128]{2,1,0:T(8,128)S(1)}) fusion(f32[32,16,128]{2,1,0:T(8,128)} %bitcast.54), kind=kLoop, calls=%fused_computation.47 | loop fusion | bytes 491520
  1.7 0.9 %constant_dynamic-update-slice_fusion.4 = (f32[53,7,128]{2,1,0:T(8,128)S(1)}, f32[53,7,128]{2,1,0:T(8,128)S(1)}) fusion(f32[53,7,128]{2,1,0:T(8,128)S(1)} %get-tuple-element.255, f32[16,16,128]{2,1,0:T(8,128)} %param.9, f32[53,7,128]{2,1,0:T(8,128)S(1)} %get-tuple-element.256), kind=kLoop, calls=%fused_computation.46 | loop fusion | bytes 245760
  2.6 0.7 %constant_dynamic-update-slice_fusion.3 = (f32[53,7,128]{2,1,0:T(8,128)S(1)}, f32[53,7,128]{2,1,0:T(8,128)S(1)}) fusion(f32[53,7,128]{2,1,0:T(8,128)S(1)} %get-tuple-element.263, f32[2,16,128]{2,1,0:T(8,128)} %param.10, f32[53,7,128]{2,1,0:T(8,128)S(1)} %get-tuple-element.264), kind=kLoop, calls=%fused_computation.45 | loop fusion | bytes 30720
  3.3 0.7 %constant_dynamic-update-slice_fusion.2 = (f32[53,7,128]{2,1,0:T(8,128)S(1)}, f32[53,7,128]{2,1,0:T(8,128)S(1)}) fusion(f32[53,7,128]{2,1,0:T(8,128)S(1)} %get-tuple-element.274, s32[1,16,128]{2,1,0:T(8,128)} %bitcast.57, f32[53,7,128]{2,1,0:T(8,128)S(1)} %get-tuple-element.275), kind=kLoop, calls=%fused_computation.44 | loop fusion | flops 1792 | bytes 15360
  4.1 0.7 %constant_dynamic-update-slice_fusion.1 = (f32[53,7,128]{2,1,0:T(8,128)S(1)}, f32[53,7,128]{2,1,0:T(8,128)S(1)}) fusion(f32[53,7,128]{2,1,0:T(8,128)S(1)} %get-tuple-element.284, s32[1,16,128]{2,1,0:T(8,128)} %bitcast.59, f32[53,7,128]{2,1,0:T(8,128)S(1)} %get-tuple-element.285), kind=kLoop, calls=%fused_computation.43 | loop fusion | flops 1792 | bytes 15360
  4.8 0.7 %constant_dynamic-update-slice_fusion = (f32[53,7,128]{2,1,0:T(8,128)S(1)}, f32[53,7,128]{2,1,0:T(8,128)S(1)}) fusion(f32[53,7,128]{2,1,0:T(8,128)S(1)} %get-tuple-element.282, f32[1,16]{1,0:T(1,128)} %param.11, f32[53,7,128]{2,1,0:T(8,128)S(1)} %get-tuple-element.283), kind=kLoop, calls=%fused_computation.42 | loop fusion | bytes 8256 | tf_op jit(solution)/shard_map/concatenate | solution.py:179
  5.4 1.3 %collective-permute-start.1 = (f32[53,7,128]{2,1,0:T(8,128)S(1)}, f32[53,7,128]{2,1,0:T(8,128)S(1)}, u32[]{:S(2)}, u32[]{:S(2)}) collective-permute-start(f32[53,7,128]{2,1,0:T(8,128)S(1)} %get-tuple-element.287), channel_id=1, source_target_pairs={{8,0},{16,8},{24,16},{9,1},{17,9},{25,17},{10,2},{18,10},{26,18},{... | collective-permute-start | bytes 569864 | tf_op jit(solution)/shard_map/ppermute | solution.py:160
  6.7 5.6 %collective-permute-start = (f32[53,7,128]{2,1,0:T(8,128)S(1)}, f32[53,7,128]{2,1,0:T(8,128)S(1)}, u32[]{:S(2)}, u32[]{:S(2)}) collective-permute-start(f32[53,7,128]{2,1,0:T(8,128)S(1)} %get-tuple-element.286), channel_id=1, source_target_pairs={{0,8},{8,16},{16,24},{1,9},{9,17},{17,25},{2,10},{10,18},{18,26},{... | collective-permute-start | bytes 569864 | tf_op jit(solution)/shard_map/ppermute | solution.py:160
  12.3 1.2 %fusion.298 = (f32[32,16,7]{2,1,0:T(8,128)S(1)}, f32[32,16,7]{2,1,0:T(8,128)S(1)}) fusion(f32[32,16,128]{2,1,0:T(8,128)} %bitcast.55), kind=kLoop, calls=%fused_computation.671 | loop fusion | bytes 57344 | tf_op jit(solution)/shard_map/slice | solution.py:170
  13.8 0.2 copy.56
  14.0 0.2 copy.65
  14.2 0.2 copy.66
  14.4 0.2 copy.57
  14.7 0.2 copy.58
  14.9 0.2 copy.49
  15.1 0.2 copy.63
  15.3 0.2 copy.64
  15.5 0.2 copy.50
  15.8 0.2 copy.51
  16.7 0.2 collective-permute-done
  17.2 1.3 %collective-permute-start.3 = (f32[52,30,7]{0,1,2:T(8,128)S(1)}, f32[52,30,7]{0,1,2:T(8,128)S(1)}, u32[]{:S(2)}, u32[]{:S(2)}) collective-permute-start(f32[52,30,7]{0,1,2:T(8,128)S(1)} %pad_maximum_fusion.6), channel_id=1, source_target_pairs={{1,0},{2,1},{3,2},{4,3},{5,4},{6,5},{7,6},{9,8},{10,9},{11,10},{12... | collective-permute-start | bytes 131048 | tf_op jit(solution)/shard_map/ppermute | solution.py:160
  18.6 0.2 copy.52
  18.8 3.0 %collective-permute-start.2 = (f32[52,30,7]{0,1,2:T(8,128)S(1)}, f32[52,30,7]{0,1,2:T(8,128)S(1)}, u32[]{:S(2)}, u32[]{:S(2)}) collective-permute-start(f32[52,30,7]{0,1,2:T(8,128)S(1)} %pad_maximum_fusion.5), channel_id=1, source_target_pairs={{0,1},{1,2},{2,3},{3,4},{4,5},{5,6},{6,7},{8,9},{9,10},{10,11},{11... | collective-permute-start | bytes 131048 | tf_op jit(solution)/shard_map/ppermute | solution.py:160
  21.9 9.2 %all-gather.1 = f32[8,3,16]{2,1,0:T(4,128)S(1)} all-gather(f32[1,3,16]{2,1,0:T(4,128)S(1)} %maximum_bitcast_fusion.2), channel_id=2, replica_groups=mesh['gx'=4,'gy'=8] {'gy'}, dimensions={0}, use_global_device_ids=true | all-gather | bytes 1728 | tf_op jit(solution)/shard_map/all_gather | solution.py:197
  31.5 0.8 %copy.62 = f32[52,30,7]{2,1,0:T(8,128)S(1)} copy(f32[52,30,7]{0,1,2:T(8,128)S(1)} %collective-permute-done.3) | data formatting | bytes 87360 | tf_op jit(solution)/shard_map/ppermute | solution.py:160
  32.4 0.9 %copy.61 = f32[52,30,7]{2,1,0:T(8,128)S(1)} copy(f32[52,30,7]{0,1,2:T(8,128)S(1)} %collective-permute-done.2) | data formatting | bytes 87360 | tf_op jit(solution)/shard_map/ppermute | solution.py:160
  33.2 1.0 %pad_maximum_fusion = f32[52,30,142]{2,1,0:T(8,128)S(1)} fusion(f32[52,30,7]{2,1,0:T(8,128)S(1)} %copy.62, f32[52,7,128]{2,1,0:T(8,128)S(1)} %slice.1162, f32[52,16,128]{2,1,0:T(8,128)S(1)} %constant_dynamic-update-slice_fusion.12, f32[52,7,128]{2,1,0:T(8,128)S(1)} %slice.1161, f32[52,30,7]{2,1,0:T(8,128)S(1)} %copy.61), kind=kLoop, calls=%fused_computation.2 | loop fusion | flops 886080 | bytes 1772160 | tf_op jit(solution)/shard_map/concatenate | solution.py:200
  34.3 0.2 pad_maximum_fusion.1
  34.5 0.3 fusion.3
  35.0 2.2 %select_reduce_fusion = f32[30,142]{1,0:T(8,128)S(1)} fusion(f32[128,30]{0,1:T(8,128)S(1)} %pad_maximum_fusion.16, s32[30,142]{1,0:T(8,128)S(1)} %get-tuple-element.245), kind=kLoop, calls=%fused_computation | loop fusion | flops 1631580 | bytes 49440 | tf_op jit(solution)/shard_map/reduce_sum | solution.py:222
  37.4 0.8 %fusion.167 = (f32[16,30,284]{2,1,0:T(8,128)S(1)}, f32[16,30,284]{2,1,0:T(8,128)S(1)}, f32[16,30,284]{2,1,0:T(8,128)S(1)}, f32[16,30,284]{2,1,0:T(8,128)S(1)}, f...) fusion(f32[16,30,142]{2,1,0:T(8,128)S(1)} %get-tuple-element.247, f32[16,30,142]{2,1,0:T(8,128)S(1)} %get-tuple-element.248, ...), kind=kLoop, calls=%fused_computation.669 | loop fusion | flops 2044800 | bytes 4500832 | tf_op jit(solution)/shard_map/add | solution.py:133
  38.2 0.4 add_add_fusion.3
  38.7 0.3 fusion.126
  39.4 0.9 %add_add_fusion.2 = f32[16,30,284]{2,1,0:T(8,128)S(1)} fusion(f32[16,30,284]{2,1,0:T(8,128)S(1)} %broadcast_multiply_fusion.1, f32[16,30,284]{2,1,0:T(8,128)S(1)} %get-tuple-element.243, f32[16,30,284]{2,1,0:T(8,128)S(1)} %get-tuple-element.242, f32[16,30,284]{2,1,0:T(8,128)S(1)} %get-tuple-element.241, f32[16,30,284]{2,1,0:T(8,128)S(1)} %get-tuple-element.240, ...), kind=kLoop, calls=%fused_computation.22 | loop fusion | flops 2044800 | bytes 3819232 | tf_op jit(solution)/shard_map/add | solution.py:133
  40.3 0.2 fusion.108
  40.9 0.2 add_multiply_fusion.5
  41.1 0.9 %add_add_fusion.1 = f32[16,30,284]{2,1,0:T(8,128)S(1)} fusion(f32[16,30,284]{2,1,0:T(8,128)S(1)} %add_multiply_fusion.5, f32[16,30,284]{2,1,0:T(8,128)S(1)} %get-tuple-element.243, f32[16,30,284]{2,1,0:T(8,128)S(1)} %get-tuple-element.242, f32[16,30,284]{2,1,0:T(8,128)S(1)} %get-tuple-element.241, f32[16,30,284]{2,1,0:T(8,128)S(1)} %get-tuple-element.240, ...), kind=kLoop, calls=%fused_computation.20 | loop fusion | flops 2044800 | bytes 3819232 | tf_op jit(solution)/shard_map/add | solution.py:133
  42.0 0.2 fusion.93
  42.2 0.2 constant_dynamic-update-slice_fusion.64
  42.6 0.2 add_multiply_fusion.4
  42.7 0.9 %add_add_fusion = f32[16,30,284]{2,1,0:T(8,128)S(1)} fusion(f32[16,30,284]{2,1,0:T(8,128)S(1)} %add_multiply_fusion.4, f32[16,30,284]{2,1,0:T(8,128)S(1)} %get-tuple-element.243, f32[16,30,284]{2,1,0:T(8,128)S(1)} %get-tuple-element.242, f32[16,30,284]{2,1,0:T(8,128)S(1)} %get-tuple-element.241, f32[16,30,284]{2,1,0:T(8,128)S(1)} %get-tuple-element.240, ...), kind=kLoop, calls=%fused_computation.18 | loop fusion | flops 2044800 | bytes 3819232 | tf_op jit(solution)/shard_map/add | solution.py:133
  43.6 0.2 fusion.78
  43.8 0.2 constant_dynamic-update-slice_fusion.80
  44.2 0.2 add_multiply_fusion.3
  44.4 0.2 fusion.60
  44.6 0.2 constant_dynamic-update-slice_fusion.96
  45.1 0.8 %multiply_add_fusion.2 = f32[16,30,284]{2,1,0:T(8,128)S(1)} fusion(f32[16,30,284]{2,1,0:T(8,128)S(1)} %broadcast_multiply_fusion, f32[16,30,284]{2,1,0:T(8,128)S(1)} %get-tuple-element.243, f32[16,30,284]{2,1,0:T(8,128)S(1)} %get-tuple-element.242, f32[16,30,284]{2,1,0:T(8,128)S(1)} %get-tuple-element.241, f32[16,30,284]{2,1,0:T(8,128)S(1)} %get-tuple-element.240, ...), kind=kLoop, calls=%fused_computation.16 | loop fusion | flops 1772160 | bytes 3273952 | tf_op jit(solution)/shard_map/add | solution.py:130
  45.9 0.2 fusion.44
  46.0 0.2 constant_dynamic-update-slice_fusion.112
  46.5 0.2 add_multiply_fusion.2
  46.6 0.8 %multiply_add_fusion.1 = f32[16,30,284]{2,1,0:T(8,128)S(1)} fusion(f32[16,30,284]{2,1,0:T(8,128)S(1)} %add_multiply_fusion.2, f32[16,30,284]{2,1,0:T(8,128)S(1)} %get-tuple-element.243, f32[16,30,284]{2,1,0:T(8,128)S(1)} %get-tuple-element.242, f32[16,30,284]{2,1,0:T(8,128)S(1)} %get-tuple-element.241, f32[16,30,284]{2,1,0:T(8,128)S(1)} %get-tuple-element.240, ...), kind=kLoop, calls=%fused_computation.14 | loop fusion | flops 1772160 | bytes 3273952 | tf_op jit(solution)/shard_map/add | solution.py:130
  47.4 0.2 fusion.28
  47.6 0.2 constant_dynamic-update-slice_fusion.128
  48.0 0.2 add_multiply_fusion.1
  48.2 0.8 %multiply_add_fusion = f32[16,30,284]{2,1,0:T(8,128)S(1)} fusion(f32[16,30,284]{2,1,0:T(8,128)S(1)} %add_multiply_fusion.1, f32[16,30,284]{2,1,0:T(8,128)S(1)} %get-tuple-element.243, f32[16,30,284]{2,1,0:T(8,128)S(1)} %get-tuple-element.242, f32[16,30,284]{2,1,0:T(8,128)S(1)} %get-tuple-element.241, f32[16,30,284]{2,1,0:T(8,128)S(1)} %get-tuple-element.240, ...), kind=kLoop, calls=%fused_computation.12 | loop fusion | flops 1772160 | bytes 3273952 | tf_op jit(solution)/shard_map/add | solution.py:130
  49.0 0.2 fusion.12
  49.2 0.2 constant_dynamic-update-slice_fusion.144
  49.6 0.2 add_multiply_fusion
  49.7 0.2 slice_bitcast_fusion.1
  50.0 0.7 %pad_maximum_fusion.3 = f32[2,16,16,128]{3,2,1,0:T(8,128)} fusion(f32[1,16,16,128]{3,2,1,0:T(8,128)S(1)} %get-tuple-element.288, f32[1,16,16,128]{3,2,1,0:T(8,128)S(1)} %get-tuple-element.289), kind=kLoop, calls=%fused_computation.37 | loop fusion | flops 65536 | bytes 524288 | tf_op jit(solution)/shard_map/stack | solution.py:252
  50.7 0.7 %pad_maximum_fusion.4 = f32[2,16,16,128]{3,2,1,0:T(8,128)} fusion(f32[1,16,16,128]{3,2,1,0:T(8,128)S(1)} %get-tuple-element.250, f32[1,16,16,128]{3,2,1,0:T(8,128)S(1)} %get-tuple-element.249), kind=kLoop, calls=%fused_computation.40 | loop fusion | flops 65536 | bytes 524288 | tf_op jit(solution)/shard_map/stack | solution.py:252
  51.6 0.5 fusion
  52.1 9.1 %all_gather.11 = f32[8,8,16]{2,1,0:T(8,128)S(1)} all-gather(f32[1,8,16]{2,1,0:T(8,128)S(1)} %add.4639), channel_id=1, replica_groups=mesh['gx'=4,'gy'=8] {'gy'}, dimensions={0}, use_global_device_ids=true | all-gather | bytes 4608 | tf_op jit(solution)/shard_map/all_gather | solution.py:272
  61.2 0.5 dynamic-slice_reduce_fusion
  (188 shorter events, 4.0 us)
Async XLA Ops:
  0.6 13.2 %copy-start = (f32[2,16,16,128]{3,2,1,0:T(8,128)S(1)}, f32[2,16,16,128]{3,2,1,0:T(8,128)}, u32[]{:S(2)}) copy-start(f32[2,16,16,128]{3,2,1,0:T(8,128)} %param.8) | copy-start | bytes 786436
  0.6 12.8 %copy-start.1 = (f32[16,16,128]{2,1,0:T(8,128)S(1)}, f32[16,16,128]{2,1,0:T(8,128)}, u32[]{:S(2)}) copy-start(f32[16,16,128]{2,1,0:T(8,128)} %param.9) | copy-start | bytes 393220
  0.7 12.9 %copy-start.2 = (f32[2,16,128]{2,1,0:T(8,128)S(1)}, f32[2,16,128]{2,1,0:T(8,128)}, u32[]{:S(2)}) copy-start(f32[2,16,128]{2,1,0:T(8,128)} %param.10) | copy-start | bytes 49156
  0.7 13.0 %copy-start.5 = (s32[16,128]{1,0:T(8,128)S(1)}, s32[16,128]{1,0:T(8,128)}, u32[]{:S(2)}) copy-start(s32[16,128]{1,0:T(8,128)} %param.12) | copy-start | bytes 24580
  0.7 13.0 %copy-start.6 = (s32[16,128]{1,0:T(8,128)S(1)}, s32[16,128]{1,0:T(8,128)}, u32[]{:S(2)}) copy-start(s32[16,128]{1,0:T(8,128)} %param.13) | copy-start | bytes 24580
  5.4 11.0 %collective-permute-start.1 = (f32[53,7,128]{2,1,0:T(8,128)S(1)}, f32[53,7,128]{2,1,0:T(8,128)S(1)}, u32[]{:S(2)}, u32[]{:S(2)}) collective-permute-start(f32[53,7,128]{2,1,0:T(8,128)S(1)} %get-tuple-element.287), channel_id=1, source_target_pairs={{8,0},{16,8},{24,16},{9,1},{17,9},{25,17},{10,2},{18,10},{26,18},{... | collective-permute-start | bytes 569864 | tf_op jit(solution)/shard_map/ppermute | solution.py:160
  6.7 10.1 %collective-permute-start = (f32[53,7,128]{2,1,0:T(8,128)S(1)}, f32[53,7,128]{2,1,0:T(8,128)S(1)}, u32[]{:S(2)}, u32[]{:S(2)}) collective-permute-start(f32[53,7,128]{2,1,0:T(8,128)S(1)} %get-tuple-element.286), channel_id=1, source_target_pairs={{0,8},{8,16},{16,24},{1,9},{9,17},{17,25},{2,10},{10,18},{18,26},{... | collective-permute-start | bytes 569864 | tf_op jit(solution)/shard_map/ppermute | solution.py:160
  16.2 5.7 %copy-start.7 = (f32[1,16]{1,0:T(1,128)S(1)}, f32[1,16]{1,0:T(1,128)}, u32[]{:S(2)}) copy-start(f32[1,16]{1,0:T(1,128)} %param.11) | copy-start | bytes 196
  17.2 14.3 %collective-permute-start.3 = (f32[52,30,7]{0,1,2:T(8,128)S(1)}, f32[52,30,7]{0,1,2:T(8,128)S(1)}, u32[]{:S(2)}, u32[]{:S(2)}) collective-permute-start(f32[52,30,7]{0,1,2:T(8,128)S(1)} %pad_maximum_fusion.6), channel_id=1, source_target_pairs={{1,0},{2,1},{3,2},{4,3},{5,4},{6,5},{7,6},{9,8},{10,9},{11,10},{12... | collective-permute-start | bytes 131048 | tf_op jit(solution)/shard_map/ppermute | solution.py:160
  18.8 13.5 %collective-permute-start.2 = (f32[52,30,7]{0,1,2:T(8,128)S(1)}, f32[52,30,7]{0,1,2:T(8,128)S(1)}, u32[]{:S(2)}, u32[]{:S(2)}) collective-permute-start(f32[52,30,7]{0,1,2:T(8,128)S(1)} %pad_maximum_fusion.5), channel_id=1, source_target_pairs={{0,1},{1,2},{2,3},{3,4},{4,5},{5,6},{6,7},{8,9},{9,10},{10,11},{11... | collective-permute-start | bytes 131048 | tf_op jit(solution)/shard_map/ppermute | solution.py:160
  34.9 2.5 %copy-start.3 = (f32[284]{0:T(512)S(1)}, f32[284]{0:T(512)}, u32[]{:S(2)}) copy-start(f32[284]{0:T(512)} %constant.51.clone.1) | copy-start | bytes 3412
  34.9 2.5 %copy-start.4 = (f32[284]{0:T(512)S(1)}, f32[284]{0:T(512)}, u32[]{:S(2)}) copy-start(f32[284]{0:T(512)} %constant.49.clone.1) | copy-start | bytes 3412
